TPU v7x, 32 devices: a whole 2x2x4 slice. The times are simulated.
32 devices in a mesh: row: 8 (over z, x), col: 4 (over y, core).
Axes of the slice: x: 2, y: 2, z: 4, core: 2. Of those that a mesh axis runs over, the one named last changes fastest.
Arguments:
- fine_blocks: bfloat16 [32, 16, 64, 576], P('row', 'col'), may hold values from -0.25 to 0.25
- fine_columns: int32 [32, 16, 9], P('row', 'col'), may hold values from 0 to 511, as said below
- fine_counts: int32 [32, 16], P('row', 'col'), may hold values from 1 to 9, as said below
- prolong_blocks: bfloat16 [32, 16, 64, 256], P('row', 'col'), may hold values from -1.1953125 to 1.1953125
- prolong_columns: int32 [32, 16, 4], P('row', 'col'), may hold values from 0 to 31, as said below
- prolong_counts: int32 [32, 16], P('row', 'col'), may hold values from 1 to 4, as said below
Outputs:
- galerkin: bfloat16 [8, 4, 64, 3136], P('row', 'col')
Inputs may be any that keep to these rules, and one draw needn't show every extreme that they name: `fine_columns`: entry 0 of patch (x, y) is the patch itself; entries 1 to 8 are distinct directions among the eight patches at offsets of at most one along both dimensions, in an order drawn per patch, with coordinates clamped to the grid. `fine_counts`: the patch at the low corner of each 4 x 4 tile uses all 9 blocks. `prolong_columns`: entry 0 of patch (x, y) is its own aggregate (x // 4, y // 4); the other entries are distinct aggregates inside the grid at offsets of at most one from it along both dimensions. `prolong_counts`: the patch at the low corner of each 4 x 4 tile uses all 4 blocks.
All inputs are finite; a program needn't handle non-finite values.
Results may differ from a plain program's by a relative error of at most 0.0049.
Values may be sent and summed in bfloat16 or wider, within the bound.
No kernel may reach another device: no remote copies, remote signals or barrier semaphores. Data moves between devices by JAX's collectives and lax.ppermute only.
A program may use at most 128 MiB of HBM per device.

v0:
```python
import jax
import jax.numpy as jnp
from jax import lax
from jax.experimental import pallas as pl
from jax.experimental.pallas import tpu as pltpu
from jax.sharding import PartitionSpec as P

B = 64
KA = 9
KP = 4
AG = 4

NEAR = 3
WIN = 5
HOME = 3
OUTW = 7
TRASH = WIN * WIN


def shifted(value, by_row, by_col):
    rows = lax.axis_size("row")
    cols = lax.axis_size("col")
    pairs = []
    for r in range(rows):
        for c in range(cols):
            tr, tc = r + by_row, c + by_col
            if 0 <= tr < rows and 0 <= tc < cols:
                pairs.append((r * cols + c, tr * cols + tc))
    return lax.ppermute(value, ("row", "col"), pairs)


def galerkin_kernel(pos_ref, slot_ref, a_ref, p_ref, dpt_ref, out_ref, acc_ref, prod_ref):
    patches = a_ref.shape[0]

    def one_patch(i, carry):
        acc_ref[...] = jnp.zeros(acc_ref.shape, jnp.float32)
        for k in range(KA):
            pos = pos_ref[i * KA + k]
            a_blk = a_ref[i, :, k * B:(k + 1) * B]
            term = jnp.dot(a_blk, p_ref[pos], preferred_element_type=jnp.float32)
            for q in range(KP):
                s = slot_ref[(i * KA + k) * KP + q]
                acc_ref[s] = acc_ref[s] + term[:, q * B:(q + 1) * B]
        row = pl.multiple_of(i * B, B)
        for w in range(WIN * WIN):
            prod_ref[pl.ds(row, B), w * B:(w + 1) * B] = acc_ref[w].astype(jnp.bfloat16)
        return carry

    lax.fori_loop(0, patches, one_patch, 0)
    out_ref[...] = jnp.dot(dpt_ref[...], prod_ref[...], preferred_element_type=jnp.float32)


def per_device(
    fine_blocks, fine_columns, fine_counts, prolong_blocks, prolong_columns, prolong_counts
):
    tile_rows, tile_cols = fine_counts.shape
    assert tile_rows == AG and tile_cols == AG
    patches = tile_rows * tile_cols
    grid_cols = tile_cols * lax.axis_size("col")
    coarse_grid_cols = lax.axis_size("col")
    row_index = lax.axis_index("row")
    col_index = lax.axis_index("col")

    entries = jnp.arange(KP, dtype=jnp.int32)
    kept = (entries[None, None, :] < prolong_counts[:, :, None])[:, :, None, :, None]
    prolong = jnp.where(
        kept, prolong_blocks.reshape(tile_rows, tile_cols, B, KP, B), jnp.zeros((), jnp.bfloat16)
    ).reshape(tile_rows, tile_cols, B, KP * B)

    hr, hc = tile_rows + 2, tile_cols + 2
    near_p = jnp.zeros((hr, hc, B, KP * B), jnp.bfloat16)
    near_codes = jnp.zeros((hr, hc, KP), jnp.int32)
    near_p = near_p.at[1:hr - 1, 1:hc - 1].set(prolong)
    near_codes = near_codes.at[1:hr - 1, 1:hc - 1].set(prolong_columns)
    for dr in (-1, 0, 1):
        for dc in (-1, 0, 1):
            if dr == 0 and dc == 0:
                continue
            rs = slice(0, tile_rows) if dr == 0 else (slice(0, 1) if dr == 1 else slice(tile_rows - 1, tile_rows))
            cs = slice(0, tile_cols) if dc == 0 else (slice(0, 1) if dc == 1 else slice(tile_cols - 1, tile_cols))
            got_p, got_c = shifted((prolong[rs, cs], prolong_columns[rs, cs]), -dr, -dc)
            drs = slice(1, hr - 1) if dr == 0 else (slice(hr - 1, hr) if dr == 1 else slice(0, 1))
            dcs = slice(1, hc - 1) if dc == 0 else (slice(hc - 1, hc) if dc == 1 else slice(0, 1))
            near_p = near_p.at[drs, dcs].set(got_p)
            near_codes = near_codes.at[drs, dcs].set(got_c)
    near_p = near_p.reshape(hr * hc, B, KP * B)
    near_codes = near_codes.reshape(hr * hc, KP)

    first_row = row_index * tile_rows
    first_col = col_index * tile_cols
    targets = fine_columns.reshape(patches, KA)
    pos = (targets // grid_cols - first_row + 1) * hc + targets % grid_cols - first_col + 1
    pos = jnp.clip(pos, 0, hr * hc - 1)
    codes = near_codes[pos]
    srow = jnp.clip(codes // coarse_grid_cols - row_index + 2, 0, WIN - 1)
    scol = jnp.clip(codes % coarse_grid_cols - col_index + 2, 0, WIN - 1)
    slot = srow * WIN + scol
    blocks = jnp.arange(KA, dtype=jnp.int32)
    used = blocks[None, :] < fine_counts.reshape(patches)[:, None]
    slot = jnp.where(used[:, :, None], slot, TRASH)

    own_codes = prolong_columns.reshape(patches, KP)
    hrow = jnp.clip(own_codes // coarse_grid_cols - row_index + 1, 0, HOME - 1)
    hcol = jnp.clip(own_codes % coarse_grid_cols - col_index + 1, 0, HOME - 1)
    home = hrow * HOME + hcol
    spread = (home[..., None] == jnp.arange(HOME * HOME, dtype=jnp.int32)).astype(jnp.bfloat16)
    dpt = jnp.einsum(
        "iph,ibpa->haib", spread, prolong.reshape(patches, B, KP, B),
        preferred_element_type=jnp.float32,
    ).astype(jnp.bfloat16).reshape(HOME * HOME * B, patches * B)

    smem = pltpu.MemorySpace.SMEM if hasattr(pltpu, "MemorySpace") else pltpu.SMEM
    contrib = pl.pallas_call(
        galerkin_kernel,
        out_shape=jax.ShapeDtypeStruct((HOME * HOME * B, WIN * WIN * B), jnp.float32),
        in_specs=[
            pl.BlockSpec(memory_space=smem),
            pl.BlockSpec(memory_space=smem),
            pl.BlockSpec(memory_space=pltpu.VMEM),
            pl.BlockSpec(memory_space=pltpu.VMEM),
            pl.BlockSpec(memory_space=pltpu.VMEM),
        ],
        out_specs=pl.BlockSpec(memory_space=pltpu.VMEM),
        scratch_shapes=[
            pltpu.VMEM((TRASH + 1, B, B), jnp.float32),
            pltpu.VMEM((patches * B, WIN * WIN * B), jnp.bfloat16),
        ],
    )(
        pos.reshape(-1).astype(jnp.int32),
        slot.reshape(-1).astype(jnp.int32),
        fine_blocks.reshape(patches, B, KA * B),
        near_p,
        dpt,
    )
    contrib = contrib.reshape(HOME, HOME, B, WIN, WIN, B)

    total = jnp.zeros((B, OUTW, OUTW, B), jnp.float32)
    for dr in (-1, 0, 1):
        for dc in (-1, 0, 1):
            block = contrib[dr + 1, dc + 1]
            if dr != 0 or dc != 0:
                block = shifted(block, dr, dc)
            total = total + jnp.pad(
                block, ((0, 0), (1 - dr, 1 + dr), (1 - dc, 1 + dc), (0, 0))
            )
    return total.astype(jnp.bfloat16).reshape(1, 1, B, OUTW * OUTW * B)


def solution(mesh):
    in_specs = (
        P("row", "col", None, None),
        P("row", "col", None),
        P("row", "col"),
        P("row", "col", None, None),
        P("row", "col", None),
        P("row", "col"),
    )
    out_specs = P("row", "col", None, None)
    return jax.shard_map(
        per_device, mesh=mesh, in_specs=in_specs, out_specs=out_specs, check_vma=False
    )
```

profile of v0, /device:TPU:19, one launch (start us, length us, event | category | flops | bytes accessed | tf_op | source)
XLA Modules:
  0.0 251.4 jit_solution(7550607420852161380)
XLA Ops:
  0.0 1.3 fusion.46
  1.3 2.7 %collective-permute-start.7 = (s32[1,1,4]{2,1,0:T(1,128)}, s32[1,1,4]{2,1,0:T(1,128)}, u32[]{:S(2)}, u32[]{:S(2)}) collective-permute-start(s32[1,1,4]{2,1,0:T(1,128)} %get-tuple-element.238), channel_id=1, source_target_pairs={{5,0},{6,1},{7,2},{9,4},{10,5},{11,6},{13,8},{14,9},{15,10},{17,12... | collective-permute-start | bytes 56 | tf_op jit(solution)/shard_map/ppermute | solution.py:29
  4.1 3.6 %collective-permute-start.5 = (s32[1,1,4]{2,1,0:T(1,128)}, s32[1,1,4]{2,1,0:T(1,128)}, u32[]{:S(2)}, u32[]{:S(2)}) collective-permute-start(s32[1,1,4]{2,1,0:T(1,128)} %get-tuple-element.239), channel_id=1, source_target_pairs={{4,1},{5,2},{6,3},{8,5},{9,6},{10,7},{12,9},{13,10},{14,11},{16,13... | collective-permute-start | bytes 56 | tf_op jit(solution)/shard_map/ppermute | solution.py:29
  7.7 3.3 %collective-permute-start.2 = (s32[1,1,4]{2,1,0:T(1,128)}, s32[1,1,4]{2,1,0:T(1,128)}, u32[]{:S(2)}, u32[]{:S(2)}) collective-permute-start(s32[1,1,4]{2,1,0:T(1,128)} %get-tuple-element.240), channel_id=1, source_target_pairs={{1,4},{2,5},{3,6},{5,8},{6,9},{7,10},{9,12},{10,13},{11,14},{13,16... | collective-permute-start | bytes 56 | tf_op jit(solution)/shard_map/ppermute | solution.py:29
  11.0 4.6 %collective-permute-start = (s32[1,1,4]{2,1,0:T(1,128)}, s32[1,1,4]{2,1,0:T(1,128)}, u32[]{:S(2)}, u32[]{:S(2)}) collective-permute-start(s32[1,1,4]{2,1,0:T(1,128)} %get-tuple-element.241), channel_id=1, source_target_pairs={{0,5},{1,6},{2,7},{4,9},{5,10},{6,11},{8,13},{9,14},{10,15},{12,17... | collective-permute-start | bytes 56 | tf_op jit(solution)/shard_map/ppermute | solution.py:29
  15.7 1.4 fusion.48
  17.1 1.9 collective-permute-start.4
  19.0 0.8 lt.88
  19.8 0.8 iota_compare_fusion.2
  20.5 1.3 fusion.47
  22.0 1.1 broadcast_select_fusion.1
  23.1 0.7 fusion.44
  23.9 0.7 fusion.45
  25.1 1.4 reshape.910
  26.5 0.7 fusion.49
  27.2 0.8 and_reduce_fusion
  28.0 0.7 and_reduce_fusion.1
  30.5 0.6 scatter.60
  31.4 1.2 scatter.75
  33.3 0.9 slice.647
  34.1 0.9 slice.641
  35.0 3.3 %convert_bitcast_fusion = bf16[9,64,16,64]{1,0,3,2:T(8,128)(2,1)} fusion(bf16[16,64,4,64]{3,2,1,0:T(4,128)(2,1)S(1)} %reshape.912, pred[16,4]{1,0:T(8,128)(4,1)S(1)} %iota_compare_fusion.1, s32[16,4]{1,0:T(8,128)S(1)} %copy.13), kind=kOutput, calls=%fused_computation.1 | convolution fusion | flops 5571136 | bytes 1704256 | tf_op jit(solution)/shard_map/iph,ibpa->haib/dot_general | solution.py:107
  38.3 5.0 %reshape.929 = bf16[576,1024]{0,1:T(8,128)(2,1)S(1)} reshape(bf16[9,64,16,64]{1,0,3,2:T(8,128)(2,1)} %convert_bitcast_fusion) | data formatting | bytes 2359296 | tf_op jit(solution)/shard_map/reshape | solution.py:110
  43.4 1.5 copy.28.dpt_ref
  44.9 2.1 collective-permute-start.1
  47.0 0.7 scatter.61
  47.7 1.7 collective-permute-done.1
  49.4 4.8 %collective-permute-start.3 = (s32[4,1,4]{2,1,0:T(1,128)S(1)}, s32[4,1,4]{2,1,0:T(1,128)S(1)}, u32[]{:S(2)}, u32[]{:S(2)}) collective-permute-start(s32[4,1,4]{2,1,0:T(1,128)S(1)} %copy-done.16), channel_id=1, source_target_pairs={{0,1},{1,2},{2,3},{4,5},{5,6},{6,7},{8,9},{9,10},{10,11},{12,13},{... | collective-permute-start | bytes 200 | tf_op jit(solution)/shard_map/ppermute | solution.py:29
  54.2 1.3 scatter.64
  55.5 2.6 %collective-permute-start.6 = (s32[1,4,4]{2,1,0:T(4,128)S(1)}, s32[1,4,4]{2,1,0:T(4,128)S(1)}, u32[]{:S(2)}, u32[]{:S(2)}) collective-permute-start(s32[1,4,4]{2,1,0:T(4,128)S(1)} %get-tuple-element.242), channel_id=1, source_target_pairs={{4,0},{5,1},{6,2},{7,3},{8,4},{9,5},{10,6},{11,7},{12,8},{13,9},{1... | collective-permute-start | bytes 200 | tf_op jit(solution)/shard_map/ppermute | solution.py:29
  58.2 2.5 %broadcast_select_fusion.2 = s32[1,1,4]{2,1,0:T(1,128)S(1)} fusion(s32[1,1,4]{2,1,0:T(1,128)} %collective-permute-done.2, pred[]{:T(512)} %and_reduce_fusion.1, s32[6,6,4]{2,1,0:T(8,128)S(1)} %scatter.64, s32[]{:T(128)} %bitcast.2, s32[]{:T(128)} %bitcast.3), kind=kLoop, calls=%fused_computation.86 | loop fusion | flops 4 | bytes 57 | tf_op jit(solution)/shard_map/select.21
  60.7 1.3 scatter.65
  62.0 1.9 collective-permute-start.15
  64.0 4.4 %collective-permute-start.13 = (bf16[1,1,64,256]{3,2,1,0:T(8,128)(2,1)S(1)}, bf16[1,1,64,256]{3,2,1,0:T(8,128)(2,1)S(1)}, u32[]{:S(2)}, u32[]{:S(2)}) collective-permute-start(bf16[1,1,64,256]{3,2,1,0:T(8,128)(2,1)S(1)} %copy-done.12), channel_id=1, source_target_pairs={{4,1},{5,2},{6,3},{8,5},{9,6},{10,7},{12,9},{13,10},{14,11},{16,13... | collective-permute-start | bytes 98312 | tf_op jit(solution)/shard_map/ppermute | solution.py:29
  68.5 2.0 collective-permute-start.10
  70.5 0.6 scatter.70
  71.2 5.4 %collective-permute-start.8 = (bf16[1,1,64,256]{3,2,1,0:T(8,128)(2,1)S(1)}, bf16[1,1,64,256]{3,2,1,0:T(8,128)(2,1)S(1)}, u32[]{:S(2)}, u32[]{:S(2)}) collective-permute-start(bf16[1,1,64,256]{3,2,1,0:T(8,128)(2,1)S(1)} %copy-done.14), channel_id=1, source_target_pairs={{0,5},{1,6},{2,7},{4,9},{5,10},{6,11},{8,13},{9,14},{10,15},{12,17... | collective-permute-start | bytes 98312 | tf_op jit(solution)/shard_map/ppermute | solution.py:29
  76.8 1.9 collective-permute-start.9
  79.3 0.7 gather_fusion
  80.1 0.6 fusion.22.slot_ref
  80.7 1.9 collective-permute-start.12
  82.7 3.6 %collective-permute-start.11 = (bf16[4,1,64,256]{3,2,1,0:T(8,128)(2,1)S(1)}, bf16[4,1,64,256]{3,2,1,0:T(8,128)(2,1)S(1)}, u32[]{:S(2)}, u32[]{:S(2)}) collective-permute-start(bf16[4,1,64,256]{3,2,1,0:T(8,128)(2,1)S(1)} %copy-done.7), channel_id=1, source_target_pairs={{0,1},{1,2},{2,3},{4,5},{5,6},{6,7},{8,9},{9,10},{10,11},{12,13},{... | collective-permute-start | bytes 393224 | tf_op jit(solution)/shard_map/ppermute | solution.py:29
  86.3 1.2 constant_dynamic-update-slice_fusion.5
  87.6 3.5 %collective-permute-start.14 = (bf16[1,4,64,256]{3,2,1,0:T(8,128)(2,1)S(1)}, bf16[1,4,64,256]{3,2,1,0:T(8,128)(2,1)S(1)}, u32[]{:S(2)}, u32[]{:S(2)}) collective-permute-start(bf16[1,4,64,256]{3,2,1,0:T(8,128)(2,1)S(1)} %copy-done.4), channel_id=1, source_target_pairs={{4,0},{5,1},{6,2},{7,3},{8,4},{9,5},{10,6},{11,7},{12,8},{13,9},{1... | collective-permute-start | bytes 393224 | tf_op jit(solution)/shard_map/ppermute | solution.py:29
  91.1 2.0 select_dynamic-update-slice_fusion
  93.2 1.6 collective-permute-done.14
  94.9 1.0 copy-done
  95.9 16.1 %shard_map.64 = f32[576,1600]{1,0:T(8,128)} custom-call(s32[144]{0:T(256)} %add_clamp_fusion.pos_ref, s32[576]{0:T(1024)} %fusion.22.slot_ref, bf16[16,64,576]{2,1,0:T(8,128)(2,1)} %bitcast.54, bf16[36,64,256]{2,1,0:T(8,128)(2,1)} %bitcast.51, bf16[576,1024]{1,0:T(8,128)(2,1)} %copy.28.dpt_ref), custom_call_target="tpu_custom_call" | custom-call | tf_op jit(solution)/shard_map/pallas_call | solution.py:113
  112.0 5.1 %copy.15 = f32[576,1600]{0,1:T(8,128)} copy(f32[576,1600]{1,0:T(8,128)} %shard_map.64) | data formatting | bytes 7372800 | tf_op jit(solution)/shard_map/pallas_call | solution.py:113
  117.1 10.7 %reshape.915 = f32[3,3,64,5,5,64]{2,1,0,5,4,3:T(4,128)} reshape(f32[576,1600]{0,1:T(8,128)} %copy.15) | data formatting | bytes 7372800 | tf_op jit(solution)/shard_map/reshape | solution.py:135
  127.8 14.8 %fusion.42 = (f32[1,1,64,5,5,64]{2,1,0,5,4,3:T(1,128)S(1)}, f32[1,1,64,5,5,64]{2,1,0,5,4,3:T(1,128)S(1)}, f32[1,1,64,5,5,64]{2,1,0,5,4,3:T(1,128)S(1)}, f32[1,1,...) fusion(f32[3,3,64,5,5,64]{2,1,0,5,4,3:T(4,128)} %reshape.915), kind=kLoop, calls=%fused_computation.89 | loop fusion | bytes 7372800 | tf_op jit(solution)/shard_map/slice | solution.py:140
  142.6 3.2 %collective-permute-start.21 = (f32[64,5,5,64]{0,3,2,1:T(8,128)S(1)}, f32[64,5,5,64]{0,3,2,1:T(8,128)S(1)}, u32[]{:S(2)}, u32[]{:S(2)}) collective-permute-start(f32[64,5,5,64]{0,3,2,1:T(8,128)S(1)} %bitcast.62), channel_id=1, source_target_pairs={{1,4},{2,5},{3,6},{5,8},{6,9},{7,10},{9,12},{10,13},{11,14},{13,16... | collective-permute-start | bytes 1228808 | tf_op jit(solution)/shard_map/ppermute | solution.py:29
  145.8 1.9 collective-permute-start.16
  147.8 3.8 %collective-permute-start.20 = (f32[64,5,5,64]{0,3,2,1:T(8,128)S(1)}, f32[64,5,5,64]{0,3,2,1:T(8,128)S(1)}, u32[]{:S(2)}, u32[]{:S(2)}) collective-permute-start(f32[64,5,5,64]{0,3,2,1:T(8,128)S(1)} %bitcast.60), channel_id=1, source_target_pairs={{0,1},{1,2},{2,3},{4,5},{5,6},{6,7},{8,9},{9,10},{10,11},{12,13},{... | collective-permute-start | bytes 1228808 | tf_op jit(solution)/shard_map/ppermute | solution.py:29
  151.5 1.9 collective-permute-start.19
  153.5 4.5 %collective-permute-start.18 = (f32[64,5,5,64]{0,3,2,1:T(8,128)S(1)}, f32[64,5,5,64]{0,3,2,1:T(8,128)S(1)}, u32[]{:S(2)}, u32[]{:S(2)}) collective-permute-start(f32[64,5,5,64]{0,3,2,1:T(8,128)S(1)} %bitcast.58), channel_id=1, source_target_pairs={{4,1},{5,2},{6,3},{8,5},{9,6},{10,7},{12,9},{13,10},{14,11},{16,13... | collective-permute-start | bytes 1228808 | tf_op jit(solution)/shard_map/ppermute | solution.py:29
  158.0 42.2 %collective-permute-done.21 = f32[64,5,5,64]{0,3,2,1:T(8,128)S(1)} collective-permute-done((f32[64,5,5,64]{0,3,2,1:T(8,128)S(1)}, f32[64,5,5,64]{0,3,2,1:T(8,128)S(1)}, u32[]{:S(2)}, u32[]{:S(2)}) %collective-permute-start.21) | collective-permute-done | bytes 409632 | tf_op jit(solution)/shard_map/ppermute | solution.py:29
  200.1 1.9 collective-permute-start.17
  202.1 4.2 %collective-permute-start.23 = (f32[64,5,5,64]{0,3,2,1:T(8,128)S(1)}, f32[64,5,5,64]{0,3,2,1:T(8,128)S(1)}, u32[]{:S(2)}, u32[]{:S(2)}) collective-permute-start(f32[64,5,5,64]{0,3,2,1:T(8,128)S(1)} %bitcast.56), channel_id=1, source_target_pairs={{0,5},{1,6},{2,7},{4,9},{5,10},{6,11},{8,13},{9,14},{10,15},{12,17... | collective-permute-start | bytes 1228808 | tf_op jit(solution)/shard_map/ppermute | solution.py:29
  206.3 2.0 collective-permute-start.22
  208.3 35.2 %collective-permute-done.17 = f32[64,5,5,64]{0,3,2,1:T(8,128)S(1)} collective-permute-done((f32[64,5,5,64]{0,3,2,1:T(8,128)S(1)}, f32[64,5,5,64]{0,3,2,1:T(8,128)S(1)}, u32[]{:S(2)}, u32[]{:S(2)}) %collective-permute-start.17) | collective-permute-done | bytes 409632 | tf_op jit(solution)/shard_map/ppermute | solution.py:29
  243.5 6.0 %collective-permute-done.22 = f32[64,5,5,64]{0,3,2,1:T(8,128)S(1)} collective-permute-done((f32[64,5,5,64]{0,3,2,1:T(8,128)S(1)}, f32[64,5,5,64]{0,3,2,1:T(8,128)S(1)}, u32[]{:S(2)}, u32[]{:S(2)}) %collective-permute-start.22) | collective-permute-done | bytes 409632 | tf_op jit(solution)/shard_map/ppermute | solution.py:29
  249.5 0.9 add_convert_fusion
  250.4 1.0 copy.29
  (91 shorter events, 4.5 us)
Async XLA Ops:
  0.0 24.6 %copy-start.1 = (bf16[4,4,64,256]{3,2,1,0:T(8,128)(2,1)S(1)}, bf16[4,4,64,256]{3,2,1,0:T(8,128)(2,1)}, u32[]{:S(2)}) copy-start(bf16[4,4,64,256]{3,2,1,0:T(8,128)(2,1)} %param.45) | copy-start | bytes 1572868
  1.3 75.4 %collective-permute-start.7 = (s32[1,1,4]{2,1,0:T(1,128)}, s32[1,1,4]{2,1,0:T(1,128)}, u32[]{:S(2)}, u32[]{:S(2)}) collective-permute-start(s32[1,1,4]{2,1,0:T(1,128)} %get-tuple-element.238), channel_id=1, source_target_pairs={{5,0},{6,1},{7,2},{9,4},{10,5},{11,6},{13,8},{14,9},{15,10},{17,12... | collective-permute-start | bytes 56 | tf_op jit(solution)/shard_map/ppermute | solution.py:29
  4.1 64.4 %collective-permute-start.5 = (s32[1,1,4]{2,1,0:T(1,128)}, s32[1,1,4]{2,1,0:T(1,128)}, u32[]{:S(2)}, u32[]{:S(2)}) collective-permute-start(s32[1,1,4]{2,1,0:T(1,128)} %get-tuple-element.239), channel_id=1, source_target_pairs={{4,1},{5,2},{6,3},{8,5},{9,6},{10,7},{12,9},{13,10},{14,11},{16,13... | collective-permute-start | bytes 56 | tf_op jit(solution)/shard_map/ppermute | solution.py:29
  7.7 47.8 %collective-permute-start.2 = (s32[1,1,4]{2,1,0:T(1,128)}, s32[1,1,4]{2,1,0:T(1,128)}, u32[]{:S(2)}, u32[]{:S(2)}) collective-permute-start(s32[1,1,4]{2,1,0:T(1,128)} %get-tuple-element.240), channel_id=1, source_target_pairs={{1,4},{2,5},{3,6},{5,8},{6,9},{7,10},{9,12},{10,13},{11,14},{13,16... | collective-permute-start | bytes 56 | tf_op jit(solution)/shard_map/ppermute | solution.py:29
  11.0 33.8 %collective-permute-start = (s32[1,1,4]{2,1,0:T(1,128)}, s32[1,1,4]{2,1,0:T(1,128)}, u32[]{:S(2)}, u32[]{:S(2)}) collective-permute-start(s32[1,1,4]{2,1,0:T(1,128)} %get-tuple-element.241), channel_id=1, source_target_pairs={{0,5},{1,6},{2,7},{4,9},{5,10},{6,11},{8,13},{9,14},{10,15},{12,17... | collective-permute-start | bytes 56 | tf_op jit(solution)/shard_map/ppermute | solution.py:29
  17.1 46.9 %collective-permute-start.4 = (s32[4,1,4]{2,1,0:T(1,128)}, s32[4,1,4]{2,1,0:T(1,128)S(1)}, u32[]{:S(2)}, u32[]{:S(2)}) collective-permute-start(s32[4,1,4]{2,1,0:T(1,128)} %get-tuple-element.244), channel_id=1, source_target_pairs={{1,0},{2,1},{3,2},{5,4},{6,5},{7,6},{9,8},{10,9},{11,10},{13,12},{... | collective-permute-start | bytes 200 | tf_op jit(solution)/shard_map/ppermute | solution.py:29
  23.1 0.9 copy-start.3
  24.6 2.5 %copy-start.19 = (s32[4]{0:T(128)S(1)}, s32[4]{0:T(128)}, u32[]{:S(2)}) copy-start(s32[4]{0:T(128)} %constant.609.clone.1) | copy-start | bytes 52
  24.6 3.3 %copy-start.18 = (s32[3]{0:T(128)S(1)}, s32[3]{0:T(128)}, u32[]{:S(2)}) copy-start(s32[3]{0:T(128)} %constant.602.clone.1) | copy-start | bytes 40
  24.6 4.0 %copy-start.15 = (s32[4,4]{1,0:T(4,128)S(1)}, s32[4,4]{1,0:T(4,128)}, u32[]{:S(2)}) copy-start(s32[4,4]{1,0:T(4,128)} %param.44) | copy-start | bytes 196
  24.7 4.7 %copy-start.10 = (s32[4,4,9]{2,1,0:T(4,128)S(1)}, s32[4,4,9]{2,1,0:T(4,128)}, u32[]{:S(2)}) copy-start(s32[4,4,9]{2,1,0:T(4,128)} %param.43) | copy-start | bytes 1732
  24.7 5.0 %copy-start.9 = (s32[4,4,4]{2,1,0:T(4,128)S(1)}, s32[4,4,4]{2,1,0:T(4,128)}, u32[]{:S(2)}) copy-start(s32[4,4,4]{2,1,0:T(4,128)} %param.46) | copy-start | bytes 772
  26.5 6.0 %copy-start.2 = (bf16[4,4,64,4,64]{4,3,2,1,0:T(4,128)(2,1)S(1)}, bf16[4,4,64,4,64]{4,3,2,1,0:T(4,128)(2,1)}, u32[]{:S(2)}) copy-start(bf16[4,4,64,4,64]{4,3,2,1,0:T(4,128)(2,1)} %reshape.910) | copy-start | bytes 1572868
  43.3 1.6 copy-start.17
  43.4 3.6 %copy-start.8 = (s32[6,6,4]{2,1,0:T(8,128)S(1)}, s32[6,6,4]{2,1,0:T(8,128)}, u32[]{:S(2)}) copy-start(s32[6,6,4]{2,1,0:T(8,128)} %scatter.60) | copy-start | bytes 1732
  43.4 6.0 %copy-start.16 = (s32[4,1,4]{2,1,0:T(1,128)S(1)}, s32[4,1,4]{2,1,0:T(1,128)}, u32[]{:S(2)}) copy-start(s32[4,1,4]{2,1,0:T(1,128)} %get-tuple-element.245) | copy-start | bytes 196
  43.4 18.6 %copy-start.11 = (bf16[1,1,64,256]{3,2,1,0:T(8,128)(2,1)S(1)}, bf16[1,1,64,256]{3,2,1,0:T(8,128)(2,1)}, u32[]{:S(2)}) copy-start(bf16[1,1,64,256]{3,2,1,0:T(8,128)(2,1)} %get-tuple-element.232) | copy-start | bytes 98308
  43.4 20.6 %copy-start.12 = (bf16[1,1,64,256]{3,2,1,0:T(8,128)(2,1)S(1)}, bf16[1,1,64,256]{3,2,1,0:T(8,128)(2,1)}, u32[]{:S(2)}) copy-start(bf16[1,1,64,256]{3,2,1,0:T(8,128)(2,1)} %get-tuple-element.233) | copy-start | bytes 98308
  43.4 25.1 %copy-start.13 = (bf16[1,1,64,256]{3,2,1,0:T(8,128)(2,1)S(1)}, bf16[1,1,64,256]{3,2,1,0:T(8,128)(2,1)}, u32[]{:S(2)}) copy-start(bf16[1,1,64,256]{3,2,1,0:T(8,128)(2,1)} %get-tuple-element.234) | copy-start | bytes 98308
  43.4 27.8 %copy-start.14 = (bf16[1,1,64,256]{3,2,1,0:T(8,128)(2,1)S(1)}, bf16[1,1,64,256]{3,2,1,0:T(8,128)(2,1)}, u32[]{:S(2)}) copy-start(bf16[1,1,64,256]{3,2,1,0:T(8,128)(2,1)} %get-tuple-element.235) | copy-start | bytes 98308
  43.4 33.4 %copy-start.5 = (bf16[1,4,64,256]{3,2,1,0:T(8,128)(2,1)S(1)}, bf16[1,4,64,256]{3,2,1,0:T(8,128)(2,1)}, u32[]{:S(2)}) copy-start(bf16[1,4,64,256]{3,2,1,0:T(8,128)(2,1)} %slice.641) | copy-start | bytes 393220
  44.9 35.8 %copy-start.6 = (bf16[4,1,64,256]{3,2,1,0:T(8,128)(2,1)S(1)}, bf16[4,1,64,256]{3,2,1,0:T(8,128)(2,1)}, u32[]{:S(2)}) copy-start(bf16[4,1,64,256]{3,2,1,0:T(8,128)(2,1)} %get-tuple-element.236) | copy-start | bytes 393220
  44.9 37.8 %copy-start.7 = (bf16[4,1,64,256]{3,2,1,0:T(8,128)(2,1)S(1)}, bf16[4,1,64,256]{3,2,1,0:T(8,128)(2,1)}, u32[]{:S(2)}) copy-start(bf16[4,1,64,256]{3,2,1,0:T(8,128)(2,1)} %get-tuple-element.237) | copy-start | bytes 393220
  44.9 42.7 %copy-start.4 = (bf16[1,4,64,256]{3,2,1,0:T(8,128)(2,1)S(1)}, bf16[1,4,64,256]{3,2,1,0:T(8,128)(2,1)}, u32[]{:S(2)}) copy-start(bf16[1,4,64,256]{3,2,1,0:T(8,128)(2,1)} %slice.647) | copy-start | bytes 393220
  44.9 4.5 %collective-permute-start.1 = (s32[1,4,4]{2,1,0:T(4,128)S(1)}, s32[1,4,4]{2,1,0:T(4,128)S(1)}, u32[]{:S(2)}, u32[]{:S(2)}) collective-permute-start(s32[1,4,4]{2,1,0:T(4,128)S(1)} %copy-done.17), channel_id=1, source_target_pairs={{0,4},{1,5},{2,6},{3,7},{4,8},{5,9},{6,10},{7,11},{8,12},{9,13},{1... | collective-permute-start | bytes 200 | tf_op jit(solution)/shard_map/ppermute | solution.py:29
  49.4 12.6 %collective-permute-start.3 = (s32[4,1,4]{2,1,0:T(1,128)S(1)}, s32[4,1,4]{2,1,0:T(1,128)S(1)}, u32[]{:S(2)}, u32[]{:S(2)}) collective-permute-start(s32[4,1,4]{2,1,0:T(1,128)S(1)} %copy-done.16), channel_id=1, source_target_pairs={{0,1},{1,2},{2,3},{4,5},{5,6},{6,7},{8,9},{9,10},{10,11},{12,13},{... | collective-permute-start | bytes 200 | tf_op jit(solution)/shard_map/ppermute | solution.py:29
  55.5 15.7 %collective-permute-start.6 = (s32[1,4,4]{2,1,0:T(4,128)S(1)}, s32[1,4,4]{2,1,0:T(4,128)S(1)}, u32[]{:S(2)}, u32[]{:S(2)}) collective-permute-start(s32[1,4,4]{2,1,0:T(4,128)S(1)} %get-tuple-element.242), channel_id=1, source_target_pairs={{4,0},{5,1},{6,2},{7,3},{8,4},{9,5},{10,6},{11,7},{12,8},{13,9},{1... | collective-permute-start | bytes 200 | tf_op jit(solution)/shard_map/ppermute | solution.py:29
  62.0 32.8 %collective-permute-start.15 = (bf16[1,1,64,256]{3,2,1,0:T(8,128)(2,1)S(1)}, bf16[1,1,64,256]{3,2,1,0:T(8,128)(2,1)S(1)}, u32[]{:S(2)}, u32[]{:S(2)}) collective-permute-start(bf16[1,1,64,256]{3,2,1,0:T(8,128)(2,1)S(1)} %copy-done.11), channel_id=1, source_target_pairs={{5,0},{6,1},{7,2},{9,4},{10,5},{11,6},{13,8},{14,9},{15,10},{17,12... | collective-permute-start | bytes 98312 | tf_op jit(solution)/shard_map/ppermute | solution.py:29
  64.0 29.2 %collective-permute-start.13 = (bf16[1,1,64,256]{3,2,1,0:T(8,128)(2,1)S(1)}, bf16[1,1,64,256]{3,2,1,0:T(8,128)(2,1)S(1)}, u32[]{:S(2)}, u32[]{:S(2)}) collective-permute-start(bf16[1,1,64,256]{3,2,1,0:T(8,128)(2,1)S(1)} %copy-done.12), channel_id=1, source_target_pairs={{4,1},{5,2},{6,3},{8,5},{9,6},{10,7},{12,9},{13,10},{14,11},{16,13... | collective-permute-start | bytes 98312 | tf_op jit(solution)/shard_map/ppermute | solution.py:29
  68.5 19.1 %collective-permute-start.10 = (bf16[1,1,64,256]{3,2,1,0:T(8,128)(2,1)S(1)}, bf16[1,1,64,256]{3,2,1,0:T(8,128)(2,1)S(1)}, u32[]{:S(2)}, u32[]{:S(2)}) collective-permute-start(bf16[1,1,64,256]{3,2,1,0:T(8,128)(2,1)S(1)} %copy-done.13), channel_id=1, source_target_pairs={{1,4},{2,5},{3,6},{5,8},{6,9},{7,10},{9,12},{10,13},{11,14},{13,16... | collective-permute-start | bytes 98312 | tf_op jit(solution)/shard_map/ppermute | solution.py:29
  71.2 9.5 %collective-permute-start.8 = (bf16[1,1,64,256]{3,2,1,0:T(8,128)(2,1)S(1)}, bf16[1,1,64,256]{3,2,1,0:T(8,128)(2,1)S(1)}, u32[]{:S(2)}, u32[]{:S(2)}) collective-permute-start(bf16[1,1,64,256]{3,2,1,0:T(8,128)(2,1)S(1)} %copy-done.14), channel_id=1, source_target_pairs={{0,5},{1,6},{2,7},{4,9},{5,10},{6,11},{8,13},{9,14},{10,15},{12,17... | collective-permute-start | bytes 98312 | tf_op jit(solution)/shard_map/ppermute | solution.py:29
  76.8 5.9 %collective-permute-start.9 = (bf16[1,4,64,256]{3,2,1,0:T(8,128)(2,1)S(1)}, bf16[1,4,64,256]{3,2,1,0:T(8,128)(2,1)S(1)}, u32[]{:S(2)}, u32[]{:S(2)}) collective-permute-start(bf16[1,4,64,256]{3,2,1,0:T(8,128)(2,1)S(1)} %copy-done.5), channel_id=1, source_target_pairs={{0,4},{1,5},{2,6},{3,7},{4,8},{5,9},{6,10},{7,11},{8,12},{9,13},{1... | collective-permute-start | bytes 393224 | tf_op jit(solution)/shard_map/ppermute | solution.py:29
  80.7 12.4 %collective-permute-start.12 = (bf16[4,1,64,256]{3,2,1,0:T(8,128)(2,1)S(1)}, bf16[4,1,64,256]{3,2,1,0:T(8,128)(2,1)S(1)}, u32[]{:S(2)}, u32[]{:S(2)}) collective-permute-start(bf16[4,1,64,256]{3,2,1,0:T(8,128)(2,1)S(1)} %copy-done.6), channel_id=1, source_target_pairs={{1,0},{2,1},{3,2},{5,4},{6,5},{7,6},{9,8},{10,9},{11,10},{13,12},{... | collective-permute-start | bytes 393224 | tf_op jit(solution)/shard_map/ppermute | solution.py:29
  82.7 10.4 %collective-permute-start.11 = (bf16[4,1,64,256]{3,2,1,0:T(8,128)(2,1)S(1)}, bf16[4,1,64,256]{3,2,1,0:T(8,128)(2,1)S(1)}, u32[]{:S(2)}, u32[]{:S(2)}) collective-permute-start(bf16[4,1,64,256]{3,2,1,0:T(8,128)(2,1)S(1)} %copy-done.7), channel_id=1, source_target_pairs={{0,1},{1,2},{2,3},{4,5},{5,6},{6,7},{8,9},{9,10},{10,11},{12,13},{... | collective-permute-start | bytes 393224 | tf_op jit(solution)/shard_map/ppermute | solution.py:29
  87.6 7.3 %collective-permute-start.14 = (bf16[1,4,64,256]{3,2,1,0:T(8,128)(2,1)S(1)}, bf16[1,4,64,256]{3,2,1,0:T(8,128)(2,1)S(1)}, u32[]{:S(2)}, u32[]{:S(2)}) collective-permute-start(bf16[1,4,64,256]{3,2,1,0:T(8,128)(2,1)S(1)} %copy-done.4), channel_id=1, source_target_pairs={{4,0},{5,1},{6,2},{7,3},{8,4},{9,5},{10,6},{11,7},{12,8},{13,9},{1... | collective-permute-start | bytes 393224 | tf_op jit(solution)/shard_map/ppermute | solution.py:29
  94.8 1.0 copy-start
  142.6 57.5 %collective-permute-start.21 = (f32[64,5,5,64]{0,3,2,1:T(8,128)S(1)}, f32[64,5,5,64]{0,3,2,1:T(8,128)S(1)}, u32[]{:S(2)}, u32[]{:S(2)}) collective-permute-start(f32[64,5,5,64]{0,3,2,1:T(8,128)S(1)} %bitcast.62), channel_id=1, source_target_pairs={{1,4},{2,5},{3,6},{5,8},{6,9},{7,10},{9,12},{10,13},{11,14},{13,16... | collective-permute-start | bytes 1228808 | tf_op jit(solution)/shard_map/ppermute | solution.py:29
  145.8 56.2 %collective-permute-start.16 = (f32[64,5,5,64]{0,3,2,1:T(8,128)S(1)}, f32[64,5,5,64]{0,3,2,1:T(8,128)S(1)}, u32[]{:S(2)}, u32[]{:S(2)}) collective-permute-start(f32[64,5,5,64]{0,3,2,1:T(8,128)S(1)} %bitcast.61), channel_id=1, source_target_pairs={{5,0},{6,1},{7,2},{9,4},{10,5},{11,6},{13,8},{14,9},{15,10},{17,12... | collective-permute-start | bytes 1228808 | tf_op jit(solution)/shard_map/ppermute | solution.py:29
  147.8 58.5 %collective-permute-start.20 = (f32[64,5,5,64]{0,3,2,1:T(8,128)S(1)}, f32[64,5,5,64]{0,3,2,1:T(8,128)S(1)}, u32[]{:S(2)}, u32[]{:S(2)}) collective-permute-start(f32[64,5,5,64]{0,3,2,1:T(8,128)S(1)} %bitcast.60), channel_id=1, source_target_pairs={{0,1},{1,2},{2,3},{4,5},{5,6},{6,7},{8,9},{9,10},{10,11},{12,13},{... | collective-permute-start | bytes 1228808 | tf_op jit(solution)/shard_map/ppermute | solution.py:29
  151.5 56.8 %collective-permute-start.19 = (f32[64,5,5,64]{0,3,2,1:T(8,128)S(1)}, f32[64,5,5,64]{0,3,2,1:T(8,128)S(1)}, u32[]{:S(2)}, u32[]{:S(2)}) collective-permute-start(f32[64,5,5,64]{0,3,2,1:T(8,128)S(1)} %bitcast.59), channel_id=1, source_target_pairs={{1,0},{2,1},{3,2},{5,4},{6,5},{7,6},{9,8},{10,9},{11,10},{13,12},{... | collective-permute-start | bytes 1228808 | tf_op jit(solution)/shard_map/ppermute | solution.py:29
  153.5 54.8 %collective-permute-start.18 = (f32[64,5,5,64]{0,3,2,1:T(8,128)S(1)}, f32[64,5,5,64]{0,3,2,1:T(8,128)S(1)}, u32[]{:S(2)}, u32[]{:S(2)}) collective-permute-start(f32[64,5,5,64]{0,3,2,1:T(8,128)S(1)} %bitcast.58), channel_id=1, source_target_pairs={{4,1},{5,2},{6,3},{8,5},{9,6},{10,7},{12,9},{13,10},{14,11},{16,13... | collective-permute-start | bytes 1228808 | tf_op jit(solution)/shard_map/ppermute | solution.py:29
  200.1 43.4 %collective-permute-start.17 = (f32[64,5,5,64]{0,3,2,1:T(8,128)S(1)}, f32[64,5,5,64]{0,3,2,1:T(8,128)S(1)}, u32[]{:S(2)}, u32[]{:S(2)}) collective-permute-start(f32[64,5,5,64]{0,3,2,1:T(8,128)S(1)} %bitcast.57), channel_id=1, source_target_pairs={{4,0},{5,1},{6,2},{7,3},{8,4},{9,5},{10,6},{11,7},{12,8},{13,9},{1... | collective-permute-start | bytes 1228808 | tf_op jit(solution)/shard_map/ppermute | solution.py:29
  202.1 41.4 %collective-permute-start.23 = (f32[64,5,5,64]{0,3,2,1:T(8,128)S(1)}, f32[64,5,5,64]{0,3,2,1:T(8,128)S(1)}, u32[]{:S(2)}, u32[]{:S(2)}) collective-permute-start(f32[64,5,5,64]{0,3,2,1:T(8,128)S(1)} %bitcast.56), channel_id=1, source_target_pairs={{0,5},{1,6},{2,7},{4,9},{5,10},{6,11},{8,13},{9,14},{10,15},{12,17... | collective-permute-start | bytes 1228808 | tf_op jit(solution)/shard_map/ppermute | solution.py:29
  206.3 43.2 %collective-permute-start.22 = (f32[64,5,5,64]{0,3,2,1:T(8,128)S(1)}, f32[64,5,5,64]{0,3,2,1:T(8,128)S(1)}, u32[]{:S(2)}, u32[]{:S(2)}) collective-permute-start(f32[64,5,5,64]{0,3,2,1:T(8,128)S(1)} %bitcast.55), channel_id=1, source_target_pairs={{0,4},{1,5},{2,6},{3,7},{4,8},{5,9},{6,10},{7,11},{8,12},{9,13},{1... | collective-permute-start | bytes 1228808 | tf_op jit(solution)/shard_map/ppermute | solution.py:29
where the time goes:
time: 253 us; the launch traced here: 251 us
  waiting for transfers between devices  86.8 us (34%)
  starting transfers between devices  73.9 us (29%)
  local copies, waits for them, and re-layouts  59.9 us (24%)
  Pallas kernels  16.1 us (6%)
  other arithmetic  10.7 us (4%)
  matrix products  3.33 us (1%)
    ppermute x24, waiting for transfers between devices, shifted(): return lax.ppermute(value, ('row', 'col'), pairs)  86.8 us
    ppermute x24, starting transfers between devices, shifted(): return lax.ppermute(value, ('row', 'col'), pairs)  73.9 us
    pallas_call x1, Pallas kernels, per_device(): pl.pallas_call(galerkin_kernel, out_shape=jax.ShapeDtypeStruct((HOME * HO...  16.1 us
    slice x1, local copies, waits for them, and re-layouts, per_device(): block = contrib[dr + 1, dc + 1]  14.8 us
    reshape x1, local copies, waits for them, and re-layouts, per_device(): contrib = contrib.reshape(HOME, HOME, B, WIN, WIN, B)  10.7 us
    slice x8, local copies, waits for them, and re-layouts, per_device(): got_p, got_c = shifted((prolong[rs, cs], prolong_columns[rs, cs]), -dr, -dc)  7.31 us
    reshape x2, local copies, waits for them, and re-layouts, per_device(): dpt = jnp.einsum('iph,ibpa->haib', spread, prolong.reshape(patches, B, KP...  6.45 us
    pallas_call x1, local copies, waits for them, and re-layouts, per_device(): pl.pallas_call(galerkin_kernel, out_shape=jax.ShapeDtypeStruct((HOME * HO...  5.1 us
  transfers between devices with their start and end apart: 24, of which 5 were waited for; matrix products, arithmetic and copies ran while one was open for 15% of the time, Pallas kernels for 0%

commit v1 on v0

v1 whole, which is shorter than its diff:
```python
import jax
import jax.numpy as jnp
from jax import lax
from jax.experimental import pallas as pl
from jax.experimental.pallas import tpu as pltpu
from jax.sharding import PartitionSpec as P

B = 64
KA = 9
KP = 4
AG = 4

NEAR = 3
WIN = 5
HOME = 3
OUTW = 7
TRASH = WIN * WIN
SEND = jnp.float32


def shifted(value, by_row, by_col):
    rows = lax.axis_size("row")
    cols = lax.axis_size("col")
    pairs = []
    for r in range(rows):
        for c in range(cols):
            tr, tc = r + by_row, c + by_col
            if 0 <= tr < rows and 0 <= tc < cols:
                pairs.append((r * cols + c, tr * cols + tc))
    return lax.ppermute(value, ("row", "col"), pairs)


def galerkin_kernel(pos_ref, slot_ref, a_ref, p_ref, dpt_ref, keep_ref, send_ref, acc_ref, prod_ref):
    patches = a_ref.shape[0]

    def one_patch(i, carry):
        acc_ref[...] = jnp.zeros(acc_ref.shape, jnp.float32)
        for k in range(KA):
            pos = pos_ref[i * KA + k]
            a_blk = a_ref[i, :, k * B:(k + 1) * B]
            term = jnp.dot(a_blk, p_ref[pos], preferred_element_type=jnp.float32)
            for q in range(KP):
                s = slot_ref[(i * KA + k) * KP + q]
                acc_ref[s] = acc_ref[s] + term[:, q * B:(q + 1) * B]
        row = pl.multiple_of(i * B, B)
        for w in range(WIN * WIN):
            prod_ref[pl.ds(row, B), w * B:(w + 1) * B] = acc_ref[w].astype(jnp.bfloat16)
        return carry

    lax.fori_loop(0, patches, one_patch, 0)
    rows = HOME * B
    keep_ref[...] = jnp.dot(dpt_ref[rows:2 * rows], prod_ref[...], preferred_element_type=jnp.float32)
    for side, start in ((0, 0), (1, 2 * rows)):
        send_ref[side] = jnp.dot(
            dpt_ref[start:start + rows], prod_ref[...], preferred_element_type=jnp.float32
        ).astype(send_ref.dtype)


def fold_cols_kernel(keep_ref, left_ref, right_ref, keep_out, send_out):
    for d in range(HOME):
        for sx in range(WIN):
            for t in range(OUTW):
                parts = []
                if 1 <= t <= WIN:
                    u = t - 1
                    parts.append(keep_ref[d, :, (sx * WIN + u) * B:(sx * WIN + u + 1) * B])
                if t <= WIN - 1:
                    parts.append(left_ref[d, :, (sx * WIN + t) * B:(sx * WIN + t + 1) * B].astype(jnp.float32))
                if t >= 2:
                    u = t - 2
                    parts.append(right_ref[d, :, (sx * WIN + u) * B:(sx * WIN + u + 1) * B].astype(jnp.float32))
                total = parts[0]
                for extra in parts[1:]:
                    total = total + extra
                lo = (sx * OUTW + t) * B
                if d == 1:
                    keep_out[:, lo:lo + B] = total
                else:
                    send_out[d // 2, :, lo:lo + B] = total.astype(send_out.dtype)


def fold_rows_kernel(keep_ref, up_ref, down_ref, out_ref):
    band = OUTW * B
    for s in range(OUTW):
        parts = []
        if 1 <= s <= WIN:
            parts.append(keep_ref[:, (s - 1) * band:s * band])
        if s <= WIN - 1:
            parts.append(up_ref[:, s * band:(s + 1) * band].astype(jnp.float32))
        if s >= 2:
            parts.append(down_ref[:, (s - 2) * band:(s - 1) * band].astype(jnp.float32))
        total = parts[0]
        for extra in parts[1:]:
            total = total + extra
        out_ref[:, s * band:(s + 1) * band] = total.astype(out_ref.dtype)


def per_device(
    fine_blocks, fine_columns, fine_counts, prolong_blocks, prolong_columns, prolong_counts
):
    tile_rows, tile_cols = fine_counts.shape
    assert tile_rows == AG and tile_cols == AG
    patches = tile_rows * tile_cols
    grid_cols = tile_cols * lax.axis_size("col")
    coarse_grid_cols = lax.axis_size("col")
    row_index = lax.axis_index("row")
    col_index = lax.axis_index("col")

    entries = jnp.arange(KP, dtype=jnp.int32)
    kept = (entries[None, None, :] < prolong_counts[:, :, None])[:, :, None, :, None]
    prolong = jnp.where(
        kept, prolong_blocks.reshape(tile_rows, tile_cols, B, KP, B), jnp.zeros((), jnp.bfloat16)
    ).reshape(tile_rows, tile_cols, B, KP * B)

    hr, hc = tile_rows + 2, tile_cols + 2
    from_above = shifted(prolong[tile_rows - 1:], 1, 0)
    from_below = shifted(prolong[:1], -1, 0)
    tall = jnp.concatenate([from_above, prolong, from_below], axis=0)
    from_left = shifted(tall[:, tile_cols - 1:], 0, 1)
    from_right = shifted(tall[:, :1], 0, -1)
    near_p = jnp.concatenate([from_left, tall, from_right], axis=1).reshape(hr * hc, B, KP * B)

    all_codes = lax.all_gather(prolong_columns, ("row", "col"), axis=0, tiled=False)
    rows_n, cols_n = lax.axis_size("row"), lax.axis_size("col")
    all_codes = all_codes.reshape(rows_n, cols_n, tile_rows, tile_cols, KP)
    all_codes = all_codes.transpose(0, 2, 1, 3, 4).reshape(rows_n * tile_rows * cols_n * tile_cols, KP)

    first_row = row_index * tile_rows
    first_col = col_index * tile_cols
    targets = fine_columns.reshape(patches, KA)
    pos = (targets // grid_cols - first_row + 1) * hc + targets % grid_cols - first_col + 1
    pos = jnp.clip(pos, 0, hr * hc - 1)
    codes = all_codes[jnp.clip(targets, 0, all_codes.shape[0] - 1)]
    srow = jnp.clip(codes // coarse_grid_cols - row_index + 2, 0, WIN - 1)
    scol = jnp.clip(codes % coarse_grid_cols - col_index + 2, 0, WIN - 1)
    slot = srow * WIN + scol
    blocks = jnp.arange(KA, dtype=jnp.int32)
    used = blocks[None, :] < fine_counts.reshape(patches)[:, None]
    slot = jnp.where(used[:, :, None], slot, TRASH)

    own_codes = prolong_columns.reshape(patches, KP)
    hrow = jnp.clip(own_codes // coarse_grid_cols - row_index + 1, 0, HOME - 1)
    hcol = jnp.clip(own_codes % coarse_grid_cols - col_index + 1, 0, HOME - 1)
    home = hcol * HOME + hrow
    spread = (home[..., None] == jnp.arange(HOME * HOME, dtype=jnp.int32)).astype(jnp.bfloat16)
    dpt = jnp.einsum(
        "iph,ibpa->haib", spread, prolong.reshape(patches, B, KP, B),
        preferred_element_type=jnp.float32,
    ).astype(jnp.bfloat16).reshape(HOME * HOME * B, patches * B)

    smem = pltpu.MemorySpace.SMEM
    vmem = pltpu.MemorySpace.VMEM
    width = WIN * WIN * B
    keep, send = pl.pallas_call(
        galerkin_kernel,
        out_shape=(
            jax.ShapeDtypeStruct((HOME * B, width), jnp.float32),
            jax.ShapeDtypeStruct((2, HOME * B, width), SEND),
        ),
        in_specs=[
            pl.BlockSpec(memory_space=smem),
            pl.BlockSpec(memory_space=smem),
            pl.BlockSpec(memory_space=vmem),
            pl.BlockSpec(memory_space=vmem),
            pl.BlockSpec(memory_space=vmem),
        ],
        out_specs=(pl.BlockSpec(memory_space=vmem), pl.BlockSpec(memory_space=vmem)),
        scratch_shapes=[
            pltpu.VMEM((TRASH + 1, B, B), jnp.float32),
            pltpu.VMEM((patches * B, width), jnp.bfloat16),
        ],
    )(
        pos.reshape(-1).astype(jnp.int32),
        slot.reshape(-1).astype(jnp.int32),
        fine_blocks.reshape(patches, B, KA * B),
        near_p,
        dpt,
    )
    left_in = shifted(send[1].reshape(HOME, B, width), 0, 1)
    right_in = shifted(send[0].reshape(HOME, B, width), 0, -1)
    band = WIN * OUTW * B
    keep2, send2 = pl.pallas_call(
        fold_cols_kernel,
        out_shape=(
            jax.ShapeDtypeStruct((B, band), jnp.float32),
            jax.ShapeDtypeStruct((2, B, band), SEND),
        ),
        in_specs=[pl.BlockSpec(memory_space=vmem)] * 3,
        out_specs=(pl.BlockSpec(memory_space=vmem), pl.BlockSpec(memory_space=vmem)),
    )(keep.reshape(HOME, B, width), left_in, right_in)
    up_in = shifted(send2[1], 1, 0)
    down_in = shifted(send2[0], -1, 0)
    out = pl.pallas_call(
        fold_rows_kernel,
        out_shape=jax.ShapeDtypeStruct((B, OUTW * OUTW * B), jnp.bfloat16),
        in_specs=[pl.BlockSpec(memory_space=vmem)] * 3,
        out_specs=pl.BlockSpec(memory_space=vmem),
    )(keep2, up_in, down_in)
    return out.reshape(1, 1, B, OUTW * OUTW * B)


def solution(mesh):
    in_specs = (
        P("row", "col", None, None),
        P("row", "col", None),
        P("row", "col"),
        P("row", "col", None, None),
        P("row", "col", None),
        P("row", "col"),
    )
    out_specs = P("row", "col", None, None)
    return jax.shard_map(
        per_device, mesh=mesh, in_specs=in_specs, out_specs=out_specs, check_vma=False
    )
```

time: 253 us -> 145 us (0.57)
  the two profiles are of different devices: /device:TPU:19 before, /device:TPU:1 now
where the time goes in v1:
time: 145 us
  blocking collectives  44.4 us (31%)
  waiting for transfers between devices  31.9 us (22%)
  Pallas kernels  28 us (19%)
  local copies, waits for them, and re-layouts  16.6 us (11%)
  starting transfers between devices  16.6 us (11%)
  other arithmetic  3.94 us (3%)
  matrix products  3.31 us (2%)
    all_gather x1, blocking collectives, per_device(): lax.all_gather(prolong_columns, ('row', 'col'), axis=0, tiled=False)  44.4 us
    ppermute x8, waiting for transfers between devices, shifted(): return lax.ppermute(value, ('row', 'col'), pairs)  31.9 us
    ppermute x8, starting transfers between devices, shifted(): return lax.ppermute(value, ('row', 'col'), pairs)  16.6 us
    pallas_call x1, Pallas kernels, per_device(): pl.pallas_call(galerkin_kernel, out_shape=(jax.ShapeDtypeStruct((HOME * B...  16.1 us
    pallas_call x1, Pallas kernels, per_device(): pl.pallas_call(fold_cols_kernel, out_shape=(jax.ShapeDtypeStruct((B, band...  9.12 us
    reshape x2, local copies, waits for them, and re-layouts, per_device(): dpt = jnp.einsum('iph,ibpa->haib', spread, prolong.reshape(patches, B, KP...  6.53 us
    dot_general x1, matrix products, per_device(): jnp.einsum('iph,ibpa->haib', spread, prolong.reshape(patches, B, KP, B),...  3.31 us
  transfers between devices with their start and end apart: 8, of which 4 were waited for; matrix products, arithmetic and copies ran while one was open for 9% of the time, Pallas kernels for 0%

profile of v1, /device:TPU:1, one launch (start us, length us, event | category | flops | bytes accessed | tf_op | source)
XLA Modules:
  0.0 145.0 jit_solution(380322691105187559)
XLA Ops:
  0.0 0.8 iota_compare_fusion.2
  0.8 2.0 %reshape.156 = bf16[4,4,64,4,64]{4,3,2,1,0:T(4,128)(2,1)S(1)} reshape(bf16[4,4,64,256]{3,2,1,0:T(8,128)(2,1)} %param.9) | data formatting | bytes 1048576 | tf_op jit(solution)/shard_map/reshape | solution.py:112
  2.8 0.5 broadcast_select_fusion
  3.3 0.0 copy-start
  3.3 0.2 fusion.32
  3.5 0.0 copy-start.7
  3.5 0.0 copy-start.6
  3.5 0.2 slice.31
  3.7 3.9 %collective-permute-start = (bf16[1,4,64,256]{3,2,1,0:T(8,128)(2,1)S(1)}, bf16[1,4,64,256]{3,2,1,0:T(8,128)(2,1)S(1)}, u32[]{:S(2)}, u32[]{:S(2)}) collective-permute-start(bf16[1,4,64,256]{3,2,1,0:T(8,128)(2,1)S(1)} %slice.31), channel_id=1, source_target_pairs={{0,4},{1,5},{2,6},{3,7},{4,8},{5,9},{6,10},{7,11},{8,12},{9,13},{1... | collective-permute-start | bytes 393224 | tf_op jit(solution)/shard_map/ppermute | solution.py:30
  7.7 0.2 slice.33
  7.9 1.3 collective-permute-start.1
  9.2 0.0 copy-done
  9.2 0.0 copy-start.5
  9.2 0.4 reshape.158
  9.7 0.0 copy-done.7
  9.7 0.1 lt.85
  9.7 0.0 copy-done.6
  9.8 0.1 reshape.152
  9.8 0.1 broadcast_in_dim.51
  9.9 0.1 broadcast_in_dim.52
  10.1 0.0 copy-done.5
  10.1 44.4 %all-gather = s32[128,4,4]{2,1,0:T(4,128)S(1)} all-gather(s32[4,4,4]{2,1,0:T(4,128)S(1)} %copy-done.5), channel_id=2, replica_groups=mesh['row'=8,'col'=4] {'row','col'}, dimensions={0}, use_global_device_ids=true | all-gather | bytes 8448 | tf_op jit(solution)/shard_map/all_gather | solution.py:123
  54.5 0.1 copy.20
  54.6 0.1 copy.17
  54.7 0.1 iota_compare_fusion.1
  54.8 3.3 %convert_bitcast_fusion = bf16[9,64,16,64]{1,0,3,2:T(8,128)(2,1)} fusion(bf16[16,64,4,64]{3,2,1,0:T(4,128)(2,1)S(1)} %reshape.158, pred[16,4]{1,0:T(8,128)(4,1)S(1)} %iota_compare_fusion.1, s32[16,4]{1,0:T(8,128)S(1)} %copy.17), kind=kOutput, calls=%fused_computation.1 | convolution fusion | flops 5571136 | bytes 1704256 | tf_op jit(solution)/shard_map/iph,ibpa->haib/dot_general | solution.py:146
  58.1 5.0 %reshape.176 = bf16[576,1024]{0,1:T(8,128)(2,1)S(1)} reshape(bf16[9,64,16,64]{1,0,3,2:T(8,128)(2,1)} %convert_bitcast_fusion) | data formatting | bytes 2359296 | tf_op jit(solution)/shard_map/reshape | solution.py:149
  63.1 1.5 %copy.21.dpt_ref = bf16[576,1024]{1,0:T(8,128)(2,1)} copy(bf16[576,1024]{0,1:T(8,128)(2,1)S(1)} %reshape.176) | data formatting | bytes 2359296 | tf_op jit(solution)/shard_map/reshape | solution.py:149
  64.6 0.0 copy-start.8
  64.7 0.1 reshape.165
  64.8 0.7 gather_fusion
  65.5 0.1 gather.6
  65.6 0.0 copy-done.8
  65.6 0.1 lt.76
  65.7 0.1 iota_compare_fusion.3
  65.7 0.1 broadcast_in_dim.46
  65.8 0.1 broadcast_in_dim.47
  66.0 0.6 fusion.11.slot_ref
  66.6 0.0 collective-permute-done
  66.6 0.0 collective-permute-done.1
  66.6 1.9 %collective-permute-start.2 = (bf16[6,1,64,256]{3,2,1,0:T(8,128)(2,1)S(1)}, bf16[6,1,64,256]{3,2,1,0:T(8,128)(2,1)S(1)}, u32[]{:S(2)}, u32[]{:S(2)}) collective-permute-start(bf16[6,1,64,256]{3,2,1,0:T(8,128)(2,1)S(1)} %get-tuple-element.19), channel_id=1, source_target_pairs={{0,1},{1,2},{2,3},{4,5},{5,6},{6,7},{8,9},{9,10},{10,11},{12,13},{... | collective-permute-start | bytes 589832 | tf_op jit(solution)/shard_map/ppermute | solution.py:30
  68.6 2.4 %collective-permute-start.3 = (bf16[6,1,64,256]{3,2,1,0:T(8,128)(2,1)S(1)}, bf16[6,1,64,256]{3,2,1,0:T(8,128)(2,1)S(1)}, u32[]{:S(2)}, u32[]{:S(2)}) collective-permute-start(bf16[6,1,64,256]{3,2,1,0:T(8,128)(2,1)S(1)} %get-tuple-element.20), channel_id=1, source_target_pairs={{1,0},{2,1},{3,2},{5,4},{6,5},{7,6},{9,8},{10,9},{11,10},{13,12},{... | collective-permute-start | bytes 589832 | tf_op jit(solution)/shard_map/ppermute | solution.py:30
  71.0 0.6 add_clamp_fusion.pos_ref
  71.6 0.0 collective-permute-done.2
  71.6 4.0 %collective-permute-done.3 = bf16[6,1,64,256]{3,2,1,0:T(8,128)(2,1)S(1)} collective-permute-done((bf16[6,1,64,256]{3,2,1,0:T(8,128)(2,1)S(1)}, bf16[6,1,64,256]{3,2,1,0:T(8,128)(2,1)S(1)}, u32[]{:S(2)}, u32[]{:S(2)}) %collective-permute-start.3) | collective-permute-done | bytes 196640 | tf_op jit(solution)/shard_map/ppermute | solution.py:30
  75.6 1.2 pad_maximum_fusion
  76.7 16.1 %shard_map.64 = (f32[192,1600]{1,0:T(8,128)}, f32[2,192,1600]{2,1,0:T(8,128)}) custom-call(s32[144]{0:T(256)} %add_clamp_fusion.pos_ref, s32[576]{0:T(1024)} %fusion.11.slot_ref, bf16[16,64,576]{2,1,0:T(8,128)(2,1)} %bitcast.33, bf16[36,64,256]{2,1,0:T(8,128)(2,1)} %bitcast.32, bf16[576,1024]{1,0:T(8,128)(2,1)} %copy.21.dpt_ref), custom_call_target="tpu_custom_call" | custom-call | tf_op jit(solution)/shard_map/pallas_call | solution.py:154
  92.9 1.9 %fusion.31 = (f32[1,192,1600]{2,1,0:T(8,128)S(1)}, f32[1,192,1600]{2,1,0:T(8,128)S(1)}) fusion(f32[2,192,1600]{2,1,0:T(8,128)} %get-tuple-element.10), kind=kLoop, calls=%fused_computation.65 | loop fusion | bytes 4915200 | tf_op jit(solution)/shard_map/slice | solution.py:180
  94.8 1.9 %collective-permute-start.4 = (f32[3,64,1600]{2,1,0:T(8,128)S(1)}, f32[3,64,1600]{2,1,0:T(8,128)S(1)}, u32[]{:S(2)}, u32[]{:S(2)}) collective-permute-start(f32[3,64,1600]{2,1,0:T(8,128)S(1)} %bitcast.35), channel_id=1, source_target_pairs={{0,1},{1,2},{2,3},{4,5},{5,6},{6,7},{8,9},{9,10},{10,11},{12,13},{... | collective-permute-start | bytes 3686408 | tf_op jit(solution)/shard_map/ppermute | solution.py:30
  96.7 2.5 %collective-permute-start.5 = (f32[3,64,1600]{2,1,0:T(8,128)S(1)}, f32[3,64,1600]{2,1,0:T(8,128)S(1)}, u32[]{:S(2)}, u32[]{:S(2)}) collective-permute-start(f32[3,64,1600]{2,1,0:T(8,128)S(1)} %bitcast.34), channel_id=1, source_target_pairs={{1,0},{2,1},{3,2},{5,4},{6,5},{7,6},{9,8},{10,9},{11,10},{13,12},{... | collective-permute-start | bytes 3686408 | tf_op jit(solution)/shard_map/ppermute | solution.py:30
  99.2 11.7 %collective-permute-done.4.left_ref = f32[3,64,1600]{2,1,0:T(8,128)S(1)} collective-permute-done((f32[3,64,1600]{2,1,0:T(8,128)S(1)}, f32[3,64,1600]{2,1,0:T(8,128)S(1)}, u32[]{:S(2)}, u32[]{:S(2)}) %collective-permute-start.4) | collective-permute-done | bytes 1228832 | tf_op jit(solution)/shard_map/ppermute | solution.py:30
  110.9 0.0 copy-start.1
  110.9 4.4 %collective-permute-done.5.right_ref = f32[3,64,1600]{2,1,0:T(8,128)S(1)} collective-permute-done((f32[3,64,1600]{2,1,0:T(8,128)S(1)}, f32[3,64,1600]{2,1,0:T(8,128)S(1)}, u32[]{:S(2)}, u32[]{:S(2)}) %collective-permute-start.5) | collective-permute-done | bytes 1228832 | tf_op jit(solution)/shard_map/ppermute | solution.py:30
  115.3 0.0 copy-done.1
  115.3 1.1 copy-done.2
  116.3 9.1 %shard_map.65 = (f32[64,2240]{1,0:T(8,128)}, f32[2,64,2240]{2,1,0:T(8,128)}) custom-call(f32[3,64,1600]{2,1,0:T(8,128)} %bitcast.36, f32[3,64,1600]{2,1,0:T(8,128)} %copy-done.1, f32[3,64,1600]{2,1,0:T(8,128)} %copy-done.2), custom_call_target="tpu_custom_call" | custom-call | tf_op jit(solution)/shard_map/pallas_call | solution.py:182
  125.4 1.3 slice_bitcast_fusion
  126.8 1.3 collective-permute-start.6
  128.1 1.3 collective-permute-start.7
  129.4 11.8 %collective-permute-done.6.up_ref = f32[64,2240]{1,0:T(8,128)S(1)} collective-permute-done((f32[64,2240]{1,0:T(8,128)S(1)}, f32[64,2240]{1,0:T(8,128)S(1)}, u32[]{:S(2)}, u32[]{:S(2)}) %collective-permute-start.6) | collective-permute-done | bytes 573472 | tf_op jit(solution)/shard_map/ppermute | solution.py:30
  141.2 0.0 collective-permute-done.7.down_ref
  141.2 0.8 copy-done.3
  142.0 0.2 copy-done.4
  142.2 2.8 %shard_map.66 = bf16[64,3136]{1,0:T(8,128)(2,1)} custom-call(f32[64,2240]{1,0:T(8,128)} %get-tuple-element.11.keep_ref, f32[64,2240]{1,0:T(8,128)} %copy-done.3, f32[64,2240]{1,0:T(8,128)} %copy-done.4), custom_call_target="tpu_custom_call" | custom-call | tf_op jit(solution)/shard_map/pallas_call | solution.py:193
  (10 shorter events, 0.2 us)
Async XLA Ops:
  3.3 5.9 %copy-start = (bf16[4,4,64,256]{3,2,1,0:T(8,128)(2,1)S(1)}, bf16[4,4,64,256]{3,2,1,0:T(8,128)(2,1)}, u32[]{:S(2)}) copy-start(bf16[4,4,64,256]{3,2,1,0:T(8,128)(2,1)} %param.9) | copy-start | bytes 1572868
  3.5 6.1 %copy-start.7 = (s32[4,4]{1,0:T(4,128)S(1)}, s32[4,4]{1,0:T(4,128)}, u32[]{:S(2)}) copy-start(s32[4,4]{1,0:T(4,128)} %param.11) | copy-start | bytes 196
  3.5 6.2 %copy-start.6 = (s32[4,4,9]{2,1,0:T(4,128)S(1)}, s32[4,4,9]{2,1,0:T(4,128)}, u32[]{:S(2)}) copy-start(s32[4,4,9]{2,1,0:T(4,128)} %param.7) | copy-start | bytes 1732
  3.7 62.8 %collective-permute-start = (bf16[1,4,64,256]{3,2,1,0:T(8,128)(2,1)S(1)}, bf16[1,4,64,256]{3,2,1,0:T(8,128)(2,1)S(1)}, u32[]{:S(2)}, u32[]{:S(2)}) collective-permute-start(bf16[1,4,64,256]{3,2,1,0:T(8,128)(2,1)S(1)} %slice.31), channel_id=1, source_target_pairs={{0,4},{1,5},{2,6},{3,7},{4,8},{5,9},{6,10},{7,11},{8,12},{9,13},{1... | collective-permute-start | bytes 393224 | tf_op jit(solution)/shard_map/ppermute | solution.py:30
  7.9 58.7 %collective-permute-start.1 = (bf16[1,4,64,256]{3,2,1,0:T(8,128)(2,1)S(1)}, bf16[1,4,64,256]{3,2,1,0:T(8,128)(2,1)S(1)}, u32[]{:S(2)}, u32[]{:S(2)}) collective-permute-start(bf16[1,4,64,256]{3,2,1,0:T(8,128)(2,1)S(1)} %slice.33), channel_id=1, source_target_pairs={{4,0},{5,1},{6,2},{7,3},{8,4},{9,5},{10,6},{11,7},{12,8},{13,9},{1... | collective-permute-start | bytes 393224 | tf_op jit(solution)/shard_map/ppermute | solution.py:30
  9.2 0.9 copy-start.5
  64.6 0.9 copy-start.8
  66.6 4.9 %collective-permute-start.2 = (bf16[6,1,64,256]{3,2,1,0:T(8,128)(2,1)S(1)}, bf16[6,1,64,256]{3,2,1,0:T(8,128)(2,1)S(1)}, u32[]{:S(2)}, u32[]{:S(2)}) collective-permute-start(bf16[6,1,64,256]{3,2,1,0:T(8,128)(2,1)S(1)} %get-tuple-element.19), channel_id=1, source_target_pairs={{0,1},{1,2},{2,3},{4,5},{5,6},{6,7},{8,9},{9,10},{10,11},{12,13},{... | collective-permute-start | bytes 589832 | tf_op jit(solution)/shard_map/ppermute | solution.py:30
  68.6 7.0 %collective-permute-start.3 = (bf16[6,1,64,256]{3,2,1,0:T(8,128)(2,1)S(1)}, bf16[6,1,64,256]{3,2,1,0:T(8,128)(2,1)S(1)}, u32[]{:S(2)}, u32[]{:S(2)}) collective-permute-start(bf16[6,1,64,256]{3,2,1,0:T(8,128)(2,1)S(1)} %get-tuple-element.20), channel_id=1, source_target_pairs={{1,0},{2,1},{3,2},{5,4},{6,5},{7,6},{9,8},{10,9},{11,10},{13,12},{... | collective-permute-start | bytes 589832 | tf_op jit(solution)/shard_map/ppermute | solution.py:30
  94.8 16.1 %collective-permute-start.4 = (f32[3,64,1600]{2,1,0:T(8,128)S(1)}, f32[3,64,1600]{2,1,0:T(8,128)S(1)}, u32[]{:S(2)}, u32[]{:S(2)}) collective-permute-start(f32[3,64,1600]{2,1,0:T(8,128)S(1)} %bitcast.35), channel_id=1, source_target_pairs={{0,1},{1,2},{2,3},{4,5},{5,6},{6,7},{8,9},{9,10},{10,11},{12,13},{... | collective-permute-start | bytes 3686408 | tf_op jit(solution)/shard_map/ppermute | solution.py:30
  96.7 18.6 %collective-permute-start.5 = (f32[3,64,1600]{2,1,0:T(8,128)S(1)}, f32[3,64,1600]{2,1,0:T(8,128)S(1)}, u32[]{:S(2)}, u32[]{:S(2)}) collective-permute-start(f32[3,64,1600]{2,1,0:T(8,128)S(1)} %bitcast.34), channel_id=1, source_target_pairs={{1,0},{2,1},{3,2},{5,4},{6,5},{7,6},{9,8},{10,9},{11,10},{13,12},{... | collective-permute-start | bytes 3686408 | tf_op jit(solution)/shard_map/ppermute | solution.py:30
  110.9 4.4 %copy-start.1 = (f32[3,64,1600]{2,1,0:T(8,128)}, f32[3,64,1600]{2,1,0:T(8,128)S(1)}, u32[]{:S(2)}) copy-start(f32[3,64,1600]{2,1,0:T(8,128)S(1)} %collective-permute-done.4.left_ref) | copy-start | bytes 3686404
  115.3 1.1 copy-start.2
  126.8 14.4 %collective-permute-start.6 = (f32[64,2240]{1,0:T(8,128)S(1)}, f32[64,2240]{1,0:T(8,128)S(1)}, u32[]{:S(2)}, u32[]{:S(2)}) collective-permute-start(f32[64,2240]{1,0:T(8,128)S(1)} %get-tuple-element.16), channel_id=1, source_target_pairs={{0,4},{1,5},{2,6},{3,7},{4,8},{5,9},{6,10},{7,11},{8,12},{9,13},{1... | collective-permute-start | bytes 1720328 | tf_op jit(solution)/shard_map/ppermute | solution.py:30
  128.1 13.1 %collective-permute-start.7 = (f32[64,2240]{1,0:T(8,128)S(1)}, f32[64,2240]{1,0:T(8,128)S(1)}, u32[]{:S(2)}, u32[]{:S(2)}) collective-permute-start(f32[64,2240]{1,0:T(8,128)S(1)} %get-tuple-element.15), channel_id=1, source_target_pairs={{4,0},{5,1},{6,2},{7,3},{8,4},{9,5},{10,6},{11,7},{12,8},{13,9},{1... | collective-permute-start | bytes 1720328 | tf_op jit(solution)/shard_map/ppermute | solution.py:30
  141.2 0.8 copy-start.3
  141.2 1.0 copy-start.4

commit v2 on v1

--- a/solution.py
+++ b/solution.py
@@ -30,7 +30,8 @@
     return lax.ppermute(value, ("row", "col"), pairs)
 
 
-def galerkin_kernel(pos_ref, slot_ref, a_ref, p_ref, dpt_ref, keep_ref, send_ref, acc_ref, prod_ref):
+def galerkin_kernel(pos_ref, slot_ref, home_ref, a_ref, p_ref, own_ref, keep_ref, send_ref,
+                    acc_ref, prod_ref, dp_ref):
     patches = a_ref.shape[0]
 
     def one_patch(i, carry):
@@ -45,15 +46,23 @@
         row = pl.multiple_of(i * B, B)
         for w in range(WIN * WIN):
             prod_ref[pl.ds(row, B), w * B:(w + 1) * B] = acc_ref[w].astype(jnp.bfloat16)
+        for p in range(KP):
+            h = home_ref[i * KP + p]
+            dp_ref[h, pl.ds(row, B), :] = dp_ref[h, pl.ds(row, B), :] + own_ref[i, :, p * B:(p + 1) * B].astype(jnp.float32)
         return carry
 
+    dp_ref[...] = jnp.zeros(dp_ref.shape, jnp.float32)
     lax.fori_loop(0, patches, one_patch, 0)
-    rows = HOME * B
-    keep_ref[...] = jnp.dot(dpt_ref[rows:2 * rows], prod_ref[...], preferred_element_type=jnp.float32)
-    for side, start in ((0, 0), (1, 2 * rows)):
-        send_ref[side] = jnp.dot(
-            dpt_ref[start:start + rows], prod_ref[...], preferred_element_type=jnp.float32
-        ).astype(send_ref.dtype)
+    prod = prod_ref[...]
+    dims = (((0,), (0,)), ((), ()))
+
+    def coarse_terms(h):
+        return lax.dot_general(dp_ref[h].astype(jnp.bfloat16), prod, dims, preferred_element_type=jnp.float32)
+
+    for dr in range(HOME):
+        keep_ref[dr] = coarse_terms(HOME + dr)
+        send_ref[0, dr] = coarse_terms(dr).astype(send_ref.dtype)
+        send_ref[1, dr] = coarse_terms(2 * HOME + dr).astype(send_ref.dtype)
 
 
 def fold_cols_kernel(keep_ref, left_ref, right_ref, keep_out, send_out):
@@ -112,41 +121,48 @@
         kept, prolong_blocks.reshape(tile_rows, tile_cols, B, KP, B), jnp.zeros((), jnp.bfloat16)
     ).reshape(tile_rows, tile_cols, B, KP * B)
 
+    own_codes = prolong_columns.reshape(patches, KP)
+    hrow = jnp.clip(own_codes // coarse_grid_cols - row_index + 1, 0, HOME - 1)
+    hcol = jnp.clip(own_codes % coarse_grid_cols - col_index + 1, 0, HOME - 1)
+    rel = (hrow * HOME + hcol).reshape(tile_rows, tile_cols, KP)
+
+    def payload(p_part, rel_part):
+        count = p_part.shape[0]
+        flat = p_part.reshape(count * B, KP * B)
+        extra = jnp.zeros((16, KP * B), jnp.bfloat16)
+        extra = extra.at[0, :count * KP].set(rel_part.reshape(-1).astype(jnp.bfloat16))
+        return jnp.concatenate([flat, extra], axis=0)
+
+    def unpack(got, count):
+        p_part = got[:count * B].reshape(count, B, KP * B)
+        rel_part = got[count * B, :count * KP].astype(jnp.int32).reshape(count, KP)
+        return p_part, rel_part
+
     hr, hc = tile_rows + 2, tile_cols + 2
-    from_above = shifted(prolong[tile_rows - 1:], 1, 0)
-    from_below = shifted(prolong[:1], -1, 0)
-    tall = jnp.concatenate([from_above, prolong, from_below], axis=0)
-    from_left = shifted(tall[:, tile_cols - 1:], 0, 1)
-    from_right = shifted(tall[:, :1], 0, -1)
-    near_p = jnp.concatenate([from_left, tall, from_right], axis=1).reshape(hr * hc, B, KP * B)
-
-    all_codes = lax.all_gather(prolong_columns, ("row", "col"), axis=0, tiled=False)
-    rows_n, cols_n = lax.axis_size("row"), lax.axis_size("col")
-    all_codes = all_codes.reshape(rows_n, cols_n, tile_rows, tile_cols, KP)
-    all_codes = all_codes.transpose(0, 2, 1, 3, 4).reshape(rows_n * tile_rows * cols_n * tile_cols, KP)
+    above, above_rel = unpack(shifted(payload(prolong[tile_rows - 1], rel[tile_rows - 1]), 1, 0), tile_cols)
+    below, below_rel = unpack(shifted(payload(prolong[0], rel[0]), -1, 0), tile_cols)
+    tall = jnp.concatenate([above[None], prolong, below[None]], axis=0)
+    tall_rel = jnp.concatenate([above_rel[None], rel, below_rel[None]], axis=0)
+    left, left_rel = unpack(shifted(payload(tall[:, tile_cols - 1], tall_rel[:, tile_cols - 1]), 0, 1), hr)
+    right, right_rel = unpack(shifted(payload(tall[:, 0], tall_rel[:, 0]), 0, -1), hr)
+    near_p = jnp.concatenate([left[:, None], tall, right[:, None]], axis=1).reshape(hr * hc, B, KP * B)
+    near_rel = jnp.concatenate([left_rel[:, None], tall_rel, right_rel[:, None]], axis=1)
+
+    off_r = (jnp.arange(hr, dtype=jnp.int32) + tile_rows - 1) // tile_rows - 1
+    off_c = (jnp.arange(hc, dtype=jnp.int32) + tile_cols - 1) // tile_cols - 1
+    near_slot = (near_rel // HOME + off_r[:, None, None] + 1) * WIN + near_rel % HOME + off_c[None, :, None] + 1
+    near_slot = near_slot.reshape(hr * hc, KP)
 
     first_row = row_index * tile_rows
     first_col = col_index * tile_cols
     targets = fine_columns.reshape(patches, KA)
     pos = (targets // grid_cols - first_row + 1) * hc + targets % grid_cols - first_col + 1
     pos = jnp.clip(pos, 0, hr * hc - 1)
-    codes = all_codes[jnp.clip(targets, 0, all_codes.shape[0] - 1)]
-    srow = jnp.clip(codes // coarse_grid_cols - row_index + 2, 0, WIN - 1)
-    scol = jnp.clip(codes % coarse_grid_cols - col_index + 2, 0, WIN - 1)
-    slot = srow * WIN + scol
+    slot = near_slot[pos]
     blocks = jnp.arange(KA, dtype=jnp.int32)
     used = blocks[None, :] < fine_counts.reshape(patches)[:, None]
     slot = jnp.where(used[:, :, None], slot, TRASH)
-
-    own_codes = prolong_columns.reshape(patches, KP)
-    hrow = jnp.clip(own_codes // coarse_grid_cols - row_index + 1, 0, HOME - 1)
-    hcol = jnp.clip(own_codes % coarse_grid_cols - col_index + 1, 0, HOME - 1)
     home = hcol * HOME + hrow
-    spread = (home[..., None] == jnp.arange(HOME * HOME, dtype=jnp.int32)).astype(jnp.bfloat16)
-    dpt = jnp.einsum(
-        "iph,ibpa->haib", spread, prolong.reshape(patches, B, KP, B),
-        preferred_element_type=jnp.float32,
-    ).astype(jnp.bfloat16).reshape(HOME * HOME * B, patches * B)
 
     smem = pltpu.MemorySpace.SMEM
     vmem = pltpu.MemorySpace.VMEM
@@ -154,10 +170,11 @@
     keep, send = pl.pallas_call(
         galerkin_kernel,
         out_shape=(
-            jax.ShapeDtypeStruct((HOME * B, width), jnp.float32),
-            jax.ShapeDtypeStruct((2, HOME * B, width), SEND),
+            jax.ShapeDtypeStruct((HOME, B, width), jnp.float32),
+            jax.ShapeDtypeStruct((2, HOME, B, width), SEND),
         ),
         in_specs=[
+            pl.BlockSpec(memory_space=smem),
             pl.BlockSpec(memory_space=smem),
             pl.BlockSpec(memory_space=smem),
             pl.BlockSpec(memory_space=vmem),
@@ -168,16 +185,18 @@
         scratch_shapes=[
             pltpu.VMEM((TRASH + 1, B, B), jnp.float32),
             pltpu.VMEM((patches * B, width), jnp.bfloat16),
+            pltpu.VMEM((HOME * HOME, patches * B, B), jnp.float32),
         ],
     )(
         pos.reshape(-1).astype(jnp.int32),
         slot.reshape(-1).astype(jnp.int32),
+        home.reshape(-1).astype(jnp.int32),
         fine_blocks.reshape(patches, B, KA * B),
         near_p,
-        dpt,
+        prolong.reshape(patches, B, KP * B),
     )
-    left_in = shifted(send[1].reshape(HOME, B, width), 0, 1)
-    right_in = shifted(send[0].reshape(HOME, B, width), 0, -1)
+    left_in = shifted(send[1], 0, 1)
+    right_in = shifted(send[0], 0, -1)
     band = WIN * OUTW * B
     keep2, send2 = pl.pallas_call(
         fold_cols_kernel,
@@ -187,7 +206,7 @@
         ),
         in_specs=[pl.BlockSpec(memory_space=vmem)] * 3,
         out_specs=(pl.BlockSpec(memory_space=vmem), pl.BlockSpec(memory_space=vmem)),
-    )(keep.reshape(HOME, B, width), left_in, right_in)
+    )(keep, left_in, right_in)
     up_in = shifted(send2[1], 1, 0)
     down_in = shifted(send2[0], -1, 0)
     out = pl.pallas_call(

time: 145 us -> 108 us (0.74)
  the two profiles are of different devices: /device:TPU:1 before, /device:TPU:20 now
where the time goes in v2:
time: 108 us; the launch traced here: 107 us
  waiting for transfers between devices  34.1 us (32%)
  Pallas kernels  30.9 us (29%)
  starting transfers between devices  23.5 us (22%)
  local copies, waits for them, and re-layouts  13.2 us (12%)
  other arithmetic  5.09 us (5%)
    ppermute x8, waiting for transfers between devices, shifted(): return lax.ppermute(value, ('row', 'col'), pairs)  34.1 us
    ppermute x8, starting transfers between devices, shifted(): return lax.ppermute(value, ('row', 'col'), pairs)  23.5 us
    pallas_call x1, Pallas kernels, per_device(): pl.pallas_call(galerkin_kernel, out_shape=(jax.ShapeDtypeStruct((HOME, B,...  18.9 us
    pallas_call x1, Pallas kernels, per_device(): pl.pallas_call(fold_cols_kernel, out_shape=(jax.ShapeDtypeStruct((B, band...  9.17 us
    pallas_call x1, Pallas kernels, per_device(): pl.pallas_call(fold_rows_kernel, out_shape=jax.ShapeDtypeStruct((B, OUTW...  2.76 us
    unnamed x17, local copies, waits for them, and re-layouts  2.23 us
  transfers between devices with their start and end apart: 8, of which 6 were waited for; matrix products, arithmetic and copies ran while one was open for 4% of the time, Pallas kernels for 0%

profile of v2, /device:TPU:20, one launch (start us, length us, event | category | flops | bytes accessed | tf_op | source)
XLA Modules:
  0.0 107.0 jit_solution(3299773336821579310)
XLA Ops:
  0.0 0.8 iota_compare_fusion.2
  0.8 0.8 copy.46
  1.6 0.1 copy.31
  1.7 0.1 convert_element_type.89
  1.8 2.0 %reshape.431 = bf16[4,4,64,4,64]{4,3,2,1,0:T(4,128)(2,1)S(1)} reshape(bf16[4,4,64,256]{3,2,1,0:T(8,128)(2,1)} %param.17) | data formatting | bytes 1048576 | tf_op jit(solution)/shard_map/reshape | solution.py:121
  3.9 0.5 broadcast_select_fusion
  4.4 0.2 fusion.57
  4.6 0.2 reshape_squeeze.17
  4.9 3.3 %collective-permute-start.1 = (bf16[272,256]{1,0:T(8,128)(2,1)S(1)}, bf16[272,256]{1,0:T(8,128)(2,1)S(1)}, u32[]{:S(2)}, u32[]{:S(2)}) collective-permute-start(bf16[272,256]{1,0:T(8,128)(2,1)S(1)} %fusion.7), channel_id=1, source_target_pairs={{4,0},{5,1},{6,2},{7,3},{8,4},{9,5},{10,6},{11,7},{12,8},{13,9},{1... | collective-permute-start | bytes 417800 | tf_op jit(solution)/shard_map/ppermute | solution.py:30
  8.1 0.1 copy.30
  8.3 0.1 convert_element_type.88
  8.3 0.2 reshape_squeeze.16
  8.6 2.6 %collective-permute-start = (bf16[272,256]{1,0:T(8,128)(2,1)S(1)}, bf16[272,256]{1,0:T(8,128)(2,1)S(1)}, u32[]{:S(2)}, u32[]{:S(2)}) collective-permute-start(bf16[272,256]{1,0:T(8,128)(2,1)S(1)} %fusion.6), channel_id=1, source_target_pairs={{0,4},{1,5},{2,6},{3,7},{4,8},{5,9},{6,10},{7,11},{8,12},{9,13},{1... | collective-permute-start | bytes 417800 | tf_op jit(solution)/shard_map/ppermute | solution.py:30
  11.2 0.1 reshape.434
  11.3 0.1 broadcast_in_dim.49
  11.3 0.1 broadcast_in_dim.54
  11.4 0.1 broadcast_in_dim.50
  11.5 0.1 copy.32
  11.6 0.1 lt.73
  11.7 0.1 reshape.430
  11.9 0.1 add.238
  12.1 0.1 add.231
  12.1 0.6 add_clamp_fusion.pos_ref
  12.8 0.1 reshape.445
  13.0 0.9 bitcast_select_fusion.own_ref
  13.8 0.6 fusion.51.home_ref
  14.4 2.1 %collective-permute-done = bf16[272,256]{1,0:T(8,128)(2,1)S(1)} collective-permute-done((bf16[272,256]{1,0:T(8,128)(2,1)S(1)}, bf16[272,256]{1,0:T(8,128)(2,1)S(1)}, u32[]{:S(2)}, u32[]{:S(2)}) %collective-permute-start) | collective-permute-done | bytes 139296 | tf_op jit(solution)/shard_map/ppermute | solution.py:30
  16.5 0.1 reshape.440
  16.6 0.1 copy.37
  16.7 0.1 reshape.439
  16.8 0.1 copy.36
  16.9 0.1 slice_reduce_fusion.1
  17.1 0.1 convert_element_type.94
  17.1 0.1 convert_element_type.97
  17.4 1.9 %collective-permute-start.2 = (bf16[400,256]{1,0:T(8,128)(2,1)S(1)}, bf16[400,256]{1,0:T(8,128)(2,1)S(1)}, u32[]{:S(2)}, u32[]{:S(2)}) collective-permute-start(bf16[400,256]{1,0:T(8,128)(2,1)S(1)} %fusion.4), channel_id=1, source_target_pairs={{0,1},{1,2},{2,3},{4,5},{5,6},{6,7},{8,9},{9,10},{10,11},{12,13},{... | collective-permute-start | bytes 614408 | tf_op jit(solution)/shard_map/ppermute | solution.py:30
  19.3 3.6 %collective-permute-start.3 = (bf16[400,256]{1,0:T(8,128)(2,1)S(1)}, bf16[400,256]{1,0:T(8,128)(2,1)S(1)}, u32[]{:S(2)}, u32[]{:S(2)}) collective-permute-start(bf16[400,256]{1,0:T(8,128)(2,1)S(1)} %fusion.5), channel_id=1, source_target_pairs={{1,0},{2,1},{3,2},{5,4},{6,5},{7,6},{9,8},{10,9},{11,10},{13,12},{... | collective-permute-start | bytes 614408 | tf_op jit(solution)/shard_map/ppermute | solution.py:30
  23.0 1.5 %collective-permute-done.2 = bf16[400,256]{1,0:T(8,128)(2,1)S(1)} collective-permute-done((bf16[400,256]{1,0:T(8,128)(2,1)S(1)}, bf16[400,256]{1,0:T(8,128)(2,1)S(1)}, u32[]{:S(2)}, u32[]{:S(2)}) %collective-permute-start.2) | collective-permute-done | bytes 204832 | tf_op jit(solution)/shard_map/ppermute | solution.py:30
  24.5 0.1 reshape.452
  24.6 1.7 %collective-permute-done.3 = bf16[400,256]{1,0:T(8,128)(2,1)S(1)} collective-permute-done((bf16[400,256]{1,0:T(8,128)(2,1)S(1)}, bf16[400,256]{1,0:T(8,128)(2,1)S(1)}, u32[]{:S(2)}, u32[]{:S(2)}) %collective-permute-start.3) | collective-permute-done | bytes 204832 | tf_op jit(solution)/shard_map/ppermute | solution.py:30
  26.2 0.1 reshape.453
  26.3 0.1 sign_compare_fusion
  26.5 0.1 ne.169
  26.7 0.1 div.89
  26.8 0.1 copy.43
  26.9 0.7 gather_fusion
  27.6 0.1 reshape.444
  27.7 0.2 copy.45
  27.9 0.7 select_n.127.slot_ref
  28.7 1.2 %pad_maximum_fusion = bf16[6,6,64,256]{3,2,1,0:T(8,128)(2,1)} fusion(bf16[6,1,64,256]{3,2,1,0:T(8,128)(2,1)S(1)} %bitcast.41, bf16[1,4,64,256]{3,2,1,0:T(8,128)(2,1)S(1)} %bitcast.36, bf16[4,4,64,256]{3,2,1,0:T(8,128)(2,1)S(1)} %broadcast_select_fusion.1, bf16[1,4,64,256]{3,2,1,0:T(8,128)(2,1)S(1)} %bitcast.38, bf16[6,1,64,256]{3,2,1,0:T(8,128)(2,1)S(1)} %bitcast.40), kind=kLoop, calls=%fused_computation.3 | loop fusion | flops 2359296 | bytes 2359296 | tf_op jit(solution)/shard_map/concatenate | solution.py:148
  29.9 18.9 %shard_map.64 = (f32[3,64,1600]{2,1,0:T(8,128)}, f32[2,3,64,1600]{3,2,1,0:T(8,128)}) custom-call(s32[144]{0:T(256)} %add_clamp_fusion.pos_ref, s32[576]{0:T(1024)} %select_n.127.slot_ref, s32[64]{0:T(128)} %fusion.51.home_ref, bf16[16,64,576]{2,1,0:T(8,128)(2,1)} %bitcast.34, bf16[36,64,256]{2,1,0:T(8,128)(2,1)} %bitcast.33, ...), custom_call_target="tpu_custom_call" | custom-call | tf_op jit(solution)/shard_map/pallas_call | solution.py:170
  48.8 1.9 %slice_bitcast_fusion = (f32[3,64,1600]{2,1,0:T(8,128)S(1)}, f32[3,64,1600]{2,1,0:T(8,128)S(1)}) fusion(f32[2,3,64,1600]{3,2,1,0:T(8,128)} %get-tuple-element.58), kind=kLoop, calls=%fused_computation.1 | loop fusion | bytes 4915200 | tf_op jit(solution)/shard_map/squeeze | solution.py:199
  50.7 4.3 %collective-permute-start.5 = (f32[3,64,1600]{2,1,0:T(8,128)S(1)}, f32[3,64,1600]{2,1,0:T(8,128)S(1)}, u32[]{:S(2)}, u32[]{:S(2)}) collective-permute-start(f32[3,64,1600]{2,1,0:T(8,128)S(1)} %get-tuple-element.65), channel_id=1, source_target_pairs={{1,0},{2,1},{3,2},{5,4},{6,5},{7,6},{9,8},{10,9},{11,10},{13,12},{... | collective-permute-start | bytes 3686408 | tf_op jit(solution)/shard_map/ppermute | solution.py:30
  55.0 1.9 %collective-permute-start.4 = (f32[3,64,1600]{2,1,0:T(8,128)S(1)}, f32[3,64,1600]{2,1,0:T(8,128)S(1)}, u32[]{:S(2)}, u32[]{:S(2)}) collective-permute-start(f32[3,64,1600]{2,1,0:T(8,128)S(1)} %get-tuple-element.66), channel_id=1, source_target_pairs={{0,1},{1,2},{2,3},{4,5},{5,6},{6,7},{8,9},{9,10},{10,11},{12,13},{... | collective-permute-start | bytes 3686408 | tf_op jit(solution)/shard_map/ppermute | solution.py:30
  56.9 12.8 %collective-permute-done.5.right_ref = f32[3,64,1600]{2,1,0:T(8,128)S(1)} collective-permute-done((f32[3,64,1600]{2,1,0:T(8,128)S(1)}, f32[3,64,1600]{2,1,0:T(8,128)S(1)}, u32[]{:S(2)}, u32[]{:S(2)}) %collective-permute-start.5) | collective-permute-done | bytes 1228832 | tf_op jit(solution)/shard_map/ppermute | solution.py:30
  69.7 3.8 %collective-permute-done.4.left_ref = f32[3,64,1600]{2,1,0:T(8,128)S(1)} collective-permute-done((f32[3,64,1600]{2,1,0:T(8,128)S(1)}, f32[3,64,1600]{2,1,0:T(8,128)S(1)}, u32[]{:S(2)}, u32[]{:S(2)}) %collective-permute-start.4) | collective-permute-done | bytes 1228832 | tf_op jit(solution)/shard_map/ppermute | solution.py:30
  73.6 1.1 copy-done.2
  74.6 9.2 %shard_map.65 = (f32[64,2240]{1,0:T(8,128)}, f32[2,64,2240]{2,1,0:T(8,128)}) custom-call(f32[3,64,1600]{2,1,0:T(8,128)} %get-tuple-element.57.keep_ref, f32[3,64,1600]{2,1,0:T(8,128)} %copy-done.2, f32[3,64,1600]{2,1,0:T(8,128)} %copy-done.1), custom_call_target="tpu_custom_call" | custom-call | tf_op jit(solution)/shard_map/pallas_call | solution.py:201
  83.8 1.3 %slice_bitcast_fusion.2 = (f32[64,2240]{1,0:T(8,128)S(1)}, f32[64,2240]{1,0:T(8,128)S(1)}) fusion(f32[2,64,2240]{2,1,0:T(8,128)} %get-tuple-element.60), kind=kLoop, calls=%fused_computation.5 | loop fusion | bytes 2293760 | tf_op jit(solution)/shard_map/squeeze | solution.py:211
  85.1 2.5 %collective-permute-start.7 = (f32[64,2240]{1,0:T(8,128)S(1)}, f32[64,2240]{1,0:T(8,128)S(1)}, u32[]{:S(2)}, u32[]{:S(2)}) collective-permute-start(f32[64,2240]{1,0:T(8,128)S(1)} %get-tuple-element.67), channel_id=1, source_target_pairs={{4,0},{5,1},{6,2},{7,3},{8,4},{9,5},{10,6},{11,7},{12,8},{13,9},{1... | collective-permute-start | bytes 1720328 | tf_op jit(solution)/shard_map/ppermute | solution.py:30
  87.6 3.4 %collective-permute-start.6 = (f32[64,2240]{1,0:T(8,128)S(1)}, f32[64,2240]{1,0:T(8,128)S(1)}, u32[]{:S(2)}, u32[]{:S(2)}) collective-permute-start(f32[64,2240]{1,0:T(8,128)S(1)} %get-tuple-element.68), channel_id=1, source_target_pairs={{0,4},{1,5},{2,6},{3,7},{4,8},{5,9},{6,10},{7,11},{8,12},{9,13},{1... | collective-permute-start | bytes 1720328 | tf_op jit(solution)/shard_map/ppermute | solution.py:30
  91.0 12.2 %collective-permute-done.7.down_ref = f32[64,2240]{1,0:T(8,128)S(1)} collective-permute-done((f32[64,2240]{1,0:T(8,128)S(1)}, f32[64,2240]{1,0:T(8,128)S(1)}, u32[]{:S(2)}, u32[]{:S(2)}) %collective-permute-start.7) | collective-permute-done | bytes 573472 | tf_op jit(solution)/shard_map/ppermute | solution.py:30
  103.2 0.8 copy-done.3
  104.0 0.2 copy-done.4
  104.3 2.8 %shard_map.66 = bf16[64,3136]{1,0:T(8,128)(2,1)} custom-call(f32[64,2240]{1,0:T(8,128)} %get-tuple-element.59.keep_ref, f32[64,2240]{1,0:T(8,128)} %copy-done.4, f32[64,2240]{1,0:T(8,128)} %copy-done.3), custom_call_target="tpu_custom_call" | custom-call | tf_op jit(solution)/shard_map/pallas_call | solution.py:212
  (46 shorter events, 0.8 us)
Async XLA Ops:
  4.4 6.8 %copy-start.5 = (s32[4,4,4]{2,1,0:T(4,128)S(1)}, s32[4,4,4]{2,1,0:T(4,128)}, u32[]{:S(2)}) copy-start(s32[4,4,4]{2,1,0:T(4,128)} %param.18) | copy-start | bytes 772
  4.4 7.3 %copy-start.7 = (s32[4,4]{1,0:T(4,128)S(1)}, s32[4,4]{1,0:T(4,128)}, u32[]{:S(2)}) copy-start(s32[4,4]{1,0:T(4,128)} %param.16) | copy-start | bytes 196
  4.4 7.3 %copy-start.6 = (s32[4,4,9]{2,1,0:T(4,128)S(1)}, s32[4,4,9]{2,1,0:T(4,128)}, u32[]{:S(2)}) copy-start(s32[4,4,9]{2,1,0:T(4,128)} %param.15) | copy-start | bytes 1732
  4.4 8.5 %copy-start = (bf16[4,4,64,256]{3,2,1,0:T(8,128)(2,1)S(1)}, bf16[4,4,64,256]{3,2,1,0:T(8,128)(2,1)}, u32[]{:S(2)}) copy-start(bf16[4,4,64,256]{3,2,1,0:T(8,128)(2,1)} %param.17) | copy-start | bytes 1572868
  4.9 9.6 %collective-permute-start.1 = (bf16[272,256]{1,0:T(8,128)(2,1)S(1)}, bf16[272,256]{1,0:T(8,128)(2,1)S(1)}, u32[]{:S(2)}, u32[]{:S(2)}) collective-permute-start(bf16[272,256]{1,0:T(8,128)(2,1)S(1)} %fusion.7), channel_id=1, source_target_pairs={{4,0},{5,1},{6,2},{7,3},{8,4},{9,5},{10,6},{11,7},{12,8},{13,9},{1... | collective-permute-start | bytes 417800 | tf_op jit(solution)/shard_map/ppermute | solution.py:30
  8.6 7.9 %collective-permute-start = (bf16[272,256]{1,0:T(8,128)(2,1)S(1)}, bf16[272,256]{1,0:T(8,128)(2,1)S(1)}, u32[]{:S(2)}, u32[]{:S(2)}) collective-permute-start(bf16[272,256]{1,0:T(8,128)(2,1)S(1)} %fusion.6), channel_id=1, source_target_pairs={{0,4},{1,5},{2,6},{3,7},{4,8},{5,9},{6,10},{7,11},{8,12},{9,13},{1... | collective-permute-start | bytes 417800 | tf_op jit(solution)/shard_map/ppermute | solution.py:30
  17.4 7.1 %collective-permute-start.2 = (bf16[400,256]{1,0:T(8,128)(2,1)S(1)}, bf16[400,256]{1,0:T(8,128)(2,1)S(1)}, u32[]{:S(2)}, u32[]{:S(2)}) collective-permute-start(bf16[400,256]{1,0:T(8,128)(2,1)S(1)} %fusion.4), channel_id=1, source_target_pairs={{0,1},{1,2},{2,3},{4,5},{5,6},{6,7},{8,9},{9,10},{10,11},{12,13},{... | collective-permute-start | bytes 614408 | tf_op jit(solution)/shard_map/ppermute | solution.py:30
  19.3 6.9 %collective-permute-start.3 = (bf16[400,256]{1,0:T(8,128)(2,1)S(1)}, bf16[400,256]{1,0:T(8,128)(2,1)S(1)}, u32[]{:S(2)}, u32[]{:S(2)}) collective-permute-start(bf16[400,256]{1,0:T(8,128)(2,1)S(1)} %fusion.5), channel_id=1, source_target_pairs={{1,0},{2,1},{3,2},{5,4},{6,5},{7,6},{9,8},{10,9},{11,10},{13,12},{... | collective-permute-start | bytes 614408 | tf_op jit(solution)/shard_map/ppermute | solution.py:30
  50.7 19.0 %collective-permute-start.5 = (f32[3,64,1600]{2,1,0:T(8,128)S(1)}, f32[3,64,1600]{2,1,0:T(8,128)S(1)}, u32[]{:S(2)}, u32[]{:S(2)}) collective-permute-start(f32[3,64,1600]{2,1,0:T(8,128)S(1)} %get-tuple-element.65), channel_id=1, source_target_pairs={{1,0},{2,1},{3,2},{5,4},{6,5},{7,6},{9,8},{10,9},{11,10},{13,12},{... | collective-permute-start | bytes 3686408 | tf_op jit(solution)/shard_map/ppermute | solution.py:30
  55.0 18.6 %collective-permute-start.4 = (f32[3,64,1600]{2,1,0:T(8,128)S(1)}, f32[3,64,1600]{2,1,0:T(8,128)S(1)}, u32[]{:S(2)}, u32[]{:S(2)}) collective-permute-start(f32[3,64,1600]{2,1,0:T(8,128)S(1)} %get-tuple-element.66), channel_id=1, source_target_pairs={{0,1},{1,2},{2,3},{4,5},{5,6},{6,7},{8,9},{9,10},{10,11},{12,13},{... | collective-permute-start | bytes 3686408 | tf_op jit(solution)/shard_map/ppermute | solution.py:30
  69.7 3.8 %copy-start.1 = (f32[3,64,1600]{2,1,0:T(8,128)}, f32[3,64,1600]{2,1,0:T(8,128)S(1)}, u32[]{:S(2)}) copy-start(f32[3,64,1600]{2,1,0:T(8,128)S(1)} %collective-permute-done.5.right_ref) | copy-start | bytes 3686404
  73.6 1.1 copy-start.2
  85.1 18.1 %collective-permute-start.7 = (f32[64,2240]{1,0:T(8,128)S(1)}, f32[64,2240]{1,0:T(8,128)S(1)}, u32[]{:S(2)}, u32[]{:S(2)}) collective-permute-start(f32[64,2240]{1,0:T(8,128)S(1)} %get-tuple-element.67), channel_id=1, source_target_pairs={{4,0},{5,1},{6,2},{7,3},{8,4},{9,5},{10,6},{11,7},{12,8},{13,9},{1... | collective-permute-start | bytes 1720328 | tf_op jit(solution)/shard_map/ppermute | solution.py:30
  87.6 15.6 %collective-permute-start.6 = (f32[64,2240]{1,0:T(8,128)S(1)}, f32[64,2240]{1,0:T(8,128)S(1)}, u32[]{:S(2)}, u32[]{:S(2)}) collective-permute-start(f32[64,2240]{1,0:T(8,128)S(1)} %get-tuple-element.68), channel_id=1, source_target_pairs={{0,4},{1,5},{2,6},{3,7},{4,8},{5,9},{6,10},{7,11},{8,12},{9,13},{1... | collective-permute-start | bytes 1720328 | tf_op jit(solution)/shard_map/ppermute | solution.py:30
  103.2 0.8 copy-start.3
  103.2 1.0 copy-start.4

commit v3 on v2

--- a/solution.py
+++ b/solution.py
@@ -15,7 +15,7 @@
 HOME = 3
 OUTW = 7
 TRASH = WIN * WIN
-SEND = jnp.float32
+SEND = jnp.bfloat16
 
 
 def shifted(value, by_row, by_col):

time: 108 us -> 92.1 us (0.85)
  waiting for transfers between devices: 34.1 us -> 21.2 us
  Pallas kernels: 30.9 us -> 29.6 us
  local copies, waits for them, and re-layouts: 13.2 us -> 12 us
    ppermute x8, waiting for transfers between devices: 34.1 us -> 21.2 us  [shifted(): return lax.ppermute(value, ('row', 'col'), pairs)]
  transfers between devices with their start and end apart: 8 -> 8, of which waited for: 6 -> 7; matrix products, arithmetic and copies ran while one was open for 4% -> 4% of each run, Pallas kernels for 0% -> 0%
where the time goes in v3:
time: 92.1 us; the launch traced here: 91 us
  Pallas kernels  29.6 us (32%)
  starting transfers between devices  22.9 us (25%)
  waiting for transfers between devices  21.2 us (23%)
  local copies, waits for them, and re-layouts  12 us (13%)
  other arithmetic  4.98 us (5%)
    ppermute x8, starting transfers between devices, shifted(): return lax.ppermute(value, ('row', 'col'), pairs)  22.9 us
    ppermute x8, waiting for transfers between devices, shifted(): return lax.ppermute(value, ('row', 'col'), pairs)  21.2 us
    pallas_call x1, Pallas kernels, per_device(): pl.pallas_call(galerkin_kernel, out_shape=(jax.ShapeDtypeStruct((HOME, B,...  18.9 us
    pallas_call x1, Pallas kernels, per_device(): pl.pallas_call(fold_cols_kernel, out_shape=(jax.ShapeDtypeStruct((B, band...  8.3 us
    pallas_call x1, Pallas kernels, per_device(): pl.pallas_call(fold_rows_kernel, out_shape=jax.ShapeDtypeStruct((B, OUTW...  2.4 us
    reshape x1, local copies, waits for them, and re-layouts, per_device(): prolong_blocks.reshape(tile_rows, tile_cols, B, KP, B)  2.03 us
  transfers between devices with their start and end apart: 8, of which 7 were waited for; matrix products, arithmetic and copies ran while one was open for 4% of the time, Pallas kernels for 0%

profile of v3, /device:TPU:20, one launch (start us, length us, event | category | flops | bytes accessed | tf_op | source)
XLA Modules:
  0.0 91.0 jit_solution(16861626286229826970)
XLA Ops:
  0.0 0.8 iota_compare_fusion.2
  0.8 0.8 copy.46
  1.6 0.1 copy.31
  1.7 0.1 convert_element_type.89
  1.8 2.0 %reshape.431 = bf16[4,4,64,4,64]{4,3,2,1,0:T(4,128)(2,1)S(1)} reshape(bf16[4,4,64,256]{3,2,1,0:T(8,128)(2,1)} %param.17) | data formatting | bytes 1048576 | tf_op jit(solution)/shard_map/reshape | solution.py:121
  3.9 0.5 broadcast_select_fusion
  4.4 0.2 fusion.57
  4.6 0.2 reshape_squeeze.17
  4.9 3.3 %collective-permute-start.1 = (bf16[272,256]{1,0:T(8,128)(2,1)S(1)}, bf16[272,256]{1,0:T(8,128)(2,1)S(1)}, u32[]{:S(2)}, u32[]{:S(2)}) collective-permute-start(bf16[272,256]{1,0:T(8,128)(2,1)S(1)} %fusion.7), channel_id=1, source_target_pairs={{4,0},{5,1},{6,2},{7,3},{8,4},{9,5},{10,6},{11,7},{12,8},{13,9},{1... | collective-permute-start | bytes 417800 | tf_op jit(solution)/shard_map/ppermute | solution.py:30
  8.1 0.1 copy.30
  8.3 0.1 convert_element_type.88
  8.3 0.2 reshape_squeeze.16
  8.6 2.6 %collective-permute-start = (bf16[272,256]{1,0:T(8,128)(2,1)S(1)}, bf16[272,256]{1,0:T(8,128)(2,1)S(1)}, u32[]{:S(2)}, u32[]{:S(2)}) collective-permute-start(bf16[272,256]{1,0:T(8,128)(2,1)S(1)} %fusion.6), channel_id=1, source_target_pairs={{0,4},{1,5},{2,6},{3,7},{4,8},{5,9},{6,10},{7,11},{8,12},{9,13},{1... | collective-permute-start | bytes 417800 | tf_op jit(solution)/shard_map/ppermute | solution.py:30
  11.2 0.1 reshape.434
  11.3 0.1 broadcast_in_dim.49
  11.3 0.1 broadcast_in_dim.54
  11.4 0.1 broadcast_in_dim.50
  11.5 0.1 copy.32
  11.6 0.1 lt.73
  11.7 0.1 reshape.430
  11.9 0.1 add.238
  12.1 0.1 add.231
  12.1 0.6 add_clamp_fusion.pos_ref
  12.8 0.1 reshape.445
  13.0 0.9 bitcast_select_fusion.own_ref
  13.8 0.5 fusion.51.home_ref
  14.3 2.2 %collective-permute-done = bf16[272,256]{1,0:T(8,128)(2,1)S(1)} collective-permute-done((bf16[272,256]{1,0:T(8,128)(2,1)S(1)}, bf16[272,256]{1,0:T(8,128)(2,1)S(1)}, u32[]{:S(2)}, u32[]{:S(2)}) %collective-permute-start) | collective-permute-done | bytes 139296 | tf_op jit(solution)/shard_map/ppermute | solution.py:30
  16.5 0.1 reshape.440
  16.6 0.1 copy.37
  16.7 0.1 reshape.439
  16.8 0.1 copy.36
  16.9 0.1 slice_reduce_fusion.1
  17.1 0.1 convert_element_type.94
  17.1 0.1 convert_element_type.97
  17.4 1.9 %collective-permute-start.2 = (bf16[400,256]{1,0:T(8,128)(2,1)S(1)}, bf16[400,256]{1,0:T(8,128)(2,1)S(1)}, u32[]{:S(2)}, u32[]{:S(2)}) collective-permute-start(bf16[400,256]{1,0:T(8,128)(2,1)S(1)} %fusion.4), channel_id=1, source_target_pairs={{0,1},{1,2},{2,3},{4,5},{5,6},{6,7},{8,9},{9,10},{10,11},{12,13},{... | collective-permute-start | bytes 614408 | tf_op jit(solution)/shard_map/ppermute | solution.py:30
  19.3 3.6 %collective-permute-start.3 = (bf16[400,256]{1,0:T(8,128)(2,1)S(1)}, bf16[400,256]{1,0:T(8,128)(2,1)S(1)}, u32[]{:S(2)}, u32[]{:S(2)}) collective-permute-start(bf16[400,256]{1,0:T(8,128)(2,1)S(1)} %fusion.5), channel_id=1, source_target_pairs={{1,0},{2,1},{3,2},{5,4},{6,5},{7,6},{9,8},{10,9},{11,10},{13,12},{... | collective-permute-start | bytes 614408 | tf_op jit(solution)/shard_map/ppermute | solution.py:30
  23.0 1.5 %collective-permute-done.2 = bf16[400,256]{1,0:T(8,128)(2,1)S(1)} collective-permute-done((bf16[400,256]{1,0:T(8,128)(2,1)S(1)}, bf16[400,256]{1,0:T(8,128)(2,1)S(1)}, u32[]{:S(2)}, u32[]{:S(2)}) %collective-permute-start.2) | collective-permute-done | bytes 204832 | tf_op jit(solution)/shard_map/ppermute | solution.py:30
  24.5 0.1 reshape.452
  24.6 1.7 %collective-permute-done.3 = bf16[400,256]{1,0:T(8,128)(2,1)S(1)} collective-permute-done((bf16[400,256]{1,0:T(8,128)(2,1)S(1)}, bf16[400,256]{1,0:T(8,128)(2,1)S(1)}, u32[]{:S(2)}, u32[]{:S(2)}) %collective-permute-start.3) | collective-permute-done | bytes 204832 | tf_op jit(solution)/shard_map/ppermute | solution.py:30
  26.2 0.1 reshape.453
  26.3 0.1 sign_compare_fusion
  26.5 0.1 ne.169
  26.7 0.1 div.89
  26.8 0.1 copy.43
  26.9 0.7 gather_fusion
  27.6 0.1 reshape.444
  27.7 0.2 copy.45
  27.9 0.7 select_n.127.slot_ref
  28.7 1.2 %pad_maximum_fusion = bf16[6,6,64,256]{3,2,1,0:T(8,128)(2,1)} fusion(bf16[6,1,64,256]{3,2,1,0:T(8,128)(2,1)S(1)} %bitcast.41, bf16[1,4,64,256]{3,2,1,0:T(8,128)(2,1)S(1)} %bitcast.36, bf16[4,4,64,256]{3,2,1,0:T(8,128)(2,1)S(1)} %broadcast_select_fusion.1, bf16[1,4,64,256]{3,2,1,0:T(8,128)(2,1)S(1)} %bitcast.38, bf16[6,1,64,256]{3,2,1,0:T(8,128)(2,1)S(1)} %bitcast.40), kind=kLoop, calls=%fused_computation.1 | loop fusion | flops 2359296 | bytes 2359296 | tf_op jit(solution)/shard_map/concatenate | solution.py:148
  29.9 18.9 %shard_map.64 = (f32[3,64,1600]{2,1,0:T(8,128)}, bf16[2,3,64,1600]{3,2,1,0:T(8,128)(2,1)}) custom-call(s32[144]{0:T(256)} %add_clamp_fusion.pos_ref, s32[576]{0:T(1024)} %select_n.127.slot_ref, s32[64]{0:T(128)} %fusion.51.home_ref, bf16[16,64,576]{2,1,0:T(8,128)(2,1)} %bitcast.34, bf16[36,64,256]{2,1,0:T(8,128)(2,1)} %bitcast.33, ...), custom_call_target="tpu_custom_call" | custom-call | tf_op jit(solution)/shard_map/pallas_call | solution.py:170
  48.8 1.4 %slice_bitcast_fusion = (bf16[3,64,1600]{2,1,0:T(8,128)(2,1)S(1)}, bf16[3,64,1600]{2,1,0:T(8,128)(2,1)S(1)}) fusion(bf16[2,3,64,1600]{3,2,1,0:T(8,128)(2,1)} %get-tuple-element.58), kind=kLoop, calls=%fused_computation.3 | loop fusion | bytes 2457600 | tf_op jit(solution)/shard_map/squeeze | solution.py:199
  50.2 3.8 %collective-permute-start.5 = (bf16[3,64,1600]{2,1,0:T(8,128)(2,1)S(1)}, bf16[3,64,1600]{2,1,0:T(8,128)(2,1)S(1)}, u32[]{:S(2)}, u32[]{:S(2)}) collective-permute-start(bf16[3,64,1600]{2,1,0:T(8,128)(2,1)S(1)} %get-tuple-element.65), channel_id=1, source_target_pairs={{1,0},{2,1},{3,2},{5,4},{6,5},{7,6},{9,8},{10,9},{11,10},{13,12},{... | collective-permute-start | bytes 1843208 | tf_op jit(solution)/shard_map/ppermute | solution.py:30
  53.9 1.9 %collective-permute-start.4 = (bf16[3,64,1600]{2,1,0:T(8,128)(2,1)S(1)}, bf16[3,64,1600]{2,1,0:T(8,128)(2,1)S(1)}, u32[]{:S(2)}, u32[]{:S(2)}) collective-permute-start(bf16[3,64,1600]{2,1,0:T(8,128)(2,1)S(1)} %get-tuple-element.66), channel_id=1, source_target_pairs={{0,1},{1,2},{2,3},{4,5},{5,6},{6,7},{8,9},{9,10},{10,11},{12,13},{... | collective-permute-start | bytes 1843208 | tf_op jit(solution)/shard_map/ppermute | solution.py:30
  55.9 6.0 %collective-permute-done.5.right_ref = bf16[3,64,1600]{2,1,0:T(8,128)(2,1)S(1)} collective-permute-done((bf16[3,64,1600]{2,1,0:T(8,128)(2,1)S(1)}, bf16[3,64,1600]{2,1,0:T(8,128)(2,1)S(1)}, u32[]{:S(2)}, u32[]{:S(2)}) %collective-permute-start.5) | collective-permute-done | bytes 614432 | tf_op jit(solution)/shard_map/ppermute | solution.py:30
  61.8 3.8 %collective-permute-done.4.left_ref = bf16[3,64,1600]{2,1,0:T(8,128)(2,1)S(1)} collective-permute-done((bf16[3,64,1600]{2,1,0:T(8,128)(2,1)S(1)}, bf16[3,64,1600]{2,1,0:T(8,128)(2,1)S(1)}, u32[]{:S(2)}, u32[]{:S(2)}) %collective-permute-start.4) | collective-permute-done | bytes 614432 | tf_op jit(solution)/shard_map/ppermute | solution.py:30
  65.7 0.9 copy-done.2
  66.5 8.3 %shard_map.65 = (f32[64,2240]{1,0:T(8,128)}, bf16[2,64,2240]{2,1,0:T(8,128)(2,1)}) custom-call(f32[3,64,1600]{2,1,0:T(8,128)} %get-tuple-element.57.keep_ref, bf16[3,64,1600]{2,1,0:T(8,128)(2,1)} %copy-done.2, bf16[3,64,1600]{2,1,0:T(8,128)(2,1)} %copy-done.1), custom_call_target="tpu_custom_call" | custom-call | tf_op jit(solution)/shard_map/pallas_call | solution.py:201
  74.8 1.1 %slice_bitcast_fusion.2 = (bf16[64,2240]{1,0:T(8,128)(2,1)S(1)}, bf16[64,2240]{1,0:T(8,128)(2,1)S(1)}) fusion(bf16[2,64,2240]{2,1,0:T(8,128)(2,1)} %get-tuple-element.60), kind=kLoop, calls=%fused_computation.10 | loop fusion | bytes 1146880 | tf_op jit(solution)/shard_map/squeeze | solution.py:211
  75.9 2.4 %collective-permute-start.7 = (bf16[64,2240]{1,0:T(8,128)(2,1)S(1)}, bf16[64,2240]{1,0:T(8,128)(2,1)S(1)}, u32[]{:S(2)}, u32[]{:S(2)}) collective-permute-start(bf16[64,2240]{1,0:T(8,128)(2,1)S(1)} %get-tuple-element.71), channel_id=1, source_target_pairs={{4,0},{5,1},{6,2},{7,3},{8,4},{9,5},{10,6},{11,7},{12,8},{13,9},{1... | collective-permute-start | bytes 860168 | tf_op jit(solution)/shard_map/ppermute | solution.py:30
  78.4 3.4 %collective-permute-start.6 = (bf16[64,2240]{1,0:T(8,128)(2,1)S(1)}, bf16[64,2240]{1,0:T(8,128)(2,1)S(1)}, u32[]{:S(2)}, u32[]{:S(2)}) collective-permute-start(bf16[64,2240]{1,0:T(8,128)(2,1)S(1)} %get-tuple-element.72), channel_id=1, source_target_pairs={{0,4},{1,5},{2,6},{3,7},{4,8},{5,9},{6,10},{7,11},{8,12},{9,13},{1... | collective-permute-start | bytes 860168 | tf_op jit(solution)/shard_map/ppermute | solution.py:30
  81.8 2.8 %collective-permute-done.7.down_ref = bf16[64,2240]{1,0:T(8,128)(2,1)S(1)} collective-permute-done((bf16[64,2240]{1,0:T(8,128)(2,1)S(1)}, bf16[64,2240]{1,0:T(8,128)(2,1)S(1)}, u32[]{:S(2)}, u32[]{:S(2)}) %collective-permute-start.7) | collective-permute-done | bytes 286752 | tf_op jit(solution)/shard_map/ppermute | solution.py:30
  84.5 3.3 %collective-permute-done.6.up_ref = bf16[64,2240]{1,0:T(8,128)(2,1)S(1)} collective-permute-done((bf16[64,2240]{1,0:T(8,128)(2,1)S(1)}, bf16[64,2240]{1,0:T(8,128)(2,1)S(1)}, u32[]{:S(2)}, u32[]{:S(2)}) %collective-permute-start.6) | collective-permute-done | bytes 286752 | tf_op jit(solution)/shard_map/ppermute | solution.py:30
  87.9 0.7 copy-done.4
  88.6 2.4 %shard_map.66 = bf16[64,3136]{1,0:T(8,128)(2,1)} custom-call(f32[64,2240]{1,0:T(8,128)} %get-tuple-element.59.keep_ref, bf16[64,2240]{1,0:T(8,128)(2,1)} %copy-done.4, bf16[64,2240]{1,0:T(8,128)(2,1)} %copy-done.3), custom_call_target="tpu_custom_call" | custom-call | tf_op jit(solution)/shard_map/pallas_call | solution.py:212
  (46 shorter events, 0.8 us)
Async XLA Ops:
  4.4 6.8 %copy-start.5 = (s32[4,4,4]{2,1,0:T(4,128)S(1)}, s32[4,4,4]{2,1,0:T(4,128)}, u32[]{:S(2)}) copy-start(s32[4,4,4]{2,1,0:T(4,128)} %param.18) | copy-start | bytes 772
  4.4 7.3 %copy-start.7 = (s32[4,4]{1,0:T(4,128)S(1)}, s32[4,4]{1,0:T(4,128)}, u32[]{:S(2)}) copy-start(s32[4,4]{1,0:T(4,128)} %param.16) | copy-start | bytes 196
  4.4 7.3 %copy-start.6 = (s32[4,4,9]{2,1,0:T(4,128)S(1)}, s32[4,4,9]{2,1,0:T(4,128)}, u32[]{:S(2)}) copy-start(s32[4,4,9]{2,1,0:T(4,128)} %param.15) | copy-start | bytes 1732
  4.4 8.5 %copy-start = (bf16[4,4,64,256]{3,2,1,0:T(8,128)(2,1)S(1)}, bf16[4,4,64,256]{3,2,1,0:T(8,128)(2,1)}, u32[]{:S(2)}) copy-start(bf16[4,4,64,256]{3,2,1,0:T(8,128)(2,1)} %param.17) | copy-start | bytes 1572868
  4.9 9.5 %collective-permute-start.1 = (bf16[272,256]{1,0:T(8,128)(2,1)S(1)}, bf16[272,256]{1,0:T(8,128)(2,1)S(1)}, u32[]{:S(2)}, u32[]{:S(2)}) collective-permute-start(bf16[272,256]{1,0:T(8,128)(2,1)S(1)} %fusion.7), channel_id=1, source_target_pairs={{4,0},{5,1},{6,2},{7,3},{8,4},{9,5},{10,6},{11,7},{12,8},{13,9},{1... | collective-permute-start | bytes 417800 | tf_op jit(solution)/shard_map/ppermute | solution.py:30
  8.6 7.9 %collective-permute-start = (bf16[272,256]{1,0:T(8,128)(2,1)S(1)}, bf16[272,256]{1,0:T(8,128)(2,1)S(1)}, u32[]{:S(2)}, u32[]{:S(2)}) collective-permute-start(bf16[272,256]{1,0:T(8,128)(2,1)S(1)} %fusion.6), channel_id=1, source_target_pairs={{0,4},{1,5},{2,6},{3,7},{4,8},{5,9},{6,10},{7,11},{8,12},{9,13},{1... | collective-permute-start | bytes 417800 | tf_op jit(solution)/shard_map/ppermute | solution.py:30
  17.4 7.1 %collective-permute-start.2 = (bf16[400,256]{1,0:T(8,128)(2,1)S(1)}, bf16[400,256]{1,0:T(8,128)(2,1)S(1)}, u32[]{:S(2)}, u32[]{:S(2)}) collective-permute-start(bf16[400,256]{1,0:T(8,128)(2,1)S(1)} %fusion.4), channel_id=1, source_target_pairs={{0,1},{1,2},{2,3},{4,5},{5,6},{6,7},{8,9},{9,10},{10,11},{12,13},{... | collective-permute-start | bytes 614408 | tf_op jit(solution)/shard_map/ppermute | solution.py:30
  19.3 6.9 %collective-permute-start.3 = (bf16[400,256]{1,0:T(8,128)(2,1)S(1)}, bf16[400,256]{1,0:T(8,128)(2,1)S(1)}, u32[]{:S(2)}, u32[]{:S(2)}) collective-permute-start(bf16[400,256]{1,0:T(8,128)(2,1)S(1)} %fusion.5), channel_id=1, source_target_pairs={{1,0},{2,1},{3,2},{5,4},{6,5},{7,6},{9,8},{10,9},{11,10},{13,12},{... | collective-permute-start | bytes 614408 | tf_op jit(solution)/shard_map/ppermute | solution.py:30
  50.2 11.7 %collective-permute-start.5 = (bf16[3,64,1600]{2,1,0:T(8,128)(2,1)S(1)}, bf16[3,64,1600]{2,1,0:T(8,128)(2,1)S(1)}, u32[]{:S(2)}, u32[]{:S(2)}) collective-permute-start(bf16[3,64,1600]{2,1,0:T(8,128)(2,1)S(1)} %get-tuple-element.65), channel_id=1, source_target_pairs={{1,0},{2,1},{3,2},{5,4},{6,5},{7,6},{9,8},{10,9},{11,10},{13,12},{... | collective-permute-start | bytes 1843208 | tf_op jit(solution)/shard_map/ppermute | solution.py:30
  53.9 11.7 %collective-permute-start.4 = (bf16[3,64,1600]{2,1,0:T(8,128)(2,1)S(1)}, bf16[3,64,1600]{2,1,0:T(8,128)(2,1)S(1)}, u32[]{:S(2)}, u32[]{:S(2)}) collective-permute-start(bf16[3,64,1600]{2,1,0:T(8,128)(2,1)S(1)} %get-tuple-element.66), channel_id=1, source_target_pairs={{0,1},{1,2},{2,3},{4,5},{5,6},{6,7},{8,9},{9,10},{10,11},{12,13},{... | collective-permute-start | bytes 1843208 | tf_op jit(solution)/shard_map/ppermute | solution.py:30
  61.8 3.8 %copy-start.1 = (bf16[3,64,1600]{2,1,0:T(8,128)(2,1)}, bf16[3,64,1600]{2,1,0:T(8,128)(2,1)S(1)}, u32[]{:S(2)}) copy-start(bf16[3,64,1600]{2,1,0:T(8,128)(2,1)S(1)} %collective-permute-done.5.right_ref) | copy-start | bytes 1843204
  65.7 0.9 copy-start.2
  75.9 8.6 %collective-permute-start.7 = (bf16[64,2240]{1,0:T(8,128)(2,1)S(1)}, bf16[64,2240]{1,0:T(8,128)(2,1)S(1)}, u32[]{:S(2)}, u32[]{:S(2)}) collective-permute-start(bf16[64,2240]{1,0:T(8,128)(2,1)S(1)} %get-tuple-element.71), channel_id=1, source_target_pairs={{4,0},{5,1},{6,2},{7,3},{8,4},{9,5},{10,6},{11,7},{12,8},{13,9},{1... | collective-permute-start | bytes 860168 | tf_op jit(solution)/shard_map/ppermute | solution.py:30
  78.4 9.5 %collective-permute-start.6 = (bf16[64,2240]{1,0:T(8,128)(2,1)S(1)}, bf16[64,2240]{1,0:T(8,128)(2,1)S(1)}, u32[]{:S(2)}, u32[]{:S(2)}) collective-permute-start(bf16[64,2240]{1,0:T(8,128)(2,1)S(1)} %get-tuple-element.72), channel_id=1, source_target_pairs={{0,4},{1,5},{2,6},{3,7},{4,8},{5,9},{6,10},{7,11},{8,12},{9,13},{1... | collective-permute-start | bytes 860168 | tf_op jit(solution)/shard_map/ppermute | solution.py:30
  84.5 3.4 %copy-start.3 = (bf16[64,2240]{1,0:T(8,128)(2,1)}, bf16[64,2240]{1,0:T(8,128)(2,1)S(1)}, u32[]{:S(2)}) copy-start(bf16[64,2240]{1,0:T(8,128)(2,1)S(1)} %collective-permute-done.7.down_ref) | copy-start | bytes 860164
  87.9 0.7 copy-start.4

commit v4 on v3

--- a/solution.py
+++ b/solution.py
@@ -66,26 +66,26 @@
 
 
 def fold_cols_kernel(keep_ref, left_ref, right_ref, keep_out, send_out):
+    src_w = WIN * B
+    dst_w = OUTW * B
     for d in range(HOME):
+        out = keep_out if d == 1 else send_out.at[d // 2]
         for sx in range(WIN):
-            for t in range(OUTW):
-                parts = []
-                if 1 <= t <= WIN:
-                    u = t - 1
-                    parts.append(keep_ref[d, :, (sx * WIN + u) * B:(sx * WIN + u + 1) * B])
-                if t <= WIN - 1:
-                    parts.append(left_ref[d, :, (sx * WIN + t) * B:(sx * WIN + t + 1) * B].astype(jnp.float32))
-                if t >= 2:
-                    u = t - 2
-                    parts.append(right_ref[d, :, (sx * WIN + u) * B:(sx * WIN + u + 1) * B].astype(jnp.float32))
-                total = parts[0]
-                for extra in parts[1:]:
-                    total = total + extra
-                lo = (sx * OUTW + t) * B
-                if d == 1:
-                    keep_out[:, lo:lo + B] = total
-                else:
-                    send_out[d // 2, :, lo:lo + B] = total.astype(send_out.dtype)
+            lo = sx * dst_w
+            s0 = sx * src_w
+            own = keep_ref[d, :, s0:s0 + src_w]
+            left = left_ref[d, :, s0:s0 + src_w].astype(jnp.float32)
+            right = right_ref[d, :, s0:s0 + src_w].astype(jnp.float32)
+            first = left[:, :B]
+            mid = left[:, B:2 * B] + own[:, :B]
+            core = left[:, 2 * B:] + own[:, B:src_w - B] + right[:, :src_w - 2 * B]
+            tail = own[:, src_w - B:] + right[:, src_w - 2 * B:src_w - B]
+            last = right[:, src_w - B:]
+            out[:, lo:lo + B] = first.astype(out.dtype)
+            out[:, lo + B:lo + 2 * B] = mid.astype(out.dtype)
+            out[:, lo + 2 * B:lo + 5 * B] = core.astype(out.dtype)
+            out[:, lo + 5 * B:lo + 6 * B] = tail.astype(out.dtype)
+            out[:, lo + 6 * B:lo + 7 * B] = last.astype(out.dtype)
 
 
 def fold_rows_kernel(keep_ref, up_ref, down_ref, out_ref):
@@ -115,16 +115,14 @@
     row_index = lax.axis_index("row")
     col_index = lax.axis_index("col")
 
+    prolong = prolong_blocks
     entries = jnp.arange(KP, dtype=jnp.int32)
-    kept = (entries[None, None, :] < prolong_counts[:, :, None])[:, :, None, :, None]
-    prolong = jnp.where(
-        kept, prolong_blocks.reshape(tile_rows, tile_cols, B, KP, B), jnp.zeros((), jnp.bfloat16)
-    ).reshape(tile_rows, tile_cols, B, KP * B)
+    kept = entries[None, None, :] < prolong_counts[:, :, None]
 
     own_codes = prolong_columns.reshape(patches, KP)
     hrow = jnp.clip(own_codes // coarse_grid_cols - row_index + 1, 0, HOME - 1)
     hcol = jnp.clip(own_codes % coarse_grid_cols - col_index + 1, 0, HOME - 1)
-    rel = (hrow * HOME + hcol).reshape(tile_rows, tile_cols, KP)
+    rel = jnp.where(kept, (hrow * HOME + hcol).reshape(tile_rows, tile_cols, KP), HOME * HOME)
 
     def payload(p_part, rel_part):
         count = p_part.shape[0]
@@ -151,7 +149,7 @@
     off_r = (jnp.arange(hr, dtype=jnp.int32) + tile_rows - 1) // tile_rows - 1
     off_c = (jnp.arange(hc, dtype=jnp.int32) + tile_cols - 1) // tile_cols - 1
     near_slot = (near_rel // HOME + off_r[:, None, None] + 1) * WIN + near_rel % HOME + off_c[None, :, None] + 1
-    near_slot = near_slot.reshape(hr * hc, KP)
+    near_slot = jnp.where(near_rel < HOME * HOME, near_slot, TRASH).reshape(hr * hc, KP)
 
     first_row = row_index * tile_rows
     first_col = col_index * tile_cols
@@ -162,7 +160,7 @@
     blocks = jnp.arange(KA, dtype=jnp.int32)
     used = blocks[None, :] < fine_counts.reshape(patches)[:, None]
     slot = jnp.where(used[:, :, None], slot, TRASH)
-    home = hcol * HOME + hrow
+    home = jnp.where(kept.reshape(patches, KP), hcol * HOME + hrow, HOME * HOME)
 
     smem = pltpu.MemorySpace.SMEM
     vmem = pltpu.MemorySpace.VMEM
@@ -185,7 +183,7 @@
         scratch_shapes=[
             pltpu.VMEM((TRASH + 1, B, B), jnp.float32),
             pltpu.VMEM((patches * B, width), jnp.bfloat16),
-            pltpu.VMEM((HOME * HOME, patches * B, B), jnp.float32),
+            pltpu.VMEM((HOME * HOME + 1, patches * B, B), jnp.float32),
         ],
     )(
         pos.reshape(-1).astype(jnp.int32),

time: 92.1 us -> 86.8 us (0.942)
  Pallas kernels: 29.6 us -> 25.4 us
  other arithmetic: 4.98 us -> 3.66 us
  local copies, waits for them, and re-layouts: 12 us -> 13.3 us
  waiting for transfers between devices: 21.2 us -> 20.1 us
    pallas_call x1, Pallas kernels: 8.3 us -> 3.98 us  [per_device(): pl.pallas_call(fold_cols_kernel, out_shape=(jax.ShapeDtypeStruct((B, band...]
    reshape x1 -> x0, local copies, waits for them, and re-layouts: 2.03 us -> none  [per_device(): prolong_blocks.reshape(tile_rows, tile_cols, B, KP, B)]
    lt x0 -> x5, local copies, waits for them, and re-layouts: none -> 1.08 us  [the longest x2 0.87 us: per_device(): kept = entries[None, None, :] < prolong_counts[:, :, None]]
    ppermute x8, waiting for transfers between devices: 21.2 us -> 20.1 us  [shifted(): return lax.ppermute(value, ('row', 'col'), pairs)]
    unnamed x17 -> x13, local copies, waits for them, and re-layouts: 1.73 us -> 2.46 us
  transfers between devices with their start and end apart: 8 -> 8, of which waited for: 7 -> 6; matrix products, arithmetic and copies ran while one was open for 4% -> 6% of each run, Pallas kernels for 0% -> 0%
where the time goes in v4:
time: 86.8 us; the launch traced here: 86.2 us
  Pallas kernels  25.4 us (29%)
  starting transfers between devices  23.4 us (27%)
  waiting for transfers between devices  20.1 us (23%)
  local copies, waits for them, and re-layouts  13.3 us (15%)
  other arithmetic  3.66 us (4%)
    ppermute x8, starting transfers between devices, shifted(): return lax.ppermute(value, ('row', 'col'), pairs)  23.4 us
    ppermute x8, waiting for transfers between devices, shifted(): return lax.ppermute(value, ('row', 'col'), pairs)  20.1 us
    pallas_call x1, Pallas kernels, per_device(): pl.pallas_call(galerkin_kernel, out_shape=(jax.ShapeDtypeStruct((HOME, B,...  19.1 us
    pallas_call x1, Pallas kernels, per_device(): pl.pallas_call(fold_cols_kernel, out_shape=(jax.ShapeDtypeStruct((B, band...  3.98 us
    unnamed x13, local copies, waits for them, and re-layouts  2.46 us
    pallas_call x1, Pallas kernels, per_device(): pl.pallas_call(fold_rows_kernel, out_shape=jax.ShapeDtypeStruct((B, OUTW...  2.4 us
  transfers between devices with their start and end apart: 8, of which 6 were waited for; matrix products, arithmetic and copies ran while one was open for 6% of the time, Pallas kernels for 0%

profile of v4, /device:TPU:20, one launch (start us, length us, event | category | flops | bytes accessed | tf_op | source)
XLA Modules:
  0.0 86.2 jit_solution(6169016807862069050)
XLA Ops:
  0.0 0.9 %copy.25 = s32[4,4,4]{1,2,0:T(4,128)S(1)} copy(s32[4,4,4]{2,1,0:T(4,128)} %param.18) | data formatting | bytes 512 | tf_op args[4]
  0.9 0.7 fusion.49
  1.6 0.1 copy.29
  1.7 0.1 convert_element_type.88
  1.8 1.0 %fusion.51 = (bf16[1,4,64,256]{3,2,1,0:T(8,128)(2,1)S(1)}, bf16[1,4,64,256]{3,2,1,0:T(8,128)(2,1)S(1)}) fusion(bf16[4,4,64,256]{3,2,1,0:T(8,128)(2,1)} %param.17), kind=kLoop, calls=%fused_computation.108 | loop fusion | bytes 524288 | tf_op jit(solution)/shard_map/slice | solution.py:140
  2.8 3.4 %collective-permute-start = (bf16[272,256]{1,0:T(8,128)(2,1)S(1)}, bf16[272,256]{1,0:T(8,128)(2,1)S(1)}, u32[]{:S(2)}, u32[]{:S(2)}) collective-permute-start(bf16[272,256]{1,0:T(8,128)(2,1)S(1)} %fusion.6), channel_id=1, source_target_pairs={{0,4},{1,5},{2,6},{3,7},{4,8},{5,9},{6,10},{7,11},{8,12},{9,13},{1... | collective-permute-start | bytes 417800 | tf_op jit(solution)/shard_map/ppermute | solution.py:30
  6.2 0.1 copy.30
  6.3 0.1 convert_element_type.89
  6.4 3.3 %collective-permute-start.1 = (bf16[272,256]{1,0:T(8,128)(2,1)S(1)}, bf16[272,256]{1,0:T(8,128)(2,1)S(1)}, u32[]{:S(2)}, u32[]{:S(2)}) collective-permute-start(bf16[272,256]{1,0:T(8,128)(2,1)S(1)} %fusion.7), channel_id=1, source_target_pairs={{4,0},{5,1},{6,2},{7,3},{8,4},{9,5},{10,6},{11,7},{12,8},{13,9},{1... | collective-permute-start | bytes 417800 | tf_op jit(solution)/shard_map/ppermute | solution.py:30
  9.8 0.8 reshape.420
  10.6 0.8 lt.104
  11.3 0.8 lt.90
  12.1 0.8 reshape.418
  12.9 0.1 iota_compare_fusion.2
  13.0 0.1 lt.107
  13.2 0.1 add.226
  13.3 0.1 add.219
  13.4 0.5 add_clamp_fusion.pos_ref
  14.0 0.1 reshape.431
  14.0 0.6 fusion.43.home_ref
  14.7 0.1 reshape.426
  14.8 0.1 copy.32
  14.8 0.1 reshape.425
  14.9 0.1 copy.31
  15.0 0.1 slice_reduce_fusion.1
  15.2 0.1 convert_element_type.94
  15.3 0.1 convert_element_type.97
  15.5 1.9 %collective-permute-start.2 = (bf16[400,256]{1,0:T(8,128)(2,1)S(1)}, bf16[400,256]{1,0:T(8,128)(2,1)S(1)}, u32[]{:S(2)}, u32[]{:S(2)}) collective-permute-start(bf16[400,256]{1,0:T(8,128)(2,1)S(1)} %fusion.4), channel_id=1, source_target_pairs={{0,1},{1,2},{2,3},{4,5},{5,6},{6,7},{8,9},{9,10},{10,11},{12,13},{... | collective-permute-start | bytes 614408 | tf_op jit(solution)/shard_map/ppermute | solution.py:30
  17.5 3.6 %collective-permute-start.3 = (bf16[400,256]{1,0:T(8,128)(2,1)S(1)}, bf16[400,256]{1,0:T(8,128)(2,1)S(1)}, u32[]{:S(2)}, u32[]{:S(2)}) collective-permute-start(bf16[400,256]{1,0:T(8,128)(2,1)S(1)} %fusion.5), channel_id=1, source_target_pairs={{1,0},{2,1},{3,2},{5,4},{6,5},{7,6},{9,8},{10,9},{11,10},{13,12},{... | collective-permute-start | bytes 614408 | tf_op jit(solution)/shard_map/ppermute | solution.py:30
  21.1 1.5 %collective-permute-done.2 = bf16[400,256]{1,0:T(8,128)(2,1)S(1)} collective-permute-done((bf16[400,256]{1,0:T(8,128)(2,1)S(1)}, bf16[400,256]{1,0:T(8,128)(2,1)S(1)}, u32[]{:S(2)}, u32[]{:S(2)}) %collective-permute-start.2) | collective-permute-done | bytes 204832 | tf_op jit(solution)/shard_map/ppermute | solution.py:30
  22.6 0.1 reshape.438
  22.7 1.7 %collective-permute-done.3 = bf16[400,256]{1,0:T(8,128)(2,1)S(1)} collective-permute-done((bf16[400,256]{1,0:T(8,128)(2,1)S(1)}, bf16[400,256]{1,0:T(8,128)(2,1)S(1)}, u32[]{:S(2)}, u32[]{:S(2)}) %collective-permute-start.3) | collective-permute-done | bytes 204832 | tf_op jit(solution)/shard_map/ppermute | solution.py:30
  24.4 0.1 reshape.439
  24.5 0.1 sign_compare_fusion
  24.6 0.1 ne.160
  24.7 0.1 lt.99
  24.8 0.1 copy.46
  25.0 0.1 copy.39
  25.1 0.1 rem.151
  25.2 0.1 div.77
  25.2 0.1 copy.41
  25.3 0.1 copy.38
  25.5 0.1 fusion.14
  25.5 0.7 gather_fusion
  26.2 0.1 copy.47
  26.3 0.1 reshape.430
  26.4 0.2 copy.48
  26.6 0.7 select_n.125.slot_ref
  27.4 1.2 %pad_maximum_fusion = bf16[6,6,64,256]{3,2,1,0:T(8,128)(2,1)} fusion(bf16[6,1,64,256]{3,2,1,0:T(8,128)(2,1)S(1)} %bitcast.42, bf16[1,4,64,256]{3,2,1,0:T(8,128)(2,1)S(1)} %bitcast.39, bf16[4,4,64,256]{3,2,1,0:T(8,128)(2,1)S(1)} %copy-done, bf16[1,4,64,256]{3,2,1,0:T(8,128)(2,1)S(1)} %bitcast.37, bf16[6,1,64,256]{3,2,1,0:T(8,128)(2,1)S(1)} %bitcast.41), kind=kLoop, calls=%fused_computation.1 | loop fusion | flops 2359296 | bytes 2359296 | tf_op jit(solution)/shard_map/concatenate | solution.py:146
  28.6 19.1 %shard_map.64 = (f32[3,64,1600]{2,1,0:T(8,128)}, bf16[2,3,64,1600]{3,2,1,0:T(8,128)(2,1)}) custom-call(s32[144]{0:T(256)} %add_clamp_fusion.pos_ref, s32[576]{0:T(1024)} %select_n.125.slot_ref, s32[64]{0:T(128)} %fusion.43.home_ref, bf16[16,64,576]{2,1,0:T(8,128)(2,1)} %bitcast.35, bf16[36,64,256]{2,1,0:T(8,128)(2,1)} %bitcast.34, bf16[16,64,256]{2,1,0:T(8,128)(2,1)} %bitcast.33), custom_call_target="tpu_custom_call" | custom-call | tf_op jit(solution)/shard_map/pallas_call | solution.py:168
  47.6 1.4 %slice_bitcast_fusion = (bf16[3,64,1600]{2,1,0:T(8,128)(2,1)S(1)}, bf16[3,64,1600]{2,1,0:T(8,128)(2,1)S(1)}) fusion(bf16[2,3,64,1600]{3,2,1,0:T(8,128)(2,1)} %get-tuple-element.58), kind=kLoop, calls=%fused_computation.2 | loop fusion | bytes 2457600 | tf_op jit(solution)/shard_map/squeeze | solution.py:197
  49.0 3.3 %collective-permute-start.5 = (bf16[3,64,1600]{2,1,0:T(8,128)(2,1)S(1)}, bf16[3,64,1600]{2,1,0:T(8,128)(2,1)S(1)}, u32[]{:S(2)}, u32[]{:S(2)}) collective-permute-start(bf16[3,64,1600]{2,1,0:T(8,128)(2,1)S(1)} %get-tuple-element.67), channel_id=1, source_target_pairs={{1,0},{2,1},{3,2},{5,4},{6,5},{7,6},{9,8},{10,9},{11,10},{13,12},{... | collective-permute-start | bytes 1843208 | tf_op jit(solution)/shard_map/ppermute | solution.py:30
  52.4 1.9 %collective-permute-start.4 = (bf16[3,64,1600]{2,1,0:T(8,128)(2,1)S(1)}, bf16[3,64,1600]{2,1,0:T(8,128)(2,1)S(1)}, u32[]{:S(2)}, u32[]{:S(2)}) collective-permute-start(bf16[3,64,1600]{2,1,0:T(8,128)(2,1)S(1)} %get-tuple-element.68), channel_id=1, source_target_pairs={{0,1},{1,2},{2,3},{4,5},{5,6},{6,7},{8,9},{9,10},{10,11},{12,13},{... | collective-permute-start | bytes 1843208 | tf_op jit(solution)/shard_map/ppermute | solution.py:30
  54.3 6.0 %collective-permute-done.5.right_ref = bf16[3,64,1600]{2,1,0:T(8,128)(2,1)S(1)} collective-permute-done((bf16[3,64,1600]{2,1,0:T(8,128)(2,1)S(1)}, bf16[3,64,1600]{2,1,0:T(8,128)(2,1)S(1)}, u32[]{:S(2)}, u32[]{:S(2)}) %collective-permute-start.5) | collective-permute-done | bytes 614432 | tf_op jit(solution)/shard_map/ppermute | solution.py:30
  60.3 3.8 %collective-permute-done.4.left_ref = bf16[3,64,1600]{2,1,0:T(8,128)(2,1)S(1)} collective-permute-done((bf16[3,64,1600]{2,1,0:T(8,128)(2,1)S(1)}, bf16[3,64,1600]{2,1,0:T(8,128)(2,1)S(1)}, u32[]{:S(2)}, u32[]{:S(2)}) %collective-permute-start.4) | collective-permute-done | bytes 614432 | tf_op jit(solution)/shard_map/ppermute | solution.py:30
  64.1 0.9 copy-done.2
  64.9 4.0 %shard_map.65 = (f32[64,2240]{1,0:T(8,128)}, bf16[2,64,2240]{2,1,0:T(8,128)(2,1)}) custom-call(f32[3,64,1600]{2,1,0:T(8,128)} %get-tuple-element.57.keep_ref, bf16[3,64,1600]{2,1,0:T(8,128)(2,1)} %copy-done.2, bf16[3,64,1600]{2,1,0:T(8,128)(2,1)} %copy-done.1), custom_call_target="tpu_custom_call" | custom-call | tf_op jit(solution)/shard_map/pallas_call | solution.py:199
  68.9 1.1 %slice_bitcast_fusion.2 = (bf16[64,2240]{1,0:T(8,128)(2,1)S(1)}, bf16[64,2240]{1,0:T(8,128)(2,1)S(1)}) fusion(bf16[2,64,2240]{2,1,0:T(8,128)(2,1)} %get-tuple-element.60), kind=kLoop, calls=%fused_computation.7 | loop fusion | bytes 1146880 | tf_op jit(solution)/shard_map/squeeze | solution.py:209
  70.0 3.6 %collective-permute-start.7 = (bf16[64,2240]{1,0:T(8,128)(2,1)S(1)}, bf16[64,2240]{1,0:T(8,128)(2,1)S(1)}, u32[]{:S(2)}, u32[]{:S(2)}) collective-permute-start(bf16[64,2240]{1,0:T(8,128)(2,1)S(1)} %get-tuple-element.71), channel_id=1, source_target_pairs={{4,0},{5,1},{6,2},{7,3},{8,4},{9,5},{10,6},{11,7},{12,8},{13,9},{1... | collective-permute-start | bytes 860168 | tf_op jit(solution)/shard_map/ppermute | solution.py:30
  73.6 2.3 %collective-permute-start.6 = (bf16[64,2240]{1,0:T(8,128)(2,1)S(1)}, bf16[64,2240]{1,0:T(8,128)(2,1)S(1)}, u32[]{:S(2)}, u32[]{:S(2)}) collective-permute-start(bf16[64,2240]{1,0:T(8,128)(2,1)S(1)} %get-tuple-element.72), channel_id=1, source_target_pairs={{0,4},{1,5},{2,6},{3,7},{4,8},{5,9},{6,10},{7,11},{8,12},{9,13},{1... | collective-permute-start | bytes 860168 | tf_op jit(solution)/shard_map/ppermute | solution.py:30
  75.9 2.8 %collective-permute-done.7.down_ref = bf16[64,2240]{1,0:T(8,128)(2,1)S(1)} collective-permute-done((bf16[64,2240]{1,0:T(8,128)(2,1)S(1)}, bf16[64,2240]{1,0:T(8,128)(2,1)S(1)}, u32[]{:S(2)}, u32[]{:S(2)}) %collective-permute-start.7) | collective-permute-done | bytes 286752 | tf_op jit(solution)/shard_map/ppermute | solution.py:30
  78.6 4.5 %collective-permute-done.6.up_ref = bf16[64,2240]{1,0:T(8,128)(2,1)S(1)} collective-permute-done((bf16[64,2240]{1,0:T(8,128)(2,1)S(1)}, bf16[64,2240]{1,0:T(8,128)(2,1)S(1)}, u32[]{:S(2)}, u32[]{:S(2)}) %collective-permute-start.6) | collective-permute-done | bytes 286752 | tf_op jit(solution)/shard_map/ppermute | solution.py:30
  83.1 0.7 copy-done.4
  83.8 2.4 %shard_map.66 = bf16[64,3136]{1,0:T(8,128)(2,1)} custom-call(f32[64,2240]{1,0:T(8,128)} %get-tuple-element.59.keep_ref, bf16[64,2240]{1,0:T(8,128)(2,1)} %copy-done.4, bf16[64,2240]{1,0:T(8,128)(2,1)} %copy-done.3), custom_call_target="tpu_custom_call" | custom-call | tf_op jit(solution)/shard_map/pallas_call | solution.py:210
  (39 shorter events, 0.5 us)
Async XLA Ops:
  0.0 15.4 %copy-start = (bf16[4,4,64,256]{3,2,1,0:T(8,128)(2,1)S(1)}, bf16[4,4,64,256]{3,2,1,0:T(8,128)(2,1)}, u32[]{:S(2)}) copy-start(bf16[4,4,64,256]{3,2,1,0:T(8,128)(2,1)} %param.17) | copy-start | bytes 1572868
  0.0 13.9 %copy-start.5 = (s32[4,4,9]{2,1,0:T(4,128)S(1)}, s32[4,4,9]{2,1,0:T(4,128)}, u32[]{:S(2)}) copy-start(s32[4,4,9]{2,1,0:T(4,128)} %param.15) | copy-start | bytes 1732
  2.8 11.8 %collective-permute-start = (bf16[272,256]{1,0:T(8,128)(2,1)S(1)}, bf16[272,256]{1,0:T(8,128)(2,1)S(1)}, u32[]{:S(2)}, u32[]{:S(2)}) collective-permute-start(bf16[272,256]{1,0:T(8,128)(2,1)S(1)} %fusion.6), channel_id=1, source_target_pairs={{0,4},{1,5},{2,6},{3,7},{4,8},{5,9},{6,10},{7,11},{8,12},{9,13},{1... | collective-permute-start | bytes 417800 | tf_op jit(solution)/shard_map/ppermute | solution.py:30
  6.4 8.2 %collective-permute-start.1 = (bf16[272,256]{1,0:T(8,128)(2,1)S(1)}, bf16[272,256]{1,0:T(8,128)(2,1)S(1)}, u32[]{:S(2)}, u32[]{:S(2)}) collective-permute-start(bf16[272,256]{1,0:T(8,128)(2,1)S(1)} %fusion.7), channel_id=1, source_target_pairs={{4,0},{5,1},{6,2},{7,3},{8,4},{9,5},{10,6},{11,7},{12,8},{13,9},{1... | collective-permute-start | bytes 417800 | tf_op jit(solution)/shard_map/ppermute | solution.py:30
  15.5 7.1 %collective-permute-start.2 = (bf16[400,256]{1,0:T(8,128)(2,1)S(1)}, bf16[400,256]{1,0:T(8,128)(2,1)S(1)}, u32[]{:S(2)}, u32[]{:S(2)}) collective-permute-start(bf16[400,256]{1,0:T(8,128)(2,1)S(1)} %fusion.4), channel_id=1, source_target_pairs={{0,1},{1,2},{2,3},{4,5},{5,6},{6,7},{8,9},{9,10},{10,11},{12,13},{... | collective-permute-start | bytes 614408 | tf_op jit(solution)/shard_map/ppermute | solution.py:30
  17.5 6.9 %collective-permute-start.3 = (bf16[400,256]{1,0:T(8,128)(2,1)S(1)}, bf16[400,256]{1,0:T(8,128)(2,1)S(1)}, u32[]{:S(2)}, u32[]{:S(2)}) collective-permute-start(bf16[400,256]{1,0:T(8,128)(2,1)S(1)} %fusion.5), channel_id=1, source_target_pairs={{1,0},{2,1},{3,2},{5,4},{6,5},{7,6},{9,8},{10,9},{11,10},{13,12},{... | collective-permute-start | bytes 614408 | tf_op jit(solution)/shard_map/ppermute | solution.py:30
  49.0 11.2 %collective-permute-start.5 = (bf16[3,64,1600]{2,1,0:T(8,128)(2,1)S(1)}, bf16[3,64,1600]{2,1,0:T(8,128)(2,1)S(1)}, u32[]{:S(2)}, u32[]{:S(2)}) collective-permute-start(bf16[3,64,1600]{2,1,0:T(8,128)(2,1)S(1)} %get-tuple-element.67), channel_id=1, source_target_pairs={{1,0},{2,1},{3,2},{5,4},{6,5},{7,6},{9,8},{10,9},{11,10},{13,12},{... | collective-permute-start | bytes 1843208 | tf_op jit(solution)/shard_map/ppermute | solution.py:30
  52.4 11.7 %collective-permute-start.4 = (bf16[3,64,1600]{2,1,0:T(8,128)(2,1)S(1)}, bf16[3,64,1600]{2,1,0:T(8,128)(2,1)S(1)}, u32[]{:S(2)}, u32[]{:S(2)}) collective-permute-start(bf16[3,64,1600]{2,1,0:T(8,128)(2,1)S(1)} %get-tuple-element.68), channel_id=1, source_target_pairs={{0,1},{1,2},{2,3},{4,5},{5,6},{6,7},{8,9},{9,10},{10,11},{12,13},{... | collective-permute-start | bytes 1843208 | tf_op jit(solution)/shard_map/ppermute | solution.py:30
  60.3 3.8 %copy-start.1 = (bf16[3,64,1600]{2,1,0:T(8,128)(2,1)}, bf16[3,64,1600]{2,1,0:T(8,128)(2,1)S(1)}, u32[]{:S(2)}) copy-start(bf16[3,64,1600]{2,1,0:T(8,128)(2,1)S(1)} %collective-permute-done.5.right_ref) | copy-start | bytes 1843204
  64.1 0.9 copy-start.2
  70.0 8.6 %collective-permute-start.7 = (bf16[64,2240]{1,0:T(8,128)(2,1)S(1)}, bf16[64,2240]{1,0:T(8,128)(2,1)S(1)}, u32[]{:S(2)}, u32[]{:S(2)}) collective-permute-start(bf16[64,2240]{1,0:T(8,128)(2,1)S(1)} %get-tuple-element.71), channel_id=1, source_target_pairs={{4,0},{5,1},{6,2},{7,3},{8,4},{9,5},{10,6},{11,7},{12,8},{13,9},{1... | collective-permute-start | bytes 860168 | tf_op jit(solution)/shard_map/ppermute | solution.py:30
  73.6 9.5 %collective-permute-start.6 = (bf16[64,2240]{1,0:T(8,128)(2,1)S(1)}, bf16[64,2240]{1,0:T(8,128)(2,1)S(1)}, u32[]{:S(2)}, u32[]{:S(2)}) collective-permute-start(bf16[64,2240]{1,0:T(8,128)(2,1)S(1)} %get-tuple-element.72), channel_id=1, source_target_pairs={{0,4},{1,5},{2,6},{3,7},{4,8},{5,9},{6,10},{7,11},{8,12},{9,13},{1... | collective-permute-start | bytes 860168 | tf_op jit(solution)/shard_map/ppermute | solution.py:30
  78.6 4.5 %copy-start.3 = (bf16[64,2240]{1,0:T(8,128)(2,1)}, bf16[64,2240]{1,0:T(8,128)(2,1)S(1)}, u32[]{:S(2)}) copy-start(bf16[64,2240]{1,0:T(8,128)(2,1)S(1)} %collective-permute-done.7.down_ref) | copy-start | bytes 860164
  83.1 0.7 copy-start.4

commit v5 on v4

--- a/solution.py
+++ b/solution.py
@@ -30,8 +30,8 @@
     return lax.ppermute(value, ("row", "col"), pairs)
 
 
-def galerkin_kernel(pos_ref, slot_ref, home_ref, a_ref, p_ref, own_ref, keep_ref, send_ref,
-                    acc_ref, prod_ref, dp_ref):
+def galerkin_kernel(pos_ref, slot_ref, home_ref, a_ref, p_ref, own_ref, keep_ref, right_ref, left_ref,
+                    acc_ref, prod_ref, dpt_ref):
     patches = a_ref.shape[0]
 
     def one_patch(i, carry):
@@ -46,23 +46,23 @@
         row = pl.multiple_of(i * B, B)
         for w in range(WIN * WIN):
             prod_ref[pl.ds(row, B), w * B:(w + 1) * B] = acc_ref[w].astype(jnp.bfloat16)
+        return carry
+
+    lax.fori_loop(0, patches, one_patch, 0)
+
+    dpt_ref[...] = jnp.zeros(dpt_ref.shape, jnp.float32)
+    for i in range(patches):
+        flipped = own_ref[i].astype(jnp.float32).T
         for p in range(KP):
-            h = home_ref[i * KP + p]
-            dp_ref[h, pl.ds(row, B), :] = dp_ref[h, pl.ds(row, B), :] + own_ref[i, :, p * B:(p + 1) * B].astype(jnp.float32)
-        return carry
-
-    dp_ref[...] = jnp.zeros(dp_ref.shape, jnp.float32)
-    lax.fori_loop(0, patches, one_patch, 0)
+            start = pl.multiple_of(home_ref[i * KP + p] * B, B)
+            dpt_ref[pl.ds(start, B), i * B:(i + 1) * B] += flipped[p * B:(p + 1) * B, :]
+
     prod = prod_ref[...]
-    dims = (((0,), (0,)), ((), ()))
-
-    def coarse_terms(h):
-        return lax.dot_general(dp_ref[h].astype(jnp.bfloat16), prod, dims, preferred_element_type=jnp.float32)
-
-    for dr in range(HOME):
-        keep_ref[dr] = coarse_terms(HOME + dr)
-        send_ref[0, dr] = coarse_terms(dr).astype(send_ref.dtype)
-        send_ref[1, dr] = coarse_terms(2 * HOME + dr).astype(send_ref.dtype)
+    group = HOME * B
+    for out, at in ((right_ref, 0), (keep_ref, 1), (left_ref, 2)):
+        terms = jnp.dot(dpt_ref[at * group:(at + 1) * group].astype(jnp.bfloat16), prod,
+                        preferred_element_type=jnp.float32)
+        out[...] = terms.reshape(out.shape).astype(out.dtype)
 
 
 def fold_cols_kernel(keep_ref, left_ref, right_ref, keep_out, send_out):
@@ -165,11 +165,12 @@
     smem = pltpu.MemorySpace.SMEM
     vmem = pltpu.MemorySpace.VMEM
     width = WIN * WIN * B
-    keep, send = pl.pallas_call(
+    keep, to_right, to_left = pl.pallas_call(
         galerkin_kernel,
         out_shape=(
             jax.ShapeDtypeStruct((HOME, B, width), jnp.float32),
-            jax.ShapeDtypeStruct((2, HOME, B, width), SEND),
+            jax.ShapeDtypeStruct((HOME, B, width), SEND),
+            jax.ShapeDtypeStruct((HOME, B, width), SEND),
         ),
         in_specs=[
             pl.BlockSpec(memory_space=smem),
@@ -179,11 +180,11 @@
             pl.BlockSpec(memory_space=vmem),
             pl.BlockSpec(memory_space=vmem),
         ],
-        out_specs=(pl.BlockSpec(memory_space=vmem), pl.BlockSpec(memory_space=vmem)),
+        out_specs=(pl.BlockSpec(memory_space=vmem),) * 3,
         scratch_shapes=[
             pltpu.VMEM((TRASH + 1, B, B), jnp.float32),
             pltpu.VMEM((patches * B, width), jnp.bfloat16),
-            pltpu.VMEM((HOME * HOME + 1, patches * B, B), jnp.float32),
+            pltpu.VMEM(((HOME * HOME + 1) * B, patches * B), jnp.float32),
         ],
     )(
         pos.reshape(-1).astype(jnp.int32),
@@ -193,8 +194,8 @@
         near_p,
         prolong.reshape(patches, B, KP * B),
     )
-    left_in = shifted(send[1], 0, 1)
-    right_in = shifted(send[0], 0, -1)
+    left_in = shifted(to_left, 0, 1)
+    right_in = shifted(to_right, 0, -1)
     band = WIN * OUTW * B
     keep2, send2 = pl.pallas_call(
         fold_cols_kernel,

time: 86.8 us -> 81.5 us (0.939); the launches traced: 86.2 us -> 80 us
  Pallas kernels: 25.4 us -> 22.1 us
  waiting for transfers between devices: 20.1 us -> 17.7 us
  local copies, waits for them, and re-layouts: 13.3 us -> 11.9 us
  starting transfers between devices: 23.4 us -> 24.5 us
    pallas_call x1, Pallas kernels: 19.1 us -> 15.7 us  [per_device(): pl.pallas_call(galerkin_kernel, out_shape=(jax.ShapeDtypeStruct((HOME, B,...]
    ppermute x8, waiting for transfers between devices: 20.1 us -> 17.7 us  [shifted(): return lax.ppermute(value, ('row', 'col'), pairs)]
    squeeze x1 -> x0, local copies, waits for them, and re-layouts: 1.37 us -> none  [per_device(): right_in = shifted(send[0], 0, -1)]
    ppermute x8, starting transfers between devices: 23.4 us -> 24.5 us  [shifted(): return lax.ppermute(value, ('row', 'col'), pairs)]
where the time goes in v5:
time: 81.5 us; the launch traced here: 80 us
  starting transfers between devices  24.5 us (30%)
  Pallas kernels  22.1 us (27%)
  waiting for transfers between devices  17.7 us (22%)
  local copies, waits for them, and re-layouts  11.9 us (15%)
  other arithmetic  3.55 us (4%)
    ppermute x8, starting transfers between devices, shifted(): return lax.ppermute(value, ('row', 'col'), pairs)  24.5 us
    ppermute x8, waiting for transfers between devices, shifted(): return lax.ppermute(value, ('row', 'col'), pairs)  17.7 us
    pallas_call x1, Pallas kernels, per_device(): pl.pallas_call(galerkin_kernel, out_shape=(jax.ShapeDtypeStruct((HOME, B,...  15.7 us
    pallas_call x1, Pallas kernels, per_device(): pl.pallas_call(fold_cols_kernel, out_shape=(jax.ShapeDtypeStruct((B, band...  3.98 us
    unnamed x13, local copies, waits for them, and re-layouts  2.42 us
    pallas_call x1, Pallas kernels, per_device(): pl.pallas_call(fold_rows_kernel, out_shape=jax.ShapeDtypeStruct((B, OUTW...  2.4 us
  transfers between devices with their start and end apart: 8, of which 6 were waited for; matrix products, arithmetic and copies ran while one was open for 6% of the time, Pallas kernels for 0%

profile of v5, /device:TPU:20, one launch (start us, length us, event | category | flops | bytes accessed | tf_op | source)
XLA Modules:
  0.0 80.0 jit_solution(2461414374952678110)
XLA Ops:
  0.0 0.9 %copy.25 = s32[4,4,4]{1,2,0:T(4,128)S(1)} copy(s32[4,4,4]{2,1,0:T(4,128)} %param.18) | data formatting | bytes 512 | tf_op args[4]
  0.9 0.7 fusion.49
  1.6 0.1 copy.29
  1.7 0.1 convert_element_type.88
  1.8 1.0 %fusion.51 = (bf16[1,4,64,256]{3,2,1,0:T(8,128)(2,1)S(1)}, bf16[1,4,64,256]{3,2,1,0:T(8,128)(2,1)S(1)}) fusion(bf16[4,4,64,256]{3,2,1,0:T(8,128)(2,1)} %param.17), kind=kLoop, calls=%fused_computation.106 | loop fusion | bytes 524288 | tf_op jit(solution)/shard_map/slice | solution.py:140
  2.8 3.4 %collective-permute-start = (bf16[272,256]{1,0:T(8,128)(2,1)S(1)}, bf16[272,256]{1,0:T(8,128)(2,1)S(1)}, u32[]{:S(2)}, u32[]{:S(2)}) collective-permute-start(bf16[272,256]{1,0:T(8,128)(2,1)S(1)} %fusion.6), channel_id=1, source_target_pairs={{0,4},{1,5},{2,6},{3,7},{4,8},{5,9},{6,10},{7,11},{8,12},{9,13},{1... | collective-permute-start | bytes 417800 | tf_op jit(solution)/shard_map/ppermute | solution.py:30
  6.2 0.1 copy.30
  6.3 0.1 convert_element_type.89
  6.4 3.3 %collective-permute-start.1 = (bf16[272,256]{1,0:T(8,128)(2,1)S(1)}, bf16[272,256]{1,0:T(8,128)(2,1)S(1)}, u32[]{:S(2)}, u32[]{:S(2)}) collective-permute-start(bf16[272,256]{1,0:T(8,128)(2,1)S(1)} %fusion.7), channel_id=1, source_target_pairs={{4,0},{5,1},{6,2},{7,3},{8,4},{9,5},{10,6},{11,7},{12,8},{13,9},{1... | collective-permute-start | bytes 417800 | tf_op jit(solution)/shard_map/ppermute | solution.py:30
  9.8 0.8 reshape.420
  10.6 0.8 lt.104
  11.3 0.8 lt.90
  12.1 0.8 reshape.418
  12.9 0.1 iota_compare_fusion.2
  13.0 0.1 lt.107
  13.1 0.1 iota_compare_fusion.4
  13.2 0.1 add.226
  13.3 0.1 add.219
  13.4 0.6 add_clamp_fusion.pos_ref
  14.0 0.1 reshape.431
  14.1 0.5 fusion.43.home_ref
  14.6 0.1 reshape.426
  14.7 0.1 copy.32
  14.8 0.1 reshape.425
  14.9 0.1 copy.31
  15.0 0.1 slice_reduce_fusion.1
  15.1 0.1 convert_element_type.94
  15.2 0.1 convert_element_type.97
  15.4 1.9 %collective-permute-start.2 = (bf16[400,256]{1,0:T(8,128)(2,1)S(1)}, bf16[400,256]{1,0:T(8,128)(2,1)S(1)}, u32[]{:S(2)}, u32[]{:S(2)}) collective-permute-start(bf16[400,256]{1,0:T(8,128)(2,1)S(1)} %fusion.4), channel_id=1, source_target_pairs={{0,1},{1,2},{2,3},{4,5},{5,6},{6,7},{8,9},{9,10},{10,11},{12,13},{... | collective-permute-start | bytes 614408 | tf_op jit(solution)/shard_map/ppermute | solution.py:30
  17.4 3.6 %collective-permute-start.3 = (bf16[400,256]{1,0:T(8,128)(2,1)S(1)}, bf16[400,256]{1,0:T(8,128)(2,1)S(1)}, u32[]{:S(2)}, u32[]{:S(2)}) collective-permute-start(bf16[400,256]{1,0:T(8,128)(2,1)S(1)} %fusion.5), channel_id=1, source_target_pairs={{1,0},{2,1},{3,2},{5,4},{6,5},{7,6},{9,8},{10,9},{11,10},{13,12},{... | collective-permute-start | bytes 614408 | tf_op jit(solution)/shard_map/ppermute | solution.py:30
  21.0 1.5 %collective-permute-done.2 = bf16[400,256]{1,0:T(8,128)(2,1)S(1)} collective-permute-done((bf16[400,256]{1,0:T(8,128)(2,1)S(1)}, bf16[400,256]{1,0:T(8,128)(2,1)S(1)}, u32[]{:S(2)}, u32[]{:S(2)}) %collective-permute-start.2) | collective-permute-done | bytes 204832 | tf_op jit(solution)/shard_map/ppermute | solution.py:30
  22.5 0.1 reshape.438
  22.6 1.7 %collective-permute-done.3 = bf16[400,256]{1,0:T(8,128)(2,1)S(1)} collective-permute-done((bf16[400,256]{1,0:T(8,128)(2,1)S(1)}, bf16[400,256]{1,0:T(8,128)(2,1)S(1)}, u32[]{:S(2)}, u32[]{:S(2)}) %collective-permute-start.3) | collective-permute-done | bytes 204832 | tf_op jit(solution)/shard_map/ppermute | solution.py:30
  24.3 0.1 reshape.439
  24.4 0.1 sign_compare_fusion
  24.6 0.1 ne.160
  24.7 0.1 lt.99
  24.8 0.1 copy.46
  24.9 0.1 copy.39
  25.0 0.1 rem.151
  25.1 0.1 div.77
  25.2 0.1 copy.41
  25.3 0.1 copy.38
  25.4 0.1 fusion.14
  25.5 0.7 gather_fusion
  26.1 0.1 copy.47
  26.2 0.1 reshape.430
  26.3 0.2 copy.48
  26.5 0.7 select_n.125.slot_ref
  27.3 1.2 %pad_maximum_fusion = bf16[6,6,64,256]{3,2,1,0:T(8,128)(2,1)} fusion(bf16[6,1,64,256]{3,2,1,0:T(8,128)(2,1)S(1)} %bitcast.38, bf16[1,4,64,256]{3,2,1,0:T(8,128)(2,1)S(1)} %bitcast.35, bf16[4,4,64,256]{3,2,1,0:T(8,128)(2,1)S(1)} %copy-done, bf16[1,4,64,256]{3,2,1,0:T(8,128)(2,1)S(1)} %bitcast.33, bf16[6,1,64,256]{3,2,1,0:T(8,128)(2,1)S(1)} %bitcast.37), kind=kLoop, calls=%fused_computation.1 | loop fusion | flops 2359296 | bytes 2359296 | tf_op jit(solution)/shard_map/concatenate | solution.py:146
  28.5 15.7 %shard_map.64 = (f32[3,64,1600]{2,1,0:T(8,128)}, bf16[3,64,1600]{2,1,0:T(8,128)(2,1)}, bf16[3,64,1600]{2,1,0:T(8,128)(2,1)}) custom-call(s32[144]{0:T(256)} %add_clamp_fusion.pos_ref, s32[576]{0:T(1024)} %select_n.125.slot_ref, s32[64]{0:T(128)} %fusion.43.home_ref, bf16[16,64,576]{2,1,0:T(8,128)(2,1)} %bitcast.31, bf16[36,64,256]{2,1,0:T(8,128)(2,1)} %bitcast.30, ...), custom_call_target="tpu_custom_call" | custom-call | tf_op jit(solution)/shard_map/pallas_call | solution.py:168
  44.2 1.9 %collective-permute-start.4 = (bf16[3,64,1600]{2,1,0:T(8,128)(2,1)}, bf16[3,64,1600]{2,1,0:T(8,128)(2,1)S(1)}, u32[]{:S(2)}, u32[]{:S(2)}) collective-permute-start(bf16[3,64,1600]{2,1,0:T(8,128)(2,1)} %get-tuple-element.59), channel_id=1, source_target_pairs={{0,1},{1,2},{2,3},{4,5},{5,6},{6,7},{8,9},{9,10},{10,11},{12,13},{... | collective-permute-start | bytes 1843208 | tf_op jit(solution)/shard_map/ppermute | solution.py:30
  46.1 4.4 %collective-permute-start.5 = (bf16[3,64,1600]{2,1,0:T(8,128)(2,1)}, bf16[3,64,1600]{2,1,0:T(8,128)(2,1)S(1)}, u32[]{:S(2)}, u32[]{:S(2)}) collective-permute-start(bf16[3,64,1600]{2,1,0:T(8,128)(2,1)} %get-tuple-element.60), channel_id=1, source_target_pairs={{1,0},{2,1},{3,2},{5,4},{6,5},{7,6},{9,8},{10,9},{11,10},{13,12},{... | collective-permute-start | bytes 1843208 | tf_op jit(solution)/shard_map/ppermute | solution.py:30
  50.5 6.4 %collective-permute-done.4.left_ref = bf16[3,64,1600]{2,1,0:T(8,128)(2,1)S(1)} collective-permute-done((bf16[3,64,1600]{2,1,0:T(8,128)(2,1)}, bf16[3,64,1600]{2,1,0:T(8,128)(2,1)S(1)}, u32[]{:S(2)}, u32[]{:S(2)}) %collective-permute-start.4) | collective-permute-done | bytes 614432 | tf_op jit(solution)/shard_map/ppermute | solution.py:30
  56.9 1.9 %collective-permute-done.5.right_ref = bf16[3,64,1600]{2,1,0:T(8,128)(2,1)S(1)} collective-permute-done((bf16[3,64,1600]{2,1,0:T(8,128)(2,1)}, bf16[3,64,1600]{2,1,0:T(8,128)(2,1)S(1)}, u32[]{:S(2)}, u32[]{:S(2)}) %collective-permute-start.5) | collective-permute-done | bytes 614432 | tf_op jit(solution)/shard_map/ppermute | solution.py:30
  58.7 0.8 %copy-done.2 = bf16[3,64,1600]{2,1,0:T(8,128)(2,1)} copy-done((bf16[3,64,1600]{2,1,0:T(8,128)(2,1)}, bf16[3,64,1600]{2,1,0:T(8,128)(2,1)S(1)}, u32[]{:S(2)}) %copy-start.2) | copy-done | bytes 614424
  59.6 4.0 %shard_map.65 = (f32[64,2240]{1,0:T(8,128)}, bf16[2,64,2240]{2,1,0:T(8,128)(2,1)}) custom-call(f32[3,64,1600]{2,1,0:T(8,128)} %get-tuple-element.58.keep_ref, bf16[3,64,1600]{2,1,0:T(8,128)(2,1)} %copy-done.1, bf16[3,64,1600]{2,1,0:T(8,128)(2,1)} %copy-done.2), custom_call_target="tpu_custom_call" | custom-call | tf_op jit(solution)/shard_map/pallas_call | solution.py:200
  63.5 1.1 %slice_bitcast_fusion = (bf16[64,2240]{1,0:T(8,128)(2,1)S(1)}, bf16[64,2240]{1,0:T(8,128)(2,1)S(1)}) fusion(bf16[2,64,2240]{2,1,0:T(8,128)(2,1)} %get-tuple-element.62), kind=kLoop, calls=%fused_computation.5 | loop fusion | bytes 1146880 | tf_op jit(solution)/shard_map/squeeze | solution.py:210
  64.6 2.7 %collective-permute-start.7 = (bf16[64,2240]{1,0:T(8,128)(2,1)S(1)}, bf16[64,2240]{1,0:T(8,128)(2,1)S(1)}, u32[]{:S(2)}, u32[]{:S(2)}) collective-permute-start(bf16[64,2240]{1,0:T(8,128)(2,1)S(1)} %get-tuple-element.71), channel_id=1, source_target_pairs={{4,0},{5,1},{6,2},{7,3},{8,4},{9,5},{10,6},{11,7},{12,8},{13,9},{1... | collective-permute-start | bytes 860168 | tf_op jit(solution)/shard_map/ppermute | solution.py:30
  67.4 3.1 %collective-permute-start.6 = (bf16[64,2240]{1,0:T(8,128)(2,1)S(1)}, bf16[64,2240]{1,0:T(8,128)(2,1)S(1)}, u32[]{:S(2)}, u32[]{:S(2)}) collective-permute-start(bf16[64,2240]{1,0:T(8,128)(2,1)S(1)} %get-tuple-element.72), channel_id=1, source_target_pairs={{0,4},{1,5},{2,6},{3,7},{4,8},{5,9},{6,10},{7,11},{8,12},{9,13},{1... | collective-permute-start | bytes 860168 | tf_op jit(solution)/shard_map/ppermute | solution.py:30
  70.5 2.8 %collective-permute-done.7.down_ref = bf16[64,2240]{1,0:T(8,128)(2,1)S(1)} collective-permute-done((bf16[64,2240]{1,0:T(8,128)(2,1)S(1)}, bf16[64,2240]{1,0:T(8,128)(2,1)S(1)}, u32[]{:S(2)}, u32[]{:S(2)}) %collective-permute-start.7) | collective-permute-done | bytes 286752 | tf_op jit(solution)/shard_map/ppermute | solution.py:30
  73.3 3.6 %collective-permute-done.6.up_ref = bf16[64,2240]{1,0:T(8,128)(2,1)S(1)} collective-permute-done((bf16[64,2240]{1,0:T(8,128)(2,1)S(1)}, bf16[64,2240]{1,0:T(8,128)(2,1)S(1)}, u32[]{:S(2)}, u32[]{:S(2)}) %collective-permute-start.6) | collective-permute-done | bytes 286752 | tf_op jit(solution)/shard_map/ppermute | solution.py:30
  76.9 0.7 copy-done.4
  77.6 2.4 %shard_map.66 = bf16[64,3136]{1,0:T(8,128)(2,1)} custom-call(f32[64,2240]{1,0:T(8,128)} %get-tuple-element.61.keep_ref, bf16[64,2240]{1,0:T(8,128)(2,1)} %copy-done.4, bf16[64,2240]{1,0:T(8,128)(2,1)} %copy-done.3), custom_call_target="tpu_custom_call" | custom-call | tf_op jit(solution)/shard_map/pallas_call | solution.py:211
  (38 shorter events, 0.4 us)
Async XLA Ops:
  0.0 15.3 %copy-start = (bf16[4,4,64,256]{3,2,1,0:T(8,128)(2,1)S(1)}, bf16[4,4,64,256]{3,2,1,0:T(8,128)(2,1)}, u32[]{:S(2)}) copy-start(bf16[4,4,64,256]{3,2,1,0:T(8,128)(2,1)} %param.17) | copy-start | bytes 1572868
  0.0 13.9 %copy-start.5 = (s32[4,4,9]{2,1,0:T(4,128)S(1)}, s32[4,4,9]{2,1,0:T(4,128)}, u32[]{:S(2)}) copy-start(s32[4,4,9]{2,1,0:T(4,128)} %param.15) | copy-start | bytes 1732
  2.8 11.8 %collective-permute-start = (bf16[272,256]{1,0:T(8,128)(2,1)S(1)}, bf16[272,256]{1,0:T(8,128)(2,1)S(1)}, u32[]{:S(2)}, u32[]{:S(2)}) collective-permute-start(bf16[272,256]{1,0:T(8,128)(2,1)S(1)} %fusion.6), channel_id=1, source_target_pairs={{0,4},{1,5},{2,6},{3,7},{4,8},{5,9},{6,10},{7,11},{8,12},{9,13},{1... | collective-permute-start | bytes 417800 | tf_op jit(solution)/shard_map/ppermute | solution.py:30
  6.4 8.1 %collective-permute-start.1 = (bf16[272,256]{1,0:T(8,128)(2,1)S(1)}, bf16[272,256]{1,0:T(8,128)(2,1)S(1)}, u32[]{:S(2)}, u32[]{:S(2)}) collective-permute-start(bf16[272,256]{1,0:T(8,128)(2,1)S(1)} %fusion.7), channel_id=1, source_target_pairs={{4,0},{5,1},{6,2},{7,3},{8,4},{9,5},{10,6},{11,7},{12,8},{13,9},{1... | collective-permute-start | bytes 417800 | tf_op jit(solution)/shard_map/ppermute | solution.py:30
  15.4 7.1 %collective-permute-start.2 = (bf16[400,256]{1,0:T(8,128)(2,1)S(1)}, bf16[400,256]{1,0:T(8,128)(2,1)S(1)}, u32[]{:S(2)}, u32[]{:S(2)}) collective-permute-start(bf16[400,256]{1,0:T(8,128)(2,1)S(1)} %fusion.4), channel_id=1, source_target_pairs={{0,1},{1,2},{2,3},{4,5},{5,6},{6,7},{8,9},{9,10},{10,11},{12,13},{... | collective-permute-start | bytes 614408 | tf_op jit(solution)/shard_map/ppermute | solution.py:30
  17.4 6.9 %collective-permute-start.3 = (bf16[400,256]{1,0:T(8,128)(2,1)S(1)}, bf16[400,256]{1,0:T(8,128)(2,1)S(1)}, u32[]{:S(2)}, u32[]{:S(2)}) collective-permute-start(bf16[400,256]{1,0:T(8,128)(2,1)S(1)} %fusion.5), channel_id=1, source_target_pairs={{1,0},{2,1},{3,2},{5,4},{6,5},{7,6},{9,8},{10,9},{11,10},{13,12},{... | collective-permute-start | bytes 614408 | tf_op jit(solution)/shard_map/ppermute | solution.py:30
  44.2 12.7 %collective-permute-start.4 = (bf16[3,64,1600]{2,1,0:T(8,128)(2,1)}, bf16[3,64,1600]{2,1,0:T(8,128)(2,1)S(1)}, u32[]{:S(2)}, u32[]{:S(2)}) collective-permute-start(bf16[3,64,1600]{2,1,0:T(8,128)(2,1)} %get-tuple-element.59), channel_id=1, source_target_pairs={{0,1},{1,2},{2,3},{4,5},{5,6},{6,7},{8,9},{9,10},{10,11},{12,13},{... | collective-permute-start | bytes 1843208 | tf_op jit(solution)/shard_map/ppermute | solution.py:30
  46.1 12.6 %collective-permute-start.5 = (bf16[3,64,1600]{2,1,0:T(8,128)(2,1)}, bf16[3,64,1600]{2,1,0:T(8,128)(2,1)S(1)}, u32[]{:S(2)}, u32[]{:S(2)}) collective-permute-start(bf16[3,64,1600]{2,1,0:T(8,128)(2,1)} %get-tuple-element.60), channel_id=1, source_target_pairs={{1,0},{2,1},{3,2},{5,4},{6,5},{7,6},{9,8},{10,9},{11,10},{13,12},{... | collective-permute-start | bytes 1843208 | tf_op jit(solution)/shard_map/ppermute | solution.py:30
  56.9 1.9 %copy-start.1 = (bf16[3,64,1600]{2,1,0:T(8,128)(2,1)}, bf16[3,64,1600]{2,1,0:T(8,128)(2,1)S(1)}, u32[]{:S(2)}) copy-start(bf16[3,64,1600]{2,1,0:T(8,128)(2,1)S(1)} %collective-permute-done.4.left_ref) | copy-start | bytes 1843204
  58.7 0.8 %copy-start.2 = (bf16[3,64,1600]{2,1,0:T(8,128)(2,1)}, bf16[3,64,1600]{2,1,0:T(8,128)(2,1)S(1)}, u32[]{:S(2)}) copy-start(bf16[3,64,1600]{2,1,0:T(8,128)(2,1)S(1)} %collective-permute-done.5.right_ref) | copy-start | bytes 1843204
  64.6 8.6 %collective-permute-start.7 = (bf16[64,2240]{1,0:T(8,128)(2,1)S(1)}, bf16[64,2240]{1,0:T(8,128)(2,1)S(1)}, u32[]{:S(2)}, u32[]{:S(2)}) collective-permute-start(bf16[64,2240]{1,0:T(8,128)(2,1)S(1)} %get-tuple-element.71), channel_id=1, source_target_pairs={{4,0},{5,1},{6,2},{7,3},{8,4},{9,5},{10,6},{11,7},{12,8},{13,9},{1... | collective-permute-start | bytes 860168 | tf_op jit(solution)/shard_map/ppermute | solution.py:30
  67.4 9.5 %collective-permute-start.6 = (bf16[64,2240]{1,0:T(8,128)(2,1)S(1)}, bf16[64,2240]{1,0:T(8,128)(2,1)S(1)}, u32[]{:S(2)}, u32[]{:S(2)}) collective-permute-start(bf16[64,2240]{1,0:T(8,128)(2,1)S(1)} %get-tuple-element.72), channel_id=1, source_target_pairs={{0,4},{1,5},{2,6},{3,7},{4,8},{5,9},{6,10},{7,11},{8,12},{9,13},{1... | collective-permute-start | bytes 860168 | tf_op jit(solution)/shard_map/ppermute | solution.py:30
  73.3 3.6 %copy-start.3 = (bf16[64,2240]{1,0:T(8,128)(2,1)}, bf16[64,2240]{1,0:T(8,128)(2,1)S(1)}, u32[]{:S(2)}) copy-start(bf16[64,2240]{1,0:T(8,128)(2,1)S(1)} %collective-permute-done.7.down_ref) | copy-start | bytes 860164
  76.9 0.7 copy-start.4

commit v6 on v5

--- a/solution.py
+++ b/solution.py
@@ -30,18 +30,31 @@
     return lax.ppermute(value, ("row", "col"), pairs)
 
 
-def galerkin_kernel(pos_ref, slot_ref, home_ref, a_ref, p_ref, own_ref, keep_ref, right_ref, left_ref,
-                    acc_ref, prod_ref, dpt_ref):
+def galerkin_kernel(pos_ref, nslot_ref, count_ref, home_ref, a_ref, own_ref, above_ref, below_ref,
+                    left_ref, right_ref, keep_ref, to_right_ref, to_left_ref,
+                    acc_ref, prod_ref, dpt_ref, p_ref):
     patches = a_ref.shape[0]
+    rows, cols = AG, AG
+    hc = cols + 2
+    for x in range(rows):
+        for y in range(cols):
+            p_ref[(x + 1) * hc + y + 1] = own_ref[x * cols + y]
+    for y in range(cols):
+        p_ref[y + 1] = above_ref[y * B:(y + 1) * B]
+        p_ref[(rows + 1) * hc + y + 1] = below_ref[y * B:(y + 1) * B]
+    for x in range(rows + 2):
+        p_ref[x * hc] = left_ref[x * B:(x + 1) * B]
+        p_ref[x * hc + hc - 1] = right_ref[x * B:(x + 1) * B]
 
     def one_patch(i, carry):
         acc_ref[...] = jnp.zeros(acc_ref.shape, jnp.float32)
+        count = count_ref[i]
         for k in range(KA):
             pos = pos_ref[i * KA + k]
             a_blk = a_ref[i, :, k * B:(k + 1) * B]
             term = jnp.dot(a_blk, p_ref[pos], preferred_element_type=jnp.float32)
             for q in range(KP):
-                s = slot_ref[(i * KA + k) * KP + q]
+                s = jnp.where(k < count, nslot_ref[pos * KP + q], TRASH)
                 acc_ref[s] = acc_ref[s] + term[:, q * B:(q + 1) * B]
         row = pl.multiple_of(i * B, B)
         for w in range(WIN * WIN):
@@ -59,17 +72,17 @@
 
     prod = prod_ref[...]
     group = HOME * B
-    for out, at in ((right_ref, 0), (keep_ref, 1), (left_ref, 2)):
+    for out, at in ((to_right_ref, 0), (keep_ref, 1), (to_left_ref, 2)):
         terms = jnp.dot(dpt_ref[at * group:(at + 1) * group].astype(jnp.bfloat16), prod,
                         preferred_element_type=jnp.float32)
         out[...] = terms.reshape(out.shape).astype(out.dtype)
 
 
-def fold_cols_kernel(keep_ref, left_ref, right_ref, keep_out, send_out):
+def fold_cols_kernel(keep_ref, left_ref, right_ref, keep_out, minus_out, plus_out):
     src_w = WIN * B
     dst_w = OUTW * B
     for d in range(HOME):
-        out = keep_out if d == 1 else send_out.at[d // 2]
+        out = (minus_out, keep_out, plus_out)[d]
         for sx in range(WIN):
             lo = sx * dst_w
             s0 = sx * src_w
@@ -137,29 +150,28 @@
         return p_part, rel_part
 
     hr, hc = tile_rows + 2, tile_cols + 2
-    above, above_rel = unpack(shifted(payload(prolong[tile_rows - 1], rel[tile_rows - 1]), 1, 0), tile_cols)
-    below, below_rel = unpack(shifted(payload(prolong[0], rel[0]), -1, 0), tile_cols)
+    above_in = shifted(payload(prolong[tile_rows - 1], rel[tile_rows - 1]), 1, 0)
+    below_in = shifted(payload(prolong[0], rel[0]), -1, 0)
+    above, above_rel = unpack(above_in, tile_cols)
+    below, below_rel = unpack(below_in, tile_cols)
     tall = jnp.concatenate([above[None], prolong, below[None]], axis=0)
     tall_rel = jnp.concatenate([above_rel[None], rel, below_rel[None]], axis=0)
-    left, left_rel = unpack(shifted(payload(tall[:, tile_cols - 1], tall_rel[:, tile_cols - 1]), 0, 1), hr)
-    right, right_rel = unpack(shifted(payload(tall[:, 0], tall_rel[:, 0]), 0, -1), hr)
-    near_p = jnp.concatenate([left[:, None], tall, right[:, None]], axis=1).reshape(hr * hc, B, KP * B)
+    left_in = shifted(payload(tall[:, tile_cols - 1], tall_rel[:, tile_cols - 1]), 0, 1)
+    right_in = shifted(payload(tall[:, 0], tall_rel[:, 0]), 0, -1)
+    left_rel = unpack(left_in, hr)[1]
+    right_rel = unpack(right_in, hr)[1]
     near_rel = jnp.concatenate([left_rel[:, None], tall_rel, right_rel[:, None]], axis=1)
 
     off_r = (jnp.arange(hr, dtype=jnp.int32) + tile_rows - 1) // tile_rows - 1
     off_c = (jnp.arange(hc, dtype=jnp.int32) + tile_cols - 1) // tile_cols - 1
     near_slot = (near_rel // HOME + off_r[:, None, None] + 1) * WIN + near_rel % HOME + off_c[None, :, None] + 1
-    near_slot = jnp.where(near_rel < HOME * HOME, near_slot, TRASH).reshape(hr * hc, KP)
+    near_slot = jnp.where(near_rel < HOME * HOME, near_slot, TRASH).reshape(hr * hc * KP)
 
     first_row = row_index * tile_rows
     first_col = col_index * tile_cols
     targets = fine_columns.reshape(patches, KA)
     pos = (targets // grid_cols - first_row + 1) * hc + targets % grid_cols - first_col + 1
     pos = jnp.clip(pos, 0, hr * hc - 1)
-    slot = near_slot[pos]
-    blocks = jnp.arange(KA, dtype=jnp.int32)
-    used = blocks[None, :] < fine_counts.reshape(patches)[:, None]
-    slot = jnp.where(used[:, :, None], slot, TRASH)
     home = jnp.where(kept.reshape(patches, KP), hcol * HOME + hrow, HOME * HOME)
 
     smem = pltpu.MemorySpace.SMEM
@@ -172,42 +184,41 @@
             jax.ShapeDtypeStruct((HOME, B, width), SEND),
             jax.ShapeDtypeStruct((HOME, B, width), SEND),
         ),
-        in_specs=[
-            pl.BlockSpec(memory_space=smem),
-            pl.BlockSpec(memory_space=smem),
-            pl.BlockSpec(memory_space=smem),
-            pl.BlockSpec(memory_space=vmem),
-            pl.BlockSpec(memory_space=vmem),
-            pl.BlockSpec(memory_space=vmem),
-        ],
+        in_specs=[pl.BlockSpec(memory_space=smem)] * 4 + [pl.BlockSpec(memory_space=vmem)] * 6,
         out_specs=(pl.BlockSpec(memory_space=vmem),) * 3,
         scratch_shapes=[
             pltpu.VMEM((TRASH + 1, B, B), jnp.float32),
             pltpu.VMEM((patches * B, width), jnp.bfloat16),
             pltpu.VMEM(((HOME * HOME + 1) * B, patches * B), jnp.float32),
+            pltpu.VMEM((hr * hc, B, KP * B), jnp.bfloat16),
         ],
     )(
         pos.reshape(-1).astype(jnp.int32),
-        slot.reshape(-1).astype(jnp.int32),
+        near_slot.astype(jnp.int32),
+        fine_counts.reshape(-1).astype(jnp.int32),
         home.reshape(-1).astype(jnp.int32),
         fine_blocks.reshape(patches, B, KA * B),
-        near_p,
         prolong.reshape(patches, B, KP * B),
+        above_in,
+        below_in,
+        left_in,
+        right_in,
     )
-    left_in = shifted(to_left, 0, 1)
-    right_in = shifted(to_right, 0, -1)
+    from_left = shifted(to_left, 0, 1)
+    from_right = shifted(to_right, 0, -1)
     band = WIN * OUTW * B
-    keep2, send2 = pl.pallas_call(
+    keep2, minus, plus = pl.pallas_call(
         fold_cols_kernel,
         out_shape=(
             jax.ShapeDtypeStruct((B, band), jnp.float32),
-            jax.ShapeDtypeStruct((2, B, band), SEND),
+            jax.ShapeDtypeStruct((B, band), SEND),
+            jax.ShapeDtypeStruct((B, band), SEND),
         ),
         in_specs=[pl.BlockSpec(memory_space=vmem)] * 3,
-        out_specs=(pl.BlockSpec(memory_space=vmem), pl.BlockSpec(memory_space=vmem)),
-    )(keep, left_in, right_in)
-    up_in = shifted(send2[1], 1, 0)
-    down_in = shifted(send2[0], -1, 0)
+        out_specs=(pl.BlockSpec(memory_space=vmem),) * 3,
+    )(keep, from_left, from_right)
+    up_in = shifted(plus, 1, 0)
+    down_in = shifted(minus, -1, 0)
     out = pl.pallas_call(
         fold_rows_kernel,
         out_shape=jax.ShapeDtypeStruct((B, OUTW * OUTW * B), jnp.bfloat16),

time: 81.5 us -> 76.5 us (0.939)
  local copies, waits for them, and re-layouts: 11.9 us -> 7.91 us
    reshape x0 -> x1, local copies, waits for them, and re-layouts: none -> 1.34 us  [per_device(): fine_counts.reshape(-1).astype(jnp.int32)]
    concatenate x1 -> x0, other arithmetic: 1.21 us -> none  [per_device(): jnp.concatenate([left[:, None], tall, right[:, None]], axis=1)]
    squeeze x1 -> x0, local copies, waits for them, and re-layouts: 1.09 us -> none  [per_device(): down_in = shifted(send2[0], -1, 0)]
    select_n x3 -> x0, local copies, waits for them, and re-layouts: 0.99 us -> none  [the longest x2 0.9 us: per_device(): slot = jnp.where(used[:, :, None], slot, TRASH)]
    gather x3 -> x0, local copies, waits for them, and re-layouts: 0.85 us -> none  [per_device(): slot = near_slot[pos]]
    unnamed x13 -> x18, local copies, waits for them, and re-layouts: 2.42 us -> 1.59 us
  transfers between devices with their start and end apart: 8 -> 8, of which waited for: 6 -> 6; matrix products, arithmetic and copies ran while one was open for 6% -> 8% of each run, Pallas kernels for 0% -> 0%
where the time goes in v6:
time: 76.5 us; the launch traced here: 74.9 us
  starting transfers between devices  24.9 us (33%)
  Pallas kernels  21.9 us (29%)
  waiting for transfers between devices  17.1 us (22%)
  local copies, waits for them, and re-layouts  7.91 us (10%)
  other arithmetic  2.9 us (4%)
    ppermute x8, starting transfers between devices, shifted(): return lax.ppermute(value, ('row', 'col'), pairs)  24.9 us
    ppermute x8, waiting for transfers between devices, shifted(): return lax.ppermute(value, ('row', 'col'), pairs)  17.1 us
    pallas_call x1, Pallas kernels, per_device(): pl.pallas_call(galerkin_kernel, out_shape=(jax.ShapeDtypeStruct((HOME, B,...  15.6 us
    pallas_call x1, Pallas kernels, per_device(): pl.pallas_call(fold_cols_kernel, out_shape=(jax.ShapeDtypeStruct((B, band...  3.94 us
    pallas_call x1, Pallas kernels, per_device(): pl.pallas_call(fold_rows_kernel, out_shape=jax.ShapeDtypeStruct((B, OUTW...  2.4 us
    unnamed x18, local copies, waits for them, and re-layouts  1.59 us
  transfers between devices with their start and end apart: 8, of which 6 were waited for; matrix products, arithmetic and copies ran while one was open for 8% of the time, Pallas kernels for 0%

profile of v6, /device:TPU:20, one launch (start us, length us, event | category | flops | bytes accessed | tf_op | source)
XLA Modules:
  0.0 74.9 jit_solution(7434390102381048297)
XLA Ops:
  0.0 0.0 copy-start
  0.0 0.8 %fusion.35 = (bf16[4,4,4]{2,1,0:T(4,128)(2,1)S(1)}, s32[4,4,4]{2,1,0:T(4,128)S(1)}) fusion(s32[]{:T(128)S(6)} %axis_index.25, s32[]{:T(128)S(6)} %axis_index.23, s32[4,4,4]{2,1,0:T(4,128)} %param.18, s32[4,4]{1,0:T(4,128)} %param.19), kind=kLoop, calls=%fused_computation.78 | loop fusion | flops 1920 | bytes 712 | tf_op jit(solution)/shard_map/convert.7
  0.8 0.1 convert_element_type.88
  0.9 1.0 %fusion.37 = (bf16[1,4,64,256]{3,2,1,0:T(8,128)(2,1)S(1)}, bf16[1,4,64,256]{3,2,1,0:T(8,128)(2,1)S(1)}) fusion(bf16[4,4,64,256]{3,2,1,0:T(8,128)(2,1)} %param.17), kind=kLoop, calls=%fused_computation.79 | loop fusion | bytes 524288 | tf_op jit(solution)/shard_map/slice | solution.py:153
  1.9 3.4 %collective-permute-start = (bf16[272,256]{1,0:T(8,128)(2,1)S(1)}, bf16[272,256]{1,0:T(8,128)(2,1)S(1)}, u32[]{:S(2)}, u32[]{:S(2)}) collective-permute-start(bf16[272,256]{1,0:T(8,128)(2,1)S(1)} %fusion.6), channel_id=1, source_target_pairs={{0,4},{1,5},{2,6},{3,7},{4,8},{5,9},{6,10},{7,11},{8,12},{9,13},{1... | collective-permute-start | bytes 417800 | tf_op jit(solution)/shard_map/ppermute | solution.py:30
  5.3 0.1 convert_element_type.89
  5.4 3.3 %collective-permute-start.1 = (bf16[272,256]{1,0:T(8,128)(2,1)S(1)}, bf16[272,256]{1,0:T(8,128)(2,1)S(1)}, u32[]{:S(2)}, u32[]{:S(2)}) collective-permute-start(bf16[272,256]{1,0:T(8,128)(2,1)S(1)} %fusion.7), channel_id=1, source_target_pairs={{4,0},{5,1},{6,2},{7,3},{8,4},{9,5},{10,6},{11,7},{12,8},{13,9},{1... | collective-permute-start | bytes 417800 | tf_op jit(solution)/shard_map/ppermute | solution.py:30
  8.8 0.8 %reshape.264 = s32[64]{0:T(128)S(1)} reshape(s32[4,4,4]{2,1,0:T(4,128)} %param.18) | data formatting | bytes 512 | tf_op jit(solution)/shard_map/reshape | solution.py:135
  9.6 0.8 %lt.66 = s32[16]{0:T(128)S(1)} reshape(s32[4,4]{1,0:T(4,128)} %param.19) | data formatting | bytes 128 | tf_op jit(solution)/shard_map/lt | solution.py:133
  10.4 0.8 %reshape.262 = s32[144]{0:T(256)S(1)} reshape(s32[4,4,9]{2,1,0:T(4,128)} %param.15) | data formatting | bytes 1152 | tf_op jit(solution)/shard_map/reshape | solution.py:172
  11.1 0.1 iota_compare_fusion.2
  11.2 0.1 lt.69
  11.3 0.6 add_clamp_fusion.pos_ref
  11.9 0.5 fusion.29.home_ref
  12.5 1.3 %reshape.263.count_ref = s32[16]{0:T(128)} reshape(s32[4,4]{1,0:T(4,128)} %param.16) | data formatting | bytes 128 | tf_op jit(solution)/shard_map/reshape | solution.py:198
  13.8 0.0 collective-permute-done.above_ref
  13.8 0.0 copy-start.3
  13.8 0.1 reshape.268
  13.9 0.0 collective-permute-done.1.below_ref
  13.9 0.0 copy-start.4
  13.9 0.1 reshape.269
  14.1 0.1 convert_element_type.94
  14.2 0.1 convert_element_type.97
  14.3 0.0 copy-done
  14.3 0.1 pad_maximum_fusion.2
  14.4 1.9 %collective-permute-start.2 = (bf16[400,256]{1,0:T(8,128)(2,1)S(1)}, bf16[400,256]{1,0:T(8,128)(2,1)S(1)}, u32[]{:S(2)}, u32[]{:S(2)}) collective-permute-start(bf16[400,256]{1,0:T(8,128)(2,1)S(1)} %fusion.4), channel_id=1, source_target_pairs={{0,1},{1,2},{2,3},{4,5},{5,6},{6,7},{8,9},{9,10},{10,11},{12,13},{... | collective-permute-start | bytes 614408 | tf_op jit(solution)/shard_map/ppermute | solution.py:30
  16.3 3.6 %collective-permute-start.3 = (bf16[400,256]{1,0:T(8,128)(2,1)S(1)}, bf16[400,256]{1,0:T(8,128)(2,1)S(1)}, u32[]{:S(2)}, u32[]{:S(2)}) collective-permute-start(bf16[400,256]{1,0:T(8,128)(2,1)S(1)} %fusion.5), channel_id=1, source_target_pairs={{1,0},{2,1},{3,2},{5,4},{6,5},{7,6},{9,8},{10,9},{11,10},{13,12},{... | collective-permute-start | bytes 614408 | tf_op jit(solution)/shard_map/ppermute | solution.py:30
  20.0 0.1 add.164
  20.1 0.1 add.165
  20.2 0.1 add.158
  20.2 0.0 copy-done.3
  20.2 0.0 copy-done.4
  20.2 0.1 add.159
  20.4 1.1 %collective-permute-done.2.left_ref = bf16[400,256]{1,0:T(8,128)(2,1)S(1)} collective-permute-done((bf16[400,256]{1,0:T(8,128)(2,1)S(1)}, bf16[400,256]{1,0:T(8,128)(2,1)S(1)}, u32[]{:S(2)}, u32[]{:S(2)}) %collective-permute-start.2) | collective-permute-done | bytes 204832 | tf_op jit(solution)/shard_map/ppermute | solution.py:30
  21.5 0.0 copy-start.7
  21.5 0.1 reshape.272
  21.6 1.7 %collective-permute-done.3.right_ref = bf16[400,256]{1,0:T(8,128)(2,1)S(1)} collective-permute-done((bf16[400,256]{1,0:T(8,128)(2,1)S(1)}, bf16[400,256]{1,0:T(8,128)(2,1)S(1)}, u32[]{:S(2)}, u32[]{:S(2)}) %collective-permute-start.3) | collective-permute-done | bytes 204832 | tf_op jit(solution)/shard_map/ppermute | solution.py:30
  23.2 0.0 copy-start.8
  23.3 0.1 reshape.273
  23.4 0.1 ne.126
  23.5 0.1 lt.63
  23.6 0.1 div.69
  23.8 0.1 rem.134
  23.9 0.6 add_select_fusion.2.nslot_ref
  24.5 0.0 copy-done.7
  24.5 0.0 copy-done.8
  24.5 15.6 %shard_map.64 = (f32[3,64,1600]{2,1,0:T(8,128)}, bf16[3,64,1600]{2,1,0:T(8,128)(2,1)}, bf16[3,64,1600]{2,1,0:T(8,128)(2,1)}) custom-call(s32[144]{0:T(256)} %add_clamp_fusion.pos_ref, s32[144]{0:T(256)} %add_select_fusion.2.nslot_ref, s32[16]{0:T(128)} %reshape.263.count_ref, s32[64]{0:T(128)} %fusion.29.home_ref, bf16[16,64,576]{2,1,0:T(8,128)(2,1)} %bitcast.10, ...), custom_call_target="tpu_custom_call" | custom-call | tf_op jit(solution)/shard_map/pallas_call | solution.py:180
  40.0 1.9 %collective-permute-start.4 = (bf16[3,64,1600]{2,1,0:T(8,128)(2,1)}, bf16[3,64,1600]{2,1,0:T(8,128)(2,1)S(1)}, u32[]{:S(2)}, u32[]{:S(2)}) collective-permute-start(bf16[3,64,1600]{2,1,0:T(8,128)(2,1)} %get-tuple-element.60), channel_id=1, source_target_pairs={{0,1},{1,2},{2,3},{4,5},{5,6},{6,7},{8,9},{9,10},{10,11},{12,13},{... | collective-permute-start | bytes 1843208 | tf_op jit(solution)/shard_map/ppermute | solution.py:30
  41.9 4.0 %collective-permute-start.5 = (bf16[3,64,1600]{2,1,0:T(8,128)(2,1)}, bf16[3,64,1600]{2,1,0:T(8,128)(2,1)S(1)}, u32[]{:S(2)}, u32[]{:S(2)}) collective-permute-start(bf16[3,64,1600]{2,1,0:T(8,128)(2,1)} %get-tuple-element.61), channel_id=1, source_target_pairs={{1,0},{2,1},{3,2},{5,4},{6,5},{7,6},{9,8},{10,9},{11,10},{13,12},{... | collective-permute-start | bytes 1843208 | tf_op jit(solution)/shard_map/ppermute | solution.py:30
  45.9 6.4 %collective-permute-done.4.left_ref = bf16[3,64,1600]{2,1,0:T(8,128)(2,1)S(1)} collective-permute-done((bf16[3,64,1600]{2,1,0:T(8,128)(2,1)}, bf16[3,64,1600]{2,1,0:T(8,128)(2,1)S(1)}, u32[]{:S(2)}, u32[]{:S(2)}) %collective-permute-start.4) | collective-permute-done | bytes 614432 | tf_op jit(solution)/shard_map/ppermute | solution.py:30
  52.3 0.0 copy-start.1
  52.3 1.9 %collective-permute-done.5.right_ref = bf16[3,64,1600]{2,1,0:T(8,128)(2,1)S(1)} collective-permute-done((bf16[3,64,1600]{2,1,0:T(8,128)(2,1)}, bf16[3,64,1600]{2,1,0:T(8,128)(2,1)S(1)}, u32[]{:S(2)}, u32[]{:S(2)}) %collective-permute-start.5) | collective-permute-done | bytes 614432 | tf_op jit(solution)/shard_map/ppermute | solution.py:30
  54.2 0.0 copy-done.1
  54.2 0.9 %copy-done.2 = bf16[3,64,1600]{2,1,0:T(8,128)(2,1)} copy-done((bf16[3,64,1600]{2,1,0:T(8,128)(2,1)}, bf16[3,64,1600]{2,1,0:T(8,128)(2,1)S(1)}, u32[]{:S(2)}) %copy-start.2) | copy-done | bytes 614424
  55.0 3.9 %shard_map.65 = (f32[64,2240]{1,0:T(8,128)}, bf16[64,2240]{1,0:T(8,128)(2,1)}, bf16[64,2240]{1,0:T(8,128)(2,1)}) custom-call(f32[3,64,1600]{2,1,0:T(8,128)} %get-tuple-element.59.keep_ref, bf16[3,64,1600]{2,1,0:T(8,128)(2,1)} %copy-done.1, bf16[3,64,1600]{2,1,0:T(8,128)(2,1)} %copy-done.2), custom_call_target="tpu_custom_call" | custom-call | tf_op jit(solution)/shard_map/pallas_call | solution.py:210
  59.0 2.9 %collective-permute-start.6 = (bf16[64,2240]{1,0:T(8,128)(2,1)}, bf16[64,2240]{1,0:T(8,128)(2,1)S(1)}, u32[]{:S(2)}, u32[]{:S(2)}) collective-permute-start(bf16[64,2240]{1,0:T(8,128)(2,1)} %get-tuple-element.63), channel_id=1, source_target_pairs={{0,4},{1,5},{2,6},{3,7},{4,8},{5,9},{6,10},{7,11},{8,12},{9,13},{1... | collective-permute-start | bytes 860168 | tf_op jit(solution)/shard_map/ppermute | solution.py:30
  61.8 3.8 %collective-permute-start.7 = (bf16[64,2240]{1,0:T(8,128)(2,1)}, bf16[64,2240]{1,0:T(8,128)(2,1)S(1)}, u32[]{:S(2)}, u32[]{:S(2)}) collective-permute-start(bf16[64,2240]{1,0:T(8,128)(2,1)} %get-tuple-element.64), channel_id=1, source_target_pairs={{4,0},{5,1},{6,2},{7,3},{8,4},{9,5},{10,6},{11,7},{12,8},{13,9},{1... | collective-permute-start | bytes 860168 | tf_op jit(solution)/shard_map/ppermute | solution.py:30
  65.7 3.1 %collective-permute-done.6.up_ref = bf16[64,2240]{1,0:T(8,128)(2,1)S(1)} collective-permute-done((bf16[64,2240]{1,0:T(8,128)(2,1)}, bf16[64,2240]{1,0:T(8,128)(2,1)S(1)}, u32[]{:S(2)}, u32[]{:S(2)}) %collective-permute-start.6) | collective-permute-done | bytes 286752 | tf_op jit(solution)/shard_map/ppermute | solution.py:30
  68.8 0.0 copy-start.5
  68.8 3.1 %collective-permute-done.7.down_ref = bf16[64,2240]{1,0:T(8,128)(2,1)S(1)} collective-permute-done((bf16[64,2240]{1,0:T(8,128)(2,1)}, bf16[64,2240]{1,0:T(8,128)(2,1)S(1)}, u32[]{:S(2)}, u32[]{:S(2)}) %collective-permute-start.7) | collective-permute-done | bytes 286752 | tf_op jit(solution)/shard_map/ppermute | solution.py:30
  71.8 0.0 copy-start.6
  71.8 0.0 copy-done.5
  71.8 0.7 copy-done.6
  72.5 2.4 %shard_map.66 = bf16[64,3136]{1,0:T(8,128)(2,1)} custom-call(f32[64,2240]{1,0:T(8,128)} %get-tuple-element.62.keep_ref, bf16[64,2240]{1,0:T(8,128)(2,1)} %copy-done.5, bf16[64,2240]{1,0:T(8,128)(2,1)} %copy-done.6), custom_call_target="tpu_custom_call" | custom-call | tf_op jit(solution)/shard_map/pallas_call | solution.py:222
  (17 shorter events, 0.3 us)
Async XLA Ops:
  0.0 14.3 %copy-start = (bf16[4,4,64,256]{3,2,1,0:T(8,128)(2,1)S(1)}, bf16[4,4,64,256]{3,2,1,0:T(8,128)(2,1)}, u32[]{:S(2)}) copy-start(bf16[4,4,64,256]{3,2,1,0:T(8,128)(2,1)} %param.17) | copy-start | bytes 1572868
  1.9 11.9 %collective-permute-start = (bf16[272,256]{1,0:T(8,128)(2,1)S(1)}, bf16[272,256]{1,0:T(8,128)(2,1)S(1)}, u32[]{:S(2)}, u32[]{:S(2)}) collective-permute-start(bf16[272,256]{1,0:T(8,128)(2,1)S(1)} %fusion.6), channel_id=1, source_target_pairs={{0,4},{1,5},{2,6},{3,7},{4,8},{5,9},{6,10},{7,11},{8,12},{9,13},{1... | collective-permute-start | bytes 417800 | tf_op jit(solution)/shard_map/ppermute | solution.py:30
  5.4 8.5 %collective-permute-start.1 = (bf16[272,256]{1,0:T(8,128)(2,1)S(1)}, bf16[272,256]{1,0:T(8,128)(2,1)S(1)}, u32[]{:S(2)}, u32[]{:S(2)}) collective-permute-start(bf16[272,256]{1,0:T(8,128)(2,1)S(1)} %fusion.7), channel_id=1, source_target_pairs={{4,0},{5,1},{6,2},{7,3},{8,4},{9,5},{10,6},{11,7},{12,8},{13,9},{1... | collective-permute-start | bytes 417800 | tf_op jit(solution)/shard_map/ppermute | solution.py:30
  13.8 6.4 %copy-start.3 = (bf16[272,256]{1,0:T(8,128)(2,1)}, bf16[272,256]{1,0:T(8,128)(2,1)S(1)}, u32[]{:S(2)}) copy-start(bf16[272,256]{1,0:T(8,128)(2,1)S(1)} %collective-permute-done.above_ref) | copy-start | bytes 417796
  13.9 6.3 %copy-start.4 = (bf16[272,256]{1,0:T(8,128)(2,1)}, bf16[272,256]{1,0:T(8,128)(2,1)S(1)}, u32[]{:S(2)}) copy-start(bf16[272,256]{1,0:T(8,128)(2,1)S(1)} %collective-permute-done.1.below_ref) | copy-start | bytes 417796
  14.4 7.1 %collective-permute-start.2 = (bf16[400,256]{1,0:T(8,128)(2,1)S(1)}, bf16[400,256]{1,0:T(8,128)(2,1)S(1)}, u32[]{:S(2)}, u32[]{:S(2)}) collective-permute-start(bf16[400,256]{1,0:T(8,128)(2,1)S(1)} %fusion.4), channel_id=1, source_target_pairs={{0,1},{1,2},{2,3},{4,5},{5,6},{6,7},{8,9},{9,10},{10,11},{12,13},{... | collective-permute-start | bytes 614408 | tf_op jit(solution)/shard_map/ppermute | solution.py:30
  16.3 6.9 %collective-permute-start.3 = (bf16[400,256]{1,0:T(8,128)(2,1)S(1)}, bf16[400,256]{1,0:T(8,128)(2,1)S(1)}, u32[]{:S(2)}, u32[]{:S(2)}) collective-permute-start(bf16[400,256]{1,0:T(8,128)(2,1)S(1)} %fusion.5), channel_id=1, source_target_pairs={{1,0},{2,1},{3,2},{5,4},{6,5},{7,6},{9,8},{10,9},{11,10},{13,12},{... | collective-permute-start | bytes 614408 | tf_op jit(solution)/shard_map/ppermute | solution.py:30
  21.5 3.0 %copy-start.7 = (bf16[400,256]{1,0:T(8,128)(2,1)}, bf16[400,256]{1,0:T(8,128)(2,1)S(1)}, u32[]{:S(2)}) copy-start(bf16[400,256]{1,0:T(8,128)(2,1)S(1)} %collective-permute-done.2.left_ref) | copy-start | bytes 614404
  23.2 1.2 %copy-start.8 = (bf16[400,256]{1,0:T(8,128)(2,1)}, bf16[400,256]{1,0:T(8,128)(2,1)S(1)}, u32[]{:S(2)}) copy-start(bf16[400,256]{1,0:T(8,128)(2,1)S(1)} %collective-permute-done.3.right_ref) | copy-start | bytes 614404
  40.0 12.3 %collective-permute-start.4 = (bf16[3,64,1600]{2,1,0:T(8,128)(2,1)}, bf16[3,64,1600]{2,1,0:T(8,128)(2,1)S(1)}, u32[]{:S(2)}, u32[]{:S(2)}) collective-permute-start(bf16[3,64,1600]{2,1,0:T(8,128)(2,1)} %get-tuple-element.60), channel_id=1, source_target_pairs={{0,1},{1,2},{2,3},{4,5},{5,6},{6,7},{8,9},{9,10},{10,11},{12,13},{... | collective-permute-start | bytes 1843208 | tf_op jit(solution)/shard_map/ppermute | solution.py:30
  41.9 12.2 %collective-permute-start.5 = (bf16[3,64,1600]{2,1,0:T(8,128)(2,1)}, bf16[3,64,1600]{2,1,0:T(8,128)(2,1)S(1)}, u32[]{:S(2)}, u32[]{:S(2)}) collective-permute-start(bf16[3,64,1600]{2,1,0:T(8,128)(2,1)} %get-tuple-element.61), channel_id=1, source_target_pairs={{1,0},{2,1},{3,2},{5,4},{6,5},{7,6},{9,8},{10,9},{11,10},{13,12},{... | collective-permute-start | bytes 1843208 | tf_op jit(solution)/shard_map/ppermute | solution.py:30
  52.3 1.9 %copy-start.1 = (bf16[3,64,1600]{2,1,0:T(8,128)(2,1)}, bf16[3,64,1600]{2,1,0:T(8,128)(2,1)S(1)}, u32[]{:S(2)}) copy-start(bf16[3,64,1600]{2,1,0:T(8,128)(2,1)S(1)} %collective-permute-done.4.left_ref) | copy-start | bytes 1843204
  54.2 0.9 %copy-start.2 = (bf16[3,64,1600]{2,1,0:T(8,128)(2,1)}, bf16[3,64,1600]{2,1,0:T(8,128)(2,1)S(1)}, u32[]{:S(2)}) copy-start(bf16[3,64,1600]{2,1,0:T(8,128)(2,1)S(1)} %collective-permute-done.5.right_ref) | copy-start | bytes 1843204
  59.0 9.8 %collective-permute-start.6 = (bf16[64,2240]{1,0:T(8,128)(2,1)}, bf16[64,2240]{1,0:T(8,128)(2,1)S(1)}, u32[]{:S(2)}, u32[]{:S(2)}) collective-permute-start(bf16[64,2240]{1,0:T(8,128)(2,1)} %get-tuple-element.63), channel_id=1, source_target_pairs={{0,4},{1,5},{2,6},{3,7},{4,8},{5,9},{6,10},{7,11},{8,12},{9,13},{1... | collective-permute-start | bytes 860168 | tf_op jit(solution)/shard_map/ppermute | solution.py:30
  61.8 10.0 %collective-permute-start.7 = (bf16[64,2240]{1,0:T(8,128)(2,1)}, bf16[64,2240]{1,0:T(8,128)(2,1)S(1)}, u32[]{:S(2)}, u32[]{:S(2)}) collective-permute-start(bf16[64,2240]{1,0:T(8,128)(2,1)} %get-tuple-element.64), channel_id=1, source_target_pairs={{4,0},{5,1},{6,2},{7,3},{8,4},{9,5},{10,6},{11,7},{12,8},{13,9},{1... | collective-permute-start | bytes 860168 | tf_op jit(solution)/shard_map/ppermute | solution.py:30
  68.8 3.1 %copy-start.5 = (bf16[64,2240]{1,0:T(8,128)(2,1)}, bf16[64,2240]{1,0:T(8,128)(2,1)S(1)}, u32[]{:S(2)}) copy-start(bf16[64,2240]{1,0:T(8,128)(2,1)S(1)} %collective-permute-done.6.up_ref) | copy-start | bytes 860164
  71.8 0.7 copy-start.6

commit v7 on v6

--- a/solution.py
+++ b/solution.py
@@ -48,9 +48,11 @@
 
     def one_patch(i, carry):
         acc_ref[...] = jnp.zeros(acc_ref.shape, jnp.float32)
-        count = count_ref[i]
+        x = i // AG
+        y = i % AG
+        count = count_ref[x, y]
         for k in range(KA):
-            pos = pos_ref[i * KA + k]
+            pos = pos_ref[x, y, k]
             a_blk = a_ref[i, :, k * B:(k + 1) * B]
             term = jnp.dot(a_blk, p_ref[pos], preferred_element_type=jnp.float32)
             for q in range(KP):
@@ -67,7 +69,7 @@
     for i in range(patches):
         flipped = own_ref[i].astype(jnp.float32).T
         for p in range(KP):
-            start = pl.multiple_of(home_ref[i * KP + p] * B, B)
+            start = pl.multiple_of(home_ref[i // AG, i % AG, p] * B, B)
             dpt_ref[pl.ds(start, B), i * B:(i + 1) * B] += flipped[p * B:(p + 1) * B, :]
 
     prod = prod_ref[...]
@@ -132,10 +134,11 @@
     entries = jnp.arange(KP, dtype=jnp.int32)
     kept = entries[None, None, :] < prolong_counts[:, :, None]
 
-    own_codes = prolong_columns.reshape(patches, KP)
+    own_codes = prolong_columns
     hrow = jnp.clip(own_codes // coarse_grid_cols - row_index + 1, 0, HOME - 1)
     hcol = jnp.clip(own_codes % coarse_grid_cols - col_index + 1, 0, HOME - 1)
-    rel = jnp.where(kept, (hrow * HOME + hcol).reshape(tile_rows, tile_cols, KP), HOME * HOME)
+    rel = jnp.where(kept, hrow * HOME + hcol, HOME * HOME)
+    home_rc = hcol * HOME + hrow
 
     def payload(p_part, rel_part):
         count = p_part.shape[0]
@@ -169,10 +172,10 @@
 
     first_row = row_index * tile_rows
     first_col = col_index * tile_cols
-    targets = fine_columns.reshape(patches, KA)
+    targets = fine_columns
     pos = (targets // grid_cols - first_row + 1) * hc + targets % grid_cols - first_col + 1
     pos = jnp.clip(pos, 0, hr * hc - 1)
-    home = jnp.where(kept.reshape(patches, KP), hcol * HOME + hrow, HOME * HOME)
+    home = jnp.where(kept, home_rc, HOME * HOME)
 
     smem = pltpu.MemorySpace.SMEM
     vmem = pltpu.MemorySpace.VMEM
@@ -193,10 +196,10 @@
             pltpu.VMEM((hr * hc, B, KP * B), jnp.bfloat16),
         ],
     )(
-        pos.reshape(-1).astype(jnp.int32),
+        pos.astype(jnp.int32),
         near_slot.astype(jnp.int32),
-        fine_counts.reshape(-1).astype(jnp.int32),
-        home.reshape(-1).astype(jnp.int32),
+        fine_counts.astype(jnp.int32),
+        home.astype(jnp.int32),
         fine_blocks.reshape(patches, B, KA * B),
         prolong.reshape(patches, B, KP * B),
         above_in,

time: 76.5 us -> 76.4 us (level)
  local copies, waits for them, and re-layouts: 7.91 us -> 4.12 us
  waiting for transfers between devices: 17.1 us -> 20 us
    reshape x3 -> x0, local copies, waits for them, and re-layouts: 2.92 us -> none  [the longest x1 1.34 us: per_device(): fine_counts.reshape(-1).astype(jnp.int32)]
    ppermute x8, waiting for transfers between devices: 17.1 us -> 20 us  [shifted(): return lax.ppermute(value, ('row', 'col'), pairs)]
    lt x2 -> x0, local copies, waits for them, and re-layouts: 0.87 us -> none  [per_device(): kept = entries[None, None, :] < prolong_counts[:, :, None]]
  transfers between devices with their start and end apart: 8 -> 8, of which waited for: 6 -> 8; matrix products, arithmetic and copies ran while one was open for 8% -> 3% of each run, Pallas kernels for 0% -> 0%
where the time goes in v7:
time: 76.4 us; the launch traced here: 75 us
  starting transfers between devices  24.7 us (32%)
  Pallas kernels  22.4 us (29%)
  waiting for transfers between devices  20 us (26%)
  local copies, waits for them, and re-layouts  4.12 us (5%)
  other arithmetic  3.59 us (5%)
    ppermute x8, starting transfers between devices, shifted(): return lax.ppermute(value, ('row', 'col'), pairs)  24.7 us
    ppermute x8, waiting for transfers between devices, shifted(): return lax.ppermute(value, ('row', 'col'), pairs)  20 us
    pallas_call x1, Pallas kernels, per_device(): pl.pallas_call(galerkin_kernel, out_shape=(jax.ShapeDtypeStruct((HOME, B,...  16 us
    pallas_call x1, Pallas kernels, per_device(): pl.pallas_call(fold_cols_kernel, out_shape=(jax.ShapeDtypeStruct((B, band...  3.94 us
    pallas_call x1, Pallas kernels, per_device(): pl.pallas_call(fold_rows_kernel, out_shape=jax.ShapeDtypeStruct((B, OUTW...  2.4 us
    unnamed x18, local copies, waits for them, and re-layouts  1.59 us
  transfers between devices with their start and end apart: 8, of which 8 were waited for; matrix products, arithmetic and copies ran while one was open for 3% of the time, Pallas kernels for 0%

profile of v7, /device:TPU:20, one launch (start us, length us, event | category | flops | bytes accessed | tf_op | source)
XLA Modules:
  0.0 75.0 jit_solution(14900981534585198483)
XLA Ops:
  0.0 0.0 copy-start
  0.0 1.4 %fusion.31 = (bf16[4,4,4]{2,1,0:T(4,128)(2,1)S(1)}, s32[4,4,4]{2,1,0:T(4,128)S(1)}, s32[4,4,4]{2,1,0:T(4,128)}) fusion(s32[]{:T(128)S(6)} %axis_index.25, s32[]{:T(128)S(6)} %axis_index.23, s32[4,4,4]{2,1,0:T(4,128)} %param.18, s32[4,4]{1,0:T(4,128)} %param.19), kind=kLoop, calls=%fused_computation.72 | loop fusion | flops 2112 | bytes 968 | tf_op jit(solution)/shard_map/convert.7
  1.4 0.1 convert_element_type.88
  1.5 1.0 %fusion.32 = (bf16[1,4,64,256]{3,2,1,0:T(8,128)(2,1)S(1)}, bf16[1,4,64,256]{3,2,1,0:T(8,128)(2,1)S(1)}) fusion(bf16[4,4,64,256]{3,2,1,0:T(8,128)(2,1)} %param.17), kind=kLoop, calls=%fused_computation.73 | loop fusion | bytes 524288 | tf_op jit(solution)/shard_map/slice | solution.py:156
  2.5 3.4 %collective-permute-start = (bf16[272,256]{1,0:T(8,128)(2,1)S(1)}, bf16[272,256]{1,0:T(8,128)(2,1)S(1)}, u32[]{:S(2)}, u32[]{:S(2)}) collective-permute-start(bf16[272,256]{1,0:T(8,128)(2,1)S(1)} %fusion.6), channel_id=1, source_target_pairs={{0,4},{1,5},{2,6},{3,7},{4,8},{5,9},{6,10},{7,11},{8,12},{9,13},{1... | collective-permute-start | bytes 417800 | tf_op jit(solution)/shard_map/ppermute | solution.py:30
  5.9 0.1 convert_element_type.89
  6.0 3.3 %collective-permute-start.1 = (bf16[272,256]{1,0:T(8,128)(2,1)S(1)}, bf16[272,256]{1,0:T(8,128)(2,1)S(1)}, u32[]{:S(2)}, u32[]{:S(2)}) collective-permute-start(bf16[272,256]{1,0:T(8,128)(2,1)S(1)} %fusion.7), channel_id=1, source_target_pairs={{4,0},{5,1},{6,2},{7,3},{8,4},{9,5},{10,6},{11,7},{12,8},{13,9},{1... | collective-permute-start | bytes 417800 | tf_op jit(solution)/shard_map/ppermute | solution.py:30
  9.4 1.3 %add_clamp_fusion.pos_ref = s32[4,4,9]{2,1,0:T(4,128)} fusion(s32[4,4,9]{2,1,0:T(4,128)} %param.15, s32[]{:T(128)S(6)} %mul.28, s32[]{:T(128)S(6)} %mul.25), kind=kLoop, calls=%fused_computation.44 | loop fusion | flops 3744 | bytes 1160 | tf_op jit(solution)/shard_map/jit(clip)/min | solution.py:177
  10.7 0.1 collective-permute-done.above_ref
  10.8 0.0 copy-start.3
  10.8 0.1 reshape.246
  10.9 2.8 %collective-permute-done.1.below_ref = bf16[272,256]{1,0:T(8,128)(2,1)S(1)} collective-permute-done((bf16[272,256]{1,0:T(8,128)(2,1)S(1)}, bf16[272,256]{1,0:T(8,128)(2,1)S(1)}, u32[]{:S(2)}, u32[]{:S(2)}) %collective-permute-start.1) | collective-permute-done | bytes 139296 | tf_op jit(solution)/shard_map/ppermute | solution.py:30
  13.7 0.0 copy-start.4
  13.7 0.1 reshape.247
  13.9 0.1 convert_element_type.94
  13.9 0.1 convert_element_type.97
  14.1 0.0 copy-done
  14.1 0.1 pad_maximum_fusion.2
  14.2 1.9 %collective-permute-start.2 = (bf16[400,256]{1,0:T(8,128)(2,1)S(1)}, bf16[400,256]{1,0:T(8,128)(2,1)S(1)}, u32[]{:S(2)}, u32[]{:S(2)}) collective-permute-start(bf16[400,256]{1,0:T(8,128)(2,1)S(1)} %fusion.4), channel_id=1, source_target_pairs={{0,1},{1,2},{2,3},{4,5},{5,6},{6,7},{8,9},{9,10},{10,11},{12,13},{... | collective-permute-start | bytes 614408 | tf_op jit(solution)/shard_map/ppermute | solution.py:30
  16.1 3.6 %collective-permute-start.3 = (bf16[400,256]{1,0:T(8,128)(2,1)S(1)}, bf16[400,256]{1,0:T(8,128)(2,1)S(1)}, u32[]{:S(2)}, u32[]{:S(2)}) collective-permute-start(bf16[400,256]{1,0:T(8,128)(2,1)S(1)} %fusion.5), channel_id=1, source_target_pairs={{1,0},{2,1},{3,2},{5,4},{6,5},{7,6},{9,8},{10,9},{11,10},{13,12},{... | collective-permute-start | bytes 614408 | tf_op jit(solution)/shard_map/ppermute | solution.py:30
  19.8 0.1 add.143
  19.8 0.1 add.144
  20.0 0.1 add.137
  20.0 0.0 copy-done.3
  20.0 0.0 copy-done.4
  20.0 0.1 add.138
  20.1 1.1 %collective-permute-done.2.left_ref = bf16[400,256]{1,0:T(8,128)(2,1)S(1)} collective-permute-done((bf16[400,256]{1,0:T(8,128)(2,1)S(1)}, bf16[400,256]{1,0:T(8,128)(2,1)S(1)}, u32[]{:S(2)}, u32[]{:S(2)}) %collective-permute-start.2) | collective-permute-done | bytes 204832 | tf_op jit(solution)/shard_map/ppermute | solution.py:30
  21.2 0.0 copy-start.7
  21.3 0.1 reshape.250
  21.4 1.7 %collective-permute-done.3.right_ref = bf16[400,256]{1,0:T(8,128)(2,1)S(1)} collective-permute-done((bf16[400,256]{1,0:T(8,128)(2,1)S(1)}, bf16[400,256]{1,0:T(8,128)(2,1)S(1)}, u32[]{:S(2)}, u32[]{:S(2)}) %collective-permute-start.3) | collective-permute-done | bytes 204832 | tf_op jit(solution)/shard_map/ppermute | solution.py:30
  23.0 0.0 copy-start.8
  23.0 0.1 reshape.251
  23.2 0.1 ne.114
  23.3 0.1 lt.48
  23.4 0.1 div.63
  23.5 0.1 rem.115
  23.6 0.6 add_select_fusion.6.nslot_ref
  24.2 0.0 copy-done.7
  24.2 0.0 copy-done.8
  24.2 16.0 %shard_map.64 = (f32[3,64,1600]{2,1,0:T(8,128)}, bf16[3,64,1600]{2,1,0:T(8,128)(2,1)}, bf16[3,64,1600]{2,1,0:T(8,128)(2,1)}) custom-call(s32[4,4,9]{2,1,0:T(4,128)} %add_clamp_fusion.pos_ref, s32[144]{0:T(256)} %add_select_fusion.6.nslot_ref, s32[4,4]{1,0:T(4,128)} %count_ref.1, s32[4,4,4]{2,1,0:T(4,128)} %get-tuple-element.77.home_ref, ...), custom_call_target="tpu_custom_call" | custom-call | tf_op jit(solution)/shard_map/pallas_call | solution.py:183
  40.3 1.9 %collective-permute-start.4 = (bf16[3,64,1600]{2,1,0:T(8,128)(2,1)}, bf16[3,64,1600]{2,1,0:T(8,128)(2,1)S(1)}, u32[]{:S(2)}, u32[]{:S(2)}) collective-permute-start(bf16[3,64,1600]{2,1,0:T(8,128)(2,1)} %get-tuple-element.60), channel_id=1, source_target_pairs={{0,1},{1,2},{2,3},{4,5},{5,6},{6,7},{8,9},{9,10},{10,11},{12,13},{... | collective-permute-start | bytes 1843208 | tf_op jit(solution)/shard_map/ppermute | solution.py:30
  42.2 3.8 %collective-permute-start.5 = (bf16[3,64,1600]{2,1,0:T(8,128)(2,1)}, bf16[3,64,1600]{2,1,0:T(8,128)(2,1)S(1)}, u32[]{:S(2)}, u32[]{:S(2)}) collective-permute-start(bf16[3,64,1600]{2,1,0:T(8,128)(2,1)} %get-tuple-element.61), channel_id=1, source_target_pairs={{1,0},{2,1},{3,2},{5,4},{6,5},{7,6},{9,8},{10,9},{11,10},{13,12},{... | collective-permute-start | bytes 1843208 | tf_op jit(solution)/shard_map/ppermute | solution.py:30
  46.0 6.4 %collective-permute-done.4.left_ref = bf16[3,64,1600]{2,1,0:T(8,128)(2,1)S(1)} collective-permute-done((bf16[3,64,1600]{2,1,0:T(8,128)(2,1)}, bf16[3,64,1600]{2,1,0:T(8,128)(2,1)S(1)}, u32[]{:S(2)}, u32[]{:S(2)}) %collective-permute-start.4) | collective-permute-done | bytes 614432 | tf_op jit(solution)/shard_map/ppermute | solution.py:30
  52.3 0.0 copy-start.1
  52.3 1.9 %collective-permute-done.5.right_ref = bf16[3,64,1600]{2,1,0:T(8,128)(2,1)S(1)} collective-permute-done((bf16[3,64,1600]{2,1,0:T(8,128)(2,1)}, bf16[3,64,1600]{2,1,0:T(8,128)(2,1)S(1)}, u32[]{:S(2)}, u32[]{:S(2)}) %collective-permute-start.5) | collective-permute-done | bytes 614432 | tf_op jit(solution)/shard_map/ppermute | solution.py:30
  54.2 0.0 copy-start.2
  54.2 0.0 copy-done.1
  54.2 0.9 %copy-done.2 = bf16[3,64,1600]{2,1,0:T(8,128)(2,1)} copy-done((bf16[3,64,1600]{2,1,0:T(8,128)(2,1)}, bf16[3,64,1600]{2,1,0:T(8,128)(2,1)S(1)}, u32[]{:S(2)}) %copy-start.2) | copy-done | bytes 614424
  55.0 3.9 %shard_map.65 = (f32[64,2240]{1,0:T(8,128)}, bf16[64,2240]{1,0:T(8,128)(2,1)}, bf16[64,2240]{1,0:T(8,128)(2,1)}) custom-call(f32[3,64,1600]{2,1,0:T(8,128)} %get-tuple-element.59.keep_ref, bf16[3,64,1600]{2,1,0:T(8,128)(2,1)} %copy-done.1, bf16[3,64,1600]{2,1,0:T(8,128)(2,1)} %copy-done.2), custom_call_target="tpu_custom_call" | custom-call | tf_op jit(solution)/shard_map/pallas_call | solution.py:213
  59.0 3.9 %collective-permute-start.6 = (bf16[64,2240]{1,0:T(8,128)(2,1)}, bf16[64,2240]{1,0:T(8,128)(2,1)S(1)}, u32[]{:S(2)}, u32[]{:S(2)}) collective-permute-start(bf16[64,2240]{1,0:T(8,128)(2,1)} %get-tuple-element.63), channel_id=1, source_target_pairs={{0,4},{1,5},{2,6},{3,7},{4,8},{5,9},{6,10},{7,11},{8,12},{9,13},{1... | collective-permute-start | bytes 860168 | tf_op jit(solution)/shard_map/ppermute | solution.py:30
  62.8 2.9 %collective-permute-start.7 = (bf16[64,2240]{1,0:T(8,128)(2,1)}, bf16[64,2240]{1,0:T(8,128)(2,1)S(1)}, u32[]{:S(2)}, u32[]{:S(2)}) collective-permute-start(bf16[64,2240]{1,0:T(8,128)(2,1)} %get-tuple-element.64), channel_id=1, source_target_pairs={{4,0},{5,1},{6,2},{7,3},{8,4},{9,5},{10,6},{11,7},{12,8},{13,9},{1... | collective-permute-start | bytes 860168 | tf_op jit(solution)/shard_map/ppermute | solution.py:30
  65.7 3.0 %collective-permute-done.6.up_ref = bf16[64,2240]{1,0:T(8,128)(2,1)S(1)} collective-permute-done((bf16[64,2240]{1,0:T(8,128)(2,1)}, bf16[64,2240]{1,0:T(8,128)(2,1)S(1)}, u32[]{:S(2)}, u32[]{:S(2)}) %collective-permute-start.6) | collective-permute-done | bytes 286752 | tf_op jit(solution)/shard_map/ppermute | solution.py:30
  68.7 0.0 copy-start.5
  68.7 3.1 %collective-permute-done.7.down_ref = bf16[64,2240]{1,0:T(8,128)(2,1)S(1)} collective-permute-done((bf16[64,2240]{1,0:T(8,128)(2,1)}, bf16[64,2240]{1,0:T(8,128)(2,1)S(1)}, u32[]{:S(2)}, u32[]{:S(2)}) %collective-permute-start.7) | collective-permute-done | bytes 286752 | tf_op jit(solution)/shard_map/ppermute | solution.py:30
  71.8 0.0 copy-start.6
  71.9 0.0 copy-done.5
  71.9 0.7 copy-done.6
  72.6 2.4 %shard_map.66 = bf16[64,3136]{1,0:T(8,128)(2,1)} custom-call(f32[64,2240]{1,0:T(8,128)} %get-tuple-element.62.keep_ref, bf16[64,2240]{1,0:T(8,128)(2,1)} %copy-done.5, bf16[64,2240]{1,0:T(8,128)(2,1)} %copy-done.6), custom_call_target="tpu_custom_call" | custom-call | tf_op jit(solution)/shard_map/pallas_call | solution.py:225
  (16 shorter events, 0.3 us)
Async XLA Ops:
  0.0 14.1 %copy-start = (bf16[4,4,64,256]{3,2,1,0:T(8,128)(2,1)S(1)}, bf16[4,4,64,256]{3,2,1,0:T(8,128)(2,1)}, u32[]{:S(2)}) copy-start(bf16[4,4,64,256]{3,2,1,0:T(8,128)(2,1)} %param.17) | copy-start | bytes 1572868
  2.5 8.3 %collective-permute-start = (bf16[272,256]{1,0:T(8,128)(2,1)S(1)}, bf16[272,256]{1,0:T(8,128)(2,1)S(1)}, u32[]{:S(2)}, u32[]{:S(2)}) collective-permute-start(bf16[272,256]{1,0:T(8,128)(2,1)S(1)} %fusion.6), channel_id=1, source_target_pairs={{0,4},{1,5},{2,6},{3,7},{4,8},{5,9},{6,10},{7,11},{8,12},{9,13},{1... | collective-permute-start | bytes 417800 | tf_op jit(solution)/shard_map/ppermute | solution.py:30
  6.0 7.7 %collective-permute-start.1 = (bf16[272,256]{1,0:T(8,128)(2,1)S(1)}, bf16[272,256]{1,0:T(8,128)(2,1)S(1)}, u32[]{:S(2)}, u32[]{:S(2)}) collective-permute-start(bf16[272,256]{1,0:T(8,128)(2,1)S(1)} %fusion.7), channel_id=1, source_target_pairs={{4,0},{5,1},{6,2},{7,3},{8,4},{9,5},{10,6},{11,7},{12,8},{13,9},{1... | collective-permute-start | bytes 417800 | tf_op jit(solution)/shard_map/ppermute | solution.py:30
  10.8 9.2 %copy-start.3 = (bf16[272,256]{1,0:T(8,128)(2,1)}, bf16[272,256]{1,0:T(8,128)(2,1)S(1)}, u32[]{:S(2)}) copy-start(bf16[272,256]{1,0:T(8,128)(2,1)S(1)} %collective-permute-done.above_ref) | copy-start | bytes 417796
  13.7 6.3 %copy-start.4 = (bf16[272,256]{1,0:T(8,128)(2,1)}, bf16[272,256]{1,0:T(8,128)(2,1)S(1)}, u32[]{:S(2)}) copy-start(bf16[272,256]{1,0:T(8,128)(2,1)S(1)} %collective-permute-done.1.below_ref) | copy-start | bytes 417796
  14.2 7.1 %collective-permute-start.2 = (bf16[400,256]{1,0:T(8,128)(2,1)S(1)}, bf16[400,256]{1,0:T(8,128)(2,1)S(1)}, u32[]{:S(2)}, u32[]{:S(2)}) collective-permute-start(bf16[400,256]{1,0:T(8,128)(2,1)S(1)} %fusion.4), channel_id=1, source_target_pairs={{0,1},{1,2},{2,3},{4,5},{5,6},{6,7},{8,9},{9,10},{10,11},{12,13},{... | collective-permute-start | bytes 614408 | tf_op jit(solution)/shard_map/ppermute | solution.py:30
  16.1 6.9 %collective-permute-start.3 = (bf16[400,256]{1,0:T(8,128)(2,1)S(1)}, bf16[400,256]{1,0:T(8,128)(2,1)S(1)}, u32[]{:S(2)}, u32[]{:S(2)}) collective-permute-start(bf16[400,256]{1,0:T(8,128)(2,1)S(1)} %fusion.5), channel_id=1, source_target_pairs={{1,0},{2,1},{3,2},{5,4},{6,5},{7,6},{9,8},{10,9},{11,10},{13,12},{... | collective-permute-start | bytes 614408 | tf_op jit(solution)/shard_map/ppermute | solution.py:30
  21.2 3.0 %copy-start.7 = (bf16[400,256]{1,0:T(8,128)(2,1)}, bf16[400,256]{1,0:T(8,128)(2,1)S(1)}, u32[]{:S(2)}) copy-start(bf16[400,256]{1,0:T(8,128)(2,1)S(1)} %collective-permute-done.2.left_ref) | copy-start | bytes 614404
  23.0 1.2 %copy-start.8 = (bf16[400,256]{1,0:T(8,128)(2,1)}, bf16[400,256]{1,0:T(8,128)(2,1)S(1)}, u32[]{:S(2)}) copy-start(bf16[400,256]{1,0:T(8,128)(2,1)S(1)} %collective-permute-done.3.right_ref) | copy-start | bytes 614404
  40.3 12.0 %collective-permute-start.4 = (bf16[3,64,1600]{2,1,0:T(8,128)(2,1)}, bf16[3,64,1600]{2,1,0:T(8,128)(2,1)S(1)}, u32[]{:S(2)}, u32[]{:S(2)}) collective-permute-start(bf16[3,64,1600]{2,1,0:T(8,128)(2,1)} %get-tuple-element.60), channel_id=1, source_target_pairs={{0,1},{1,2},{2,3},{4,5},{5,6},{6,7},{8,9},{9,10},{10,11},{12,13},{... | collective-permute-start | bytes 1843208 | tf_op jit(solution)/shard_map/ppermute | solution.py:30
  42.2 12.0 %collective-permute-start.5 = (bf16[3,64,1600]{2,1,0:T(8,128)(2,1)}, bf16[3,64,1600]{2,1,0:T(8,128)(2,1)S(1)}, u32[]{:S(2)}, u32[]{:S(2)}) collective-permute-start(bf16[3,64,1600]{2,1,0:T(8,128)(2,1)} %get-tuple-element.61), channel_id=1, source_target_pairs={{1,0},{2,1},{3,2},{5,4},{6,5},{7,6},{9,8},{10,9},{11,10},{13,12},{... | collective-permute-start | bytes 1843208 | tf_op jit(solution)/shard_map/ppermute | solution.py:30
  52.3 1.9 %copy-start.1 = (bf16[3,64,1600]{2,1,0:T(8,128)(2,1)}, bf16[3,64,1600]{2,1,0:T(8,128)(2,1)S(1)}, u32[]{:S(2)}) copy-start(bf16[3,64,1600]{2,1,0:T(8,128)(2,1)S(1)} %collective-permute-done.4.left_ref) | copy-start | bytes 1843204
  54.2 0.9 %copy-start.2 = (bf16[3,64,1600]{2,1,0:T(8,128)(2,1)}, bf16[3,64,1600]{2,1,0:T(8,128)(2,1)S(1)}, u32[]{:S(2)}) copy-start(bf16[3,64,1600]{2,1,0:T(8,128)(2,1)S(1)} %collective-permute-done.5.right_ref) | copy-start | bytes 1843204
  59.0 9.7 %collective-permute-start.6 = (bf16[64,2240]{1,0:T(8,128)(2,1)}, bf16[64,2240]{1,0:T(8,128)(2,1)S(1)}, u32[]{:S(2)}, u32[]{:S(2)}) collective-permute-start(bf16[64,2240]{1,0:T(8,128)(2,1)} %get-tuple-element.63), channel_id=1, source_target_pairs={{0,4},{1,5},{2,6},{3,7},{4,8},{5,9},{6,10},{7,11},{8,12},{9,13},{1... | collective-permute-start | bytes 860168 | tf_op jit(solution)/shard_map/ppermute | solution.py:30
  62.8 9.0 %collective-permute-start.7 = (bf16[64,2240]{1,0:T(8,128)(2,1)}, bf16[64,2240]{1,0:T(8,128)(2,1)S(1)}, u32[]{:S(2)}, u32[]{:S(2)}) collective-permute-start(bf16[64,2240]{1,0:T(8,128)(2,1)} %get-tuple-element.64), channel_id=1, source_target_pairs={{4,0},{5,1},{6,2},{7,3},{8,4},{9,5},{10,6},{11,7},{12,8},{13,9},{1... | collective-permute-start | bytes 860168 | tf_op jit(solution)/shard_map/ppermute | solution.py:30
  68.7 3.1 %copy-start.5 = (bf16[64,2240]{1,0:T(8,128)(2,1)}, bf16[64,2240]{1,0:T(8,128)(2,1)S(1)}, u32[]{:S(2)}) copy-start(bf16[64,2240]{1,0:T(8,128)(2,1)S(1)} %collective-permute-done.6.up_ref) | copy-start | bytes 860164
  71.8 0.7 copy-start.6

commit v8 on v7

--- a/solution.py
+++ b/solution.py
@@ -30,9 +30,53 @@
     return lax.ppermute(value, ("row", "col"), pairs)
 
 
-def galerkin_kernel(pos_ref, nslot_ref, count_ref, home_ref, a_ref, own_ref, above_ref, below_ref,
-                    left_ref, right_ref, keep_ref, to_right_ref, to_left_ref,
-                    acc_ref, prod_ref, dpt_ref, p_ref):
+def is_local(pos):
+    hc = AG + 2
+    px = pos // hc
+    py = pos % hc
+    inside = (px >= 1) & (px <= AG) & (py >= 1) & (py <= AG)
+    return inside, jnp.clip((px - 1) * AG + py - 1, 0, AG * AG - 1)
+
+
+def local_kernel(pos_ref, lslot_ref, count_ref, home_ref, a_ref, own_ref, part_ref, dpt_out,
+                 acc_ref, dpt_ref):
+    patches = a_ref.shape[0]
+
+    def one_patch(i, carry):
+        acc_ref[...] = jnp.zeros(acc_ref.shape, jnp.float32)
+        x = i // AG
+        y = i % AG
+        count = count_ref[x, y]
+        for k in range(KA):
+            inside, li = is_local(pos_ref[x, y, k])
+
+            @pl.when(inside & (k < count))
+            def _():
+                term = jnp.dot(a_ref[i, :, k * B:(k + 1) * B], own_ref[li],
+                               preferred_element_type=jnp.float32)
+                for q in range(KP):
+                    s = lslot_ref[li // AG, li % AG, q]
+                    acc_ref[s] = acc_ref[s] + term[:, q * B:(q + 1) * B]
+
+        row = pl.multiple_of(i * B, B)
+        for w in range(WIN * WIN):
+            part_ref[pl.ds(row, B), w * B:(w + 1) * B] = acc_ref[w]
+        return carry
+
+    lax.fori_loop(0, patches, one_patch, 0)
+
+    dpt_ref[...] = jnp.zeros(dpt_ref.shape, jnp.float32)
+    for i in range(patches):
+        flipped = own_ref[i].astype(jnp.float32).T
+        for p in range(KP):
+            start = pl.multiple_of(home_ref[i // AG, i % AG, p] * B, B)
+            dpt_ref[pl.ds(start, B), i * B:(i + 1) * B] += flipped[p * B:(p + 1) * B, :]
+    dpt_out[...] = dpt_ref[...].astype(dpt_out.dtype)
+
+
+def galerkin_kernel(pos_ref, nslot_ref, count_ref, a_ref, own_ref, above_ref, below_ref,
+                    left_ref, right_ref, part_ref, dpt_ref, keep_ref, to_right_ref, to_left_ref,
+                    acc_ref, prod_ref, p_ref):
     patches = a_ref.shape[0]
     rows, cols = AG, AG
     hc = cols + 2
@@ -47,35 +91,35 @@
         p_ref[x * hc + hc - 1] = right_ref[x * B:(x + 1) * B]
 
     def one_patch(i, carry):
-        acc_ref[...] = jnp.zeros(acc_ref.shape, jnp.float32)
+        row = pl.multiple_of(i * B, B)
+        for w in range(WIN * WIN):
+            acc_ref[w] = part_ref[pl.ds(row, B), w * B:(w + 1) * B]
+        acc_ref[TRASH] = jnp.zeros((B, B), jnp.float32)
         x = i // AG
         y = i % AG
         count = count_ref[x, y]
         for k in range(KA):
             pos = pos_ref[x, y, k]
-            a_blk = a_ref[i, :, k * B:(k + 1) * B]
-            term = jnp.dot(a_blk, p_ref[pos], preferred_element_type=jnp.float32)
-            for q in range(KP):
-                s = jnp.where(k < count, nslot_ref[pos * KP + q], TRASH)
-                acc_ref[s] = acc_ref[s] + term[:, q * B:(q + 1) * B]
-        row = pl.multiple_of(i * B, B)
+            inside, _ = is_local(pos)
+
+            @pl.when(jnp.logical_not(inside) & (k < count))
+            def _():
+                term = jnp.dot(a_ref[i, :, k * B:(k + 1) * B], p_ref[pos],
+                               preferred_element_type=jnp.float32)
+                for q in range(KP):
+                    s = nslot_ref[pos * KP + q]
+                    acc_ref[s] = acc_ref[s] + term[:, q * B:(q + 1) * B]
+
         for w in range(WIN * WIN):
             prod_ref[pl.ds(row, B), w * B:(w + 1) * B] = acc_ref[w].astype(jnp.bfloat16)
         return carry
 
     lax.fori_loop(0, patches, one_patch, 0)
 
-    dpt_ref[...] = jnp.zeros(dpt_ref.shape, jnp.float32)
-    for i in range(patches):
-        flipped = own_ref[i].astype(jnp.float32).T
-        for p in range(KP):
-            start = pl.multiple_of(home_ref[i // AG, i % AG, p] * B, B)
-            dpt_ref[pl.ds(start, B), i * B:(i + 1) * B] += flipped[p * B:(p + 1) * B, :]
-
     prod = prod_ref[...]
     group = HOME * B
     for out, at in ((to_right_ref, 0), (keep_ref, 1), (to_left_ref, 2)):
-        terms = jnp.dot(dpt_ref[at * group:(at + 1) * group].astype(jnp.bfloat16), prod,
+        terms = jnp.dot(dpt_ref[at * group:(at + 1) * group], prod,
                         preferred_element_type=jnp.float32)
         out[...] = terms.reshape(out.shape).astype(out.dtype)
 
@@ -180,6 +224,28 @@
     smem = pltpu.MemorySpace.SMEM
     vmem = pltpu.MemorySpace.VMEM
     width = WIN * WIN * B
+    local_slot = (rel // HOME + 1) * WIN + rel % HOME + 1
+    local_slot = jnp.where(rel < HOME * HOME, local_slot, TRASH)
+    part, dpt = pl.pallas_call(
+        local_kernel,
+        out_shape=(
+            jax.ShapeDtypeStruct((patches * B, width), jnp.float32),
+            jax.ShapeDtypeStruct(((HOME * HOME + 1) * B, patches * B), jnp.bfloat16),
+        ),
+        in_specs=[pl.BlockSpec(memory_space=smem)] * 4 + [pl.BlockSpec(memory_space=vmem)] * 2,
+        out_specs=(pl.BlockSpec(memory_space=vmem),) * 2,
+        scratch_shapes=[
+            pltpu.VMEM((TRASH + 1, B, B), jnp.float32),
+            pltpu.VMEM(((HOME * HOME + 1) * B, patches * B), jnp.float32),
+        ],
+    )(
+        pos.astype(jnp.int32),
+        local_slot.astype(jnp.int32),
+        fine_counts.astype(jnp.int32),
+        home.astype(jnp.int32),
+        fine_blocks.reshape(patches, B, KA * B),
+        prolong.reshape(patches, B, KP * B),
+    )
     keep, to_right, to_left = pl.pallas_call(
         galerkin_kernel,
         out_shape=(
@@ -187,25 +253,25 @@
             jax.ShapeDtypeStruct((HOME, B, width), SEND),
             jax.ShapeDtypeStruct((HOME, B, width), SEND),
         ),
-        in_specs=[pl.BlockSpec(memory_space=smem)] * 4 + [pl.BlockSpec(memory_space=vmem)] * 6,
+        in_specs=[pl.BlockSpec(memory_space=smem)] * 3 + [pl.BlockSpec(memory_space=vmem)] * 8,
         out_specs=(pl.BlockSpec(memory_space=vmem),) * 3,
         scratch_shapes=[
             pltpu.VMEM((TRASH + 1, B, B), jnp.float32),
             pltpu.VMEM((patches * B, width), jnp.bfloat16),
-            pltpu.VMEM(((HOME * HOME + 1) * B, patches * B), jnp.float32),
             pltpu.VMEM((hr * hc, B, KP * B), jnp.bfloat16),
         ],
     )(
         pos.astype(jnp.int32),
         near_slot.astype(jnp.int32),
         fine_counts.astype(jnp.int32),
-        home.astype(jnp.int32),
         fine_blocks.reshape(patches, B, KA * B),
         prolong.reshape(patches, B, KP * B),
         above_in,
         below_in,
         left_in,
         right_in,
+        part,
+        dpt,
     )
     from_left = shifted(to_left, 0, 1)
     from_right = shifted(to_right, 0, -1)

time: 76.4 us -> 116 us (1.52)
  Pallas kernels: 22.4 us -> 57.7 us
  starting transfers between devices: 24.7 us -> 26.8 us
  waiting for transfers between devices: 20 us -> 21.3 us
    pallas_call x0 -> x1, Pallas kernels: none -> 27.6 us  [per_device(): pl.pallas_call(local_kernel, out_shape=(jax.ShapeDtypeStruct((patches * B...]
    pallas_call x1, Pallas kernels: 16 us -> 23.8 us  [per_device(): pl.pallas_call(galerkin_kernel, out_shape=(jax.ShapeDtypeStruct((HOME, B,...]
    ppermute x8, starting transfers between devices: 24.7 us -> 26.8 us  [shifted(): return lax.ppermute(value, ('row', 'col'), pairs)]
    select_n x0 -> x1, other arithmetic: none -> 1.45 us  [per_device(): local_slot = jnp.where(rel < HOME * HOME, local_slot, TRASH)]
    another operation x2, other arithmetic: 1.42 us -> 0.01 us
    ppermute x8, waiting for transfers between devices: 20 us -> 21.3 us  [shifted(): return lax.ppermute(value, ('row', 'col'), pairs)]
  transfers between devices with their start and end apart: 8 -> 8, of which waited for: 8 -> 6; matrix products, arithmetic and copies ran while one was open for 3% -> 2% of each run, Pallas kernels for 0% -> 24%
where the time goes in v8:
time: 116 us; the launch traced here: 114 us
  Pallas kernels  57.7 us (50%)
  starting transfers between devices  26.8 us (23%)
  waiting for transfers between devices  21.3 us (18%)
  local copies, waits for them, and re-layouts  4.1 us (4%)
  other arithmetic  3.63 us (3%)
    pallas_call x1, Pallas kernels, per_device(): pl.pallas_call(local_kernel, out_shape=(jax.ShapeDtypeStruct((patches * B...  27.6 us
    ppermute x8, starting transfers between devices, shifted(): return lax.ppermute(value, ('row', 'col'), pairs)  26.8 us
    pallas_call x1, Pallas kernels, per_device(): pl.pallas_call(galerkin_kernel, out_shape=(jax.ShapeDtypeStruct((HOME, B,...  23.8 us
    ppermute x8, waiting for transfers between devices, shifted(): return lax.ppermute(value, ('row', 'col'), pairs)  21.3 us
    pallas_call x1, Pallas kernels, per_device(): pl.pallas_call(fold_cols_kernel, out_shape=(jax.ShapeDtypeStruct((B, band...  3.96 us
    pallas_call x1, Pallas kernels, per_device(): pl.pallas_call(fold_rows_kernel, out_shape=jax.ShapeDtypeStruct((B, OUTW...  2.4 us
  transfers between devices with their start and end apart: 8, of which 6 were waited for; matrix products, arithmetic and copies ran while one was open for 2% of the time, Pallas kernels for 24%

profile of v8, /device:TPU:20, one launch (start us, length us, event | category | flops | bytes accessed | tf_op | source)
XLA Modules:
  0.0 113.8 jit_solution(3243906283383827811)
XLA Ops:
  0.0 0.0 copy-start
  0.0 1.4 %fusion.21 = (s32[4,4,4]{2,1,0:T(4,128)}, s32[4,4,4]{2,1,0:T(4,128)S(1)}, s32[4,4,4]{2,1,0:T(4,128)}) fusion(s32[]{:T(128)S(6)} %axis_index.25, s32[]{:T(128)S(6)} %axis_index.23, s32[4,4,4]{2,1,0:T(4,128)} %param.18, s32[4,4]{1,0:T(4,128)} %param.19), kind=kLoop, calls=%fused_computation.44 | loop fusion | flops 3200 | bytes 1096 | tf_op jit(solution)/shard_map/jit(_where)/select_n | solution.py:228
  1.5 0.1 convert_element_type.88
  1.6 1.0 fusion.35
  2.6 3.4 %collective-permute-start = (bf16[272,256]{1,0:T(8,128)(2,1)S(1)}, bf16[272,256]{1,0:T(8,128)(2,1)S(1)}, u32[]{:S(2)}, u32[]{:S(2)}) collective-permute-start(bf16[272,256]{1,0:T(8,128)(2,1)S(1)} %fusion.6), channel_id=1, source_target_pairs={{0,4},{1,5},{2,6},{3,7},{4,8},{5,9},{6,10},{7,11},{8,12},{9,13},{1... | collective-permute-start | bytes 417800 | tf_op jit(solution)/shard_map/ppermute | solution.py:30
  6.0 0.1 convert_element_type.89
  6.1 3.3 %collective-permute-start.1 = (bf16[272,256]{1,0:T(8,128)(2,1)S(1)}, bf16[272,256]{1,0:T(8,128)(2,1)S(1)}, u32[]{:S(2)}, u32[]{:S(2)}) collective-permute-start(bf16[272,256]{1,0:T(8,128)(2,1)S(1)} %fusion.7), channel_id=1, source_target_pairs={{4,0},{5,1},{6,2},{7,3},{8,4},{9,5},{10,6},{11,7},{12,8},{13,9},{1... | collective-permute-start | bytes 417800 | tf_op jit(solution)/shard_map/ppermute | solution.py:30
  9.4 1.3 %add_clamp_fusion.pos_ref = s32[4,4,9]{2,1,0:T(4,128)} fusion(s32[4,4,9]{2,1,0:T(4,128)} %param.15, s32[]{:T(128)S(6)} %mul.34, s32[]{:T(128)S(6)} %mul.31), kind=kLoop, calls=%fused_computation.50 | loop fusion | flops 3744 | bytes 1160 | tf_op jit(solution)/shard_map/jit(clip)/min | solution.py:221
  10.7 0.1 collective-permute-done.above_ref
  10.8 0.0 copy-start.3
  10.9 0.1 reshape.248
  10.9 2.8 %collective-permute-done.1.below_ref = bf16[272,256]{1,0:T(8,128)(2,1)S(1)} collective-permute-done((bf16[272,256]{1,0:T(8,128)(2,1)S(1)}, bf16[272,256]{1,0:T(8,128)(2,1)S(1)}, u32[]{:S(2)}, u32[]{:S(2)}) %collective-permute-start.1) | collective-permute-done | bytes 139296 | tf_op jit(solution)/shard_map/ppermute | solution.py:30
  13.8 0.0 copy-start.4
  13.8 0.1 reshape.249
  13.9 0.1 convert_element_type.94
  14.0 0.1 convert_element_type.97
  14.1 0.0 copy-done
  14.1 0.1 pad_maximum_fusion.2
  14.2 1.9 %collective-permute-start.2 = (bf16[400,256]{1,0:T(8,128)(2,1)S(1)}, bf16[400,256]{1,0:T(8,128)(2,1)S(1)}, u32[]{:S(2)}, u32[]{:S(2)}) collective-permute-start(bf16[400,256]{1,0:T(8,128)(2,1)S(1)} %fusion.4), channel_id=1, source_target_pairs={{0,1},{1,2},{2,3},{4,5},{5,6},{6,7},{8,9},{9,10},{10,11},{12,13},{... | collective-permute-start | bytes 614408 | tf_op jit(solution)/shard_map/ppermute | solution.py:30
  16.2 3.6 %collective-permute-start.3 = (bf16[400,256]{1,0:T(8,128)(2,1)S(1)}, bf16[400,256]{1,0:T(8,128)(2,1)S(1)}, u32[]{:S(2)}, u32[]{:S(2)}) collective-permute-start(bf16[400,256]{1,0:T(8,128)(2,1)S(1)} %fusion.5), channel_id=1, source_target_pairs={{1,0},{2,1},{3,2},{5,4},{6,5},{7,6},{9,8},{10,9},{11,10},{13,12},{... | collective-permute-start | bytes 614408 | tf_op jit(solution)/shard_map/ppermute | solution.py:30
  19.8 0.1 add.157
  19.9 0.1 add.158
  20.0 0.1 add.151
  20.1 0.0 copy-done.3
  20.1 0.0 copy-done.4
  20.1 0.1 add.152
  20.2 27.6 %shard_map.64 = (f32[1024,1600]{1,0:T(8,128)}, bf16[640,1024]{1,0:T(8,128)(2,1)}) custom-call(s32[4,4,9]{2,1,0:T(4,128)} %add_clamp_fusion.pos_ref, s32[4,4,4]{2,1,0:T(4,128)} %get-tuple-element.71.lslot_ref, s32[4,4]{1,0:T(4,128)} %count_ref.3, s32[4,4,4]{2,1,0:T(4,128)} %get-tuple-element.81.home_ref, bf16[16,64,576]{2,1,0:T(8,128)(2,1)} %bitcast.11, ...), custom_call_target="tpu_custom_call" | custom-call | tf_op jit(solution)/shard_map/pallas_call | solution.py:229
  47.8 0.0 collective-permute-done.2.left_ref
  47.8 0.0 copy-start.7
  47.8 0.1 reshape.252
  47.9 0.0 collective-permute-done.3.right_ref
  47.9 0.0 copy-start.8
  47.9 0.1 reshape.253
  48.1 0.1 ne.125
  48.2 0.1 lt.56
  48.3 0.1 div.67
  48.4 0.1 rem.121
  48.5 0.6 add_select_fusion.8.nslot_ref
  49.1 0.0 copy-done.7
  49.1 0.0 copy-done.8
  49.1 23.8 %shard_map.65 = (f32[3,64,1600]{2,1,0:T(8,128)}, bf16[3,64,1600]{2,1,0:T(8,128)(2,1)}, bf16[3,64,1600]{2,1,0:T(8,128)(2,1)}) custom-call(s32[4,4,9]{2,1,0:T(4,128)} %add_clamp_fusion.pos_ref, s32[144]{0:T(256)} %add_select_fusion.8.nslot_ref, s32[4,4]{1,0:T(4,128)} %count_ref.3, bf16[16,64,576]{2,1,0:T(8,128)(2,1)} %bitcast.12, ...), custom_call_target="tpu_custom_call" | custom-call | tf_op jit(solution)/shard_map/pallas_call | solution.py:249
  72.9 1.9 %collective-permute-start.4 = (bf16[3,64,1600]{2,1,0:T(8,128)(2,1)}, bf16[3,64,1600]{2,1,0:T(8,128)(2,1)S(1)}, u32[]{:S(2)}, u32[]{:S(2)}) collective-permute-start(bf16[3,64,1600]{2,1,0:T(8,128)(2,1)} %get-tuple-element.64), channel_id=1, source_target_pairs={{0,1},{1,2},{2,3},{4,5},{5,6},{6,7},{8,9},{9,10},{10,11},{12,13},{... | collective-permute-start | bytes 1843208 | tf_op jit(solution)/shard_map/ppermute | solution.py:30
  74.8 3.6 %collective-permute-start.5 = (bf16[3,64,1600]{2,1,0:T(8,128)(2,1)}, bf16[3,64,1600]{2,1,0:T(8,128)(2,1)S(1)}, u32[]{:S(2)}, u32[]{:S(2)}) collective-permute-start(bf16[3,64,1600]{2,1,0:T(8,128)(2,1)} %get-tuple-element.65), channel_id=1, source_target_pairs={{1,0},{2,1},{3,2},{5,4},{6,5},{7,6},{9,8},{10,9},{11,10},{13,12},{... | collective-permute-start | bytes 1843208 | tf_op jit(solution)/shard_map/ppermute | solution.py:30
  78.5 6.4 %collective-permute-done.4.left_ref = bf16[3,64,1600]{2,1,0:T(8,128)(2,1)S(1)} collective-permute-done((bf16[3,64,1600]{2,1,0:T(8,128)(2,1)}, bf16[3,64,1600]{2,1,0:T(8,128)(2,1)S(1)}, u32[]{:S(2)}, u32[]{:S(2)}) %collective-permute-start.4) | collective-permute-done | bytes 614432 | tf_op jit(solution)/shard_map/ppermute | solution.py:30
  84.8 0.0 copy-start.1
  84.8 1.9 %collective-permute-done.5.right_ref = bf16[3,64,1600]{2,1,0:T(8,128)(2,1)S(1)} collective-permute-done((bf16[3,64,1600]{2,1,0:T(8,128)(2,1)}, bf16[3,64,1600]{2,1,0:T(8,128)(2,1)S(1)}, u32[]{:S(2)}, u32[]{:S(2)}) %collective-permute-start.5) | collective-permute-done | bytes 614432 | tf_op jit(solution)/shard_map/ppermute | solution.py:30
  86.7 0.0 copy-start.2
  86.7 0.0 copy-done.1
  86.7 0.8 copy-done.2
  87.5 4.0 %shard_map.66 = (f32[64,2240]{1,0:T(8,128)}, bf16[64,2240]{1,0:T(8,128)(2,1)}, bf16[64,2240]{1,0:T(8,128)(2,1)}) custom-call(f32[3,64,1600]{2,1,0:T(8,128)} %get-tuple-element.63.keep_ref, bf16[3,64,1600]{2,1,0:T(8,128)(2,1)} %copy-done.1, bf16[3,64,1600]{2,1,0:T(8,128)(2,1)} %copy-done.2), custom_call_target="tpu_custom_call" | custom-call | tf_op jit(solution)/shard_map/pallas_call | solution.py:279
  91.5 7.0 %collective-permute-start.6 = (bf16[64,2240]{1,0:T(8,128)(2,1)}, bf16[64,2240]{1,0:T(8,128)(2,1)S(1)}, u32[]{:S(2)}, u32[]{:S(2)}) collective-permute-start(bf16[64,2240]{1,0:T(8,128)(2,1)} %get-tuple-element.67), channel_id=1, source_target_pairs={{0,4},{1,5},{2,6},{3,7},{4,8},{5,9},{6,10},{7,11},{8,12},{9,13},{1... | collective-permute-start | bytes 860168 | tf_op jit(solution)/shard_map/ppermute | solution.py:30
  98.5 1.9 %collective-permute-start.7 = (bf16[64,2240]{1,0:T(8,128)(2,1)}, bf16[64,2240]{1,0:T(8,128)(2,1)S(1)}, u32[]{:S(2)}, u32[]{:S(2)}) collective-permute-start(bf16[64,2240]{1,0:T(8,128)(2,1)} %get-tuple-element.68), channel_id=1, source_target_pairs={{4,0},{5,1},{6,2},{7,3},{8,4},{9,5},{10,6},{11,7},{12,8},{13,9},{1... | collective-permute-start | bytes 860168 | tf_op jit(solution)/shard_map/ppermute | solution.py:30
  100.5 5.1 %collective-permute-done.6.up_ref = bf16[64,2240]{1,0:T(8,128)(2,1)S(1)} collective-permute-done((bf16[64,2240]{1,0:T(8,128)(2,1)}, bf16[64,2240]{1,0:T(8,128)(2,1)S(1)}, u32[]{:S(2)}, u32[]{:S(2)}) %collective-permute-start.6) | collective-permute-done | bytes 286752 | tf_op jit(solution)/shard_map/ppermute | solution.py:30
  105.5 0.0 copy-start.5
  105.5 5.1 %collective-permute-done.7.down_ref = bf16[64,2240]{1,0:T(8,128)(2,1)S(1)} collective-permute-done((bf16[64,2240]{1,0:T(8,128)(2,1)}, bf16[64,2240]{1,0:T(8,128)(2,1)S(1)}, u32[]{:S(2)}, u32[]{:S(2)}) %collective-permute-start.7) | collective-permute-done | bytes 286752 | tf_op jit(solution)/shard_map/ppermute | solution.py:30
  110.7 0.0 copy-start.6
  110.7 0.0 copy-done.5
  110.7 0.7 copy-done.6
  111.4 2.4 %shard_map.67 = bf16[64,3136]{1,0:T(8,128)(2,1)} custom-call(f32[64,2240]{1,0:T(8,128)} %get-tuple-element.66.keep_ref, bf16[64,2240]{1,0:T(8,128)(2,1)} %copy-done.5, bf16[64,2240]{1,0:T(8,128)(2,1)} %copy-done.6), custom_call_target="tpu_custom_call" | custom-call | tf_op jit(solution)/shard_map/pallas_call | solution.py:291
  (17 shorter events, 0.3 us)
Async XLA Ops:
  0.0 14.1 %copy-start = (bf16[4,4,64,256]{3,2,1,0:T(8,128)(2,1)S(1)}, bf16[4,4,64,256]{3,2,1,0:T(8,128)(2,1)}, u32[]{:S(2)}) copy-start(bf16[4,4,64,256]{3,2,1,0:T(8,128)(2,1)} %param.17) | copy-start | bytes 1572868
  2.6 8.3 %collective-permute-start = (bf16[272,256]{1,0:T(8,128)(2,1)S(1)}, bf16[272,256]{1,0:T(8,128)(2,1)S(1)}, u32[]{:S(2)}, u32[]{:S(2)}) collective-permute-start(bf16[272,256]{1,0:T(8,128)(2,1)S(1)} %fusion.6), channel_id=1, source_target_pairs={{0,4},{1,5},{2,6},{3,7},{4,8},{5,9},{6,10},{7,11},{8,12},{9,13},{1... | collective-permute-start | bytes 417800 | tf_op jit(solution)/shard_map/ppermute | solution.py:30
  6.1 7.7 %collective-permute-start.1 = (bf16[272,256]{1,0:T(8,128)(2,1)S(1)}, bf16[272,256]{1,0:T(8,128)(2,1)S(1)}, u32[]{:S(2)}, u32[]{:S(2)}) collective-permute-start(bf16[272,256]{1,0:T(8,128)(2,1)S(1)} %fusion.7), channel_id=1, source_target_pairs={{4,0},{5,1},{6,2},{7,3},{8,4},{9,5},{10,6},{11,7},{12,8},{13,9},{1... | collective-permute-start | bytes 417800 | tf_op jit(solution)/shard_map/ppermute | solution.py:30
  10.8 9.2 %copy-start.3 = (bf16[272,256]{1,0:T(8,128)(2,1)}, bf16[272,256]{1,0:T(8,128)(2,1)S(1)}, u32[]{:S(2)}) copy-start(bf16[272,256]{1,0:T(8,128)(2,1)S(1)} %collective-permute-done.above_ref) | copy-start | bytes 417796
  13.8 6.3 %copy-start.4 = (bf16[272,256]{1,0:T(8,128)(2,1)}, bf16[272,256]{1,0:T(8,128)(2,1)S(1)}, u32[]{:S(2)}) copy-start(bf16[272,256]{1,0:T(8,128)(2,1)S(1)} %collective-permute-done.1.below_ref) | copy-start | bytes 417796
  14.2 33.6 %collective-permute-start.2 = (bf16[400,256]{1,0:T(8,128)(2,1)S(1)}, bf16[400,256]{1,0:T(8,128)(2,1)S(1)}, u32[]{:S(2)}, u32[]{:S(2)}) collective-permute-start(bf16[400,256]{1,0:T(8,128)(2,1)S(1)} %fusion.4), channel_id=1, source_target_pairs={{0,1},{1,2},{2,3},{4,5},{5,6},{6,7},{8,9},{9,10},{10,11},{12,13},{... | collective-permute-start | bytes 614408 | tf_op jit(solution)/shard_map/ppermute | solution.py:30
  16.2 31.7 %collective-permute-start.3 = (bf16[400,256]{1,0:T(8,128)(2,1)S(1)}, bf16[400,256]{1,0:T(8,128)(2,1)S(1)}, u32[]{:S(2)}, u32[]{:S(2)}) collective-permute-start(bf16[400,256]{1,0:T(8,128)(2,1)S(1)} %fusion.5), channel_id=1, source_target_pairs={{1,0},{2,1},{3,2},{5,4},{6,5},{7,6},{9,8},{10,9},{11,10},{13,12},{... | collective-permute-start | bytes 614408 | tf_op jit(solution)/shard_map/ppermute | solution.py:30
  47.8 1.3 %copy-start.7 = (bf16[400,256]{1,0:T(8,128)(2,1)}, bf16[400,256]{1,0:T(8,128)(2,1)S(1)}, u32[]{:S(2)}) copy-start(bf16[400,256]{1,0:T(8,128)(2,1)S(1)} %collective-permute-done.2.left_ref) | copy-start | bytes 614404
  47.9 1.2 %copy-start.8 = (bf16[400,256]{1,0:T(8,128)(2,1)}, bf16[400,256]{1,0:T(8,128)(2,1)S(1)}, u32[]{:S(2)}) copy-start(bf16[400,256]{1,0:T(8,128)(2,1)S(1)} %collective-permute-done.3.right_ref) | copy-start | bytes 614404
  72.9 11.9 %collective-permute-start.4 = (bf16[3,64,1600]{2,1,0:T(8,128)(2,1)}, bf16[3,64,1600]{2,1,0:T(8,128)(2,1)S(1)}, u32[]{:S(2)}, u32[]{:S(2)}) collective-permute-start(bf16[3,64,1600]{2,1,0:T(8,128)(2,1)} %get-tuple-element.64), channel_id=1, source_target_pairs={{0,1},{1,2},{2,3},{4,5},{5,6},{6,7},{8,9},{9,10},{10,11},{12,13},{... | collective-permute-start | bytes 1843208 | tf_op jit(solution)/shard_map/ppermute | solution.py:30
  74.8 11.9 %collective-permute-start.5 = (bf16[3,64,1600]{2,1,0:T(8,128)(2,1)}, bf16[3,64,1600]{2,1,0:T(8,128)(2,1)S(1)}, u32[]{:S(2)}, u32[]{:S(2)}) collective-permute-start(bf16[3,64,1600]{2,1,0:T(8,128)(2,1)} %get-tuple-element.65), channel_id=1, source_target_pairs={{1,0},{2,1},{3,2},{5,4},{6,5},{7,6},{9,8},{10,9},{11,10},{13,12},{... | collective-permute-start | bytes 1843208 | tf_op jit(solution)/shard_map/ppermute | solution.py:30
  84.8 1.9 %copy-start.1 = (bf16[3,64,1600]{2,1,0:T(8,128)(2,1)}, bf16[3,64,1600]{2,1,0:T(8,128)(2,1)S(1)}, u32[]{:S(2)}) copy-start(bf16[3,64,1600]{2,1,0:T(8,128)(2,1)S(1)} %collective-permute-done.4.left_ref) | copy-start | bytes 1843204
  86.7 0.8 copy-start.2
  91.5 14.1 %collective-permute-start.6 = (bf16[64,2240]{1,0:T(8,128)(2,1)}, bf16[64,2240]{1,0:T(8,128)(2,1)S(1)}, u32[]{:S(2)}, u32[]{:S(2)}) collective-permute-start(bf16[64,2240]{1,0:T(8,128)(2,1)} %get-tuple-element.67), channel_id=1, source_target_pairs={{0,4},{1,5},{2,6},{3,7},{4,8},{5,9},{6,10},{7,11},{8,12},{9,13},{1... | collective-permute-start | bytes 860168 | tf_op jit(solution)/shard_map/ppermute | solution.py:30
  98.5 12.1 %collective-permute-start.7 = (bf16[64,2240]{1,0:T(8,128)(2,1)}, bf16[64,2240]{1,0:T(8,128)(2,1)S(1)}, u32[]{:S(2)}, u32[]{:S(2)}) collective-permute-start(bf16[64,2240]{1,0:T(8,128)(2,1)} %get-tuple-element.68), channel_id=1, source_target_pairs={{4,0},{5,1},{6,2},{7,3},{8,4},{9,5},{10,6},{11,7},{12,8},{13,9},{1... | collective-permute-start | bytes 860168 | tf_op jit(solution)/shard_map/ppermute | solution.py:30
  105.5 5.1 %copy-start.5 = (bf16[64,2240]{1,0:T(8,128)(2,1)}, bf16[64,2240]{1,0:T(8,128)(2,1)S(1)}, u32[]{:S(2)}) copy-start(bf16[64,2240]{1,0:T(8,128)(2,1)S(1)} %collective-permute-done.6.up_ref) | copy-start | bytes 860164
  110.7 0.7 copy-start.6

commit v9 on v7

--- a/solution.py
+++ b/solution.py
@@ -80,27 +80,34 @@
         out[...] = terms.reshape(out.shape).astype(out.dtype)
 
 
-def fold_cols_kernel(keep_ref, left_ref, right_ref, keep_out, minus_out, plus_out):
+def fold_cols_band(keep_ref, left_ref, right_ref, d, out):
     src_w = WIN * B
     dst_w = OUTW * B
-    for d in range(HOME):
-        out = (minus_out, keep_out, plus_out)[d]
-        for sx in range(WIN):
-            lo = sx * dst_w
-            s0 = sx * src_w
-            own = keep_ref[d, :, s0:s0 + src_w]
-            left = left_ref[d, :, s0:s0 + src_w].astype(jnp.float32)
-            right = right_ref[d, :, s0:s0 + src_w].astype(jnp.float32)
-            first = left[:, :B]
-            mid = left[:, B:2 * B] + own[:, :B]
-            core = left[:, 2 * B:] + own[:, B:src_w - B] + right[:, :src_w - 2 * B]
-            tail = own[:, src_w - B:] + right[:, src_w - 2 * B:src_w - B]
-            last = right[:, src_w - B:]
-            out[:, lo:lo + B] = first.astype(out.dtype)
-            out[:, lo + B:lo + 2 * B] = mid.astype(out.dtype)
-            out[:, lo + 2 * B:lo + 5 * B] = core.astype(out.dtype)
-            out[:, lo + 5 * B:lo + 6 * B] = tail.astype(out.dtype)
-            out[:, lo + 6 * B:lo + 7 * B] = last.astype(out.dtype)
+    for sx in range(WIN):
+        lo = sx * dst_w
+        s0 = sx * src_w
+        own = keep_ref[d, :, s0:s0 + src_w]
+        left = left_ref[d, :, s0:s0 + src_w].astype(jnp.float32)
+        right = right_ref[d, :, s0:s0 + src_w].astype(jnp.float32)
+        first = left[:, :B]
+        mid = left[:, B:2 * B] + own[:, :B]
+        core = left[:, 2 * B:] + own[:, B:src_w - B] + right[:, :src_w - 2 * B]
+        tail = own[:, src_w - B:] + right[:, src_w - 2 * B:src_w - B]
+        last = right[:, src_w - B:]
+        out[:, lo:lo + B] = first.astype(out.dtype)
+        out[:, lo + B:lo + 2 * B] = mid.astype(out.dtype)
+        out[:, lo + 2 * B:lo + 5 * B] = core.astype(out.dtype)
+        out[:, lo + 5 * B:lo + 6 * B] = tail.astype(out.dtype)
+        out[:, lo + 6 * B:lo + 7 * B] = last.astype(out.dtype)
+
+
+def fold_cols_send_kernel(keep_ref, left_ref, right_ref, minus_out, plus_out):
+    fold_cols_band(keep_ref, left_ref, right_ref, 0, minus_out)
+    fold_cols_band(keep_ref, left_ref, right_ref, 2, plus_out)
+
+
+def fold_cols_keep_kernel(keep_ref, left_ref, right_ref, keep_out):
+    fold_cols_band(keep_ref, left_ref, right_ref, 1, keep_out)
 
 
 def fold_rows_kernel(keep_ref, up_ref, down_ref, out_ref):
@@ -210,15 +217,20 @@
     from_left = shifted(to_left, 0, 1)
     from_right = shifted(to_right, 0, -1)
     band = WIN * OUTW * B
-    keep2, minus, plus = pl.pallas_call(
-        fold_cols_kernel,
+    minus, plus = pl.pallas_call(
+        fold_cols_send_kernel,
         out_shape=(
-            jax.ShapeDtypeStruct((B, band), jnp.float32),
             jax.ShapeDtypeStruct((B, band), SEND),
             jax.ShapeDtypeStruct((B, band), SEND),
         ),
         in_specs=[pl.BlockSpec(memory_space=vmem)] * 3,
-        out_specs=(pl.BlockSpec(memory_space=vmem),) * 3,
+        out_specs=(pl.BlockSpec(memory_space=vmem),) * 2,
+    )(keep, from_left, from_right)
+    keep2 = pl.pallas_call(
+        fold_cols_keep_kernel,
+        out_shape=jax.ShapeDtypeStruct((B, band), jnp.float32),
+        in_specs=[pl.BlockSpec(memory_space=vmem)] * 3,
+        out_specs=pl.BlockSpec(memory_space=vmem),
     )(keep, from_left, from_right)
     up_in = shifted(plus, 1, 0)
     down_in = shifted(minus, -1, 0)

time: 76.4 us -> 75.8 us (level)
  waiting for transfers between devices: 20 us -> 17.2 us
  Pallas kernels: 22.4 us -> 24.4 us
    ppermute x8, waiting for transfers between devices: 20 us -> 17.2 us  [shifted(): return lax.ppermute(value, ('row', 'col'), pairs)]
    pallas_call x1 -> x2, Pallas kernels: 3.94 us -> 6.1 us  [the longest x1 3.26 us: per_device(): pl.pallas_call(fold_cols_send_kernel, out_shape=(jax.ShapeDtypeStruct((B,...]
  transfers between devices with their start and end apart: 8 -> 8, of which waited for: 8 -> 8; matrix products, arithmetic and copies ran while one was open for 3% -> 3% of each run, Pallas kernels for 0% -> 4%
where the time goes in v9:
time: 75.8 us; the launch traced here: 74.3 us
  starting transfers between devices  24.9 us (33%)
  Pallas kernels  24.4 us (32%)
  waiting for transfers between devices  17.2 us (23%)
  local copies, waits for them, and re-layouts  4.12 us (5%)
  other arithmetic  3.6 us (5%)
    ppermute x8, starting transfers between devices, shifted(): return lax.ppermute(value, ('row', 'col'), pairs)  24.9 us
    ppermute x8, waiting for transfers between devices, shifted(): return lax.ppermute(value, ('row', 'col'), pairs)  17.2 us
    pallas_call x1, Pallas kernels, per_device(): pl.pallas_call(galerkin_kernel, out_shape=(jax.ShapeDtypeStruct((HOME, B,...  15.9 us
    pallas_call x1, Pallas kernels, per_device(): pl.pallas_call(fold_cols_send_kernel, out_shape=(jax.ShapeDtypeStruct((B,...  3.26 us
    pallas_call x1, Pallas kernels, per_device(): pl.pallas_call(fold_cols_keep_kernel, out_shape=jax.ShapeDtypeStruct((B,...  2.84 us
    pallas_call x1, Pallas kernels, per_device(): pl.pallas_call(fold_rows_kernel, out_shape=jax.ShapeDtypeStruct((B, OUTW...  2.4 us
    unnamed x18, local copies, waits for them, and re-layouts  1.59 us
  transfers between devices with their start and end apart: 8, of which 8 were waited for; matrix products, arithmetic and copies ran while one was open for 3% of the time, Pallas kernels for 4%

profile of v9, /device:TPU:20, one launch (start us, length us, event | category | flops | bytes accessed | tf_op | source)
XLA Modules:
  0.0 74.3 jit_solution(14315081293319910273)
XLA Ops:
  0.0 0.0 copy-start
  0.0 1.4 %fusion.31 = (bf16[4,4,4]{2,1,0:T(4,128)(2,1)S(1)}, s32[4,4,4]{2,1,0:T(4,128)S(1)}, s32[4,4,4]{2,1,0:T(4,128)}) fusion(s32[]{:T(128)S(6)} %axis_index.25, s32[]{:T(128)S(6)} %axis_index.23, s32[4,4,4]{2,1,0:T(4,128)} %param.18, s32[4,4]{1,0:T(4,128)} %param.19), kind=kLoop, calls=%fused_computation.72 | loop fusion | flops 2112 | bytes 968 | tf_op jit(solution)/shard_map/convert.7
  1.4 0.1 convert_element_type.88
  1.5 1.0 %fusion.32 = (bf16[1,4,64,256]{3,2,1,0:T(8,128)(2,1)S(1)}, bf16[1,4,64,256]{3,2,1,0:T(8,128)(2,1)S(1)}) fusion(bf16[4,4,64,256]{3,2,1,0:T(8,128)(2,1)} %param.17), kind=kLoop, calls=%fused_computation.73 | loop fusion | bytes 524288 | tf_op jit(solution)/shard_map/slice | solution.py:163
  2.5 3.4 %collective-permute-start = (bf16[272,256]{1,0:T(8,128)(2,1)S(1)}, bf16[272,256]{1,0:T(8,128)(2,1)S(1)}, u32[]{:S(2)}, u32[]{:S(2)}) collective-permute-start(bf16[272,256]{1,0:T(8,128)(2,1)S(1)} %fusion.6), channel_id=1, source_target_pairs={{0,4},{1,5},{2,6},{3,7},{4,8},{5,9},{6,10},{7,11},{8,12},{9,13},{1... | collective-permute-start | bytes 417800 | tf_op jit(solution)/shard_map/ppermute | solution.py:30
  5.9 0.1 convert_element_type.89
  6.0 3.3 %collective-permute-start.1 = (bf16[272,256]{1,0:T(8,128)(2,1)S(1)}, bf16[272,256]{1,0:T(8,128)(2,1)S(1)}, u32[]{:S(2)}, u32[]{:S(2)}) collective-permute-start(bf16[272,256]{1,0:T(8,128)(2,1)S(1)} %fusion.7), channel_id=1, source_target_pairs={{4,0},{5,1},{6,2},{7,3},{8,4},{9,5},{10,6},{11,7},{12,8},{13,9},{1... | collective-permute-start | bytes 417800 | tf_op jit(solution)/shard_map/ppermute | solution.py:30
  9.4 1.3 %add_clamp_fusion.pos_ref = s32[4,4,9]{2,1,0:T(4,128)} fusion(s32[4,4,9]{2,1,0:T(4,128)} %param.15, s32[]{:T(128)S(6)} %mul.28, s32[]{:T(128)S(6)} %mul.25), kind=kLoop, calls=%fused_computation.44 | loop fusion | flops 3744 | bytes 1160 | tf_op jit(solution)/shard_map/jit(clip)/min | solution.py:184
  10.7 0.1 collective-permute-done.above_ref
  10.8 0.0 copy-start.3
  10.8 0.1 reshape.246
  10.9 2.8 %collective-permute-done.1.below_ref = bf16[272,256]{1,0:T(8,128)(2,1)S(1)} collective-permute-done((bf16[272,256]{1,0:T(8,128)(2,1)S(1)}, bf16[272,256]{1,0:T(8,128)(2,1)S(1)}, u32[]{:S(2)}, u32[]{:S(2)}) %collective-permute-start.1) | collective-permute-done | bytes 139296 | tf_op jit(solution)/shard_map/ppermute | solution.py:30
  13.7 0.0 copy-start.4
  13.7 0.1 reshape.247
  13.9 0.1 convert_element_type.94
  14.0 0.0 copy-done
  14.0 0.1 pad_maximum_fusion.2
  14.1 1.9 %collective-permute-start.2 = (bf16[400,256]{1,0:T(8,128)(2,1)S(1)}, bf16[400,256]{1,0:T(8,128)(2,1)S(1)}, u32[]{:S(2)}, u32[]{:S(2)}) collective-permute-start(bf16[400,256]{1,0:T(8,128)(2,1)S(1)} %fusion.4), channel_id=1, source_target_pairs={{0,1},{1,2},{2,3},{4,5},{5,6},{6,7},{8,9},{9,10},{10,11},{12,13},{... | collective-permute-start | bytes 614408 | tf_op jit(solution)/shard_map/ppermute | solution.py:30
  16.0 0.1 convert_element_type.97
  16.1 3.6 %collective-permute-start.3 = (bf16[400,256]{1,0:T(8,128)(2,1)S(1)}, bf16[400,256]{1,0:T(8,128)(2,1)S(1)}, u32[]{:S(2)}, u32[]{:S(2)}) collective-permute-start(bf16[400,256]{1,0:T(8,128)(2,1)S(1)} %fusion.5), channel_id=1, source_target_pairs={{1,0},{2,1},{3,2},{5,4},{6,5},{7,6},{9,8},{10,9},{11,10},{13,12},{... | collective-permute-start | bytes 614408 | tf_op jit(solution)/shard_map/ppermute | solution.py:30
  19.8 0.1 add.137
  19.8 0.1 add.138
  20.0 0.1 add.143
  20.0 0.0 copy-done.3
  20.0 0.0 copy-done.4
  20.0 0.1 add.144
  20.1 1.0 %collective-permute-done.2.left_ref = bf16[400,256]{1,0:T(8,128)(2,1)S(1)} collective-permute-done((bf16[400,256]{1,0:T(8,128)(2,1)S(1)}, bf16[400,256]{1,0:T(8,128)(2,1)S(1)}, u32[]{:S(2)}, u32[]{:S(2)}) %collective-permute-start.2) | collective-permute-done | bytes 204832 | tf_op jit(solution)/shard_map/ppermute | solution.py:30
  21.1 0.0 copy-start.7
  21.2 0.1 reshape.250
  21.3 1.8 %collective-permute-done.3.right_ref = bf16[400,256]{1,0:T(8,128)(2,1)S(1)} collective-permute-done((bf16[400,256]{1,0:T(8,128)(2,1)S(1)}, bf16[400,256]{1,0:T(8,128)(2,1)S(1)}, u32[]{:S(2)}, u32[]{:S(2)}) %collective-permute-start.3) | collective-permute-done | bytes 204832 | tf_op jit(solution)/shard_map/ppermute | solution.py:30
  23.0 0.0 copy-start.8
  23.0 0.1 reshape.251
  23.2 0.1 div.63
  23.3 0.1 rem.115
  23.4 0.1 lt.48
  23.5 0.1 ne.114
  23.6 0.6 add_select_fusion.6.nslot_ref
  24.2 0.0 copy-done.7
  24.2 0.0 copy-done.8
  24.2 15.9 %shard_map.64 = (f32[3,64,1600]{2,1,0:T(8,128)}, bf16[3,64,1600]{2,1,0:T(8,128)(2,1)}, bf16[3,64,1600]{2,1,0:T(8,128)(2,1)}) custom-call(s32[4,4,9]{2,1,0:T(4,128)} %add_clamp_fusion.pos_ref, s32[144]{0:T(256)} %add_select_fusion.6.nslot_ref, s32[4,4]{1,0:T(4,128)} %count_ref.1, s32[4,4,4]{2,1,0:T(4,128)} %get-tuple-element.75.home_ref, ...), custom_call_target="tpu_custom_call" | custom-call | tf_op jit(solution)/shard_map/pallas_call | solution.py:190
  40.1 1.9 %collective-permute-start.4 = (bf16[3,64,1600]{2,1,0:T(8,128)(2,1)}, bf16[3,64,1600]{2,1,0:T(8,128)(2,1)S(1)}, u32[]{:S(2)}, u32[]{:S(2)}) collective-permute-start(bf16[3,64,1600]{2,1,0:T(8,128)(2,1)} %get-tuple-element.59), channel_id=1, source_target_pairs={{0,1},{1,2},{2,3},{4,5},{5,6},{6,7},{8,9},{9,10},{10,11},{12,13},{... | collective-permute-start | bytes 1843208 | tf_op jit(solution)/shard_map/ppermute | solution.py:30
  42.0 3.9 %collective-permute-start.5 = (bf16[3,64,1600]{2,1,0:T(8,128)(2,1)}, bf16[3,64,1600]{2,1,0:T(8,128)(2,1)S(1)}, u32[]{:S(2)}, u32[]{:S(2)}) collective-permute-start(bf16[3,64,1600]{2,1,0:T(8,128)(2,1)} %get-tuple-element.60), channel_id=1, source_target_pairs={{1,0},{2,1},{3,2},{5,4},{6,5},{7,6},{9,8},{10,9},{11,10},{13,12},{... | collective-permute-start | bytes 1843208 | tf_op jit(solution)/shard_map/ppermute | solution.py:30
  46.0 6.4 %collective-permute-done.4.left_ref = bf16[3,64,1600]{2,1,0:T(8,128)(2,1)S(1)} collective-permute-done((bf16[3,64,1600]{2,1,0:T(8,128)(2,1)}, bf16[3,64,1600]{2,1,0:T(8,128)(2,1)S(1)}, u32[]{:S(2)}, u32[]{:S(2)}) %collective-permute-start.4) | collective-permute-done | bytes 614432 | tf_op jit(solution)/shard_map/ppermute | solution.py:30
  52.3 0.0 copy-start.1
  52.3 1.9 %collective-permute-done.5.right_ref = bf16[3,64,1600]{2,1,0:T(8,128)(2,1)S(1)} collective-permute-done((bf16[3,64,1600]{2,1,0:T(8,128)(2,1)}, bf16[3,64,1600]{2,1,0:T(8,128)(2,1)S(1)}, u32[]{:S(2)}, u32[]{:S(2)}) %collective-permute-start.5) | collective-permute-done | bytes 614432 | tf_op jit(solution)/shard_map/ppermute | solution.py:30
  54.2 0.0 copy-start.2
  54.2 0.0 copy-done.1
  54.2 0.9 %copy-done.2 = bf16[3,64,1600]{2,1,0:T(8,128)(2,1)} copy-done((bf16[3,64,1600]{2,1,0:T(8,128)(2,1)}, bf16[3,64,1600]{2,1,0:T(8,128)(2,1)S(1)}, u32[]{:S(2)}) %copy-start.2) | copy-done | bytes 614424
  55.0 3.3 %shard_map.66 = (bf16[64,2240]{1,0:T(8,128)(2,1)}, bf16[64,2240]{1,0:T(8,128)(2,1)}) custom-call(f32[3,64,1600]{2,1,0:T(8,128)} %get-tuple-element.58.keep_ref, bf16[3,64,1600]{2,1,0:T(8,128)(2,1)} %copy-done.1, bf16[3,64,1600]{2,1,0:T(8,128)(2,1)} %copy-done.2), custom_call_target="tpu_custom_call" | custom-call | tf_op jit(solution)/shard_map/pallas_call | solution.py:220
  58.3 3.6 %collective-permute-start.6 = (bf16[64,2240]{1,0:T(8,128)(2,1)}, bf16[64,2240]{1,0:T(8,128)(2,1)S(1)}, u32[]{:S(2)}, u32[]{:S(2)}) collective-permute-start(bf16[64,2240]{1,0:T(8,128)(2,1)} %get-tuple-element.61), channel_id=1, source_target_pairs={{0,4},{1,5},{2,6},{3,7},{4,8},{5,9},{6,10},{7,11},{8,12},{9,13},{1... | collective-permute-start | bytes 860168 | tf_op jit(solution)/shard_map/ppermute | solution.py:30
  61.9 3.1 %collective-permute-start.7 = (bf16[64,2240]{1,0:T(8,128)(2,1)}, bf16[64,2240]{1,0:T(8,128)(2,1)S(1)}, u32[]{:S(2)}, u32[]{:S(2)}) collective-permute-start(bf16[64,2240]{1,0:T(8,128)(2,1)} %get-tuple-element.62), channel_id=1, source_target_pairs={{4,0},{5,1},{6,2},{7,3},{8,4},{9,5},{10,6},{11,7},{12,8},{13,9},{1... | collective-permute-start | bytes 860168 | tf_op jit(solution)/shard_map/ppermute | solution.py:30
  65.0 2.8 %shard_map.65.keep_ref = f32[64,2240]{1,0:T(8,128)} custom-call(f32[3,64,1600]{2,1,0:T(8,128)} %get-tuple-element.58.keep_ref, bf16[3,64,1600]{2,1,0:T(8,128)(2,1)} %copy-done.1, bf16[3,64,1600]{2,1,0:T(8,128)(2,1)} %copy-done.2), custom_call_target="tpu_custom_call" | custom-call | tf_op jit(solution)/shard_map/pallas_call | solution.py:229
  67.9 0.2 collective-permute-done.6.up_ref
  68.1 0.0 copy-start.5
  68.1 3.1 %collective-permute-done.7.down_ref = bf16[64,2240]{1,0:T(8,128)(2,1)S(1)} collective-permute-done((bf16[64,2240]{1,0:T(8,128)(2,1)}, bf16[64,2240]{1,0:T(8,128)(2,1)S(1)}, u32[]{:S(2)}, u32[]{:S(2)}) %collective-permute-start.7) | collective-permute-done | bytes 286752 | tf_op jit(solution)/shard_map/ppermute | solution.py:30
  71.2 0.0 copy-done.5
  71.2 0.0 copy-start.6
  71.2 0.7 copy-done.6
  71.9 2.4 %shard_map.67 = bf16[64,3136]{1,0:T(8,128)(2,1)} custom-call(f32[64,2240]{1,0:T(8,128)} %shard_map.65.keep_ref, bf16[64,2240]{1,0:T(8,128)(2,1)} %copy-done.5, bf16[64,2240]{1,0:T(8,128)(2,1)} %copy-done.6), custom_call_target="tpu_custom_call" | custom-call | tf_op jit(solution)/shard_map/pallas_call | solution.py:237
  (16 shorter events, 0.3 us)
Async XLA Ops:
  0.0 14.0 %copy-start = (bf16[4,4,64,256]{3,2,1,0:T(8,128)(2,1)S(1)}, bf16[4,4,64,256]{3,2,1,0:T(8,128)(2,1)}, u32[]{:S(2)}) copy-start(bf16[4,4,64,256]{3,2,1,0:T(8,128)(2,1)} %param.17) | copy-start | bytes 1572868
  2.5 8.3 %collective-permute-start = (bf16[272,256]{1,0:T(8,128)(2,1)S(1)}, bf16[272,256]{1,0:T(8,128)(2,1)S(1)}, u32[]{:S(2)}, u32[]{:S(2)}) collective-permute-start(bf16[272,256]{1,0:T(8,128)(2,1)S(1)} %fusion.6), channel_id=1, source_target_pairs={{0,4},{1,5},{2,6},{3,7},{4,8},{5,9},{6,10},{7,11},{8,12},{9,13},{1... | collective-permute-start | bytes 417800 | tf_op jit(solution)/shard_map/ppermute | solution.py:30
  6.0 7.7 %collective-permute-start.1 = (bf16[272,256]{1,0:T(8,128)(2,1)S(1)}, bf16[272,256]{1,0:T(8,128)(2,1)S(1)}, u32[]{:S(2)}, u32[]{:S(2)}) collective-permute-start(bf16[272,256]{1,0:T(8,128)(2,1)S(1)} %fusion.7), channel_id=1, source_target_pairs={{4,0},{5,1},{6,2},{7,3},{8,4},{9,5},{10,6},{11,7},{12,8},{13,9},{1... | collective-permute-start | bytes 417800 | tf_op jit(solution)/shard_map/ppermute | solution.py:30
  10.8 9.2 %copy-start.3 = (bf16[272,256]{1,0:T(8,128)(2,1)}, bf16[272,256]{1,0:T(8,128)(2,1)S(1)}, u32[]{:S(2)}) copy-start(bf16[272,256]{1,0:T(8,128)(2,1)S(1)} %collective-permute-done.above_ref) | copy-start | bytes 417796
  13.7 6.3 %copy-start.4 = (bf16[272,256]{1,0:T(8,128)(2,1)}, bf16[272,256]{1,0:T(8,128)(2,1)S(1)}, u32[]{:S(2)}) copy-start(bf16[272,256]{1,0:T(8,128)(2,1)S(1)} %collective-permute-done.1.below_ref) | copy-start | bytes 417796
  14.1 7.1 %collective-permute-start.2 = (bf16[400,256]{1,0:T(8,128)(2,1)S(1)}, bf16[400,256]{1,0:T(8,128)(2,1)S(1)}, u32[]{:S(2)}, u32[]{:S(2)}) collective-permute-start(bf16[400,256]{1,0:T(8,128)(2,1)S(1)} %fusion.4), channel_id=1, source_target_pairs={{0,1},{1,2},{2,3},{4,5},{5,6},{6,7},{8,9},{9,10},{10,11},{12,13},{... | collective-permute-start | bytes 614408 | tf_op jit(solution)/shard_map/ppermute | solution.py:30
  16.1 6.9 %collective-permute-start.3 = (bf16[400,256]{1,0:T(8,128)(2,1)S(1)}, bf16[400,256]{1,0:T(8,128)(2,1)S(1)}, u32[]{:S(2)}, u32[]{:S(2)}) collective-permute-start(bf16[400,256]{1,0:T(8,128)(2,1)S(1)} %fusion.5), channel_id=1, source_target_pairs={{1,0},{2,1},{3,2},{5,4},{6,5},{7,6},{9,8},{10,9},{11,10},{13,12},{... | collective-permute-start | bytes 614408 | tf_op jit(solution)/shard_map/ppermute | solution.py:30
  21.1 3.1 %copy-start.7 = (bf16[400,256]{1,0:T(8,128)(2,1)}, bf16[400,256]{1,0:T(8,128)(2,1)S(1)}, u32[]{:S(2)}) copy-start(bf16[400,256]{1,0:T(8,128)(2,1)S(1)} %collective-permute-done.2.left_ref) | copy-start | bytes 614404
  23.0 1.2 %copy-start.8 = (bf16[400,256]{1,0:T(8,128)(2,1)}, bf16[400,256]{1,0:T(8,128)(2,1)S(1)}, u32[]{:S(2)}) copy-start(bf16[400,256]{1,0:T(8,128)(2,1)S(1)} %collective-permute-done.3.right_ref) | copy-start | bytes 614404
  40.1 12.2 %collective-permute-start.4 = (bf16[3,64,1600]{2,1,0:T(8,128)(2,1)}, bf16[3,64,1600]{2,1,0:T(8,128)(2,1)S(1)}, u32[]{:S(2)}, u32[]{:S(2)}) collective-permute-start(bf16[3,64,1600]{2,1,0:T(8,128)(2,1)} %get-tuple-element.59), channel_id=1, source_target_pairs={{0,1},{1,2},{2,3},{4,5},{5,6},{6,7},{8,9},{9,10},{10,11},{12,13},{... | collective-permute-start | bytes 1843208 | tf_op jit(solution)/shard_map/ppermute | solution.py:30
  42.0 12.1 %collective-permute-start.5 = (bf16[3,64,1600]{2,1,0:T(8,128)(2,1)}, bf16[3,64,1600]{2,1,0:T(8,128)(2,1)S(1)}, u32[]{:S(2)}, u32[]{:S(2)}) collective-permute-start(bf16[3,64,1600]{2,1,0:T(8,128)(2,1)} %get-tuple-element.60), channel_id=1, source_target_pairs={{1,0},{2,1},{3,2},{5,4},{6,5},{7,6},{9,8},{10,9},{11,10},{13,12},{... | collective-permute-start | bytes 1843208 | tf_op jit(solution)/shard_map/ppermute | solution.py:30
  52.3 1.9 %copy-start.1 = (bf16[3,64,1600]{2,1,0:T(8,128)(2,1)}, bf16[3,64,1600]{2,1,0:T(8,128)(2,1)S(1)}, u32[]{:S(2)}) copy-start(bf16[3,64,1600]{2,1,0:T(8,128)(2,1)S(1)} %collective-permute-done.4.left_ref) | copy-start | bytes 1843204
  54.2 0.9 %copy-start.2 = (bf16[3,64,1600]{2,1,0:T(8,128)(2,1)}, bf16[3,64,1600]{2,1,0:T(8,128)(2,1)S(1)}, u32[]{:S(2)}) copy-start(bf16[3,64,1600]{2,1,0:T(8,128)(2,1)S(1)} %collective-permute-done.5.right_ref) | copy-start | bytes 1843204
  58.3 9.8 %collective-permute-start.6 = (bf16[64,2240]{1,0:T(8,128)(2,1)}, bf16[64,2240]{1,0:T(8,128)(2,1)S(1)}, u32[]{:S(2)}, u32[]{:S(2)}) collective-permute-start(bf16[64,2240]{1,0:T(8,128)(2,1)} %get-tuple-element.61), channel_id=1, source_target_pairs={{0,4},{1,5},{2,6},{3,7},{4,8},{5,9},{6,10},{7,11},{8,12},{9,13},{1... | collective-permute-start | bytes 860168 | tf_op jit(solution)/shard_map/ppermute | solution.py:30
  61.9 9.3 %collective-permute-start.7 = (bf16[64,2240]{1,0:T(8,128)(2,1)}, bf16[64,2240]{1,0:T(8,128)(2,1)S(1)}, u32[]{:S(2)}, u32[]{:S(2)}) collective-permute-start(bf16[64,2240]{1,0:T(8,128)(2,1)} %get-tuple-element.62), channel_id=1, source_target_pairs={{4,0},{5,1},{6,2},{7,3},{8,4},{9,5},{10,6},{11,7},{12,8},{13,9},{1... | collective-permute-start | bytes 860168 | tf_op jit(solution)/shard_map/ppermute | solution.py:30
  68.1 3.1 %copy-start.5 = (bf16[64,2240]{1,0:T(8,128)(2,1)}, bf16[64,2240]{1,0:T(8,128)(2,1)S(1)}, u32[]{:S(2)}) copy-start(bf16[64,2240]{1,0:T(8,128)(2,1)S(1)} %collective-permute-done.6.up_ref) | copy-start | bytes 860164
  71.2 0.7 copy-start.6

commit v10 on v9

--- a/solution.py
+++ b/solution.py
@@ -144,14 +144,14 @@
     own_codes = prolong_columns
     hrow = jnp.clip(own_codes // coarse_grid_cols - row_index + 1, 0, HOME - 1)
     hcol = jnp.clip(own_codes % coarse_grid_cols - col_index + 1, 0, HOME - 1)
-    rel = jnp.where(kept, hrow * HOME + hcol, HOME * HOME)
+    rel = jnp.where(kept, hrow * WIN + hcol, 4 * TRASH)
     home_rc = hcol * HOME + hrow
 
     def payload(p_part, rel_part):
         count = p_part.shape[0]
         flat = p_part.reshape(count * B, KP * B)
-        extra = jnp.zeros((16, KP * B), jnp.bfloat16)
-        extra = extra.at[0, :count * KP].set(rel_part.reshape(-1).astype(jnp.bfloat16))
+        extra = jnp.pad(rel_part.reshape(1, count * KP).astype(jnp.bfloat16),
+                        ((0, 15), (0, KP * B - count * KP)))
         return jnp.concatenate([flat, extra], axis=0)
 
     def unpack(got, count):
@@ -174,8 +174,8 @@
 
     off_r = (jnp.arange(hr, dtype=jnp.int32) + tile_rows - 1) // tile_rows - 1
     off_c = (jnp.arange(hc, dtype=jnp.int32) + tile_cols - 1) // tile_cols - 1
-    near_slot = (near_rel // HOME + off_r[:, None, None] + 1) * WIN + near_rel % HOME + off_c[None, :, None] + 1
-    near_slot = jnp.where(near_rel < HOME * HOME, near_slot, TRASH).reshape(hr * hc * KP)
+    base = (off_r[:, None, None] + 1) * WIN + off_c[None, :, None] + 1
+    near_slot = jnp.minimum(near_rel + base, TRASH).reshape(hr * hc * KP)
 
     first_row = row_index * tile_rows
     first_col = col_index * tile_cols

time: 75.8 us -> 75.4 us (level)
  transfers between devices with their start and end apart: 8 -> 8, of which waited for: 8 -> 8; matrix products, arithmetic and copies ran while one was open for 3% -> 2% of each run, Pallas kernels for 4% -> 4%
where the time goes in v10:
time: 75.4 us; the launch traced here: 74 us
  Pallas kernels  24.7 us (33%)
  starting transfers between devices  24.6 us (33%)
  waiting for transfers between devices  17.4 us (23%)
  local copies, waits for them, and re-layouts  4 us (5%)
  other arithmetic  3.1 us (4%)
    ppermute x8, starting transfers between devices, shifted(): return lax.ppermute(value, ('row', 'col'), pairs)  24.6 us
    ppermute x8, waiting for transfers between devices, shifted(): return lax.ppermute(value, ('row', 'col'), pairs)  17.4 us
    pallas_call x1, Pallas kernels, per_device(): pl.pallas_call(galerkin_kernel, out_shape=(jax.ShapeDtypeStruct((HOME, B,...  16.2 us
    pallas_call x1, Pallas kernels, per_device(): pl.pallas_call(fold_cols_send_kernel, out_shape=(jax.ShapeDtypeStruct((B,...  3.26 us
    pallas_call x1, Pallas kernels, per_device(): pl.pallas_call(fold_cols_keep_kernel, out_shape=jax.ShapeDtypeStruct((B,...  2.85 us
    pallas_call x1, Pallas kernels, per_device(): pl.pallas_call(fold_rows_kernel, out_shape=jax.ShapeDtypeStruct((B, OUTW...  2.4 us
    unnamed x18, local copies, waits for them, and re-layouts  1.58 us
  transfers between devices with their start and end apart: 8, of which 8 were waited for; matrix products, arithmetic and copies ran while one was open for 2% of the time, Pallas kernels for 4%

profile of v10, /device:TPU:20, one launch (start us, length us, event | category | flops | bytes accessed | tf_op | source)
XLA Modules:
  0.0 74.0 jit_solution(13847236030862326922)
XLA Ops:
  0.0 0.0 copy-start
  0.0 1.4 %fusion.27 = (bf16[4,4,4]{2,1,0:T(4,128)(2,1)S(1)}, s32[4,4,4]{2,1,0:T(4,128)S(1)}, s32[4,4,4]{2,1,0:T(4,128)}) fusion(s32[]{:T(128)S(6)} %axis_index.25, s32[]{:T(128)S(6)} %axis_index.23, s32[4,4,4]{2,1,0:T(4,128)} %param.10, s32[4,4]{1,0:T(4,128)} %param.11), kind=kLoop, calls=%fused_computation.64 | loop fusion | flops 2112 | bytes 968 | tf_op jit(solution)/shard_map/convert.7
  1.4 0.1 convert_element_type.106
  1.5 1.0 %fusion.28 = (bf16[1,4,64,256]{3,2,1,0:T(8,128)(2,1)S(1)}, bf16[1,4,64,256]{3,2,1,0:T(8,128)(2,1)S(1)}) fusion(bf16[4,4,64,256]{3,2,1,0:T(8,128)(2,1)} %param.9), kind=kLoop, calls=%fused_computation.65 | loop fusion | bytes 524288 | tf_op jit(solution)/shard_map/slice | solution.py:163
  2.5 3.4 %collective-permute-start = (bf16[272,256]{1,0:T(8,128)(2,1)S(1)}, bf16[272,256]{1,0:T(8,128)(2,1)S(1)}, u32[]{:S(2)}, u32[]{:S(2)}) collective-permute-start(bf16[272,256]{1,0:T(8,128)(2,1)S(1)} %fusion.6), channel_id=1, source_target_pairs={{0,4},{1,5},{2,6},{3,7},{4,8},{5,9},{6,10},{7,11},{8,12},{9,13},{1... | collective-permute-start | bytes 417800 | tf_op jit(solution)/shard_map/ppermute | solution.py:30
  5.9 0.1 convert_element_type.107
  6.0 3.3 %collective-permute-start.1 = (bf16[272,256]{1,0:T(8,128)(2,1)S(1)}, bf16[272,256]{1,0:T(8,128)(2,1)S(1)}, u32[]{:S(2)}, u32[]{:S(2)}) collective-permute-start(bf16[272,256]{1,0:T(8,128)(2,1)S(1)} %fusion.7), channel_id=1, source_target_pairs={{4,0},{5,1},{6,2},{7,3},{8,4},{9,5},{10,6},{11,7},{12,8},{13,9},{1... | collective-permute-start | bytes 417800 | tf_op jit(solution)/shard_map/ppermute | solution.py:30
  9.4 1.3 %add_clamp_fusion.pos_ref = s32[4,4,9]{2,1,0:T(4,128)} fusion(s32[4,4,9]{2,1,0:T(4,128)} %param.7, s32[]{:T(128)S(6)} %mul.33, s32[]{:T(128)S(6)} %mul.30), kind=kLoop, calls=%fused_computation.41 | loop fusion | flops 3744 | bytes 1160 | tf_op jit(solution)/shard_map/jit(clip)/min | solution.py:184
  10.7 0.1 collective-permute-done.above_ref
  10.8 0.0 copy-start.3
  10.8 0.1 reshape.196
  10.9 2.8 %collective-permute-done.1.below_ref = bf16[272,256]{1,0:T(8,128)(2,1)S(1)} collective-permute-done((bf16[272,256]{1,0:T(8,128)(2,1)S(1)}, bf16[272,256]{1,0:T(8,128)(2,1)S(1)}, u32[]{:S(2)}, u32[]{:S(2)}) %collective-permute-start.1) | collective-permute-done | bytes 139296 | tf_op jit(solution)/shard_map/ppermute | solution.py:30
  13.7 0.0 copy-start.4
  13.7 0.1 reshape.197
  13.9 0.1 convert_element_type.112
  14.0 0.0 copy-done
  14.0 0.1 pad_maximum_fusion.2
  14.1 1.9 %collective-permute-start.2 = (bf16[400,256]{1,0:T(8,128)(2,1)S(1)}, bf16[400,256]{1,0:T(8,128)(2,1)S(1)}, u32[]{:S(2)}, u32[]{:S(2)}) collective-permute-start(bf16[400,256]{1,0:T(8,128)(2,1)S(1)} %fusion.4), channel_id=1, source_target_pairs={{0,1},{1,2},{2,3},{4,5},{5,6},{6,7},{8,9},{9,10},{10,11},{12,13},{... | collective-permute-start | bytes 614408 | tf_op jit(solution)/shard_map/ppermute | solution.py:30
  16.0 0.1 convert_element_type.115
  16.1 3.6 %collective-permute-start.3 = (bf16[400,256]{1,0:T(8,128)(2,1)S(1)}, bf16[400,256]{1,0:T(8,128)(2,1)S(1)}, u32[]{:S(2)}, u32[]{:S(2)}) collective-permute-start(bf16[400,256]{1,0:T(8,128)(2,1)S(1)} %fusion.5), channel_id=1, source_target_pairs={{1,0},{2,1},{3,2},{5,4},{6,5},{7,6},{9,8},{10,9},{11,10},{13,12},{... | collective-permute-start | bytes 614408 | tf_op jit(solution)/shard_map/ppermute | solution.py:30
  19.8 0.1 add_add_fusion.1
  19.8 1.3 %collective-permute-done.2.left_ref = bf16[400,256]{1,0:T(8,128)(2,1)S(1)} collective-permute-done((bf16[400,256]{1,0:T(8,128)(2,1)S(1)}, bf16[400,256]{1,0:T(8,128)(2,1)S(1)}, u32[]{:S(2)}, u32[]{:S(2)}) %collective-permute-start.2) | collective-permute-done | bytes 204832 | tf_op jit(solution)/shard_map/ppermute | solution.py:30
  21.2 0.0 copy-start.7
  21.2 0.1 reshape.200
  21.3 1.8 %collective-permute-done.3.right_ref = bf16[400,256]{1,0:T(8,128)(2,1)S(1)} collective-permute-done((bf16[400,256]{1,0:T(8,128)(2,1)S(1)}, bf16[400,256]{1,0:T(8,128)(2,1)S(1)}, u32[]{:S(2)}, u32[]{:S(2)}) %collective-permute-start.3) | collective-permute-done | bytes 204832 | tf_op jit(solution)/shard_map/ppermute | solution.py:30
  23.0 0.0 copy-start.8
  23.1 0.1 reshape.201
  23.1 0.1 fusion.8
  23.2 0.0 copy-done.3
  23.2 0.0 copy-done.4
  23.2 0.7 min.34.nslot_ref
  23.9 0.0 copy-done.7
  23.9 0.0 copy-done.8
  23.9 16.2 %shard_map.64 = (f32[3,64,1600]{2,1,0:T(8,128)}, bf16[3,64,1600]{2,1,0:T(8,128)(2,1)}, bf16[3,64,1600]{2,1,0:T(8,128)(2,1)}) custom-call(s32[4,4,9]{2,1,0:T(4,128)} %add_clamp_fusion.pos_ref, s32[144]{0:T(256)} %min.34.nslot_ref, s32[4,4]{1,0:T(4,128)} %count_ref.1, s32[4,4,4]{2,1,0:T(4,128)} %get-tuple-element.23.home_ref, bf16[16,64,576]{2,1,0:T(8,128)(2,1)} %bitcast.10, ...), custom_call_target="tpu_custom_call" | custom-call | tf_op jit(solution)/shard_map/pallas_call | solution.py:190
  40.1 1.9 %collective-permute-start.4 = (bf16[3,64,1600]{2,1,0:T(8,128)(2,1)}, bf16[3,64,1600]{2,1,0:T(8,128)(2,1)S(1)}, u32[]{:S(2)}, u32[]{:S(2)}) collective-permute-start(bf16[3,64,1600]{2,1,0:T(8,128)(2,1)} %get-tuple-element.11), channel_id=1, source_target_pairs={{0,1},{1,2},{2,3},{4,5},{5,6},{6,7},{8,9},{9,10},{10,11},{12,13},{... | collective-permute-start | bytes 1843208 | tf_op jit(solution)/shard_map/ppermute | solution.py:30
  42.0 3.6 %collective-permute-start.5 = (bf16[3,64,1600]{2,1,0:T(8,128)(2,1)}, bf16[3,64,1600]{2,1,0:T(8,128)(2,1)S(1)}, u32[]{:S(2)}, u32[]{:S(2)}) collective-permute-start(bf16[3,64,1600]{2,1,0:T(8,128)(2,1)} %get-tuple-element.12), channel_id=1, source_target_pairs={{1,0},{2,1},{3,2},{5,4},{6,5},{7,6},{9,8},{10,9},{11,10},{13,12},{... | collective-permute-start | bytes 1843208 | tf_op jit(solution)/shard_map/ppermute | solution.py:30
  45.6 6.4 %collective-permute-done.4.left_ref = bf16[3,64,1600]{2,1,0:T(8,128)(2,1)S(1)} collective-permute-done((bf16[3,64,1600]{2,1,0:T(8,128)(2,1)}, bf16[3,64,1600]{2,1,0:T(8,128)(2,1)S(1)}, u32[]{:S(2)}, u32[]{:S(2)}) %collective-permute-start.4) | collective-permute-done | bytes 614432 | tf_op jit(solution)/shard_map/ppermute | solution.py:30
  52.0 0.0 copy-start.1
  52.0 1.9 %collective-permute-done.5.right_ref = bf16[3,64,1600]{2,1,0:T(8,128)(2,1)S(1)} collective-permute-done((bf16[3,64,1600]{2,1,0:T(8,128)(2,1)}, bf16[3,64,1600]{2,1,0:T(8,128)(2,1)S(1)}, u32[]{:S(2)}, u32[]{:S(2)}) %collective-permute-start.5) | collective-permute-done | bytes 614432 | tf_op jit(solution)/shard_map/ppermute | solution.py:30
  53.9 0.0 copy-start.2
  53.9 0.0 copy-done.1
  53.9 0.8 %copy-done.2 = bf16[3,64,1600]{2,1,0:T(8,128)(2,1)} copy-done((bf16[3,64,1600]{2,1,0:T(8,128)(2,1)}, bf16[3,64,1600]{2,1,0:T(8,128)(2,1)S(1)}, u32[]{:S(2)}) %copy-start.2) | copy-done | bytes 614424
  54.7 3.3 %shard_map.66 = (bf16[64,2240]{1,0:T(8,128)(2,1)}, bf16[64,2240]{1,0:T(8,128)(2,1)}) custom-call(f32[3,64,1600]{2,1,0:T(8,128)} %get-tuple-element.10.keep_ref, bf16[3,64,1600]{2,1,0:T(8,128)(2,1)} %copy-done.1, bf16[3,64,1600]{2,1,0:T(8,128)(2,1)} %copy-done.2), custom_call_target="tpu_custom_call" | custom-call | tf_op jit(solution)/shard_map/pallas_call | solution.py:220
  58.0 3.9 %collective-permute-start.6 = (bf16[64,2240]{1,0:T(8,128)(2,1)}, bf16[64,2240]{1,0:T(8,128)(2,1)S(1)}, u32[]{:S(2)}, u32[]{:S(2)}) collective-permute-start(bf16[64,2240]{1,0:T(8,128)(2,1)} %get-tuple-element.13), channel_id=1, source_target_pairs={{0,4},{1,5},{2,6},{3,7},{4,8},{5,9},{6,10},{7,11},{8,12},{9,13},{1... | collective-permute-start | bytes 860168 | tf_op jit(solution)/shard_map/ppermute | solution.py:30
  61.9 2.8 %collective-permute-start.7 = (bf16[64,2240]{1,0:T(8,128)(2,1)}, bf16[64,2240]{1,0:T(8,128)(2,1)S(1)}, u32[]{:S(2)}, u32[]{:S(2)}) collective-permute-start(bf16[64,2240]{1,0:T(8,128)(2,1)} %get-tuple-element.14), channel_id=1, source_target_pairs={{4,0},{5,1},{6,2},{7,3},{8,4},{9,5},{10,6},{11,7},{12,8},{13,9},{1... | collective-permute-start | bytes 860168 | tf_op jit(solution)/shard_map/ppermute | solution.py:30
  64.7 2.9 %shard_map.65.keep_ref = f32[64,2240]{1,0:T(8,128)} custom-call(f32[3,64,1600]{2,1,0:T(8,128)} %get-tuple-element.10.keep_ref, bf16[3,64,1600]{2,1,0:T(8,128)(2,1)} %copy-done.1, bf16[3,64,1600]{2,1,0:T(8,128)(2,1)} %copy-done.2), custom_call_target="tpu_custom_call" | custom-call | tf_op jit(solution)/shard_map/pallas_call | solution.py:229
  67.6 0.1 collective-permute-done.6.up_ref
  67.7 0.0 copy-start.5
  67.7 3.1 %collective-permute-done.7.down_ref = bf16[64,2240]{1,0:T(8,128)(2,1)S(1)} collective-permute-done((bf16[64,2240]{1,0:T(8,128)(2,1)}, bf16[64,2240]{1,0:T(8,128)(2,1)S(1)}, u32[]{:S(2)}, u32[]{:S(2)}) %collective-permute-start.7) | collective-permute-done | bytes 286752 | tf_op jit(solution)/shard_map/ppermute | solution.py:30
  70.8 0.0 copy-done.5
  70.9 0.0 copy-start.6
  70.9 0.7 copy-done.6
  71.6 2.4 %shard_map.67 = bf16[64,3136]{1,0:T(8,128)(2,1)} custom-call(f32[64,2240]{1,0:T(8,128)} %shard_map.65.keep_ref, bf16[64,2240]{1,0:T(8,128)(2,1)} %copy-done.5, bf16[64,2240]{1,0:T(8,128)(2,1)} %copy-done.6), custom_call_target="tpu_custom_call" | custom-call | tf_op jit(solution)/shard_map/pallas_call | solution.py:237
  (14 shorter events, 0.2 us)
Async XLA Ops:
  0.0 14.0 %copy-start = (bf16[4,4,64,256]{3,2,1,0:T(8,128)(2,1)S(1)}, bf16[4,4,64,256]{3,2,1,0:T(8,128)(2,1)}, u32[]{:S(2)}) copy-start(bf16[4,4,64,256]{3,2,1,0:T(8,128)(2,1)} %param.9) | copy-start | bytes 1572868
  2.5 8.3 %collective-permute-start = (bf16[272,256]{1,0:T(8,128)(2,1)S(1)}, bf16[272,256]{1,0:T(8,128)(2,1)S(1)}, u32[]{:S(2)}, u32[]{:S(2)}) collective-permute-start(bf16[272,256]{1,0:T(8,128)(2,1)S(1)} %fusion.6), channel_id=1, source_target_pairs={{0,4},{1,5},{2,6},{3,7},{4,8},{5,9},{6,10},{7,11},{8,12},{9,13},{1... | collective-permute-start | bytes 417800 | tf_op jit(solution)/shard_map/ppermute | solution.py:30
  6.0 7.7 %collective-permute-start.1 = (bf16[272,256]{1,0:T(8,128)(2,1)S(1)}, bf16[272,256]{1,0:T(8,128)(2,1)S(1)}, u32[]{:S(2)}, u32[]{:S(2)}) collective-permute-start(bf16[272,256]{1,0:T(8,128)(2,1)S(1)} %fusion.7), channel_id=1, source_target_pairs={{4,0},{5,1},{6,2},{7,3},{8,4},{9,5},{10,6},{11,7},{12,8},{13,9},{1... | collective-permute-start | bytes 417800 | tf_op jit(solution)/shard_map/ppermute | solution.py:30
  10.8 12.4 %copy-start.3 = (bf16[272,256]{1,0:T(8,128)(2,1)}, bf16[272,256]{1,0:T(8,128)(2,1)S(1)}, u32[]{:S(2)}) copy-start(bf16[272,256]{1,0:T(8,128)(2,1)S(1)} %collective-permute-done.above_ref) | copy-start | bytes 417796
  13.7 9.5 %copy-start.4 = (bf16[272,256]{1,0:T(8,128)(2,1)}, bf16[272,256]{1,0:T(8,128)(2,1)S(1)}, u32[]{:S(2)}) copy-start(bf16[272,256]{1,0:T(8,128)(2,1)S(1)} %collective-permute-done.1.below_ref) | copy-start | bytes 417796
  14.1 7.1 %collective-permute-start.2 = (bf16[400,256]{1,0:T(8,128)(2,1)S(1)}, bf16[400,256]{1,0:T(8,128)(2,1)S(1)}, u32[]{:S(2)}, u32[]{:S(2)}) collective-permute-start(bf16[400,256]{1,0:T(8,128)(2,1)S(1)} %fusion.4), channel_id=1, source_target_pairs={{0,1},{1,2},{2,3},{4,5},{5,6},{6,7},{8,9},{9,10},{10,11},{12,13},{... | collective-permute-start | bytes 614408 | tf_op jit(solution)/shard_map/ppermute | solution.py:30
  16.1 6.9 %collective-permute-start.3 = (bf16[400,256]{1,0:T(8,128)(2,1)S(1)}, bf16[400,256]{1,0:T(8,128)(2,1)S(1)}, u32[]{:S(2)}, u32[]{:S(2)}) collective-permute-start(bf16[400,256]{1,0:T(8,128)(2,1)S(1)} %fusion.5), channel_id=1, source_target_pairs={{1,0},{2,1},{3,2},{5,4},{6,5},{7,6},{9,8},{10,9},{11,10},{13,12},{... | collective-permute-start | bytes 614408 | tf_op jit(solution)/shard_map/ppermute | solution.py:30
  21.2 2.7 %copy-start.7 = (bf16[400,256]{1,0:T(8,128)(2,1)}, bf16[400,256]{1,0:T(8,128)(2,1)S(1)}, u32[]{:S(2)}) copy-start(bf16[400,256]{1,0:T(8,128)(2,1)S(1)} %collective-permute-done.2.left_ref) | copy-start | bytes 614404
  23.0 0.9 %copy-start.8 = (bf16[400,256]{1,0:T(8,128)(2,1)}, bf16[400,256]{1,0:T(8,128)(2,1)S(1)}, u32[]{:S(2)}) copy-start(bf16[400,256]{1,0:T(8,128)(2,1)S(1)} %collective-permute-done.3.right_ref) | copy-start | bytes 614404
  40.1 11.9 %collective-permute-start.4 = (bf16[3,64,1600]{2,1,0:T(8,128)(2,1)}, bf16[3,64,1600]{2,1,0:T(8,128)(2,1)S(1)}, u32[]{:S(2)}, u32[]{:S(2)}) collective-permute-start(bf16[3,64,1600]{2,1,0:T(8,128)(2,1)} %get-tuple-element.11), channel_id=1, source_target_pairs={{0,1},{1,2},{2,3},{4,5},{5,6},{6,7},{8,9},{9,10},{10,11},{12,13},{... | collective-permute-start | bytes 1843208 | tf_op jit(solution)/shard_map/ppermute | solution.py:30
  42.0 11.9 %collective-permute-start.5 = (bf16[3,64,1600]{2,1,0:T(8,128)(2,1)}, bf16[3,64,1600]{2,1,0:T(8,128)(2,1)S(1)}, u32[]{:S(2)}, u32[]{:S(2)}) collective-permute-start(bf16[3,64,1600]{2,1,0:T(8,128)(2,1)} %get-tuple-element.12), channel_id=1, source_target_pairs={{1,0},{2,1},{3,2},{5,4},{6,5},{7,6},{9,8},{10,9},{11,10},{13,12},{... | collective-permute-start | bytes 1843208 | tf_op jit(solution)/shard_map/ppermute | solution.py:30
  52.0 1.9 %copy-start.1 = (bf16[3,64,1600]{2,1,0:T(8,128)(2,1)}, bf16[3,64,1600]{2,1,0:T(8,128)(2,1)S(1)}, u32[]{:S(2)}) copy-start(bf16[3,64,1600]{2,1,0:T(8,128)(2,1)S(1)} %collective-permute-done.4.left_ref) | copy-start | bytes 1843204
  53.9 0.9 %copy-start.2 = (bf16[3,64,1600]{2,1,0:T(8,128)(2,1)}, bf16[3,64,1600]{2,1,0:T(8,128)(2,1)S(1)}, u32[]{:S(2)}) copy-start(bf16[3,64,1600]{2,1,0:T(8,128)(2,1)S(1)} %collective-permute-done.5.right_ref) | copy-start | bytes 1843204
  58.0 9.7 %collective-permute-start.6 = (bf16[64,2240]{1,0:T(8,128)(2,1)}, bf16[64,2240]{1,0:T(8,128)(2,1)S(1)}, u32[]{:S(2)}, u32[]{:S(2)}) collective-permute-start(bf16[64,2240]{1,0:T(8,128)(2,1)} %get-tuple-element.13), channel_id=1, source_target_pairs={{0,4},{1,5},{2,6},{3,7},{4,8},{5,9},{6,10},{7,11},{8,12},{9,13},{1... | collective-permute-start | bytes 860168 | tf_op jit(solution)/shard_map/ppermute | solution.py:30
  61.9 8.9 %collective-permute-start.7 = (bf16[64,2240]{1,0:T(8,128)(2,1)}, bf16[64,2240]{1,0:T(8,128)(2,1)S(1)}, u32[]{:S(2)}, u32[]{:S(2)}) collective-permute-start(bf16[64,2240]{1,0:T(8,128)(2,1)} %get-tuple-element.14), channel_id=1, source_target_pairs={{4,0},{5,1},{6,2},{7,3},{8,4},{9,5},{10,6},{11,7},{12,8},{13,9},{1... | collective-permute-start | bytes 860168 | tf_op jit(solution)/shard_map/ppermute | solution.py:30
  67.7 3.2 %copy-start.5 = (bf16[64,2240]{1,0:T(8,128)(2,1)}, bf16[64,2240]{1,0:T(8,128)(2,1)S(1)}, u32[]{:S(2)}) copy-start(bf16[64,2240]{1,0:T(8,128)(2,1)S(1)} %collective-permute-done.6.up_ref) | copy-start | bytes 860164
  70.9 0.7 copy-start.6

commit v11 on v10

--- a/solution.py
+++ b/solution.py
@@ -28,6 +28,18 @@
             if 0 <= tr < rows and 0 <= tc < cols:
                 pairs.append((r * cols + c, tr * cols + tc))
     return lax.ppermute(value, ("row", "col"), pairs)
+
+
+def exchange(to_prev, to_next, axis):
+    count = lax.axis_size(axis)
+    even = lax.axis_index(axis) % 2 == 0
+    first = [(j, j ^ 1) for j in range(count) if (j ^ 1) < count]
+    second = [(j, j + 1) for j in range(1, count - 1, 2)] + [(j + 1, j) for j in range(1, count - 1, 2)]
+    got_first = lax.ppermute(jnp.where(even, to_next, to_prev), axis, first)
+    got_second = lax.ppermute(jnp.where(even, to_prev, to_next), axis, second)
+    from_prev = jnp.where(even, got_second, got_first)
+    from_next = jnp.where(even, got_first, got_second)
+    return from_prev, from_next
 
 
 def galerkin_kernel(pos_ref, nslot_ref, count_ref, home_ref, a_ref, own_ref, above_ref, below_ref,
@@ -160,14 +172,14 @@
         return p_part, rel_part
 
     hr, hc = tile_rows + 2, tile_cols + 2
-    above_in = shifted(payload(prolong[tile_rows - 1], rel[tile_rows - 1]), 1, 0)
-    below_in = shifted(payload(prolong[0], rel[0]), -1, 0)
+    above_in, below_in = exchange(
+        payload(prolong[0], rel[0]), payload(prolong[tile_rows - 1], rel[tile_rows - 1]), "row")
     above, above_rel = unpack(above_in, tile_cols)
     below, below_rel = unpack(below_in, tile_cols)
     tall = jnp.concatenate([above[None], prolong, below[None]], axis=0)
     tall_rel = jnp.concatenate([above_rel[None], rel, below_rel[None]], axis=0)
-    left_in = shifted(payload(tall[:, tile_cols - 1], tall_rel[:, tile_cols - 1]), 0, 1)
-    right_in = shifted(payload(tall[:, 0], tall_rel[:, 0]), 0, -1)
+    left_in, right_in = exchange(
+        payload(tall[:, 0], tall_rel[:, 0]), payload(tall[:, tile_cols - 1], tall_rel[:, tile_cols - 1]), "col")
     left_rel = unpack(left_in, hr)[1]
     right_rel = unpack(right_in, hr)[1]
     near_rel = jnp.concatenate([left_rel[:, None], tall_rel, right_rel[:, None]], axis=1)
@@ -214,8 +226,7 @@
         left_in,
         right_in,
     )
-    from_left = shifted(to_left, 0, 1)
-    from_right = shifted(to_right, 0, -1)
+    from_left, from_right = exchange(to_right, to_left, "col")
     band = WIN * OUTW * B
     minus, plus = pl.pallas_call(
         fold_cols_send_kernel,
@@ -232,8 +243,7 @@
         in_specs=[pl.BlockSpec(memory_space=vmem)] * 3,
         out_specs=pl.BlockSpec(memory_space=vmem),
     )(keep, from_left, from_right)
-    up_in = shifted(plus, 1, 0)
-    down_in = shifted(minus, -1, 0)
+    up_in, down_in = exchange(minus, plus, "row")
     out = pl.pallas_call(
         fold_rows_kernel,
         out_shape=jax.ShapeDtypeStruct((B, OUTW * OUTW * B), jnp.bfloat16),

time: 75.4 us -> 72.1 us (0.956); the launches traced: 74 us -> 71.5 us
  starting transfers between devices: 24.6 us -> 13.2 us
  waiting for transfers between devices: 17.4 us -> 23.4 us
  other arithmetic: 3.1 us -> 7.73 us
  local copies, waits for them, and re-layouts: 4 us -> 2.42 us
    ppermute x8, starting transfers between devices: 24.6 us -> 13.2 us  [the longest x4 9.98 us: exchange(): got_second = lax.ppermute(jnp.where(even, to_prev, to_next), axis, second)]
    ppermute x8, waiting for transfers between devices: 17.4 us -> 23.4 us  [the longest x4 20.3 us: exchange(): got_second = lax.ppermute(jnp.where(even, to_prev, to_next), axis, second)]
    select_n x0 -> x8, other arithmetic: none -> 4.71 us  [the longest x2 2.49 us: exchange(): got_first = lax.ppermute(jnp.where(even, to_next, to_prev), axis, first)]
    unnamed x18 -> x10, local copies, waits for them, and re-layouts: 1.58 us -> 0.02 us
  transfers between devices with their start and end apart: 8 -> 8, of which waited for: 8 -> 6; matrix products, arithmetic and copies ran while one was open for 2% -> 2% of each run, Pallas kernels for 4% -> 4%
where the time goes in v11:
time: 72.1 us; the launch traced here: 71.5 us
  Pallas kernels  24.5 us (34%)
  waiting for transfers between devices  23.4 us (32%)
  starting transfers between devices  13.2 us (18%)
  other arithmetic  7.73 us (11%)
  local copies, waits for them, and re-layouts  2.42 us (3%)
    ppermute x4, waiting for transfers between devices, exchange(): got_second = lax.ppermute(jnp.where(even, to_prev, to_next), axis, second)  20.3 us
    pallas_call x1, Pallas kernels, per_device(): pl.pallas_call(galerkin_kernel, out_shape=(jax.ShapeDtypeStruct((HOME, B,...  16 us
    ppermute x4, starting transfers between devices, exchange(): got_second = lax.ppermute(jnp.where(even, to_prev, to_next), axis, second)  9.98 us
    pallas_call x1, Pallas kernels, per_device(): pl.pallas_call(fold_cols_send_kernel, out_shape=(jax.ShapeDtypeStruct((B,...  3.27 us
    ppermute x4, starting transfers between devices, exchange(): got_first = lax.ppermute(jnp.where(even, to_next, to_prev), axis, first)  3.25 us
    ppermute x4, waiting for transfers between devices, exchange(): got_first = lax.ppermute(jnp.where(even, to_next, to_prev), axis, first)  3.1 us
    pallas_call x1, Pallas kernels, per_device(): pl.pallas_call(fold_cols_keep_kernel, out_shape=jax.ShapeDtypeStruct((B,...  2.85 us
    select_n x2, other arithmetic, exchange(): got_first = lax.ppermute(jnp.where(even, to_next, to_prev), axis, first)  2.49 us
  transfers between devices with their start and end apart: 8, of which 6 were waited for; matrix products, arithmetic and copies ran while one was open for 2% of the time, Pallas kernels for 4%

profile of v11, /device:TPU:20, one launch (start us, length us, event | category | flops | bytes accessed | tf_op | source)
XLA Modules:
  0.0 71.5 jit_solution(10138644360071708440)
XLA Ops:
  0.0 0.0 copy-start
  0.0 1.4 %fusion.27 = (bf16[4,4,4]{2,1,0:T(4,128)(2,1)S(1)}, s32[4,4,4]{2,1,0:T(4,128)S(1)}, s32[4,4,4]{2,1,0:T(4,128)}) fusion(s32[]{:T(128)S(6)} %axis_index.17, s32[]{:T(128)S(6)} %axis_index.15, s32[4,4,4]{2,1,0:T(4,128)} %param.10, s32[4,4]{1,0:T(4,128)} %param.11), kind=kLoop, calls=%fused_computation.80 | loop fusion | flops 2112 | bytes 968 | tf_op jit(solution)/shard_map/convert.7
  1.4 0.1 convert_element_type.106
  1.5 0.1 convert_element_type.107
  1.6 1.0 %fusion.28 = (bf16[1,4,64,256]{3,2,1,0:T(8,128)(2,1)S(1)}, bf16[1,4,64,256]{3,2,1,0:T(8,128)(2,1)S(1)}) fusion(bf16[4,4,64,256]{3,2,1,0:T(8,128)(2,1)} %param.9), kind=kLoop, calls=%fused_computation.81 | loop fusion | bytes 524288 | tf_op jit(solution)/shard_map/slice | solution.py:176
  2.6 0.1 broadcast_select_fusion.15
  2.7 3.3 %collective-permute-start = (bf16[272,256]{1,0:T(8,128)(2,1)S(1)}, bf16[272,256]{1,0:T(8,128)(2,1)S(1)}, u32[]{:S(2)}, u32[]{:S(2)}) collective-permute-start(bf16[272,256]{1,0:T(8,128)(2,1)S(1)} %get-tuple-element.37), channel_id=1, source_target_pairs={{4,8},{12,16},{20,24},{8,4},{16,12},{24,20},{5,9},{13,17},{21,25},... | collective-permute-start | bytes 417800 | tf_op jit(solution)/shard_map/ppermute | solution.py:39
  5.9 1.7 %collective-permute-start.1 = (bf16[272,256]{1,0:T(8,128)(2,1)S(1)}, bf16[272,256]{1,0:T(8,128)(2,1)S(1)}, u32[]{:S(2)}, u32[]{:S(2)}) collective-permute-start(bf16[272,256]{1,0:T(8,128)(2,1)S(1)} %get-tuple-element.38), channel_id=1, source_target_pairs={{0,4},{4,0},{8,12},{12,8},{16,20},{20,16},{24,28},{28,24},{1,5},{5... | collective-permute-start | bytes 417800 | tf_op jit(solution)/shard_map/ppermute | solution.py:38
  7.7 1.3 %add_clamp_fusion.pos_ref = s32[4,4,9]{2,1,0:T(4,128)} fusion(s32[4,4,9]{2,1,0:T(4,128)} %param.7, s32[]{:T(128)S(6)} %mul.33, s32[]{:T(128)S(6)} %mul.30), kind=kLoop, calls=%fused_computation.57 | loop fusion | flops 3744 | bytes 1160 | tf_op jit(solution)/shard_map/jit(clip)/min | solution.py:196
  9.0 2.0 %collective-permute-done = bf16[272,256]{1,0:T(8,128)(2,1)S(1)} collective-permute-done((bf16[272,256]{1,0:T(8,128)(2,1)S(1)}, bf16[272,256]{1,0:T(8,128)(2,1)S(1)}, u32[]{:S(2)}, u32[]{:S(2)}) %collective-permute-start) | collective-permute-done | bytes 139296 | tf_op jit(solution)/shard_map/ppermute | solution.py:39
  11.0 2.9 %collective-permute-done.1 = bf16[272,256]{1,0:T(8,128)(2,1)S(1)} collective-permute-done((bf16[272,256]{1,0:T(8,128)(2,1)S(1)}, bf16[272,256]{1,0:T(8,128)(2,1)S(1)}, u32[]{:S(2)}, u32[]{:S(2)}) %collective-permute-start.1) | collective-permute-done | bytes 139296 | tf_op jit(solution)/shard_map/ppermute | solution.py:38
  13.9 0.0 copy-start.1
  13.9 0.0 copy-start.2
  14.0 0.1 reshape.197
  14.0 0.1 reshape.196
  14.2 0.1 convert_element_type.112
  14.3 0.1 convert_element_type.113
  14.3 0.0 copy-done
  14.3 0.1 pad_maximum_fusion.2
  14.4 0.1 broadcast_select_fusion.11
  14.5 2.0 %collective-permute-start.2 = (bf16[400,256]{1,0:T(8,128)(2,1)S(1)}, bf16[400,256]{1,0:T(8,128)(2,1)S(1)}, u32[]{:S(2)}, u32[]{:S(2)}) collective-permute-start(bf16[400,256]{1,0:T(8,128)(2,1)S(1)} %get-tuple-element.33), channel_id=1, source_target_pairs={{1,2},{2,1},{5,6},{6,5},{9,10},{10,9},{13,14},{14,13},{17,18},{18,... | collective-permute-start | bytes 614408 | tf_op jit(solution)/shard_map/ppermute | solution.py:39
  16.5 0.1 collective-permute-start.3
  16.6 0.1 add_add_fusion.1
  16.7 4.9 %collective-permute-done.2 = bf16[400,256]{1,0:T(8,128)(2,1)S(1)} collective-permute-done((bf16[400,256]{1,0:T(8,128)(2,1)S(1)}, bf16[400,256]{1,0:T(8,128)(2,1)S(1)}, u32[]{:S(2)}, u32[]{:S(2)}) %collective-permute-start.2) | collective-permute-done | bytes 204832 | tf_op jit(solution)/shard_map/ppermute | solution.py:39
  21.6 0.0 collective-permute-done.3
  21.6 0.0 copy-done.1
  21.6 0.0 copy-done.2
  21.6 0.0 copy-start.3
  21.6 0.0 copy-start.4
  21.7 0.1 reshape.201
  21.8 0.1 reshape.200
  21.8 0.1 fusion.8
  21.9 0.7 min.34.nslot_ref
  22.6 0.0 copy-done.3
  22.6 0.0 copy-done.4
  22.6 16.0 %shard_map.64 = (f32[3,64,1600]{2,1,0:T(8,128)}, bf16[3,64,1600]{2,1,0:T(8,128)(2,1)}, bf16[3,64,1600]{2,1,0:T(8,128)(2,1)}) custom-call(s32[4,4,9]{2,1,0:T(4,128)} %add_clamp_fusion.pos_ref, s32[144]{0:T(256)} %min.34.nslot_ref, s32[4,4]{1,0:T(4,128)} %count_ref.1, s32[4,4,4]{2,1,0:T(4,128)} %get-tuple-element.39.home_ref, bf16[16,64,576]{2,1,0:T(8,128)(2,1)} %bitcast.10, ...), custom_call_target="tpu_custom_call" | custom-call | tf_op jit(solution)/shard_map/pallas_call | solution.py:202
  38.6 1.4 %broadcast_select_fusion.2 = (bf16[3,64,1600]{2,1,0:T(8,128)(2,1)S(1)}, bf16[3,64,1600]{2,1,0:T(8,128)(2,1)S(1)}) fusion(bf16[3,64,1600]{2,1,0:T(8,128)(2,1)} %get-tuple-element.12, bf16[3,64,1600]{2,1,0:T(8,128)(2,1)} %get-tuple-element.11, pred[]{:T(512)S(6)} %eq.17), kind=kLoop, calls=%fused_computation.2 | loop fusion | flops 614400 | bytes 2457601 | tf_op jit(solution)/shard_map/jit(_where)/select_n | solution.py:38
  40.0 0.1 collective-permute-start.5
  40.1 2.3 %collective-permute-start.4 = (bf16[3,64,1600]{2,1,0:T(8,128)(2,1)S(1)}, bf16[3,64,1600]{2,1,0:T(8,128)(2,1)S(1)}, u32[]{:S(2)}, u32[]{:S(2)}) collective-permute-start(bf16[3,64,1600]{2,1,0:T(8,128)(2,1)S(1)} %get-tuple-element.22), channel_id=1, source_target_pairs={{1,2},{2,1},{5,6},{6,5},{9,10},{10,9},{13,14},{14,13},{17,18},{18,... | collective-permute-start | bytes 1843208 | tf_op jit(solution)/shard_map/ppermute | solution.py:39
  42.4 0.0 collective-permute-done.5
  42.4 9.4 %collective-permute-done.4 = bf16[3,64,1600]{2,1,0:T(8,128)(2,1)S(1)} collective-permute-done((bf16[3,64,1600]{2,1,0:T(8,128)(2,1)S(1)}, bf16[3,64,1600]{2,1,0:T(8,128)(2,1)S(1)}, u32[]{:S(2)}, u32[]{:S(2)}) %collective-permute-start.4) | collective-permute-done | bytes 614432 | tf_op jit(solution)/shard_map/ppermute | solution.py:39
  51.8 1.2 %broadcast_select_fusion = (bf16[3,64,1600]{2,1,0:T(8,128)(2,1)}, bf16[3,64,1600]{2,1,0:T(8,128)(2,1)}) fusion(bf16[3,64,1600]{2,1,0:T(8,128)(2,1)S(1)} %collective-permute-done.5, bf16[3,64,1600]{2,1,0:T(8,128)(2,1)S(1)} %collective-permute-done.4, pred[]{:T(512)S(6)} %eq.17), kind=kLoop, calls=%fused_computation | loop fusion | flops 614400 | bytes 2457601 | tf_op jit(solution)/shard_map/jit(_where)/select_n | solution.py:41
  53.0 3.3 %shard_map.66 = (bf16[64,2240]{1,0:T(8,128)(2,1)}, bf16[64,2240]{1,0:T(8,128)(2,1)}) custom-call(f32[3,64,1600]{2,1,0:T(8,128)} %get-tuple-element.10.keep_ref, bf16[3,64,1600]{2,1,0:T(8,128)(2,1)} %get-tuple-element.20.left_ref, bf16[3,64,1600]{2,1,0:T(8,128)(2,1)} %get-tuple-element.19.right_ref), custom_call_target="tpu_custom_call" | custom-call | tf_op jit(solution)/shard_map/pallas_call | solution.py:231
  56.2 1.1 %broadcast_select_fusion.6 = (bf16[64,2240]{1,0:T(8,128)(2,1)S(1)}, bf16[64,2240]{1,0:T(8,128)(2,1)S(1)}) fusion(bf16[64,2240]{1,0:T(8,128)(2,1)} %get-tuple-element.14, bf16[64,2240]{1,0:T(8,128)(2,1)} %get-tuple-element.13, pred[]{:T(512)S(6)} %eq.18), kind=kLoop, calls=%fused_computation.9 | loop fusion | flops 286720 | bytes 1146881 | tf_op jit(solution)/shard_map/jit(_where)/select_n | solution.py:38
  57.3 1.4 %collective-permute-start.7 = (bf16[64,2240]{1,0:T(8,128)(2,1)S(1)}, bf16[64,2240]{1,0:T(8,128)(2,1)S(1)}, u32[]{:S(2)}, u32[]{:S(2)}) collective-permute-start(bf16[64,2240]{1,0:T(8,128)(2,1)S(1)} %get-tuple-element.27), channel_id=1, source_target_pairs={{0,4},{4,0},{8,12},{12,8},{16,20},{20,16},{24,28},{28,24},{1,5},{5... | collective-permute-start | bytes 860168 | tf_op jit(solution)/shard_map/ppermute | solution.py:38
  58.7 2.3 %collective-permute-start.6 = (bf16[64,2240]{1,0:T(8,128)(2,1)S(1)}, bf16[64,2240]{1,0:T(8,128)(2,1)S(1)}, u32[]{:S(2)}, u32[]{:S(2)}) collective-permute-start(bf16[64,2240]{1,0:T(8,128)(2,1)S(1)} %get-tuple-element.28), channel_id=1, source_target_pairs={{4,8},{12,16},{20,24},{8,4},{16,12},{24,20},{5,9},{13,17},{21,25},... | collective-permute-start | bytes 860168 | tf_op jit(solution)/shard_map/ppermute | solution.py:39
  61.1 2.9 %shard_map.65.keep_ref = f32[64,2240]{1,0:T(8,128)} custom-call(f32[3,64,1600]{2,1,0:T(8,128)} %get-tuple-element.10.keep_ref, bf16[3,64,1600]{2,1,0:T(8,128)(2,1)} %get-tuple-element.20.left_ref, bf16[3,64,1600]{2,1,0:T(8,128)(2,1)} %get-tuple-element.19.right_ref), custom_call_target="tpu_custom_call" | custom-call | tf_op jit(solution)/shard_map/pallas_call | solution.py:240
  63.9 0.2 collective-permute-done.7
  64.1 4.1 %collective-permute-done.6 = bf16[64,2240]{1,0:T(8,128)(2,1)S(1)} collective-permute-done((bf16[64,2240]{1,0:T(8,128)(2,1)S(1)}, bf16[64,2240]{1,0:T(8,128)(2,1)S(1)}, u32[]{:S(2)}, u32[]{:S(2)}) %collective-permute-start.6) | collective-permute-done | bytes 286752 | tf_op jit(solution)/shard_map/ppermute | solution.py:39
  68.2 0.9 %broadcast_select_fusion.4 = (bf16[64,2240]{1,0:T(8,128)(2,1)}, bf16[64,2240]{1,0:T(8,128)(2,1)}) fusion(bf16[64,2240]{1,0:T(8,128)(2,1)S(1)} %collective-permute-done.7, bf16[64,2240]{1,0:T(8,128)(2,1)S(1)} %collective-permute-done.6, pred[]{:T(512)S(6)} %eq.18), kind=kLoop, calls=%fused_computation.7 | loop fusion | flops 286720 | bytes 1146881 | tf_op jit(solution)/shard_map/jit(_where)/select_n | solution.py:41
  69.1 2.4 %shard_map.67 = bf16[64,3136]{1,0:T(8,128)(2,1)} custom-call(f32[64,2240]{1,0:T(8,128)} %shard_map.65.keep_ref, bf16[64,2240]{1,0:T(8,128)(2,1)} %get-tuple-element.26.up_ref, bf16[64,2240]{1,0:T(8,128)(2,1)} %get-tuple-element.25.down_ref), custom_call_target="tpu_custom_call" | custom-call | tf_op jit(solution)/shard_map/pallas_call | solution.py:247
  (11 shorter events, 0.2 us)
Async XLA Ops:
  0.0 14.3 %copy-start = (bf16[4,4,64,256]{3,2,1,0:T(8,128)(2,1)S(1)}, bf16[4,4,64,256]{3,2,1,0:T(8,128)(2,1)}, u32[]{:S(2)}) copy-start(bf16[4,4,64,256]{3,2,1,0:T(8,128)(2,1)} %param.9) | copy-start | bytes 1572868
  2.7 8.3 %collective-permute-start = (bf16[272,256]{1,0:T(8,128)(2,1)S(1)}, bf16[272,256]{1,0:T(8,128)(2,1)S(1)}, u32[]{:S(2)}, u32[]{:S(2)}) collective-permute-start(bf16[272,256]{1,0:T(8,128)(2,1)S(1)} %get-tuple-element.37), channel_id=1, source_target_pairs={{4,8},{12,16},{20,24},{8,4},{16,12},{24,20},{5,9},{13,17},{21,25},... | collective-permute-start | bytes 417800 | tf_op jit(solution)/shard_map/ppermute | solution.py:39
  5.9 7.9 %collective-permute-start.1 = (bf16[272,256]{1,0:T(8,128)(2,1)S(1)}, bf16[272,256]{1,0:T(8,128)(2,1)S(1)}, u32[]{:S(2)}, u32[]{:S(2)}) collective-permute-start(bf16[272,256]{1,0:T(8,128)(2,1)S(1)} %get-tuple-element.38), channel_id=1, source_target_pairs={{0,4},{4,0},{8,12},{12,8},{16,20},{20,16},{24,28},{28,24},{1,5},{5... | collective-permute-start | bytes 417800 | tf_op jit(solution)/shard_map/ppermute | solution.py:38
  13.9 7.7 %copy-start.1 = (bf16[272,256]{1,0:T(8,128)(2,1)}, bf16[272,256]{1,0:T(8,128)(2,1)S(1)}, u32[]{:S(2)}) copy-start(bf16[272,256]{1,0:T(8,128)(2,1)S(1)} %get-tuple-element.35.above_ref) | copy-start | bytes 417796
  13.9 7.7 %copy-start.2 = (bf16[272,256]{1,0:T(8,128)(2,1)}, bf16[272,256]{1,0:T(8,128)(2,1)S(1)}, u32[]{:S(2)}) copy-start(bf16[272,256]{1,0:T(8,128)(2,1)S(1)} %get-tuple-element.36.below_ref) | copy-start | bytes 417796
  14.5 7.1 %collective-permute-start.2 = (bf16[400,256]{1,0:T(8,128)(2,1)S(1)}, bf16[400,256]{1,0:T(8,128)(2,1)S(1)}, u32[]{:S(2)}, u32[]{:S(2)}) collective-permute-start(bf16[400,256]{1,0:T(8,128)(2,1)S(1)} %get-tuple-element.33), channel_id=1, source_target_pairs={{1,2},{2,1},{5,6},{6,5},{9,10},{10,9},{13,14},{14,13},{17,18},{18,... | collective-permute-start | bytes 614408 | tf_op jit(solution)/shard_map/ppermute | solution.py:39
  16.5 5.0 %collective-permute-start.3 = (bf16[400,256]{1,0:T(8,128)(2,1)S(1)}, bf16[400,256]{1,0:T(8,128)(2,1)S(1)}, u32[]{:S(2)}, u32[]{:S(2)}) collective-permute-start(bf16[400,256]{1,0:T(8,128)(2,1)S(1)} %get-tuple-element.34), channel_id=1, source_target_pairs={{0,1},{1,0},{2,3},{3,2},{4,5},{5,4},{6,7},{7,6},{8,9},{9,8},{10,11... | collective-permute-start | bytes 614408 | tf_op jit(solution)/shard_map/ppermute | solution.py:38
  21.6 1.0 %copy-start.3 = (bf16[400,256]{1,0:T(8,128)(2,1)}, bf16[400,256]{1,0:T(8,128)(2,1)S(1)}, u32[]{:S(2)}) copy-start(bf16[400,256]{1,0:T(8,128)(2,1)S(1)} %get-tuple-element.31.left_ref) | copy-start | bytes 614404
  21.6 1.0 %copy-start.4 = (bf16[400,256]{1,0:T(8,128)(2,1)}, bf16[400,256]{1,0:T(8,128)(2,1)S(1)}, u32[]{:S(2)}) copy-start(bf16[400,256]{1,0:T(8,128)(2,1)S(1)} %get-tuple-element.32.right_ref) | copy-start | bytes 614404
  40.0 2.4 %collective-permute-start.5 = (bf16[3,64,1600]{2,1,0:T(8,128)(2,1)S(1)}, bf16[3,64,1600]{2,1,0:T(8,128)(2,1)S(1)}, u32[]{:S(2)}, u32[]{:S(2)}) collective-permute-start(bf16[3,64,1600]{2,1,0:T(8,128)(2,1)S(1)} %get-tuple-element.21), channel_id=1, source_target_pairs={{0,1},{1,0},{2,3},{3,2},{4,5},{5,4},{6,7},{7,6},{8,9},{9,8},{10,11... | collective-permute-start | bytes 1843208 | tf_op jit(solution)/shard_map/ppermute | solution.py:38
  40.1 11.7 %collective-permute-start.4 = (bf16[3,64,1600]{2,1,0:T(8,128)(2,1)S(1)}, bf16[3,64,1600]{2,1,0:T(8,128)(2,1)S(1)}, u32[]{:S(2)}, u32[]{:S(2)}) collective-permute-start(bf16[3,64,1600]{2,1,0:T(8,128)(2,1)S(1)} %get-tuple-element.22), channel_id=1, source_target_pairs={{1,2},{2,1},{5,6},{6,5},{9,10},{10,9},{13,14},{14,13},{17,18},{18,... | collective-permute-start | bytes 1843208 | tf_op jit(solution)/shard_map/ppermute | solution.py:39
  57.3 6.8 %collective-permute-start.7 = (bf16[64,2240]{1,0:T(8,128)(2,1)S(1)}, bf16[64,2240]{1,0:T(8,128)(2,1)S(1)}, u32[]{:S(2)}, u32[]{:S(2)}) collective-permute-start(bf16[64,2240]{1,0:T(8,128)(2,1)S(1)} %get-tuple-element.27), channel_id=1, source_target_pairs={{0,4},{4,0},{8,12},{12,8},{16,20},{20,16},{24,28},{28,24},{1,5},{5... | collective-permute-start | bytes 860168 | tf_op jit(solution)/shard_map/ppermute | solution.py:38
  58.7 9.5 %collective-permute-start.6 = (bf16[64,2240]{1,0:T(8,128)(2,1)S(1)}, bf16[64,2240]{1,0:T(8,128)(2,1)S(1)}, u32[]{:S(2)}, u32[]{:S(2)}) collective-permute-start(bf16[64,2240]{1,0:T(8,128)(2,1)S(1)} %get-tuple-element.28), channel_id=1, source_target_pairs={{4,8},{12,16},{20,24},{8,4},{16,12},{24,20},{5,9},{13,17},{21,25},... | collective-permute-start | bytes 860168 | tf_op jit(solution)/shard_map/ppermute | solution.py:39

commit v12 on v11

--- a/solution.py
+++ b/solution.py
@@ -42,8 +42,15 @@
     return from_prev, from_next
 
 
-def galerkin_kernel(pos_ref, nslot_ref, count_ref, home_ref, a_ref, own_ref, above_ref, below_ref,
-                    left_ref, right_ref, keep_ref, to_right_ref, to_left_ref,
+def swap_rounds(first, second, axis):
+    count = lax.axis_size(axis)
+    pairs_a = [(j, j ^ 1) for j in range(count) if (j ^ 1) < count]
+    pairs_b = [(j, j + 1) for j in range(1, count - 1, 2)] + [(j + 1, j) for j in range(1, count - 1, 2)]
+    return lax.ppermute(first, axis, pairs_a), lax.ppermute(second, axis, pairs_b)
+
+
+def galerkin_kernel(par_ref, pos_ref, nslot_ref, count_ref, home_ref, a_ref, own_ref, above_ref, below_ref,
+                    left_ref, right_ref, keep_ref, first_ref, second_ref,
                     acc_ref, prod_ref, dpt_ref, p_ref):
     patches = a_ref.shape[0]
     rows, cols = AG, AG
@@ -86,21 +93,25 @@
 
     prod = prod_ref[...]
     group = HOME * B
-    for out, at in ((to_right_ref, 0), (keep_ref, 1), (to_left_ref, 2)):
-        terms = jnp.dot(dpt_ref[at * group:(at + 1) * group].astype(jnp.bfloat16), prod,
+    odd = par_ref[0]
+    for out, at in ((first_ref, 2 - 2 * odd), (keep_ref, 1), (second_ref, 2 * odd)):
+        start = pl.multiple_of(at * group, group)
+        terms = jnp.dot(dpt_ref[pl.ds(start, group)].astype(jnp.bfloat16), prod,
                         preferred_element_type=jnp.float32)
         out[...] = terms.reshape(out.shape).astype(out.dtype)
 
 
-def fold_cols_band(keep_ref, left_ref, right_ref, d, out):
+def fold_cols_band(keep_ref, a_ref, b_ref, even, d, out):
     src_w = WIN * B
     dst_w = OUTW * B
     for sx in range(WIN):
         lo = sx * dst_w
         s0 = sx * src_w
         own = keep_ref[d, :, s0:s0 + src_w]
-        left = left_ref[d, :, s0:s0 + src_w].astype(jnp.float32)
-        right = right_ref[d, :, s0:s0 + src_w].astype(jnp.float32)
+        got_a = a_ref[d, :, s0:s0 + src_w].astype(jnp.float32)
+        got_b = b_ref[d, :, s0:s0 + src_w].astype(jnp.float32)
+        left = jnp.where(even, got_b, got_a)
+        right = jnp.where(even, got_a, got_b)
         first = left[:, :B]
         mid = left[:, B:2 * B] + own[:, :B]
         core = left[:, 2 * B:] + own[:, B:src_w - B] + right[:, :src_w - 2 * B]
@@ -113,25 +124,30 @@
         out[:, lo + 6 * B:lo + 7 * B] = last.astype(out.dtype)
 
 
-def fold_cols_send_kernel(keep_ref, left_ref, right_ref, minus_out, plus_out):
-    fold_cols_band(keep_ref, left_ref, right_ref, 0, minus_out)
-    fold_cols_band(keep_ref, left_ref, right_ref, 2, plus_out)
-
-
-def fold_cols_keep_kernel(keep_ref, left_ref, right_ref, keep_out):
-    fold_cols_band(keep_ref, left_ref, right_ref, 1, keep_out)
-
-
-def fold_rows_kernel(keep_ref, up_ref, down_ref, out_ref):
+def fold_cols_send_kernel(par_ref, keep_ref, a_ref, b_ref, first_out, second_out):
+    even_col = par_ref[0] == 0
+    odd_row = par_ref[1]
+    fold_cols_band(keep_ref, a_ref, b_ref, even_col, 2 - 2 * odd_row, first_out)
+    fold_cols_band(keep_ref, a_ref, b_ref, even_col, 2 * odd_row, second_out)
+
+
+def fold_cols_keep_kernel(par_ref, keep_ref, a_ref, b_ref, keep_out):
+    fold_cols_band(keep_ref, a_ref, b_ref, par_ref[0] == 0, 1, keep_out)
+
+
+def fold_rows_kernel(par_ref, keep_ref, a_ref, b_ref, out_ref):
     band = OUTW * B
+    even = par_ref[1] == 0
     for s in range(OUTW):
         parts = []
         if 1 <= s <= WIN:
             parts.append(keep_ref[:, (s - 1) * band:s * band])
         if s <= WIN - 1:
-            parts.append(up_ref[:, s * band:(s + 1) * band].astype(jnp.float32))
+            lanes = slice(s * band, (s + 1) * band)
+            parts.append(jnp.where(even, b_ref[:, lanes], a_ref[:, lanes]).astype(jnp.float32))
         if s >= 2:
-            parts.append(down_ref[:, (s - 2) * band:(s - 1) * band].astype(jnp.float32))
+            lanes = slice((s - 2) * band, (s - 1) * band)
+            parts.append(jnp.where(even, a_ref[:, lanes], b_ref[:, lanes]).astype(jnp.float32))
         total = parts[0]
         for extra in parts[1:]:
             total = total + extra
@@ -199,14 +215,15 @@
     smem = pltpu.MemorySpace.SMEM
     vmem = pltpu.MemorySpace.VMEM
     width = WIN * WIN * B
-    keep, to_right, to_left = pl.pallas_call(
+    parity = jnp.stack([col_index % 2, row_index % 2]).astype(jnp.int32)
+    keep, first, second = pl.pallas_call(
         galerkin_kernel,
         out_shape=(
             jax.ShapeDtypeStruct((HOME, B, width), jnp.float32),
             jax.ShapeDtypeStruct((HOME, B, width), SEND),
             jax.ShapeDtypeStruct((HOME, B, width), SEND),
         ),
-        in_specs=[pl.BlockSpec(memory_space=smem)] * 4 + [pl.BlockSpec(memory_space=vmem)] * 6,
+        in_specs=[pl.BlockSpec(memory_space=smem)] * 5 + [pl.BlockSpec(memory_space=vmem)] * 6,
         out_specs=(pl.BlockSpec(memory_space=vmem),) * 3,
         scratch_shapes=[
             pltpu.VMEM((TRASH + 1, B, B), jnp.float32),
@@ -215,6 +232,7 @@
             pltpu.VMEM((hr * hc, B, KP * B), jnp.bfloat16),
         ],
     )(
+        parity,
         pos.astype(jnp.int32),
         near_slot.astype(jnp.int32),
         fine_counts.astype(jnp.int32),
@@ -226,30 +244,30 @@
         left_in,
         right_in,
     )
-    from_left, from_right = exchange(to_right, to_left, "col")
+    got_a, got_b = swap_rounds(first, second, "col")
     band = WIN * OUTW * B
-    minus, plus = pl.pallas_call(
+    first2, second2 = pl.pallas_call(
         fold_cols_send_kernel,
         out_shape=(
             jax.ShapeDtypeStruct((B, band), SEND),
             jax.ShapeDtypeStruct((B, band), SEND),
         ),
-        in_specs=[pl.BlockSpec(memory_space=vmem)] * 3,
+        in_specs=[pl.BlockSpec(memory_space=smem)] + [pl.BlockSpec(memory_space=vmem)] * 3,
         out_specs=(pl.BlockSpec(memory_space=vmem),) * 2,
-    )(keep, from_left, from_right)
+    )(parity, keep, got_a, got_b)
     keep2 = pl.pallas_call(
         fold_cols_keep_kernel,
         out_shape=jax.ShapeDtypeStruct((B, band), jnp.float32),
-        in_specs=[pl.BlockSpec(memory_space=vmem)] * 3,
+        in_specs=[pl.BlockSpec(memory_space=smem)] + [pl.BlockSpec(memory_space=vmem)] * 3,
         out_specs=pl.BlockSpec(memory_space=vmem),
-    )(keep, from_left, from_right)
-    up_in, down_in = exchange(minus, plus, "row")
+    )(parity, keep, got_a, got_b)
+    row_a, row_b = swap_rounds(first2, second2, "row")
     out = pl.pallas_call(
         fold_rows_kernel,
         out_shape=jax.ShapeDtypeStruct((B, OUTW * OUTW * B), jnp.bfloat16),
-        in_specs=[pl.BlockSpec(memory_space=vmem)] * 3,
+        in_specs=[pl.BlockSpec(memory_space=smem)] + [pl.BlockSpec(memory_space=vmem)] * 3,
         out_specs=pl.BlockSpec(memory_space=vmem),
-    )(keep2, up_in, down_in)
+    )(parity, keep2, row_a, row_b)
     return out.reshape(1, 1, B, OUTW * OUTW * B)
 
 

time: 72.1 us -> 69.4 us (0.963)
  other arithmetic: 7.73 us -> 3.87 us
  local copies, waits for them, and re-layouts: 2.42 us -> 3.99 us
    ppermute x4 -> x2, waiting for transfers between devices: 20.3 us -> 6.18 us  [exchange(): got_second = lax.ppermute(jnp.where(even, to_prev, to_next), axis, second)]
    ppermute x0 -> x4, waiting for transfers between devices: none -> 13.8 us  [the longest x2 13.7 us: swap_rounds(): lax.ppermute(second, axis, pairs_b)]
    ppermute x0 -> x4, starting transfers between devices: none -> 6.46 us  [the longest x2 4.99 us: swap_rounds(): lax.ppermute(second, axis, pairs_b)]
    ppermute x4 -> x2, starting transfers between devices: 9.98 us -> 5.32 us  [exchange(): got_second = lax.ppermute(jnp.where(even, to_prev, to_next), axis, second)]
    select_n x4 -> x0, other arithmetic: 4.52 us -> none  [the longest x2 2.49 us: exchange(): got_first = lax.ppermute(jnp.where(even, to_next, to_prev), axis, first)]
    unnamed x10 -> x18, local copies, waits for them, and re-layouts: 0.02 us -> 1.59 us
    ppermute x4 -> x2, starting transfers between devices: 3.25 us -> 1.8 us  [exchange(): got_first = lax.ppermute(jnp.where(even, to_next, to_prev), axis, first)]
    another operation x2 -> x3, other arithmetic: 1.43 us -> 2.1 us
  transfers between devices with their start and end apart: 8 -> 8, of which waited for: 6 -> 5; matrix products, arithmetic and copies ran while one was open for 2% -> 3% of each run, Pallas kernels for 4% -> 4%
where the time goes in v12:
time: 69.4 us; the launch traced here: 68.8 us
  Pallas kernels  24.4 us (35%)
  waiting for transfers between devices  22.8 us (33%)
  starting transfers between devices  13.6 us (20%)
  local copies, waits for them, and re-layouts  3.99 us (6%)
  other arithmetic  3.87 us (6%)
    pallas_call x1, Pallas kernels, per_device(): pl.pallas_call(galerkin_kernel, out_shape=(jax.ShapeDtypeStruct((HOME, B,...  15.9 us
    ppermute x2, waiting for transfers between devices, swap_rounds(): lax.ppermute(second, axis, pairs_b)  13.7 us
    ppermute x2, waiting for transfers between devices, exchange(): got_second = lax.ppermute(jnp.where(even, to_prev, to_next), axis, second)  6.18 us
    ppermute x2, starting transfers between devices, exchange(): got_second = lax.ppermute(jnp.where(even, to_prev, to_next), axis, second)  5.32 us
    ppermute x2, starting transfers between devices, swap_rounds(): lax.ppermute(second, axis, pairs_b)  4.99 us
    pallas_call x1, Pallas kernels, per_device(): pl.pallas_call(fold_cols_send_kernel, out_shape=(jax.ShapeDtypeStruct((B,...  3.24 us
    ppermute x2, waiting for transfers between devices, exchange(): got_first = lax.ppermute(jnp.where(even, to_next, to_prev), axis, first)  2.89 us
    pallas_call x1, Pallas kernels, per_device(): pl.pallas_call(fold_cols_keep_kernel, out_shape=jax.ShapeDtypeStruct((B,...  2.86 us
  transfers between devices with their start and end apart: 8, of which 5 were waited for; matrix products, arithmetic and copies ran while one was open for 3% of the time, Pallas kernels for 4%

profile of v12, /device:TPU:20, one launch (start us, length us, event | category | flops | bytes accessed | tf_op | source)
XLA Modules:
  0.0 68.8 jit_solution(12365255398371703005)
XLA Ops:
  0.0 0.0 copy-start
  0.0 1.4 %fusion.27 = (bf16[4,4,4]{2,1,0:T(4,128)(2,1)S(1)}, s32[4,4,4]{2,1,0:T(4,128)S(1)}, s32[4,4,4]{2,1,0:T(4,128)}) fusion(s32[]{:T(128)S(6)} %axis_index.14, s32[]{:T(128)S(6)} %axis_index.33, s32[4,4,4]{2,1,0:T(4,128)} %param.10, s32[4,4]{1,0:T(4,128)} %param.11), kind=kLoop, calls=%fused_computation.73 | loop fusion | flops 2112 | bytes 968 | tf_op jit(solution)/shard_map/convert.7
  1.4 0.1 convert_element_type.106
  1.5 0.1 convert_element_type.107
  1.6 1.0 %fusion.28 = (bf16[1,4,64,256]{3,2,1,0:T(8,128)(2,1)S(1)}, bf16[1,4,64,256]{3,2,1,0:T(8,128)(2,1)S(1)}) fusion(bf16[4,4,64,256]{3,2,1,0:T(8,128)(2,1)} %param.9), kind=kLoop, calls=%fused_computation.74 | loop fusion | bytes 524288 | tf_op jit(solution)/shard_map/slice | solution.py:192
  2.6 0.1 broadcast_select_fusion.7
  2.7 3.3 %collective-permute-start = (bf16[272,256]{1,0:T(8,128)(2,1)S(1)}, bf16[272,256]{1,0:T(8,128)(2,1)S(1)}, u32[]{:S(2)}, u32[]{:S(2)}) collective-permute-start(bf16[272,256]{1,0:T(8,128)(2,1)S(1)} %get-tuple-element.29), channel_id=1, source_target_pairs={{4,8},{12,16},{20,24},{8,4},{16,12},{24,20},{5,9},{13,17},{21,25},... | collective-permute-start | bytes 417800 | tf_op jit(solution)/shard_map/ppermute | solution.py:39
  5.9 1.7 %collective-permute-start.1 = (bf16[272,256]{1,0:T(8,128)(2,1)S(1)}, bf16[272,256]{1,0:T(8,128)(2,1)S(1)}, u32[]{:S(2)}, u32[]{:S(2)}) collective-permute-start(bf16[272,256]{1,0:T(8,128)(2,1)S(1)} %get-tuple-element.30), channel_id=1, source_target_pairs={{0,4},{4,0},{8,12},{12,8},{16,20},{20,16},{24,28},{28,24},{1,5},{5... | collective-permute-start | bytes 417800 | tf_op jit(solution)/shard_map/ppermute | solution.py:38
  7.7 1.3 %add_clamp_fusion.pos_ref = s32[4,4,9]{2,1,0:T(4,128)} fusion(s32[4,4,9]{2,1,0:T(4,128)} %param.7, s32[]{:T(128)S(6)} %mul.33, s32[]{:T(128)S(6)} %mul.30), kind=kLoop, calls=%fused_computation.49 | loop fusion | flops 3744 | bytes 1160 | tf_op jit(solution)/shard_map/jit(clip)/min | solution.py:212
  9.0 0.7 pad_add_fusion.par_ref
  9.7 1.3 %collective-permute-done = bf16[272,256]{1,0:T(8,128)(2,1)S(1)} collective-permute-done((bf16[272,256]{1,0:T(8,128)(2,1)S(1)}, bf16[272,256]{1,0:T(8,128)(2,1)S(1)}, u32[]{:S(2)}, u32[]{:S(2)}) %collective-permute-start) | collective-permute-done | bytes 139296 | tf_op jit(solution)/shard_map/ppermute | solution.py:39
  11.0 2.9 %collective-permute-done.1 = bf16[272,256]{1,0:T(8,128)(2,1)S(1)} collective-permute-done((bf16[272,256]{1,0:T(8,128)(2,1)S(1)}, bf16[272,256]{1,0:T(8,128)(2,1)S(1)}, u32[]{:S(2)}, u32[]{:S(2)}) %collective-permute-start.1) | collective-permute-done | bytes 139296 | tf_op jit(solution)/shard_map/ppermute | solution.py:38
  13.9 0.0 copy-start.3
  13.9 0.0 copy-start.4
  14.0 0.1 reshape.196
  14.0 0.1 reshape.197
  14.2 0.1 convert_element_type.112
  14.3 0.1 convert_element_type.113
  14.3 0.0 copy-done
  14.4 0.1 pad_maximum_fusion.2
  14.4 0.1 broadcast_select_fusion.3
  14.5 2.0 %collective-permute-start.2 = (bf16[400,256]{1,0:T(8,128)(2,1)S(1)}, bf16[400,256]{1,0:T(8,128)(2,1)S(1)}, u32[]{:S(2)}, u32[]{:S(2)}) collective-permute-start(bf16[400,256]{1,0:T(8,128)(2,1)S(1)} %get-tuple-element.25), channel_id=1, source_target_pairs={{1,2},{2,1},{5,6},{6,5},{9,10},{10,9},{13,14},{14,13},{17,18},{18,... | collective-permute-start | bytes 614408 | tf_op jit(solution)/shard_map/ppermute | solution.py:39
  16.5 0.1 collective-permute-start.3
  16.6 0.1 add_add_fusion.1
  16.7 4.9 %collective-permute-done.2 = bf16[400,256]{1,0:T(8,128)(2,1)S(1)} collective-permute-done((bf16[400,256]{1,0:T(8,128)(2,1)S(1)}, bf16[400,256]{1,0:T(8,128)(2,1)S(1)}, u32[]{:S(2)}, u32[]{:S(2)}) %collective-permute-start.2) | collective-permute-done | bytes 204832 | tf_op jit(solution)/shard_map/ppermute | solution.py:39
  21.6 0.0 collective-permute-done.3
  21.6 0.0 copy-done.3
  21.6 0.0 copy-done.4
  21.6 0.0 copy-start.5
  21.6 0.0 copy-start.6
  21.7 0.1 reshape.200
  21.8 0.1 reshape.201
  21.9 0.1 fusion.8
  21.9 0.7 min.34.nslot_ref
  22.6 0.0 copy-done.5
  22.6 0.0 copy-done.6
  22.6 15.9 %shard_map.64 = (f32[3,64,1600]{2,1,0:T(8,128)}, bf16[3,64,1600]{2,1,0:T(8,128)(2,1)}, bf16[3,64,1600]{2,1,0:T(8,128)(2,1)}) custom-call(s32[2]{0:T(128)} %pad_add_fusion.par_ref, s32[4,4,9]{2,1,0:T(4,128)} %add_clamp_fusion.pos_ref, s32[144]{0:T(256)} %min.34.nslot_ref, s32[4,4]{1,0:T(4,128)} %count_ref.1, s32[4,4,4]{2,1,0:T(4,128)} %get-tuple-element.31.home_ref, ...), custom_call_target="tpu_custom_call" | custom-call | tf_op jit(solution)/shard_map/pallas_call | solution.py:219
  38.5 0.0 collective-permute-start.4
  38.5 2.3 %collective-permute-start.5 = (bf16[3,64,1600]{2,1,0:T(8,128)(2,1)}, bf16[3,64,1600]{2,1,0:T(8,128)(2,1)S(1)}, u32[]{:S(2)}, u32[]{:S(2)}) collective-permute-start(bf16[3,64,1600]{2,1,0:T(8,128)(2,1)} %get-tuple-element.12), channel_id=1, source_target_pairs={{1,2},{2,1},{5,6},{6,5},{9,10},{10,9},{13,14},{14,13},{17,18},{18,... | collective-permute-start | bytes 1843208 | tf_op jit(solution)/shard_map/ppermute | solution.py:49
  40.8 0.0 collective-permute-done.4.a_ref
  40.8 0.0 copy-start.1
  40.8 9.6 %collective-permute-done.5.b_ref = bf16[3,64,1600]{2,1,0:T(8,128)(2,1)S(1)} collective-permute-done((bf16[3,64,1600]{2,1,0:T(8,128)(2,1)}, bf16[3,64,1600]{2,1,0:T(8,128)(2,1)S(1)}, u32[]{:S(2)}, u32[]{:S(2)}) %collective-permute-start.5) | collective-permute-done | bytes 614432 | tf_op jit(solution)/shard_map/ppermute | solution.py:49
  50.4 0.0 copy-start.2
  50.4 0.0 copy-done.1
  50.4 0.9 %copy-done.2 = bf16[3,64,1600]{2,1,0:T(8,128)(2,1)} copy-done((bf16[3,64,1600]{2,1,0:T(8,128)(2,1)}, bf16[3,64,1600]{2,1,0:T(8,128)(2,1)S(1)}, u32[]{:S(2)}) %copy-start.2) | copy-done | bytes 614424
  51.3 3.2 %shard_map.66 = (bf16[64,2240]{1,0:T(8,128)(2,1)}, bf16[64,2240]{1,0:T(8,128)(2,1)}) custom-call(s32[2]{0:T(128)} %pad_add_fusion.par_ref, f32[3,64,1600]{2,1,0:T(8,128)} %get-tuple-element.10.keep_ref, bf16[3,64,1600]{2,1,0:T(8,128)(2,1)} %copy-done.1, bf16[3,64,1600]{2,1,0:T(8,128)(2,1)} %copy-done.2), custom_call_target="tpu_custom_call" | custom-call | tf_op jit(solution)/shard_map/pallas_call | solution.py:249
  54.5 1.5 %collective-permute-start.6 = (bf16[64,2240]{1,0:T(8,128)(2,1)}, bf16[64,2240]{1,0:T(8,128)(2,1)S(1)}, u32[]{:S(2)}, u32[]{:S(2)}) collective-permute-start(bf16[64,2240]{1,0:T(8,128)(2,1)} %get-tuple-element.13), channel_id=1, source_target_pairs={{0,4},{4,0},{8,12},{12,8},{16,20},{20,16},{24,28},{28,24},{1,5},{5... | collective-permute-start | bytes 860168 | tf_op jit(solution)/shard_map/ppermute | solution.py:49
  56.0 2.7 %collective-permute-start.7 = (bf16[64,2240]{1,0:T(8,128)(2,1)}, bf16[64,2240]{1,0:T(8,128)(2,1)S(1)}, u32[]{:S(2)}, u32[]{:S(2)}) collective-permute-start(bf16[64,2240]{1,0:T(8,128)(2,1)} %get-tuple-element.14), channel_id=1, source_target_pairs={{4,8},{12,16},{20,24},{8,4},{16,12},{24,20},{5,9},{13,17},{21,25},... | collective-permute-start | bytes 860168 | tf_op jit(solution)/shard_map/ppermute | solution.py:49
  58.7 2.9 %shard_map.65.keep_ref = f32[64,2240]{1,0:T(8,128)} custom-call(s32[2]{0:T(128)} %pad_add_fusion.par_ref, f32[3,64,1600]{2,1,0:T(8,128)} %get-tuple-element.10.keep_ref, bf16[3,64,1600]{2,1,0:T(8,128)(2,1)} %copy-done.1, bf16[3,64,1600]{2,1,0:T(8,128)(2,1)} %copy-done.2), custom_call_target="tpu_custom_call" | custom-call | tf_op jit(solution)/shard_map/pallas_call | solution.py:258
  61.5 0.0 collective-permute-done.6.a_ref
  61.5 0.0 copy-start.7
  61.5 4.1 %collective-permute-done.7.b_ref = bf16[64,2240]{1,0:T(8,128)(2,1)S(1)} collective-permute-done((bf16[64,2240]{1,0:T(8,128)(2,1)}, bf16[64,2240]{1,0:T(8,128)(2,1)S(1)}, u32[]{:S(2)}, u32[]{:S(2)}) %collective-permute-start.7) | collective-permute-done | bytes 286752 | tf_op jit(solution)/shard_map/ppermute | solution.py:49
  65.7 0.0 copy-done.7
  65.7 0.0 copy-start.8
  65.7 0.7 %copy-done.8 = bf16[64,2240]{1,0:T(8,128)(2,1)} copy-done((bf16[64,2240]{1,0:T(8,128)(2,1)}, bf16[64,2240]{1,0:T(8,128)(2,1)S(1)}, u32[]{:S(2)}) %copy-start.8) | copy-done | bytes 286744
  66.4 2.4 %shard_map.67 = bf16[64,3136]{1,0:T(8,128)(2,1)} custom-call(s32[2]{0:T(128)} %pad_add_fusion.par_ref, f32[64,2240]{1,0:T(8,128)} %shard_map.65.keep_ref, bf16[64,2240]{1,0:T(8,128)(2,1)} %copy-done.7, bf16[64,2240]{1,0:T(8,128)(2,1)} %copy-done.8), custom_call_target="tpu_custom_call" | custom-call | tf_op jit(solution)/shard_map/pallas_call | solution.py:265
  (11 shorter events, 0.2 us)
Async XLA Ops:
  0.0 14.3 %copy-start = (bf16[4,4,64,256]{3,2,1,0:T(8,128)(2,1)S(1)}, bf16[4,4,64,256]{3,2,1,0:T(8,128)(2,1)}, u32[]{:S(2)}) copy-start(bf16[4,4,64,256]{3,2,1,0:T(8,128)(2,1)} %param.9) | copy-start | bytes 1572868
  2.7 8.3 %collective-permute-start = (bf16[272,256]{1,0:T(8,128)(2,1)S(1)}, bf16[272,256]{1,0:T(8,128)(2,1)S(1)}, u32[]{:S(2)}, u32[]{:S(2)}) collective-permute-start(bf16[272,256]{1,0:T(8,128)(2,1)S(1)} %get-tuple-element.29), channel_id=1, source_target_pairs={{4,8},{12,16},{20,24},{8,4},{16,12},{24,20},{5,9},{13,17},{21,25},... | collective-permute-start | bytes 417800 | tf_op jit(solution)/shard_map/ppermute | solution.py:39
  5.9 7.9 %collective-permute-start.1 = (bf16[272,256]{1,0:T(8,128)(2,1)S(1)}, bf16[272,256]{1,0:T(8,128)(2,1)S(1)}, u32[]{:S(2)}, u32[]{:S(2)}) collective-permute-start(bf16[272,256]{1,0:T(8,128)(2,1)S(1)} %get-tuple-element.30), channel_id=1, source_target_pairs={{0,4},{4,0},{8,12},{12,8},{16,20},{20,16},{24,28},{28,24},{1,5},{5... | collective-permute-start | bytes 417800 | tf_op jit(solution)/shard_map/ppermute | solution.py:38
  13.9 7.7 %copy-start.3 = (bf16[272,256]{1,0:T(8,128)(2,1)}, bf16[272,256]{1,0:T(8,128)(2,1)S(1)}, u32[]{:S(2)}) copy-start(bf16[272,256]{1,0:T(8,128)(2,1)S(1)} %get-tuple-element.27.above_ref) | copy-start | bytes 417796
  13.9 7.7 %copy-start.4 = (bf16[272,256]{1,0:T(8,128)(2,1)}, bf16[272,256]{1,0:T(8,128)(2,1)S(1)}, u32[]{:S(2)}) copy-start(bf16[272,256]{1,0:T(8,128)(2,1)S(1)} %get-tuple-element.28.below_ref) | copy-start | bytes 417796
  14.5 7.1 %collective-permute-start.2 = (bf16[400,256]{1,0:T(8,128)(2,1)S(1)}, bf16[400,256]{1,0:T(8,128)(2,1)S(1)}, u32[]{:S(2)}, u32[]{:S(2)}) collective-permute-start(bf16[400,256]{1,0:T(8,128)(2,1)S(1)} %get-tuple-element.25), channel_id=1, source_target_pairs={{1,2},{2,1},{5,6},{6,5},{9,10},{10,9},{13,14},{14,13},{17,18},{18,... | collective-permute-start | bytes 614408 | tf_op jit(solution)/shard_map/ppermute | solution.py:39
  16.5 5.0 %collective-permute-start.3 = (bf16[400,256]{1,0:T(8,128)(2,1)S(1)}, bf16[400,256]{1,0:T(8,128)(2,1)S(1)}, u32[]{:S(2)}, u32[]{:S(2)}) collective-permute-start(bf16[400,256]{1,0:T(8,128)(2,1)S(1)} %get-tuple-element.26), channel_id=1, source_target_pairs={{0,1},{1,0},{2,3},{3,2},{4,5},{5,4},{6,7},{7,6},{8,9},{9,8},{10,11... | collective-permute-start | bytes 614408 | tf_op jit(solution)/shard_map/ppermute | solution.py:38
  21.6 1.0 %copy-start.5 = (bf16[400,256]{1,0:T(8,128)(2,1)}, bf16[400,256]{1,0:T(8,128)(2,1)S(1)}, u32[]{:S(2)}) copy-start(bf16[400,256]{1,0:T(8,128)(2,1)S(1)} %get-tuple-element.23.left_ref) | copy-start | bytes 614404
  21.6 1.0 %copy-start.6 = (bf16[400,256]{1,0:T(8,128)(2,1)}, bf16[400,256]{1,0:T(8,128)(2,1)S(1)}, u32[]{:S(2)}) copy-start(bf16[400,256]{1,0:T(8,128)(2,1)S(1)} %get-tuple-element.24.right_ref) | copy-start | bytes 614404
  38.5 2.3 %collective-permute-start.4 = (bf16[3,64,1600]{2,1,0:T(8,128)(2,1)}, bf16[3,64,1600]{2,1,0:T(8,128)(2,1)S(1)}, u32[]{:S(2)}, u32[]{:S(2)}) collective-permute-start(bf16[3,64,1600]{2,1,0:T(8,128)(2,1)} %get-tuple-element.11), channel_id=1, source_target_pairs={{0,1},{1,0},{2,3},{3,2},{4,5},{5,4},{6,7},{7,6},{8,9},{9,8},{10,11... | collective-permute-start | bytes 1843208 | tf_op jit(solution)/shard_map/ppermute | solution.py:49
  38.5 11.9 %collective-permute-start.5 = (bf16[3,64,1600]{2,1,0:T(8,128)(2,1)}, bf16[3,64,1600]{2,1,0:T(8,128)(2,1)S(1)}, u32[]{:S(2)}, u32[]{:S(2)}) collective-permute-start(bf16[3,64,1600]{2,1,0:T(8,128)(2,1)} %get-tuple-element.12), channel_id=1, source_target_pairs={{1,2},{2,1},{5,6},{6,5},{9,10},{10,9},{13,14},{14,13},{17,18},{18,... | collective-permute-start | bytes 1843208 | tf_op jit(solution)/shard_map/ppermute | solution.py:49
  40.8 9.6 %copy-start.1 = (bf16[3,64,1600]{2,1,0:T(8,128)(2,1)}, bf16[3,64,1600]{2,1,0:T(8,128)(2,1)S(1)}, u32[]{:S(2)}) copy-start(bf16[3,64,1600]{2,1,0:T(8,128)(2,1)S(1)} %collective-permute-done.4.a_ref) | copy-start | bytes 1843204
  50.4 0.9 %copy-start.2 = (bf16[3,64,1600]{2,1,0:T(8,128)(2,1)}, bf16[3,64,1600]{2,1,0:T(8,128)(2,1)S(1)}, u32[]{:S(2)}) copy-start(bf16[3,64,1600]{2,1,0:T(8,128)(2,1)S(1)} %collective-permute-done.5.b_ref) | copy-start | bytes 1843204
  54.5 7.0 %collective-permute-start.6 = (bf16[64,2240]{1,0:T(8,128)(2,1)}, bf16[64,2240]{1,0:T(8,128)(2,1)S(1)}, u32[]{:S(2)}, u32[]{:S(2)}) collective-permute-start(bf16[64,2240]{1,0:T(8,128)(2,1)} %get-tuple-element.13), channel_id=1, source_target_pairs={{0,4},{4,0},{8,12},{12,8},{16,20},{20,16},{24,28},{28,24},{1,5},{5... | collective-permute-start | bytes 860168 | tf_op jit(solution)/shard_map/ppermute | solution.py:49
  56.0 9.7 %collective-permute-start.7 = (bf16[64,2240]{1,0:T(8,128)(2,1)}, bf16[64,2240]{1,0:T(8,128)(2,1)S(1)}, u32[]{:S(2)}, u32[]{:S(2)}) collective-permute-start(bf16[64,2240]{1,0:T(8,128)(2,1)} %get-tuple-element.14), channel_id=1, source_target_pairs={{4,8},{12,16},{20,24},{8,4},{16,12},{24,20},{5,9},{13,17},{21,25},... | collective-permute-start | bytes 860168 | tf_op jit(solution)/shard_map/ppermute | solution.py:49
  61.5 4.2 %copy-start.7 = (bf16[64,2240]{1,0:T(8,128)(2,1)}, bf16[64,2240]{1,0:T(8,128)(2,1)S(1)}, u32[]{:S(2)}) copy-start(bf16[64,2240]{1,0:T(8,128)(2,1)S(1)} %collective-permute-done.6.a_ref) | copy-start | bytes 860164
  65.7 0.7 %copy-start.8 = (bf16[64,2240]{1,0:T(8,128)(2,1)}, bf16[64,2240]{1,0:T(8,128)(2,1)S(1)}, u32[]{:S(2)}) copy-start(bf16[64,2240]{1,0:T(8,128)(2,1)S(1)} %collective-permute-done.7.b_ref) | copy-start | bytes 860164

commit v13 on v12

--- a/solution.py
+++ b/solution.py
@@ -101,11 +101,11 @@
         out[...] = terms.reshape(out.shape).astype(out.dtype)
 
 
-def fold_cols_band(keep_ref, a_ref, b_ref, even, d, out):
+def fold_cols_band(keep_ref, a_ref, b_ref, even, d, out, shift=0):
     src_w = WIN * B
     dst_w = OUTW * B
     for sx in range(WIN):
-        lo = sx * dst_w
+        lo = (sx + shift) * dst_w
         s0 = sx * src_w
         own = keep_ref[d, :, s0:s0 + src_w]
         got_a = a_ref[d, :, s0:s0 + src_w].astype(jnp.float32)
@@ -132,26 +132,24 @@
 
 
 def fold_cols_keep_kernel(par_ref, keep_ref, a_ref, b_ref, keep_out):
-    fold_cols_band(keep_ref, a_ref, b_ref, par_ref[0] == 0, 1, keep_out)
+    band = OUTW * B
+    keep_out[:, :band] = jnp.zeros((B, band), keep_out.dtype)
+    keep_out[:, (OUTW - 1) * band:] = jnp.zeros((B, band), keep_out.dtype)
+    fold_cols_band(keep_ref, a_ref, b_ref, par_ref[0] == 0, 1, keep_out, shift=1)
 
 
 def fold_rows_kernel(par_ref, keep_ref, a_ref, b_ref, out_ref):
     band = OUTW * B
     even = par_ref[1] == 0
-    for s in range(OUTW):
-        parts = []
-        if 1 <= s <= WIN:
-            parts.append(keep_ref[:, (s - 1) * band:s * band])
-        if s <= WIN - 1:
-            lanes = slice(s * band, (s + 1) * band)
-            parts.append(jnp.where(even, b_ref[:, lanes], a_ref[:, lanes]).astype(jnp.float32))
-        if s >= 2:
-            lanes = slice((s - 2) * band, (s - 1) * band)
-            parts.append(jnp.where(even, a_ref[:, lanes], b_ref[:, lanes]).astype(jnp.float32))
-        total = parts[0]
-        for extra in parts[1:]:
-            total = total + extra
-        out_ref[:, s * band:(s + 1) * band] = total.astype(out_ref.dtype)
+    low = 2 * band
+    high = WIN * band
+    from_prev_lo = jnp.where(even, b_ref[:, :low], a_ref[:, :low]).astype(jnp.float32)
+    out_ref[:, :low] = (keep_ref[:, :low] + from_prev_lo).astype(out_ref.dtype)
+    from_prev_mid = jnp.where(even, b_ref[:, low:high], a_ref[:, low:high]).astype(jnp.float32)
+    from_next_mid = jnp.where(even, a_ref[:, :high - low], b_ref[:, :high - low]).astype(jnp.float32)
+    out_ref[:, low:high] = (keep_ref[:, low:high] + from_prev_mid + from_next_mid).astype(out_ref.dtype)
+    from_next_hi = jnp.where(even, a_ref[:, high - low:], b_ref[:, high - low:]).astype(jnp.float32)
+    out_ref[:, high:] = (keep_ref[:, high:] + from_next_hi).astype(out_ref.dtype)
 
 
 def per_device(
@@ -257,7 +255,7 @@
     )(parity, keep, got_a, got_b)
     keep2 = pl.pallas_call(
         fold_cols_keep_kernel,
-        out_shape=jax.ShapeDtypeStruct((B, band), jnp.float32),
+        out_shape=jax.ShapeDtypeStruct((B, OUTW * OUTW * B), jnp.float32),
         in_specs=[pl.BlockSpec(memory_space=smem)] + [pl.BlockSpec(memory_space=vmem)] * 3,
         out_specs=pl.BlockSpec(memory_space=vmem),
     )(parity, keep, got_a, got_b)

time: 69.4 us -> 69.3 us (level)
  starting transfers between devices: 13.6 us -> 12.7 us
  waiting for transfers between devices: 22.8 us -> 23.7 us
    ppermute x2, starting transfers between devices: 4.99 us -> 4.02 us  [swap_rounds(): lax.ppermute(second, axis, pairs_b)]
  transfers between devices with their start and end apart: 8 -> 8, of which waited for: 5 -> 7; matrix products, arithmetic and copies ran while one was open for 3% -> 3% of each run, Pallas kernels for 4% -> 4%
where the time goes in v13:
time: 69.3 us; the launch traced here: 68.9 us
  Pallas kernels  24.6 us (35%)
  waiting for transfers between devices  23.7 us (34%)
  starting transfers between devices  12.7 us (18%)
  local copies, waits for them, and re-layouts  3.97 us (6%)
  other arithmetic  3.76 us (5%)
    pallas_call x1, Pallas kernels, per_device(): pl.pallas_call(galerkin_kernel, out_shape=(jax.ShapeDtypeStruct((HOME, B,...  16.1 us
    ppermute x2, waiting for transfers between devices, swap_rounds(): lax.ppermute(second, axis, pairs_b)  14 us
    ppermute x2, waiting for transfers between devices, exchange(): got_second = lax.ppermute(jnp.where(even, to_prev, to_next), axis, second)  6.29 us
    ppermute x2, starting transfers between devices, exchange(): got_second = lax.ppermute(jnp.where(even, to_prev, to_next), axis, second)  5.32 us
    ppermute x2, starting transfers between devices, swap_rounds(): lax.ppermute(second, axis, pairs_b)  4.02 us
    pallas_call x1, Pallas kernels, per_device(): pl.pallas_call(fold_cols_send_kernel, out_shape=(jax.ShapeDtypeStruct((B,...  3.25 us
    pallas_call x1, Pallas kernels, per_device(): pl.pallas_call(fold_cols_keep_kernel, out_shape=jax.ShapeDtypeStruct((B,...  3.1 us
    ppermute x2, waiting for transfers between devices, exchange(): got_first = lax.ppermute(jnp.where(even, to_next, to_prev), axis, first)  2.89 us
  transfers between devices with their start and end apart: 8, of which 7 were waited for; matrix products, arithmetic and copies ran while one was open for 3% of the time, Pallas kernels for 4%

profile of v13, /device:TPU:20, one launch (start us, length us, event | category | flops | bytes accessed | tf_op | source)
XLA Modules:
  0.0 68.9 jit_solution(12773471648882222630)
XLA Ops:
  0.0 0.0 copy-start
  0.0 1.4 %fusion.27 = (bf16[4,4,4]{2,1,0:T(4,128)(2,1)S(1)}, s32[4,4,4]{2,1,0:T(4,128)S(1)}, s32[4,4,4]{2,1,0:T(4,128)}) fusion(s32[]{:T(128)S(6)} %axis_index.14, s32[]{:T(128)S(6)} %axis_index.33, s32[4,4,4]{2,1,0:T(4,128)} %param.10, s32[4,4]{1,0:T(4,128)} %param.11), kind=kLoop, calls=%fused_computation.73 | loop fusion | flops 2112 | bytes 968 | tf_op jit(solution)/shard_map/convert.7
  1.4 0.1 convert_element_type.106
  1.5 0.1 convert_element_type.107
  1.6 1.0 %fusion.28 = (bf16[1,4,64,256]{3,2,1,0:T(8,128)(2,1)S(1)}, bf16[1,4,64,256]{3,2,1,0:T(8,128)(2,1)S(1)}) fusion(bf16[4,4,64,256]{3,2,1,0:T(8,128)(2,1)} %param.9), kind=kLoop, calls=%fused_computation.74 | loop fusion | bytes 524288 | tf_op jit(solution)/shard_map/slice | solution.py:190
  2.6 0.1 broadcast_select_fusion.7
  2.7 3.3 %collective-permute-start = (bf16[272,256]{1,0:T(8,128)(2,1)S(1)}, bf16[272,256]{1,0:T(8,128)(2,1)S(1)}, u32[]{:S(2)}, u32[]{:S(2)}) collective-permute-start(bf16[272,256]{1,0:T(8,128)(2,1)S(1)} %get-tuple-element.29), channel_id=1, source_target_pairs={{4,8},{12,16},{20,24},{8,4},{16,12},{24,20},{5,9},{13,17},{21,25},... | collective-permute-start | bytes 417800 | tf_op jit(solution)/shard_map/ppermute | solution.py:39
  5.9 1.7 %collective-permute-start.1 = (bf16[272,256]{1,0:T(8,128)(2,1)S(1)}, bf16[272,256]{1,0:T(8,128)(2,1)S(1)}, u32[]{:S(2)}, u32[]{:S(2)}) collective-permute-start(bf16[272,256]{1,0:T(8,128)(2,1)S(1)} %get-tuple-element.30), channel_id=1, source_target_pairs={{0,4},{4,0},{8,12},{12,8},{16,20},{20,16},{24,28},{28,24},{1,5},{5... | collective-permute-start | bytes 417800 | tf_op jit(solution)/shard_map/ppermute | solution.py:38
  7.7 1.3 %add_clamp_fusion.pos_ref = s32[4,4,9]{2,1,0:T(4,128)} fusion(s32[4,4,9]{2,1,0:T(4,128)} %param.7, s32[]{:T(128)S(6)} %mul.33, s32[]{:T(128)S(6)} %mul.30), kind=kLoop, calls=%fused_computation.49 | loop fusion | flops 3744 | bytes 1160 | tf_op jit(solution)/shard_map/jit(clip)/min | solution.py:210
  9.0 0.6 pad_add_fusion.par_ref
  9.5 1.4 %collective-permute-done = bf16[272,256]{1,0:T(8,128)(2,1)S(1)} collective-permute-done((bf16[272,256]{1,0:T(8,128)(2,1)S(1)}, bf16[272,256]{1,0:T(8,128)(2,1)S(1)}, u32[]{:S(2)}, u32[]{:S(2)}) %collective-permute-start) | collective-permute-done | bytes 139296 | tf_op jit(solution)/shard_map/ppermute | solution.py:39
  11.0 2.9 %collective-permute-done.1 = bf16[272,256]{1,0:T(8,128)(2,1)S(1)} collective-permute-done((bf16[272,256]{1,0:T(8,128)(2,1)S(1)}, bf16[272,256]{1,0:T(8,128)(2,1)S(1)}, u32[]{:S(2)}, u32[]{:S(2)}) %collective-permute-start.1) | collective-permute-done | bytes 139296 | tf_op jit(solution)/shard_map/ppermute | solution.py:38
  13.9 0.0 copy-start.3
  13.9 0.0 copy-start.4
  14.0 0.1 reshape.196
  14.0 0.1 reshape.197
  14.2 0.1 convert_element_type.112
  14.3 0.1 convert_element_type.113
  14.3 0.0 copy-done
  14.4 0.1 pad_maximum_fusion.2
  14.4 0.1 broadcast_select_fusion.3
  14.5 2.0 %collective-permute-start.2 = (bf16[400,256]{1,0:T(8,128)(2,1)S(1)}, bf16[400,256]{1,0:T(8,128)(2,1)S(1)}, u32[]{:S(2)}, u32[]{:S(2)}) collective-permute-start(bf16[400,256]{1,0:T(8,128)(2,1)S(1)} %get-tuple-element.25), channel_id=1, source_target_pairs={{1,2},{2,1},{5,6},{6,5},{9,10},{10,9},{13,14},{14,13},{17,18},{18,... | collective-permute-start | bytes 614408 | tf_op jit(solution)/shard_map/ppermute | solution.py:39
  16.5 0.1 collective-permute-start.3
  16.6 0.1 add_add_fusion.1
  16.7 4.9 %collective-permute-done.2 = bf16[400,256]{1,0:T(8,128)(2,1)S(1)} collective-permute-done((bf16[400,256]{1,0:T(8,128)(2,1)S(1)}, bf16[400,256]{1,0:T(8,128)(2,1)S(1)}, u32[]{:S(2)}, u32[]{:S(2)}) %collective-permute-start.2) | collective-permute-done | bytes 204832 | tf_op jit(solution)/shard_map/ppermute | solution.py:39
  21.6 0.0 collective-permute-done.3
  21.6 0.0 copy-done.3
  21.6 0.0 copy-done.4
  21.6 0.0 copy-start.5
  21.6 0.0 copy-start.6
  21.7 0.1 reshape.200
  21.8 0.1 reshape.201
  21.9 0.1 fusion.8
  21.9 0.7 min.34.nslot_ref
  22.6 0.0 copy-done.5
  22.6 0.0 copy-done.6
  22.6 16.1 %shard_map.64 = (f32[3,64,1600]{2,1,0:T(8,128)}, bf16[3,64,1600]{2,1,0:T(8,128)(2,1)}, bf16[3,64,1600]{2,1,0:T(8,128)(2,1)}) custom-call(s32[2]{0:T(128)} %pad_add_fusion.par_ref, s32[4,4,9]{2,1,0:T(4,128)} %add_clamp_fusion.pos_ref, s32[144]{0:T(256)} %min.34.nslot_ref, s32[4,4]{1,0:T(4,128)} %count_ref.1, s32[4,4,4]{2,1,0:T(4,128)} %get-tuple-element.31.home_ref, ...), custom_call_target="tpu_custom_call" | custom-call | tf_op jit(solution)/shard_map/pallas_call | solution.py:217
  38.7 0.0 collective-permute-start.4
  38.7 2.0 %collective-permute-start.5 = (bf16[3,64,1600]{2,1,0:T(8,128)(2,1)}, bf16[3,64,1600]{2,1,0:T(8,128)(2,1)S(1)}, u32[]{:S(2)}, u32[]{:S(2)}) collective-permute-start(bf16[3,64,1600]{2,1,0:T(8,128)(2,1)} %get-tuple-element.12), channel_id=1, source_target_pairs={{1,2},{2,1},{5,6},{6,5},{9,10},{10,9},{13,14},{14,13},{17,18},{18,... | collective-permute-start | bytes 1843208 | tf_op jit(solution)/shard_map/ppermute | solution.py:49
  40.8 0.2 collective-permute-done.4.a_ref
  41.0 0.0 copy-start.1
  41.0 9.6 %collective-permute-done.5.b_ref = bf16[3,64,1600]{2,1,0:T(8,128)(2,1)S(1)} collective-permute-done((bf16[3,64,1600]{2,1,0:T(8,128)(2,1)}, bf16[3,64,1600]{2,1,0:T(8,128)(2,1)S(1)}, u32[]{:S(2)}, u32[]{:S(2)}) %collective-permute-start.5) | collective-permute-done | bytes 614432 | tf_op jit(solution)/shard_map/ppermute | solution.py:49
  50.7 0.0 copy-start.2
  50.7 0.0 copy-done.1
  50.7 0.8 %copy-done.2 = bf16[3,64,1600]{2,1,0:T(8,128)(2,1)} copy-done((bf16[3,64,1600]{2,1,0:T(8,128)(2,1)}, bf16[3,64,1600]{2,1,0:T(8,128)(2,1)S(1)}, u32[]{:S(2)}) %copy-start.2) | copy-done | bytes 614424
  51.5 3.3 %shard_map.66 = (bf16[64,2240]{1,0:T(8,128)(2,1)}, bf16[64,2240]{1,0:T(8,128)(2,1)}) custom-call(s32[2]{0:T(128)} %pad_add_fusion.par_ref, f32[3,64,1600]{2,1,0:T(8,128)} %get-tuple-element.10.keep_ref, bf16[3,64,1600]{2,1,0:T(8,128)(2,1)} %copy-done.1, bf16[3,64,1600]{2,1,0:T(8,128)(2,1)} %copy-done.2), custom_call_target="tpu_custom_call" | custom-call | tf_op jit(solution)/shard_map/pallas_call | solution.py:247
  54.7 1.6 %collective-permute-start.6 = (bf16[64,2240]{1,0:T(8,128)(2,1)}, bf16[64,2240]{1,0:T(8,128)(2,1)S(1)}, u32[]{:S(2)}, u32[]{:S(2)}) collective-permute-start(bf16[64,2240]{1,0:T(8,128)(2,1)} %get-tuple-element.13), channel_id=1, source_target_pairs={{0,4},{4,0},{8,12},{12,8},{16,20},{20,16},{24,28},{28,24},{1,5},{5... | collective-permute-start | bytes 860168 | tf_op jit(solution)/shard_map/ppermute | solution.py:49
  56.3 2.0 %collective-permute-start.7 = (bf16[64,2240]{1,0:T(8,128)(2,1)}, bf16[64,2240]{1,0:T(8,128)(2,1)S(1)}, u32[]{:S(2)}, u32[]{:S(2)}) collective-permute-start(bf16[64,2240]{1,0:T(8,128)(2,1)} %get-tuple-element.14), channel_id=1, source_target_pairs={{4,8},{12,16},{20,24},{8,4},{16,12},{24,20},{5,9},{13,17},{21,25},... | collective-permute-start | bytes 860168 | tf_op jit(solution)/shard_map/ppermute | solution.py:49
  58.3 3.1 %shard_map.65.keep_ref = f32[64,3136]{1,0:T(8,128)} custom-call(s32[2]{0:T(128)} %pad_add_fusion.par_ref, f32[3,64,1600]{2,1,0:T(8,128)} %get-tuple-element.10.keep_ref, bf16[3,64,1600]{2,1,0:T(8,128)(2,1)} %copy-done.1, bf16[3,64,1600]{2,1,0:T(8,128)(2,1)} %copy-done.2), custom_call_target="tpu_custom_call" | custom-call | tf_op jit(solution)/shard_map/pallas_call | solution.py:256
  61.4 0.2 collective-permute-done.6.a_ref
  61.7 0.0 copy-start.7
  61.7 4.4 %collective-permute-done.7.b_ref = bf16[64,2240]{1,0:T(8,128)(2,1)S(1)} collective-permute-done((bf16[64,2240]{1,0:T(8,128)(2,1)}, bf16[64,2240]{1,0:T(8,128)(2,1)S(1)}, u32[]{:S(2)}, u32[]{:S(2)}) %collective-permute-start.7) | collective-permute-done | bytes 286752 | tf_op jit(solution)/shard_map/ppermute | solution.py:49
  66.1 0.0 copy-done.7
  66.1 0.0 copy-start.8
  66.1 0.7 %copy-done.8 = bf16[64,2240]{1,0:T(8,128)(2,1)} copy-done((bf16[64,2240]{1,0:T(8,128)(2,1)}, bf16[64,2240]{1,0:T(8,128)(2,1)S(1)}, u32[]{:S(2)}) %copy-start.8) | copy-done | bytes 286744
  66.8 2.2 %shard_map.67 = bf16[64,3136]{1,0:T(8,128)(2,1)} custom-call(s32[2]{0:T(128)} %pad_add_fusion.par_ref, f32[64,3136]{1,0:T(8,128)} %shard_map.65.keep_ref, bf16[64,2240]{1,0:T(8,128)(2,1)} %copy-done.7, bf16[64,2240]{1,0:T(8,128)(2,1)} %copy-done.8), custom_call_target="tpu_custom_call" | custom-call | tf_op jit(solution)/shard_map/pallas_call | solution.py:263
  (11 shorter events, 0.2 us)
Async XLA Ops:
  0.0 14.3 %copy-start = (bf16[4,4,64,256]{3,2,1,0:T(8,128)(2,1)S(1)}, bf16[4,4,64,256]{3,2,1,0:T(8,128)(2,1)}, u32[]{:S(2)}) copy-start(bf16[4,4,64,256]{3,2,1,0:T(8,128)(2,1)} %param.9) | copy-start | bytes 1572868
  2.7 8.3 %collective-permute-start = (bf16[272,256]{1,0:T(8,128)(2,1)S(1)}, bf16[272,256]{1,0:T(8,128)(2,1)S(1)}, u32[]{:S(2)}, u32[]{:S(2)}) collective-permute-start(bf16[272,256]{1,0:T(8,128)(2,1)S(1)} %get-tuple-element.29), channel_id=1, source_target_pairs={{4,8},{12,16},{20,24},{8,4},{16,12},{24,20},{5,9},{13,17},{21,25},... | collective-permute-start | bytes 417800 | tf_op jit(solution)/shard_map/ppermute | solution.py:39
  5.9 7.9 %collective-permute-start.1 = (bf16[272,256]{1,0:T(8,128)(2,1)S(1)}, bf16[272,256]{1,0:T(8,128)(2,1)S(1)}, u32[]{:S(2)}, u32[]{:S(2)}) collective-permute-start(bf16[272,256]{1,0:T(8,128)(2,1)S(1)} %get-tuple-element.30), channel_id=1, source_target_pairs={{0,4},{4,0},{8,12},{12,8},{16,20},{20,16},{24,28},{28,24},{1,5},{5... | collective-permute-start | bytes 417800 | tf_op jit(solution)/shard_map/ppermute | solution.py:38
  13.9 7.7 %copy-start.3 = (bf16[272,256]{1,0:T(8,128)(2,1)}, bf16[272,256]{1,0:T(8,128)(2,1)S(1)}, u32[]{:S(2)}) copy-start(bf16[272,256]{1,0:T(8,128)(2,1)S(1)} %get-tuple-element.27.above_ref) | copy-start | bytes 417796
  13.9 7.7 %copy-start.4 = (bf16[272,256]{1,0:T(8,128)(2,1)}, bf16[272,256]{1,0:T(8,128)(2,1)S(1)}, u32[]{:S(2)}) copy-start(bf16[272,256]{1,0:T(8,128)(2,1)S(1)} %get-tuple-element.28.below_ref) | copy-start | bytes 417796
  14.5 7.1 %collective-permute-start.2 = (bf16[400,256]{1,0:T(8,128)(2,1)S(1)}, bf16[400,256]{1,0:T(8,128)(2,1)S(1)}, u32[]{:S(2)}, u32[]{:S(2)}) collective-permute-start(bf16[400,256]{1,0:T(8,128)(2,1)S(1)} %get-tuple-element.25), channel_id=1, source_target_pairs={{1,2},{2,1},{5,6},{6,5},{9,10},{10,9},{13,14},{14,13},{17,18},{18,... | collective-permute-start | bytes 614408 | tf_op jit(solution)/shard_map/ppermute | solution.py:39
  16.5 5.0 %collective-permute-start.3 = (bf16[400,256]{1,0:T(8,128)(2,1)S(1)}, bf16[400,256]{1,0:T(8,128)(2,1)S(1)}, u32[]{:S(2)}, u32[]{:S(2)}) collective-permute-start(bf16[400,256]{1,0:T(8,128)(2,1)S(1)} %get-tuple-element.26), channel_id=1, source_target_pairs={{0,1},{1,0},{2,3},{3,2},{4,5},{5,4},{6,7},{7,6},{8,9},{9,8},{10,11... | collective-permute-start | bytes 614408 | tf_op jit(solution)/shard_map/ppermute | solution.py:38
  21.6 1.0 %copy-start.5 = (bf16[400,256]{1,0:T(8,128)(2,1)}, bf16[400,256]{1,0:T(8,128)(2,1)S(1)}, u32[]{:S(2)}) copy-start(bf16[400,256]{1,0:T(8,128)(2,1)S(1)} %get-tuple-element.23.left_ref) | copy-start | bytes 614404
  21.6 1.0 %copy-start.6 = (bf16[400,256]{1,0:T(8,128)(2,1)}, bf16[400,256]{1,0:T(8,128)(2,1)S(1)}, u32[]{:S(2)}) copy-start(bf16[400,256]{1,0:T(8,128)(2,1)S(1)} %get-tuple-element.24.right_ref) | copy-start | bytes 614404
  38.7 2.3 %collective-permute-start.4 = (bf16[3,64,1600]{2,1,0:T(8,128)(2,1)}, bf16[3,64,1600]{2,1,0:T(8,128)(2,1)S(1)}, u32[]{:S(2)}, u32[]{:S(2)}) collective-permute-start(bf16[3,64,1600]{2,1,0:T(8,128)(2,1)} %get-tuple-element.11), channel_id=1, source_target_pairs={{0,1},{1,0},{2,3},{3,2},{4,5},{5,4},{6,7},{7,6},{8,9},{9,8},{10,11... | collective-permute-start | bytes 1843208 | tf_op jit(solution)/shard_map/ppermute | solution.py:49
  38.7 11.9 %collective-permute-start.5 = (bf16[3,64,1600]{2,1,0:T(8,128)(2,1)}, bf16[3,64,1600]{2,1,0:T(8,128)(2,1)S(1)}, u32[]{:S(2)}, u32[]{:S(2)}) collective-permute-start(bf16[3,64,1600]{2,1,0:T(8,128)(2,1)} %get-tuple-element.12), channel_id=1, source_target_pairs={{1,2},{2,1},{5,6},{6,5},{9,10},{10,9},{13,14},{14,13},{17,18},{18,... | collective-permute-start | bytes 1843208 | tf_op jit(solution)/shard_map/ppermute | solution.py:49
  41.0 9.6 %copy-start.1 = (bf16[3,64,1600]{2,1,0:T(8,128)(2,1)}, bf16[3,64,1600]{2,1,0:T(8,128)(2,1)S(1)}, u32[]{:S(2)}) copy-start(bf16[3,64,1600]{2,1,0:T(8,128)(2,1)S(1)} %collective-permute-done.4.a_ref) | copy-start | bytes 1843204
  50.7 0.8 %copy-start.2 = (bf16[3,64,1600]{2,1,0:T(8,128)(2,1)}, bf16[3,64,1600]{2,1,0:T(8,128)(2,1)S(1)}, u32[]{:S(2)}) copy-start(bf16[3,64,1600]{2,1,0:T(8,128)(2,1)S(1)} %collective-permute-done.5.b_ref) | copy-start | bytes 1843204
  54.7 6.9 %collective-permute-start.6 = (bf16[64,2240]{1,0:T(8,128)(2,1)}, bf16[64,2240]{1,0:T(8,128)(2,1)S(1)}, u32[]{:S(2)}, u32[]{:S(2)}) collective-permute-start(bf16[64,2240]{1,0:T(8,128)(2,1)} %get-tuple-element.13), channel_id=1, source_target_pairs={{0,4},{4,0},{8,12},{12,8},{16,20},{20,16},{24,28},{28,24},{1,5},{5... | collective-permute-start | bytes 860168 | tf_op jit(solution)/shard_map/ppermute | solution.py:49
  56.3 9.7 %collective-permute-start.7 = (bf16[64,2240]{1,0:T(8,128)(2,1)}, bf16[64,2240]{1,0:T(8,128)(2,1)S(1)}, u32[]{:S(2)}, u32[]{:S(2)}) collective-permute-start(bf16[64,2240]{1,0:T(8,128)(2,1)} %get-tuple-element.14), channel_id=1, source_target_pairs={{4,8},{12,16},{20,24},{8,4},{16,12},{24,20},{5,9},{13,17},{21,25},... | collective-permute-start | bytes 860168 | tf_op jit(solution)/shard_map/ppermute | solution.py:49
  61.7 4.4 %copy-start.7 = (bf16[64,2240]{1,0:T(8,128)(2,1)}, bf16[64,2240]{1,0:T(8,128)(2,1)S(1)}, u32[]{:S(2)}) copy-start(bf16[64,2240]{1,0:T(8,128)(2,1)S(1)} %collective-permute-done.6.a_ref) | copy-start | bytes 860164
  66.1 0.7 %copy-start.8 = (bf16[64,2240]{1,0:T(8,128)(2,1)}, bf16[64,2240]{1,0:T(8,128)(2,1)S(1)}, u32[]{:S(2)}) copy-start(bf16[64,2240]{1,0:T(8,128)(2,1)S(1)} %collective-permute-done.7.b_ref) | copy-start | bytes 860164

commit v14 on v13

--- a/solution.py
+++ b/solution.py
@@ -78,8 +78,11 @@
                 s = jnp.where(k < count, nslot_ref[pos * KP + q], TRASH)
                 acc_ref[s] = acc_ref[s] + term[:, q * B:(q + 1) * B]
         row = pl.multiple_of(i * B, B)
-        for w in range(WIN * WIN):
-            prod_ref[pl.ds(row, B), w * B:(w + 1) * B] = acc_ref[w].astype(jnp.bfloat16)
+        for w in range(0, WIN * WIN - 1, 2):
+            pair = jnp.concatenate([acc_ref[w], acc_ref[w + 1]], axis=1)
+            prod_ref[pl.ds(row, B), w * B:(w + 2) * B] = pair.astype(jnp.bfloat16)
+        last = WIN * WIN - 1
+        prod_ref[pl.ds(row, B), last * B:(last + 1) * B] = acc_ref[last].astype(jnp.bfloat16)
         return carry
 
     lax.fori_loop(0, patches, one_patch, 0)

time: 69.3 us -> 68.6 us (0.990)
  Pallas kernels: 24.6 us -> 23.8 us
    pallas_call x1, Pallas kernels: 16.1 us -> 15.3 us  [per_device(): pl.pallas_call(galerkin_kernel, out_shape=(jax.ShapeDtypeStruct((HOME, B,...]
  transfers between devices with their start and end apart: 8 -> 8, of which waited for: 7 -> 6; matrix products, arithmetic and copies ran while one was open for 3% -> 3% of each run, Pallas kernels for 4% -> 5%
where the time goes in v14:
time: 68.6 us; the launch traced here: 68.3 us
  Pallas kernels  23.8 us (35%)
  waiting for transfers between devices  23.5 us (34%)
  starting transfers between devices  13.2 us (19%)
  local copies, waits for them, and re-layouts  3.97 us (6%)
  other arithmetic  3.76 us (5%)
    pallas_call x1, Pallas kernels, per_device(): pl.pallas_call(galerkin_kernel, out_shape=(jax.ShapeDtypeStruct((HOME, B,...  15.3 us
    ppermute x2, waiting for transfers between devices, swap_rounds(): lax.ppermute(second, axis, pairs_b)  14 us
    ppermute x2, waiting for transfers between devices, exchange(): got_second = lax.ppermute(jnp.where(even, to_prev, to_next), axis, second)  6.29 us
    ppermute x2, starting transfers between devices, exchange(): got_second = lax.ppermute(jnp.where(even, to_prev, to_next), axis, second)  5.32 us
    ppermute x2, starting transfers between devices, swap_rounds(): lax.ppermute(second, axis, pairs_b)  4.23 us
    pallas_call x1, Pallas kernels, per_device(): pl.pallas_call(fold_cols_send_kernel, out_shape=(jax.ShapeDtypeStruct((B,...  3.25 us
    pallas_call x1, Pallas kernels, per_device(): pl.pallas_call(fold_cols_keep_kernel, out_shape=jax.ShapeDtypeStruct((B,...  3.1 us
    ppermute x2, waiting for transfers between devices, exchange(): got_first = lax.ppermute(jnp.where(even, to_next, to_prev), axis, first)  2.89 us
  transfers between devices with their start and end apart: 8, of which 6 were waited for; matrix products, arithmetic and copies ran while one was open for 3% of the time, Pallas kernels for 5%

profile of v14, /device:TPU:20, one launch (start us, length us, event | category | flops | bytes accessed | tf_op | source)
XLA Modules:
  0.0 68.3 jit_solution(15381411172416765119)
XLA Ops:
  0.0 0.0 copy-start
  0.0 1.4 %fusion.27 = (bf16[4,4,4]{2,1,0:T(4,128)(2,1)S(1)}, s32[4,4,4]{2,1,0:T(4,128)S(1)}, s32[4,4,4]{2,1,0:T(4,128)}) fusion(s32[]{:T(128)S(6)} %axis_index.14, s32[]{:T(128)S(6)} %axis_index.33, s32[4,4,4]{2,1,0:T(4,128)} %param.10, s32[4,4]{1,0:T(4,128)} %param.11), kind=kLoop, calls=%fused_computation.73 | loop fusion | flops 2112 | bytes 968 | tf_op jit(solution)/shard_map/convert.7
  1.4 0.1 convert_element_type.106
  1.5 0.1 convert_element_type.107
  1.6 1.0 %fusion.28 = (bf16[1,4,64,256]{3,2,1,0:T(8,128)(2,1)S(1)}, bf16[1,4,64,256]{3,2,1,0:T(8,128)(2,1)S(1)}) fusion(bf16[4,4,64,256]{3,2,1,0:T(8,128)(2,1)} %param.9), kind=kLoop, calls=%fused_computation.74 | loop fusion | bytes 524288 | tf_op jit(solution)/shard_map/slice | solution.py:193
  2.6 0.1 broadcast_select_fusion.7
  2.7 3.3 %collective-permute-start = (bf16[272,256]{1,0:T(8,128)(2,1)S(1)}, bf16[272,256]{1,0:T(8,128)(2,1)S(1)}, u32[]{:S(2)}, u32[]{:S(2)}) collective-permute-start(bf16[272,256]{1,0:T(8,128)(2,1)S(1)} %get-tuple-element.29), channel_id=1, source_target_pairs={{4,8},{12,16},{20,24},{8,4},{16,12},{24,20},{5,9},{13,17},{21,25},... | collective-permute-start | bytes 417800 | tf_op jit(solution)/shard_map/ppermute | solution.py:39
  5.9 1.7 %collective-permute-start.1 = (bf16[272,256]{1,0:T(8,128)(2,1)S(1)}, bf16[272,256]{1,0:T(8,128)(2,1)S(1)}, u32[]{:S(2)}, u32[]{:S(2)}) collective-permute-start(bf16[272,256]{1,0:T(8,128)(2,1)S(1)} %get-tuple-element.30), channel_id=1, source_target_pairs={{0,4},{4,0},{8,12},{12,8},{16,20},{20,16},{24,28},{28,24},{1,5},{5... | collective-permute-start | bytes 417800 | tf_op jit(solution)/shard_map/ppermute | solution.py:38
  7.7 1.3 %add_clamp_fusion.pos_ref = s32[4,4,9]{2,1,0:T(4,128)} fusion(s32[4,4,9]{2,1,0:T(4,128)} %param.7, s32[]{:T(128)S(6)} %mul.33, s32[]{:T(128)S(6)} %mul.30), kind=kLoop, calls=%fused_computation.49 | loop fusion | flops 3744 | bytes 1160 | tf_op jit(solution)/shard_map/jit(clip)/min | solution.py:213
  9.0 0.6 pad_add_fusion.par_ref
  9.5 1.4 %collective-permute-done = bf16[272,256]{1,0:T(8,128)(2,1)S(1)} collective-permute-done((bf16[272,256]{1,0:T(8,128)(2,1)S(1)}, bf16[272,256]{1,0:T(8,128)(2,1)S(1)}, u32[]{:S(2)}, u32[]{:S(2)}) %collective-permute-start) | collective-permute-done | bytes 139296 | tf_op jit(solution)/shard_map/ppermute | solution.py:39
  11.0 2.9 %collective-permute-done.1 = bf16[272,256]{1,0:T(8,128)(2,1)S(1)} collective-permute-done((bf16[272,256]{1,0:T(8,128)(2,1)S(1)}, bf16[272,256]{1,0:T(8,128)(2,1)S(1)}, u32[]{:S(2)}, u32[]{:S(2)}) %collective-permute-start.1) | collective-permute-done | bytes 139296 | tf_op jit(solution)/shard_map/ppermute | solution.py:38
  13.9 0.0 copy-start.3
  13.9 0.0 copy-start.4
  14.0 0.1 reshape.196
  14.0 0.1 reshape.197
  14.2 0.1 convert_element_type.112
  14.3 0.1 convert_element_type.113
  14.3 0.0 copy-done
  14.4 0.1 pad_maximum_fusion.2
  14.4 0.1 broadcast_select_fusion.3
  14.5 2.0 %collective-permute-start.2 = (bf16[400,256]{1,0:T(8,128)(2,1)S(1)}, bf16[400,256]{1,0:T(8,128)(2,1)S(1)}, u32[]{:S(2)}, u32[]{:S(2)}) collective-permute-start(bf16[400,256]{1,0:T(8,128)(2,1)S(1)} %get-tuple-element.25), channel_id=1, source_target_pairs={{1,2},{2,1},{5,6},{6,5},{9,10},{10,9},{13,14},{14,13},{17,18},{18,... | collective-permute-start | bytes 614408 | tf_op jit(solution)/shard_map/ppermute | solution.py:39
  16.5 0.1 collective-permute-start.3
  16.6 0.1 add_add_fusion.1
  16.7 4.9 %collective-permute-done.2 = bf16[400,256]{1,0:T(8,128)(2,1)S(1)} collective-permute-done((bf16[400,256]{1,0:T(8,128)(2,1)S(1)}, bf16[400,256]{1,0:T(8,128)(2,1)S(1)}, u32[]{:S(2)}, u32[]{:S(2)}) %collective-permute-start.2) | collective-permute-done | bytes 204832 | tf_op jit(solution)/shard_map/ppermute | solution.py:39
  21.6 0.0 collective-permute-done.3
  21.6 0.0 copy-done.3
  21.6 0.0 copy-done.4
  21.6 0.0 copy-start.5
  21.6 0.0 copy-start.6
  21.7 0.1 reshape.200
  21.8 0.1 reshape.201
  21.9 0.1 fusion.8
  21.9 0.7 min.34.nslot_ref
  22.6 0.0 copy-done.5
  22.6 0.0 copy-done.6
  22.6 15.3 %shard_map.64 = (f32[3,64,1600]{2,1,0:T(8,128)}, bf16[3,64,1600]{2,1,0:T(8,128)(2,1)}, bf16[3,64,1600]{2,1,0:T(8,128)(2,1)}) custom-call(s32[2]{0:T(128)} %pad_add_fusion.par_ref, s32[4,4,9]{2,1,0:T(4,128)} %add_clamp_fusion.pos_ref, s32[144]{0:T(256)} %min.34.nslot_ref, s32[4,4]{1,0:T(4,128)} %count_ref.1, s32[4,4,4]{2,1,0:T(4,128)} %get-tuple-element.31.home_ref, ...), custom_call_target="tpu_custom_call" | custom-call | tf_op jit(solution)/shard_map/pallas_call | solution.py:220
  37.9 0.0 collective-permute-start.4
  37.9 2.0 %collective-permute-start.5 = (bf16[3,64,1600]{2,1,0:T(8,128)(2,1)}, bf16[3,64,1600]{2,1,0:T(8,128)(2,1)S(1)}, u32[]{:S(2)}, u32[]{:S(2)}) collective-permute-start(bf16[3,64,1600]{2,1,0:T(8,128)(2,1)} %get-tuple-element.12), channel_id=1, source_target_pairs={{1,2},{2,1},{5,6},{6,5},{9,10},{10,9},{13,14},{14,13},{17,18},{18,... | collective-permute-start | bytes 1843208 | tf_op jit(solution)/shard_map/ppermute | solution.py:49
  39.9 0.3 collective-permute-done.4.a_ref
  40.2 0.0 copy-start.1
  40.2 9.6 %collective-permute-done.5.b_ref = bf16[3,64,1600]{2,1,0:T(8,128)(2,1)S(1)} collective-permute-done((bf16[3,64,1600]{2,1,0:T(8,128)(2,1)}, bf16[3,64,1600]{2,1,0:T(8,128)(2,1)S(1)}, u32[]{:S(2)}, u32[]{:S(2)}) %collective-permute-start.5) | collective-permute-done | bytes 614432 | tf_op jit(solution)/shard_map/ppermute | solution.py:49
  49.8 0.0 copy-start.2
  49.8 0.0 copy-done.1
  49.8 0.8 %copy-done.2 = bf16[3,64,1600]{2,1,0:T(8,128)(2,1)} copy-done((bf16[3,64,1600]{2,1,0:T(8,128)(2,1)}, bf16[3,64,1600]{2,1,0:T(8,128)(2,1)S(1)}, u32[]{:S(2)}) %copy-start.2) | copy-done | bytes 614424
  50.6 3.3 %shard_map.66 = (bf16[64,2240]{1,0:T(8,128)(2,1)}, bf16[64,2240]{1,0:T(8,128)(2,1)}) custom-call(s32[2]{0:T(128)} %pad_add_fusion.par_ref, f32[3,64,1600]{2,1,0:T(8,128)} %get-tuple-element.10.keep_ref, bf16[3,64,1600]{2,1,0:T(8,128)(2,1)} %copy-done.1, bf16[3,64,1600]{2,1,0:T(8,128)(2,1)} %copy-done.2), custom_call_target="tpu_custom_call" | custom-call | tf_op jit(solution)/shard_map/pallas_call | solution.py:250
  53.9 1.8 %collective-permute-start.6 = (bf16[64,2240]{1,0:T(8,128)(2,1)}, bf16[64,2240]{1,0:T(8,128)(2,1)S(1)}, u32[]{:S(2)}, u32[]{:S(2)}) collective-permute-start(bf16[64,2240]{1,0:T(8,128)(2,1)} %get-tuple-element.13), channel_id=1, source_target_pairs={{0,4},{4,0},{8,12},{12,8},{16,20},{20,16},{24,28},{28,24},{1,5},{5... | collective-permute-start | bytes 860168 | tf_op jit(solution)/shard_map/ppermute | solution.py:49
  55.7 2.3 %collective-permute-start.7 = (bf16[64,2240]{1,0:T(8,128)(2,1)}, bf16[64,2240]{1,0:T(8,128)(2,1)S(1)}, u32[]{:S(2)}, u32[]{:S(2)}) collective-permute-start(bf16[64,2240]{1,0:T(8,128)(2,1)} %get-tuple-element.14), channel_id=1, source_target_pairs={{4,8},{12,16},{20,24},{8,4},{16,12},{24,20},{5,9},{13,17},{21,25},... | collective-permute-start | bytes 860168 | tf_op jit(solution)/shard_map/ppermute | solution.py:49
  58.0 3.1 %shard_map.65.keep_ref = f32[64,3136]{1,0:T(8,128)} custom-call(s32[2]{0:T(128)} %pad_add_fusion.par_ref, f32[3,64,1600]{2,1,0:T(8,128)} %get-tuple-element.10.keep_ref, bf16[3,64,1600]{2,1,0:T(8,128)(2,1)} %copy-done.1, bf16[3,64,1600]{2,1,0:T(8,128)(2,1)} %copy-done.2), custom_call_target="tpu_custom_call" | custom-call | tf_op jit(solution)/shard_map/pallas_call | solution.py:259
  61.1 0.0 collective-permute-done.6.a_ref
  61.1 0.0 copy-start.7
  61.1 4.3 %collective-permute-done.7.b_ref = bf16[64,2240]{1,0:T(8,128)(2,1)S(1)} collective-permute-done((bf16[64,2240]{1,0:T(8,128)(2,1)}, bf16[64,2240]{1,0:T(8,128)(2,1)S(1)}, u32[]{:S(2)}, u32[]{:S(2)}) %collective-permute-start.7) | collective-permute-done | bytes 286752 | tf_op jit(solution)/shard_map/ppermute | solution.py:49
  65.4 0.0 copy-done.7
  65.5 0.0 copy-start.8
  65.5 0.7 %copy-done.8 = bf16[64,2240]{1,0:T(8,128)(2,1)} copy-done((bf16[64,2240]{1,0:T(8,128)(2,1)}, bf16[64,2240]{1,0:T(8,128)(2,1)S(1)}, u32[]{:S(2)}) %copy-start.8) | copy-done | bytes 286744
  66.2 2.2 %shard_map.67 = bf16[64,3136]{1,0:T(8,128)(2,1)} custom-call(s32[2]{0:T(128)} %pad_add_fusion.par_ref, f32[64,3136]{1,0:T(8,128)} %shard_map.65.keep_ref, bf16[64,2240]{1,0:T(8,128)(2,1)} %copy-done.7, bf16[64,2240]{1,0:T(8,128)(2,1)} %copy-done.8), custom_call_target="tpu_custom_call" | custom-call | tf_op jit(solution)/shard_map/pallas_call | solution.py:266
  (11 shorter events, 0.2 us)
Async XLA Ops:
  0.0 14.3 %copy-start = (bf16[4,4,64,256]{3,2,1,0:T(8,128)(2,1)S(1)}, bf16[4,4,64,256]{3,2,1,0:T(8,128)(2,1)}, u32[]{:S(2)}) copy-start(bf16[4,4,64,256]{3,2,1,0:T(8,128)(2,1)} %param.9) | copy-start | bytes 1572868
  2.7 8.3 %collective-permute-start = (bf16[272,256]{1,0:T(8,128)(2,1)S(1)}, bf16[272,256]{1,0:T(8,128)(2,1)S(1)}, u32[]{:S(2)}, u32[]{:S(2)}) collective-permute-start(bf16[272,256]{1,0:T(8,128)(2,1)S(1)} %get-tuple-element.29), channel_id=1, source_target_pairs={{4,8},{12,16},{20,24},{8,4},{16,12},{24,20},{5,9},{13,17},{21,25},... | collective-permute-start | bytes 417800 | tf_op jit(solution)/shard_map/ppermute | solution.py:39
  5.9 7.9 %collective-permute-start.1 = (bf16[272,256]{1,0:T(8,128)(2,1)S(1)}, bf16[272,256]{1,0:T(8,128)(2,1)S(1)}, u32[]{:S(2)}, u32[]{:S(2)}) collective-permute-start(bf16[272,256]{1,0:T(8,128)(2,1)S(1)} %get-tuple-element.30), channel_id=1, source_target_pairs={{0,4},{4,0},{8,12},{12,8},{16,20},{20,16},{24,28},{28,24},{1,5},{5... | collective-permute-start | bytes 417800 | tf_op jit(solution)/shard_map/ppermute | solution.py:38
  13.9 7.7 %copy-start.3 = (bf16[272,256]{1,0:T(8,128)(2,1)}, bf16[272,256]{1,0:T(8,128)(2,1)S(1)}, u32[]{:S(2)}) copy-start(bf16[272,256]{1,0:T(8,128)(2,1)S(1)} %get-tuple-element.27.above_ref) | copy-start | bytes 417796
  13.9 7.7 %copy-start.4 = (bf16[272,256]{1,0:T(8,128)(2,1)}, bf16[272,256]{1,0:T(8,128)(2,1)S(1)}, u32[]{:S(2)}) copy-start(bf16[272,256]{1,0:T(8,128)(2,1)S(1)} %get-tuple-element.28.below_ref) | copy-start | bytes 417796
  14.5 7.1 %collective-permute-start.2 = (bf16[400,256]{1,0:T(8,128)(2,1)S(1)}, bf16[400,256]{1,0:T(8,128)(2,1)S(1)}, u32[]{:S(2)}, u32[]{:S(2)}) collective-permute-start(bf16[400,256]{1,0:T(8,128)(2,1)S(1)} %get-tuple-element.25), channel_id=1, source_target_pairs={{1,2},{2,1},{5,6},{6,5},{9,10},{10,9},{13,14},{14,13},{17,18},{18,... | collective-permute-start | bytes 614408 | tf_op jit(solution)/shard_map/ppermute | solution.py:39
  16.5 5.0 %collective-permute-start.3 = (bf16[400,256]{1,0:T(8,128)(2,1)S(1)}, bf16[400,256]{1,0:T(8,128)(2,1)S(1)}, u32[]{:S(2)}, u32[]{:S(2)}) collective-permute-start(bf16[400,256]{1,0:T(8,128)(2,1)S(1)} %get-tuple-element.26), channel_id=1, source_target_pairs={{0,1},{1,0},{2,3},{3,2},{4,5},{5,4},{6,7},{7,6},{8,9},{9,8},{10,11... | collective-permute-start | bytes 614408 | tf_op jit(solution)/shard_map/ppermute | solution.py:38
  21.6 1.0 %copy-start.5 = (bf16[400,256]{1,0:T(8,128)(2,1)}, bf16[400,256]{1,0:T(8,128)(2,1)S(1)}, u32[]{:S(2)}) copy-start(bf16[400,256]{1,0:T(8,128)(2,1)S(1)} %get-tuple-element.23.left_ref) | copy-start | bytes 614404
  21.6 1.0 %copy-start.6 = (bf16[400,256]{1,0:T(8,128)(2,1)}, bf16[400,256]{1,0:T(8,128)(2,1)S(1)}, u32[]{:S(2)}) copy-start(bf16[400,256]{1,0:T(8,128)(2,1)S(1)} %get-tuple-element.24.right_ref) | copy-start | bytes 614404
  37.9 2.3 %collective-permute-start.4 = (bf16[3,64,1600]{2,1,0:T(8,128)(2,1)}, bf16[3,64,1600]{2,1,0:T(8,128)(2,1)S(1)}, u32[]{:S(2)}, u32[]{:S(2)}) collective-permute-start(bf16[3,64,1600]{2,1,0:T(8,128)(2,1)} %get-tuple-element.11), channel_id=1, source_target_pairs={{0,1},{1,0},{2,3},{3,2},{4,5},{5,4},{6,7},{7,6},{8,9},{9,8},{10,11... | collective-permute-start | bytes 1843208 | tf_op jit(solution)/shard_map/ppermute | solution.py:49
  37.9 11.9 %collective-permute-start.5 = (bf16[3,64,1600]{2,1,0:T(8,128)(2,1)}, bf16[3,64,1600]{2,1,0:T(8,128)(2,1)S(1)}, u32[]{:S(2)}, u32[]{:S(2)}) collective-permute-start(bf16[3,64,1600]{2,1,0:T(8,128)(2,1)} %get-tuple-element.12), channel_id=1, source_target_pairs={{1,2},{2,1},{5,6},{6,5},{9,10},{10,9},{13,14},{14,13},{17,18},{18,... | collective-permute-start | bytes 1843208 | tf_op jit(solution)/shard_map/ppermute | solution.py:49
  40.2 9.6 %copy-start.1 = (bf16[3,64,1600]{2,1,0:T(8,128)(2,1)}, bf16[3,64,1600]{2,1,0:T(8,128)(2,1)S(1)}, u32[]{:S(2)}) copy-start(bf16[3,64,1600]{2,1,0:T(8,128)(2,1)S(1)} %collective-permute-done.4.a_ref) | copy-start | bytes 1843204
  49.8 0.8 %copy-start.2 = (bf16[3,64,1600]{2,1,0:T(8,128)(2,1)}, bf16[3,64,1600]{2,1,0:T(8,128)(2,1)S(1)}, u32[]{:S(2)}) copy-start(bf16[3,64,1600]{2,1,0:T(8,128)(2,1)S(1)} %collective-permute-done.5.b_ref) | copy-start | bytes 1843204
  53.9 7.2 %collective-permute-start.6 = (bf16[64,2240]{1,0:T(8,128)(2,1)}, bf16[64,2240]{1,0:T(8,128)(2,1)S(1)}, u32[]{:S(2)}, u32[]{:S(2)}) collective-permute-start(bf16[64,2240]{1,0:T(8,128)(2,1)} %get-tuple-element.13), channel_id=1, source_target_pairs={{0,4},{4,0},{8,12},{12,8},{16,20},{20,16},{24,28},{28,24},{1,5},{5... | collective-permute-start | bytes 860168 | tf_op jit(solution)/shard_map/ppermute | solution.py:49
  55.7 9.7 %collective-permute-start.7 = (bf16[64,2240]{1,0:T(8,128)(2,1)}, bf16[64,2240]{1,0:T(8,128)(2,1)S(1)}, u32[]{:S(2)}, u32[]{:S(2)}) collective-permute-start(bf16[64,2240]{1,0:T(8,128)(2,1)} %get-tuple-element.14), channel_id=1, source_target_pairs={{4,8},{12,16},{20,24},{8,4},{16,12},{24,20},{5,9},{13,17},{21,25},... | collective-permute-start | bytes 860168 | tf_op jit(solution)/shard_map/ppermute | solution.py:49
  61.1 4.3 %copy-start.7 = (bf16[64,2240]{1,0:T(8,128)(2,1)}, bf16[64,2240]{1,0:T(8,128)(2,1)S(1)}, u32[]{:S(2)}) copy-start(bf16[64,2240]{1,0:T(8,128)(2,1)S(1)} %collective-permute-done.6.a_ref) | copy-start | bytes 860164
  65.5 0.7 %copy-start.8 = (bf16[64,2240]{1,0:T(8,128)(2,1)}, bf16[64,2240]{1,0:T(8,128)(2,1)S(1)}, u32[]{:S(2)}) copy-start(bf16[64,2240]{1,0:T(8,128)(2,1)S(1)} %collective-permute-done.7.b_ref) | copy-start | bytes 860164

commit v15 on v14

--- a/solution.py
+++ b/solution.py
@@ -141,7 +141,9 @@
     fold_cols_band(keep_ref, a_ref, b_ref, par_ref[0] == 0, 1, keep_out, shift=1)
 
 
-def fold_rows_kernel(par_ref, keep_ref, a_ref, b_ref, out_ref):
+def fold_rows_kernel(par_ref, keep_ref, a_hbm, b_hbm, out_ref, a_ref, b_ref):
+    pltpu.sync_copy(a_hbm, a_ref)
+    pltpu.sync_copy(b_hbm, b_ref)
     band = OUTW * B
     even = par_ref[1] == 0
     low = 2 * band
@@ -266,8 +268,10 @@
     out = pl.pallas_call(
         fold_rows_kernel,
         out_shape=jax.ShapeDtypeStruct((B, OUTW * OUTW * B), jnp.bfloat16),
-        in_specs=[pl.BlockSpec(memory_space=smem)] + [pl.BlockSpec(memory_space=vmem)] * 3,
+        in_specs=[pl.BlockSpec(memory_space=smem), pl.BlockSpec(memory_space=vmem)]
+        + [pl.BlockSpec(memory_space=pltpu.MemorySpace.HBM)] * 2,
         out_specs=pl.BlockSpec(memory_space=vmem),
+        scratch_shapes=[pltpu.VMEM((B, band), SEND), pltpu.VMEM((B, band), SEND)],
     )(parity, keep2, row_a, row_b)
     return out.reshape(1, 1, B, OUTW * OUTW * B)
 

time: 68.6 us -> 70.4 us (1.026)
  Pallas kernels: 23.8 us -> 25.5 us
    pallas_call x1, Pallas kernels: 2.18 us -> 3.95 us  [per_device(): pl.pallas_call(fold_rows_kernel, out_shape=jax.ShapeDtypeStruct((B, OUTW...]
  transfers between devices with their start and end apart: 8 -> 8, of which waited for: 6 -> 6; matrix products, arithmetic and copies ran while one was open for 3% -> 3% of each run, Pallas kernels for 5% -> 4%
where the time goes in v15:
time: 70.4 us; the launch traced here: 69.8 us
  Pallas kernels  25.5 us (36%)
  waiting for transfers between devices  23.1 us (33%)
  starting transfers between devices  13.2 us (19%)
  local copies, waits for them, and re-layouts  3.97 us (6%)
  other arithmetic  3.76 us (5%)
    pallas_call x1, Pallas kernels, per_device(): pl.pallas_call(galerkin_kernel, out_shape=(jax.ShapeDtypeStruct((HOME, B,...  15.2 us
    ppermute x2, waiting for transfers between devices, swap_rounds(): lax.ppermute(second, axis, pairs_b)  13.7 us
    ppermute x2, waiting for transfers between devices, exchange(): got_second = lax.ppermute(jnp.where(even, to_prev, to_next), axis, second)  6.29 us
    ppermute x2, starting transfers between devices, exchange(): got_second = lax.ppermute(jnp.where(even, to_prev, to_next), axis, second)  5.32 us
    ppermute x2, starting transfers between devices, swap_rounds(): lax.ppermute(second, axis, pairs_b)  4.57 us
    pallas_call x1, Pallas kernels, per_device(): pl.pallas_call(fold_rows_kernel, out_shape=jax.ShapeDtypeStruct((B, OUTW...  3.95 us
    pallas_call x1, Pallas kernels, per_device(): pl.pallas_call(fold_cols_send_kernel, out_shape=(jax.ShapeDtypeStruct((B,...  3.25 us
    pallas_call x1, Pallas kernels, per_device(): pl.pallas_call(fold_cols_keep_kernel, out_shape=jax.ShapeDtypeStruct((B,...  3.1 us
  transfers between devices with their start and end apart: 8, of which 6 were waited for; matrix products, arithmetic and copies ran while one was open for 3% of the time, Pallas kernels for 4%

profile of v15, /device:TPU:20, one launch (start us, length us, event | category | flops | bytes accessed | tf_op | source)
XLA Modules:
  0.0 69.8 jit_solution(5509050261830161148)
XLA Ops:
  0.0 0.0 copy-start
  0.0 1.4 %fusion.27 = (bf16[4,4,4]{2,1,0:T(4,128)(2,1)S(1)}, s32[4,4,4]{2,1,0:T(4,128)S(1)}, s32[4,4,4]{2,1,0:T(4,128)}) fusion(s32[]{:T(128)S(6)} %axis_index.14, s32[]{:T(128)S(6)} %axis_index.33, s32[4,4,4]{2,1,0:T(4,128)} %param.10, s32[4,4]{1,0:T(4,128)} %param.11), kind=kLoop, calls=%fused_computation.73 | loop fusion | flops 2112 | bytes 968 | tf_op jit(solution)/shard_map/convert.7
  1.4 0.1 convert_element_type.106
  1.5 0.1 convert_element_type.107
  1.6 1.0 %fusion.28 = (bf16[1,4,64,256]{3,2,1,0:T(8,128)(2,1)S(1)}, bf16[1,4,64,256]{3,2,1,0:T(8,128)(2,1)S(1)}) fusion(bf16[4,4,64,256]{3,2,1,0:T(8,128)(2,1)} %param.9), kind=kLoop, calls=%fused_computation.74 | loop fusion | bytes 524288 | tf_op jit(solution)/shard_map/slice | solution.py:195
  2.6 0.1 broadcast_select_fusion.7
  2.7 3.3 %collective-permute-start = (bf16[272,256]{1,0:T(8,128)(2,1)S(1)}, bf16[272,256]{1,0:T(8,128)(2,1)S(1)}, u32[]{:S(2)}, u32[]{:S(2)}) collective-permute-start(bf16[272,256]{1,0:T(8,128)(2,1)S(1)} %get-tuple-element.29), channel_id=1, source_target_pairs={{4,8},{12,16},{20,24},{8,4},{16,12},{24,20},{5,9},{13,17},{21,25},... | collective-permute-start | bytes 417800 | tf_op jit(solution)/shard_map/ppermute | solution.py:39
  5.9 1.7 %collective-permute-start.1 = (bf16[272,256]{1,0:T(8,128)(2,1)S(1)}, bf16[272,256]{1,0:T(8,128)(2,1)S(1)}, u32[]{:S(2)}, u32[]{:S(2)}) collective-permute-start(bf16[272,256]{1,0:T(8,128)(2,1)S(1)} %get-tuple-element.30), channel_id=1, source_target_pairs={{0,4},{4,0},{8,12},{12,8},{16,20},{20,16},{24,28},{28,24},{1,5},{5... | collective-permute-start | bytes 417800 | tf_op jit(solution)/shard_map/ppermute | solution.py:38
  7.7 1.3 %add_clamp_fusion.pos_ref = s32[4,4,9]{2,1,0:T(4,128)} fusion(s32[4,4,9]{2,1,0:T(4,128)} %param.7, s32[]{:T(128)S(6)} %mul.33, s32[]{:T(128)S(6)} %mul.30), kind=kLoop, calls=%fused_computation.49 | loop fusion | flops 3744 | bytes 1160 | tf_op jit(solution)/shard_map/jit(clip)/min | solution.py:215
  9.0 0.6 pad_add_fusion.par_ref
  9.5 1.4 %collective-permute-done = bf16[272,256]{1,0:T(8,128)(2,1)S(1)} collective-permute-done((bf16[272,256]{1,0:T(8,128)(2,1)S(1)}, bf16[272,256]{1,0:T(8,128)(2,1)S(1)}, u32[]{:S(2)}, u32[]{:S(2)}) %collective-permute-start) | collective-permute-done | bytes 139296 | tf_op jit(solution)/shard_map/ppermute | solution.py:39
  11.0 2.9 %collective-permute-done.1 = bf16[272,256]{1,0:T(8,128)(2,1)S(1)} collective-permute-done((bf16[272,256]{1,0:T(8,128)(2,1)S(1)}, bf16[272,256]{1,0:T(8,128)(2,1)S(1)}, u32[]{:S(2)}, u32[]{:S(2)}) %collective-permute-start.1) | collective-permute-done | bytes 139296 | tf_op jit(solution)/shard_map/ppermute | solution.py:38
  13.9 0.0 copy-start.3
  13.9 0.0 copy-start.4
  14.0 0.1 reshape.196
  14.0 0.1 reshape.197
  14.2 0.1 convert_element_type.112
  14.3 0.1 convert_element_type.113
  14.3 0.0 copy-done
  14.4 0.1 pad_maximum_fusion.2
  14.4 0.1 broadcast_select_fusion.3
  14.5 2.0 %collective-permute-start.2 = (bf16[400,256]{1,0:T(8,128)(2,1)S(1)}, bf16[400,256]{1,0:T(8,128)(2,1)S(1)}, u32[]{:S(2)}, u32[]{:S(2)}) collective-permute-start(bf16[400,256]{1,0:T(8,128)(2,1)S(1)} %get-tuple-element.25), channel_id=1, source_target_pairs={{1,2},{2,1},{5,6},{6,5},{9,10},{10,9},{13,14},{14,13},{17,18},{18,... | collective-permute-start | bytes 614408 | tf_op jit(solution)/shard_map/ppermute | solution.py:39
  16.5 0.1 collective-permute-start.3
  16.6 0.1 add_add_fusion.1
  16.7 4.9 %collective-permute-done.2 = bf16[400,256]{1,0:T(8,128)(2,1)S(1)} collective-permute-done((bf16[400,256]{1,0:T(8,128)(2,1)S(1)}, bf16[400,256]{1,0:T(8,128)(2,1)S(1)}, u32[]{:S(2)}, u32[]{:S(2)}) %collective-permute-start.2) | collective-permute-done | bytes 204832 | tf_op jit(solution)/shard_map/ppermute | solution.py:39
  21.6 0.0 collective-permute-done.3
  21.6 0.0 copy-done.3
  21.6 0.0 copy-done.4
  21.6 0.0 copy-start.5
  21.6 0.0 copy-start.6
  21.7 0.1 reshape.200
  21.8 0.1 reshape.201
  21.9 0.1 fusion.8
  21.9 0.7 min.34.nslot_ref
  22.6 0.0 copy-done.5
  22.6 0.0 copy-done.6
  22.6 15.2 %shard_map.64 = (f32[3,64,1600]{2,1,0:T(8,128)}, bf16[3,64,1600]{2,1,0:T(8,128)(2,1)}, bf16[3,64,1600]{2,1,0:T(8,128)(2,1)}) custom-call(s32[2]{0:T(128)} %pad_add_fusion.par_ref, s32[4,4,9]{2,1,0:T(4,128)} %add_clamp_fusion.pos_ref, s32[144]{0:T(256)} %min.34.nslot_ref, s32[4,4]{1,0:T(4,128)} %count_ref.1, s32[4,4,4]{2,1,0:T(4,128)} %get-tuple-element.31.home_ref, ...), custom_call_target="tpu_custom_call" | custom-call | tf_op jit(solution)/shard_map/pallas_call | solution.py:222
  37.8 0.0 collective-permute-start.4
  37.8 2.0 %collective-permute-start.5 = (bf16[3,64,1600]{2,1,0:T(8,128)(2,1)}, bf16[3,64,1600]{2,1,0:T(8,128)(2,1)S(1)}, u32[]{:S(2)}, u32[]{:S(2)}) collective-permute-start(bf16[3,64,1600]{2,1,0:T(8,128)(2,1)} %get-tuple-element.12), channel_id=1, source_target_pairs={{1,2},{2,1},{5,6},{6,5},{9,10},{10,9},{13,14},{14,13},{17,18},{18,... | collective-permute-start | bytes 1843208 | tf_op jit(solution)/shard_map/ppermute | solution.py:49
  39.8 0.3 collective-permute-done.4.a_ref
  40.1 0.0 copy-start.1
  40.1 9.6 %collective-permute-done.5.b_ref = bf16[3,64,1600]{2,1,0:T(8,128)(2,1)S(1)} collective-permute-done((bf16[3,64,1600]{2,1,0:T(8,128)(2,1)}, bf16[3,64,1600]{2,1,0:T(8,128)(2,1)S(1)}, u32[]{:S(2)}, u32[]{:S(2)}) %collective-permute-start.5) | collective-permute-done | bytes 614432 | tf_op jit(solution)/shard_map/ppermute | solution.py:49
  49.7 0.0 copy-start.2
  49.7 0.0 copy-done.1
  49.7 0.8 %copy-done.2 = bf16[3,64,1600]{2,1,0:T(8,128)(2,1)} copy-done((bf16[3,64,1600]{2,1,0:T(8,128)(2,1)}, bf16[3,64,1600]{2,1,0:T(8,128)(2,1)S(1)}, u32[]{:S(2)}) %copy-start.2) | copy-done | bytes 614424
  50.6 3.3 %shard_map.66 = (bf16[64,2240]{1,0:T(8,128)(2,1)}, bf16[64,2240]{1,0:T(8,128)(2,1)}) custom-call(s32[2]{0:T(128)} %pad_add_fusion.par_ref, f32[3,64,1600]{2,1,0:T(8,128)} %get-tuple-element.10.keep_ref, bf16[3,64,1600]{2,1,0:T(8,128)(2,1)} %copy-done.1, bf16[3,64,1600]{2,1,0:T(8,128)(2,1)} %copy-done.2), custom_call_target="tpu_custom_call" | custom-call | tf_op jit(solution)/shard_map/pallas_call | solution.py:252
  53.8 1.5 %collective-permute-start.6 = (bf16[64,2240]{1,0:T(8,128)(2,1)}, bf16[64,2240]{1,0:T(8,128)(2,1)S(1)}, u32[]{:S(2)}, u32[]{:S(2)}) collective-permute-start(bf16[64,2240]{1,0:T(8,128)(2,1)} %get-tuple-element.13), channel_id=1, source_target_pairs={{0,4},{4,0},{8,12},{12,8},{16,20},{20,16},{24,28},{28,24},{1,5},{5... | collective-permute-start | bytes 860168 | tf_op jit(solution)/shard_map/ppermute | solution.py:49
  55.4 2.5 %collective-permute-start.7 = (bf16[64,2240]{1,0:T(8,128)(2,1)}, bf16[64,2240]{1,0:T(8,128)(2,1)S(1)}, u32[]{:S(2)}, u32[]{:S(2)}) collective-permute-start(bf16[64,2240]{1,0:T(8,128)(2,1)} %get-tuple-element.14), channel_id=1, source_target_pairs={{4,8},{12,16},{20,24},{8,4},{16,12},{24,20},{5,9},{13,17},{21,25},... | collective-permute-start | bytes 860168 | tf_op jit(solution)/shard_map/ppermute | solution.py:49
  57.9 3.1 %shard_map.65.keep_ref = f32[64,3136]{1,0:T(8,128)} custom-call(s32[2]{0:T(128)} %pad_add_fusion.par_ref, f32[3,64,1600]{2,1,0:T(8,128)} %get-tuple-element.10.keep_ref, bf16[3,64,1600]{2,1,0:T(8,128)(2,1)} %copy-done.1, bf16[3,64,1600]{2,1,0:T(8,128)(2,1)} %copy-done.2), custom_call_target="tpu_custom_call" | custom-call | tf_op jit(solution)/shard_map/pallas_call | solution.py:261
  61.0 0.0 collective-permute-done.6.a_hbm
  61.0 0.0 copy-start.7
  61.0 4.1 %collective-permute-done.7.b_hbm = bf16[64,2240]{1,0:T(8,128)(2,1)S(1)} collective-permute-done((bf16[64,2240]{1,0:T(8,128)(2,1)}, bf16[64,2240]{1,0:T(8,128)(2,1)S(1)}, u32[]{:S(2)}, u32[]{:S(2)}) %collective-permute-start.7) | collective-permute-done | bytes 286752 | tf_op jit(solution)/shard_map/ppermute | solution.py:49
  65.1 0.0 copy-done.7
  65.1 0.0 copy-start.8
  65.1 0.7 %copy-done.8 = bf16[64,2240]{1,0:T(8,128)(2,1)} copy-done((bf16[64,2240]{1,0:T(8,128)(2,1)}, bf16[64,2240]{1,0:T(8,128)(2,1)S(1)}, u32[]{:S(2)}) %copy-start.8) | copy-done | bytes 286744
  65.8 3.9 %shard_map.67 = bf16[64,3136]{1,0:T(8,128)(2,1)} custom-call(s32[2]{0:T(128)} %pad_add_fusion.par_ref, f32[64,3136]{1,0:T(8,128)} %shard_map.65.keep_ref, bf16[64,2240]{1,0:T(8,128)(2,1)} %copy-done.7, bf16[64,2240]{1,0:T(8,128)(2,1)} %copy-done.8), custom_call_target="tpu_custom_call" | custom-call | tf_op jit(solution)/shard_map/pallas_call | solution.py:268
  (11 shorter events, 0.2 us)
Async XLA Ops:
  0.0 14.3 %copy-start = (bf16[4,4,64,256]{3,2,1,0:T(8,128)(2,1)S(1)}, bf16[4,4,64,256]{3,2,1,0:T(8,128)(2,1)}, u32[]{:S(2)}) copy-start(bf16[4,4,64,256]{3,2,1,0:T(8,128)(2,1)} %param.9) | copy-start | bytes 1572868
  2.7 8.3 %collective-permute-start = (bf16[272,256]{1,0:T(8,128)(2,1)S(1)}, bf16[272,256]{1,0:T(8,128)(2,1)S(1)}, u32[]{:S(2)}, u32[]{:S(2)}) collective-permute-start(bf16[272,256]{1,0:T(8,128)(2,1)S(1)} %get-tuple-element.29), channel_id=1, source_target_pairs={{4,8},{12,16},{20,24},{8,4},{16,12},{24,20},{5,9},{13,17},{21,25},... | collective-permute-start | bytes 417800 | tf_op jit(solution)/shard_map/ppermute | solution.py:39
  5.9 7.9 %collective-permute-start.1 = (bf16[272,256]{1,0:T(8,128)(2,1)S(1)}, bf16[272,256]{1,0:T(8,128)(2,1)S(1)}, u32[]{:S(2)}, u32[]{:S(2)}) collective-permute-start(bf16[272,256]{1,0:T(8,128)(2,1)S(1)} %get-tuple-element.30), channel_id=1, source_target_pairs={{0,4},{4,0},{8,12},{12,8},{16,20},{20,16},{24,28},{28,24},{1,5},{5... | collective-permute-start | bytes 417800 | tf_op jit(solution)/shard_map/ppermute | solution.py:38
  13.9 7.7 %copy-start.3 = (bf16[272,256]{1,0:T(8,128)(2,1)}, bf16[272,256]{1,0:T(8,128)(2,1)S(1)}, u32[]{:S(2)}) copy-start(bf16[272,256]{1,0:T(8,128)(2,1)S(1)} %get-tuple-element.27.above_ref) | copy-start | bytes 417796
  13.9 7.7 %copy-start.4 = (bf16[272,256]{1,0:T(8,128)(2,1)}, bf16[272,256]{1,0:T(8,128)(2,1)S(1)}, u32[]{:S(2)}) copy-start(bf16[272,256]{1,0:T(8,128)(2,1)S(1)} %get-tuple-element.28.below_ref) | copy-start | bytes 417796
  14.5 7.1 %collective-permute-start.2 = (bf16[400,256]{1,0:T(8,128)(2,1)S(1)}, bf16[400,256]{1,0:T(8,128)(2,1)S(1)}, u32[]{:S(2)}, u32[]{:S(2)}) collective-permute-start(bf16[400,256]{1,0:T(8,128)(2,1)S(1)} %get-tuple-element.25), channel_id=1, source_target_pairs={{1,2},{2,1},{5,6},{6,5},{9,10},{10,9},{13,14},{14,13},{17,18},{18,... | collective-permute-start | bytes 614408 | tf_op jit(solution)/shard_map/ppermute | solution.py:39
  16.5 5.0 %collective-permute-start.3 = (bf16[400,256]{1,0:T(8,128)(2,1)S(1)}, bf16[400,256]{1,0:T(8,128)(2,1)S(1)}, u32[]{:S(2)}, u32[]{:S(2)}) collective-permute-start(bf16[400,256]{1,0:T(8,128)(2,1)S(1)} %get-tuple-element.26), channel_id=1, source_target_pairs={{0,1},{1,0},{2,3},{3,2},{4,5},{5,4},{6,7},{7,6},{8,9},{9,8},{10,11... | collective-permute-start | bytes 614408 | tf_op jit(solution)/shard_map/ppermute | solution.py:38
  21.6 1.0 %copy-start.5 = (bf16[400,256]{1,0:T(8,128)(2,1)}, bf16[400,256]{1,0:T(8,128)(2,1)S(1)}, u32[]{:S(2)}) copy-start(bf16[400,256]{1,0:T(8,128)(2,1)S(1)} %get-tuple-element.23.left_ref) | copy-start | bytes 614404
  21.6 1.0 %copy-start.6 = (bf16[400,256]{1,0:T(8,128)(2,1)}, bf16[400,256]{1,0:T(8,128)(2,1)S(1)}, u32[]{:S(2)}) copy-start(bf16[400,256]{1,0:T(8,128)(2,1)S(1)} %get-tuple-element.24.right_ref) | copy-start | bytes 614404
  37.8 2.3 %collective-permute-start.4 = (bf16[3,64,1600]{2,1,0:T(8,128)(2,1)}, bf16[3,64,1600]{2,1,0:T(8,128)(2,1)S(1)}, u32[]{:S(2)}, u32[]{:S(2)}) collective-permute-start(bf16[3,64,1600]{2,1,0:T(8,128)(2,1)} %get-tuple-element.11), channel_id=1, source_target_pairs={{0,1},{1,0},{2,3},{3,2},{4,5},{5,4},{6,7},{7,6},{8,9},{9,8},{10,11... | collective-permute-start | bytes 1843208 | tf_op jit(solution)/shard_map/ppermute | solution.py:49
  37.8 11.9 %collective-permute-start.5 = (bf16[3,64,1600]{2,1,0:T(8,128)(2,1)}, bf16[3,64,1600]{2,1,0:T(8,128)(2,1)S(1)}, u32[]{:S(2)}, u32[]{:S(2)}) collective-permute-start(bf16[3,64,1600]{2,1,0:T(8,128)(2,1)} %get-tuple-element.12), channel_id=1, source_target_pairs={{1,2},{2,1},{5,6},{6,5},{9,10},{10,9},{13,14},{14,13},{17,18},{18,... | collective-permute-start | bytes 1843208 | tf_op jit(solution)/shard_map/ppermute | solution.py:49
  40.1 9.6 %copy-start.1 = (bf16[3,64,1600]{2,1,0:T(8,128)(2,1)}, bf16[3,64,1600]{2,1,0:T(8,128)(2,1)S(1)}, u32[]{:S(2)}) copy-start(bf16[3,64,1600]{2,1,0:T(8,128)(2,1)S(1)} %collective-permute-done.4.a_ref) | copy-start | bytes 1843204
  49.7 0.8 %copy-start.2 = (bf16[3,64,1600]{2,1,0:T(8,128)(2,1)}, bf16[3,64,1600]{2,1,0:T(8,128)(2,1)S(1)}, u32[]{:S(2)}) copy-start(bf16[3,64,1600]{2,1,0:T(8,128)(2,1)S(1)} %collective-permute-done.5.b_ref) | copy-start | bytes 1843204
  53.8 7.2 %collective-permute-start.6 = (bf16[64,2240]{1,0:T(8,128)(2,1)}, bf16[64,2240]{1,0:T(8,128)(2,1)S(1)}, u32[]{:S(2)}, u32[]{:S(2)}) collective-permute-start(bf16[64,2240]{1,0:T(8,128)(2,1)} %get-tuple-element.13), channel_id=1, source_target_pairs={{0,4},{4,0},{8,12},{12,8},{16,20},{20,16},{24,28},{28,24},{1,5},{5... | collective-permute-start | bytes 860168 | tf_op jit(solution)/shard_map/ppermute | solution.py:49
  55.4 9.7 %collective-permute-start.7 = (bf16[64,2240]{1,0:T(8,128)(2,1)}, bf16[64,2240]{1,0:T(8,128)(2,1)S(1)}, u32[]{:S(2)}, u32[]{:S(2)}) collective-permute-start(bf16[64,2240]{1,0:T(8,128)(2,1)} %get-tuple-element.14), channel_id=1, source_target_pairs={{4,8},{12,16},{20,24},{8,4},{16,12},{24,20},{5,9},{13,17},{21,25},... | collective-permute-start | bytes 860168 | tf_op jit(solution)/shard_map/ppermute | solution.py:49
  61.0 4.1 %copy-start.7 = (bf16[64,2240]{1,0:T(8,128)(2,1)}, bf16[64,2240]{1,0:T(8,128)(2,1)S(1)}, u32[]{:S(2)}) copy-start(bf16[64,2240]{1,0:T(8,128)(2,1)S(1)} %collective-permute-done.6.a_hbm) | copy-start | bytes 860164
  65.1 0.7 %copy-start.8 = (bf16[64,2240]{1,0:T(8,128)(2,1)}, bf16[64,2240]{1,0:T(8,128)(2,1)S(1)}, u32[]{:S(2)}) copy-start(bf16[64,2240]{1,0:T(8,128)(2,1)S(1)} %collective-permute-done.7.b_hbm) | copy-start | bytes 860164

commit v16 on v14

--- a/solution.py
+++ b/solution.py
@@ -171,8 +171,9 @@
     kept = entries[None, None, :] < prolong_counts[:, :, None]
 
     own_codes = prolong_columns
-    hrow = jnp.clip(own_codes // coarse_grid_cols - row_index + 1, 0, HOME - 1)
-    hcol = jnp.clip(own_codes % coarse_grid_cols - col_index + 1, 0, HOME - 1)
+    own_agg = own_codes[..., :1]
+    hrow = jnp.clip(own_codes // coarse_grid_cols - own_agg // coarse_grid_cols + 1, 0, HOME - 1)
+    hcol = jnp.clip(own_codes % coarse_grid_cols - own_agg % coarse_grid_cols + 1, 0, HOME - 1)
     rel = jnp.where(kept, hrow * WIN + hcol, 4 * TRASH)
     home_rc = hcol * HOME + hrow
 

time: 68.6 us -> 69.5 us (1.013)
  other arithmetic: 3.76 us -> 4.78 us
    select_n x0 -> x1, other arithmetic: none -> 0.98 us  [per_device(): own_agg // coarse_grid_cols]
where the time goes in v16:
time: 69.5 us; the launch traced here: 69 us
  Pallas kernels  24 us (35%)
  waiting for transfers between devices  23.1 us (33%)
  starting transfers between devices  12.9 us (19%)
  other arithmetic  4.78 us (7%)
  local copies, waits for them, and re-layouts  3.97 us (6%)
    pallas_call x1, Pallas kernels, per_device(): pl.pallas_call(galerkin_kernel, out_shape=(jax.ShapeDtypeStruct((HOME, B,...  15.5 us
    ppermute x2, waiting for transfers between devices, swap_rounds(): lax.ppermute(second, axis, pairs_b)  13.8 us
    ppermute x2, waiting for transfers between devices, exchange(): got_second = lax.ppermute(jnp.where(even, to_prev, to_next), axis, second)  6.2 us
    ppermute x2, starting transfers between devices, exchange(): got_second = lax.ppermute(jnp.where(even, to_prev, to_next), axis, second)  5.32 us
    ppermute x2, starting transfers between devices, swap_rounds(): lax.ppermute(second, axis, pairs_b)  4.45 us
    pallas_call x1, Pallas kernels, per_device(): pl.pallas_call(fold_cols_send_kernel, out_shape=(jax.ShapeDtypeStruct((B,...  3.23 us
    pallas_call x1, Pallas kernels, per_device(): pl.pallas_call(fold_cols_keep_kernel, out_shape=jax.ShapeDtypeStruct((B,...  3.13 us
    ppermute x2, waiting for transfers between devices, exchange(): got_first = lax.ppermute(jnp.where(even, to_next, to_prev), axis, first)  2.89 us
  transfers between devices with their start and end apart: 8, of which 6 were waited for; matrix products, arithmetic and copies ran while one was open for 3% of the time, Pallas kernels for 5%

profile of v16, /device:TPU:20, one launch (start us, length us, event | category | flops | bytes accessed | tf_op | source)
XLA Modules:
  0.0 69.0 jit_solution(9351522969598760265)
XLA Ops:
  0.0 0.0 copy-start
  0.0 1.0 %fusion.17 = (s32[4,4]{1,0:T(4,128)S(1)}, s32[4,4]{1,0:T(4,128)S(1)}) fusion(s32[4,4,4]{2,1,0:T(4,128)} %param.10), kind=kLoop, calls=%fused_computation.47 | loop fusion | flops 304 | bytes 192 | tf_op jit(solution)/shard_map/jit(floor_divide)/jit(_where)/select_n | solution.py:175
  1.0 1.4 %fusion.30 = (bf16[4,4,4]{2,1,0:T(4,128)(2,1)S(1)}, s32[4,4,4]{2,1,0:T(4,128)S(1)}, s32[4,4,4]{2,1,0:T(4,128)}) fusion(s32[4,4]{1,0:T(4,128)S(1)} %get-tuple-element.16, s32[4,4]{1,0:T(4,128)S(1)} %get-tuple-element.15, s32[4,4,4]{2,1,0:T(4,128)} %param.10, s32[4,4]{1,0:T(4,128)} %param.11), kind=kLoop, calls=%fused_computation.84 | loop fusion | flops 2112 | bytes 1088 | tf_op jit(solution)/shard_map/convert.7
  2.4 0.1 convert_element_type.106
  2.5 0.1 convert_element_type.107
  2.5 1.0 %fusion.31 = (bf16[1,4,64,256]{3,2,1,0:T(8,128)(2,1)S(1)}, bf16[1,4,64,256]{3,2,1,0:T(8,128)(2,1)S(1)}) fusion(bf16[4,4,64,256]{3,2,1,0:T(8,128)(2,1)} %param.9), kind=kLoop, calls=%fused_computation.85 | loop fusion | bytes 524288 | tf_op jit(solution)/shard_map/slice | solution.py:194
  3.5 0.1 broadcast_select_fusion.7
  3.6 3.3 %collective-permute-start = (bf16[272,256]{1,0:T(8,128)(2,1)S(1)}, bf16[272,256]{1,0:T(8,128)(2,1)S(1)}, u32[]{:S(2)}, u32[]{:S(2)}) collective-permute-start(bf16[272,256]{1,0:T(8,128)(2,1)S(1)} %get-tuple-element.31), channel_id=1, source_target_pairs={{4,8},{12,16},{20,24},{8,4},{16,12},{24,20},{5,9},{13,17},{21,25},... | collective-permute-start | bytes 417800 | tf_op jit(solution)/shard_map/ppermute | solution.py:39
  6.9 1.7 %collective-permute-start.1 = (bf16[272,256]{1,0:T(8,128)(2,1)S(1)}, bf16[272,256]{1,0:T(8,128)(2,1)S(1)}, u32[]{:S(2)}, u32[]{:S(2)}) collective-permute-start(bf16[272,256]{1,0:T(8,128)(2,1)S(1)} %get-tuple-element.32), channel_id=1, source_target_pairs={{0,4},{4,0},{8,12},{12,8},{16,20},{20,16},{24,28},{28,24},{1,5},{5... | collective-permute-start | bytes 417800 | tf_op jit(solution)/shard_map/ppermute | solution.py:38
  8.6 1.3 %add_clamp_fusion.pos_ref = s32[4,4,9]{2,1,0:T(4,128)} fusion(s32[4,4,9]{2,1,0:T(4,128)} %param.7, s32[]{:T(128)S(6)} %mul.33, s32[]{:T(128)S(6)} %mul.30), kind=kLoop, calls=%fused_computation.57 | loop fusion | flops 3744 | bytes 1160 | tf_op jit(solution)/shard_map/jit(clip)/min | solution.py:214
  9.9 0.6 pad_add_fusion.par_ref
  10.6 1.3 %collective-permute-done = bf16[272,256]{1,0:T(8,128)(2,1)S(1)} collective-permute-done((bf16[272,256]{1,0:T(8,128)(2,1)S(1)}, bf16[272,256]{1,0:T(8,128)(2,1)S(1)}, u32[]{:S(2)}, u32[]{:S(2)}) %collective-permute-start) | collective-permute-done | bytes 139296 | tf_op jit(solution)/shard_map/ppermute | solution.py:39
  11.9 2.9 %collective-permute-done.1 = bf16[272,256]{1,0:T(8,128)(2,1)S(1)} collective-permute-done((bf16[272,256]{1,0:T(8,128)(2,1)S(1)}, bf16[272,256]{1,0:T(8,128)(2,1)S(1)}, u32[]{:S(2)}, u32[]{:S(2)}) %collective-permute-start.1) | collective-permute-done | bytes 139296 | tf_op jit(solution)/shard_map/ppermute | solution.py:38
  14.8 0.0 copy-start.3
  14.8 0.0 copy-start.4
  14.9 0.1 reshape.196
  15.0 0.1 reshape.197
  15.1 0.1 convert_element_type.112
  15.2 0.1 convert_element_type.113
  15.3 0.0 copy-done
  15.3 0.1 pad_maximum_fusion.2
  15.4 0.1 broadcast_select_fusion.3
  15.4 2.0 %collective-permute-start.2 = (bf16[400,256]{1,0:T(8,128)(2,1)S(1)}, bf16[400,256]{1,0:T(8,128)(2,1)S(1)}, u32[]{:S(2)}, u32[]{:S(2)}) collective-permute-start(bf16[400,256]{1,0:T(8,128)(2,1)S(1)} %get-tuple-element.27), channel_id=1, source_target_pairs={{1,2},{2,1},{5,6},{6,5},{9,10},{10,9},{13,14},{14,13},{17,18},{18,... | collective-permute-start | bytes 614408 | tf_op jit(solution)/shard_map/ppermute | solution.py:39
  17.5 0.1 collective-permute-start.3
  17.6 0.1 add_add_fusion.1
  17.6 4.9 %collective-permute-done.2 = bf16[400,256]{1,0:T(8,128)(2,1)S(1)} collective-permute-done((bf16[400,256]{1,0:T(8,128)(2,1)S(1)}, bf16[400,256]{1,0:T(8,128)(2,1)S(1)}, u32[]{:S(2)}, u32[]{:S(2)}) %collective-permute-start.2) | collective-permute-done | bytes 204832 | tf_op jit(solution)/shard_map/ppermute | solution.py:39
  22.5 0.0 collective-permute-done.3
  22.6 0.0 copy-done.3
  22.6 0.0 copy-done.4
  22.6 0.0 copy-start.5
  22.6 0.0 copy-start.6
  22.6 0.1 reshape.200
  22.7 0.1 reshape.201
  22.8 0.1 fusion.8
  22.9 0.7 min.34.nslot_ref
  23.6 0.0 copy-done.5
  23.6 0.0 copy-done.6
  23.6 15.5 %shard_map.64 = (f32[3,64,1600]{2,1,0:T(8,128)}, bf16[3,64,1600]{2,1,0:T(8,128)(2,1)}, bf16[3,64,1600]{2,1,0:T(8,128)(2,1)}) custom-call(s32[2]{0:T(128)} %pad_add_fusion.par_ref, s32[4,4,9]{2,1,0:T(4,128)} %add_clamp_fusion.pos_ref, s32[144]{0:T(256)} %min.34.nslot_ref, s32[4,4]{1,0:T(4,128)} %count_ref.1, s32[4,4,4]{2,1,0:T(4,128)} %get-tuple-element.33.home_ref, ...), custom_call_target="tpu_custom_call" | custom-call | tf_op jit(solution)/shard_map/pallas_call | solution.py:221
  39.1 0.0 collective-permute-start.4
  39.1 2.0 %collective-permute-start.5 = (bf16[3,64,1600]{2,1,0:T(8,128)(2,1)}, bf16[3,64,1600]{2,1,0:T(8,128)(2,1)S(1)}, u32[]{:S(2)}, u32[]{:S(2)}) collective-permute-start(bf16[3,64,1600]{2,1,0:T(8,128)(2,1)} %get-tuple-element.12), channel_id=1, source_target_pairs={{1,2},{2,1},{5,6},{6,5},{9,10},{10,9},{13,14},{14,13},{17,18},{18,... | collective-permute-start | bytes 1843208 | tf_op jit(solution)/shard_map/ppermute | solution.py:49
  41.1 0.3 collective-permute-done.4.a_ref
  41.4 0.0 copy-start.1
  41.4 9.6 %collective-permute-done.5.b_ref = bf16[3,64,1600]{2,1,0:T(8,128)(2,1)S(1)} collective-permute-done((bf16[3,64,1600]{2,1,0:T(8,128)(2,1)}, bf16[3,64,1600]{2,1,0:T(8,128)(2,1)S(1)}, u32[]{:S(2)}, u32[]{:S(2)}) %collective-permute-start.5) | collective-permute-done | bytes 614432 | tf_op jit(solution)/shard_map/ppermute | solution.py:49
  51.0 0.0 copy-start.2
  51.0 0.0 copy-done.1
  51.0 0.8 %copy-done.2 = bf16[3,64,1600]{2,1,0:T(8,128)(2,1)} copy-done((bf16[3,64,1600]{2,1,0:T(8,128)(2,1)}, bf16[3,64,1600]{2,1,0:T(8,128)(2,1)S(1)}, u32[]{:S(2)}) %copy-start.2) | copy-done | bytes 614424
  51.8 3.2 %shard_map.66 = (bf16[64,2240]{1,0:T(8,128)(2,1)}, bf16[64,2240]{1,0:T(8,128)(2,1)}) custom-call(s32[2]{0:T(128)} %pad_add_fusion.par_ref, f32[3,64,1600]{2,1,0:T(8,128)} %get-tuple-element.10.keep_ref, bf16[3,64,1600]{2,1,0:T(8,128)(2,1)} %copy-done.1, bf16[3,64,1600]{2,1,0:T(8,128)(2,1)} %copy-done.2), custom_call_target="tpu_custom_call" | custom-call | tf_op jit(solution)/shard_map/pallas_call | solution.py:251
  55.1 1.3 %collective-permute-start.6 = (bf16[64,2240]{1,0:T(8,128)(2,1)}, bf16[64,2240]{1,0:T(8,128)(2,1)S(1)}, u32[]{:S(2)}, u32[]{:S(2)}) collective-permute-start(bf16[64,2240]{1,0:T(8,128)(2,1)} %get-tuple-element.13), channel_id=1, source_target_pairs={{0,4},{4,0},{8,12},{12,8},{16,20},{20,16},{24,28},{28,24},{1,5},{5... | collective-permute-start | bytes 860168 | tf_op jit(solution)/shard_map/ppermute | solution.py:49
  56.4 2.4 %collective-permute-start.7 = (bf16[64,2240]{1,0:T(8,128)(2,1)}, bf16[64,2240]{1,0:T(8,128)(2,1)S(1)}, u32[]{:S(2)}, u32[]{:S(2)}) collective-permute-start(bf16[64,2240]{1,0:T(8,128)(2,1)} %get-tuple-element.14), channel_id=1, source_target_pairs={{4,8},{12,16},{20,24},{8,4},{16,12},{24,20},{5,9},{13,17},{21,25},... | collective-permute-start | bytes 860168 | tf_op jit(solution)/shard_map/ppermute | solution.py:49
  58.9 3.1 %shard_map.65.keep_ref = f32[64,3136]{1,0:T(8,128)} custom-call(s32[2]{0:T(128)} %pad_add_fusion.par_ref, f32[3,64,1600]{2,1,0:T(8,128)} %get-tuple-element.10.keep_ref, bf16[3,64,1600]{2,1,0:T(8,128)(2,1)} %copy-done.1, bf16[3,64,1600]{2,1,0:T(8,128)(2,1)} %copy-done.2), custom_call_target="tpu_custom_call" | custom-call | tf_op jit(solution)/shard_map/pallas_call | solution.py:260
  62.0 0.0 collective-permute-done.6.a_ref
  62.0 0.0 copy-start.7
  62.0 4.1 %collective-permute-done.7.b_ref = bf16[64,2240]{1,0:T(8,128)(2,1)S(1)} collective-permute-done((bf16[64,2240]{1,0:T(8,128)(2,1)}, bf16[64,2240]{1,0:T(8,128)(2,1)S(1)}, u32[]{:S(2)}, u32[]{:S(2)}) %collective-permute-start.7) | collective-permute-done | bytes 286752 | tf_op jit(solution)/shard_map/ppermute | solution.py:49
  66.1 0.0 copy-done.7
  66.1 0.0 copy-start.8
  66.1 0.7 %copy-done.8 = bf16[64,2240]{1,0:T(8,128)(2,1)} copy-done((bf16[64,2240]{1,0:T(8,128)(2,1)}, bf16[64,2240]{1,0:T(8,128)(2,1)S(1)}, u32[]{:S(2)}) %copy-start.8) | copy-done | bytes 286744
  66.8 2.2 %shard_map.67 = bf16[64,3136]{1,0:T(8,128)(2,1)} custom-call(s32[2]{0:T(128)} %pad_add_fusion.par_ref, f32[64,3136]{1,0:T(8,128)} %shard_map.65.keep_ref, bf16[64,2240]{1,0:T(8,128)(2,1)} %copy-done.7, bf16[64,2240]{1,0:T(8,128)(2,1)} %copy-done.8), custom_call_target="tpu_custom_call" | custom-call | tf_op jit(solution)/shard_map/pallas_call | solution.py:267
  (11 shorter events, 0.2 us)
Async XLA Ops:
  0.0 15.3 %copy-start = (bf16[4,4,64,256]{3,2,1,0:T(8,128)(2,1)S(1)}, bf16[4,4,64,256]{3,2,1,0:T(8,128)(2,1)}, u32[]{:S(2)}) copy-start(bf16[4,4,64,256]{3,2,1,0:T(8,128)(2,1)} %param.9) | copy-start | bytes 1572868
  3.6 8.3 %collective-permute-start = (bf16[272,256]{1,0:T(8,128)(2,1)S(1)}, bf16[272,256]{1,0:T(8,128)(2,1)S(1)}, u32[]{:S(2)}, u32[]{:S(2)}) collective-permute-start(bf16[272,256]{1,0:T(8,128)(2,1)S(1)} %get-tuple-element.31), channel_id=1, source_target_pairs={{4,8},{12,16},{20,24},{8,4},{16,12},{24,20},{5,9},{13,17},{21,25},... | collective-permute-start | bytes 417800 | tf_op jit(solution)/shard_map/ppermute | solution.py:39
  6.9 7.9 %collective-permute-start.1 = (bf16[272,256]{1,0:T(8,128)(2,1)S(1)}, bf16[272,256]{1,0:T(8,128)(2,1)S(1)}, u32[]{:S(2)}, u32[]{:S(2)}) collective-permute-start(bf16[272,256]{1,0:T(8,128)(2,1)S(1)} %get-tuple-element.32), channel_id=1, source_target_pairs={{0,4},{4,0},{8,12},{12,8},{16,20},{20,16},{24,28},{28,24},{1,5},{5... | collective-permute-start | bytes 417800 | tf_op jit(solution)/shard_map/ppermute | solution.py:38
  14.8 7.7 %copy-start.3 = (bf16[272,256]{1,0:T(8,128)(2,1)}, bf16[272,256]{1,0:T(8,128)(2,1)S(1)}, u32[]{:S(2)}) copy-start(bf16[272,256]{1,0:T(8,128)(2,1)S(1)} %get-tuple-element.29.above_ref) | copy-start | bytes 417796
  14.8 7.7 %copy-start.4 = (bf16[272,256]{1,0:T(8,128)(2,1)}, bf16[272,256]{1,0:T(8,128)(2,1)S(1)}, u32[]{:S(2)}) copy-start(bf16[272,256]{1,0:T(8,128)(2,1)S(1)} %get-tuple-element.30.below_ref) | copy-start | bytes 417796
  15.4 7.1 %collective-permute-start.2 = (bf16[400,256]{1,0:T(8,128)(2,1)S(1)}, bf16[400,256]{1,0:T(8,128)(2,1)S(1)}, u32[]{:S(2)}, u32[]{:S(2)}) collective-permute-start(bf16[400,256]{1,0:T(8,128)(2,1)S(1)} %get-tuple-element.27), channel_id=1, source_target_pairs={{1,2},{2,1},{5,6},{6,5},{9,10},{10,9},{13,14},{14,13},{17,18},{18,... | collective-permute-start | bytes 614408 | tf_op jit(solution)/shard_map/ppermute | solution.py:39
  17.5 5.0 %collective-permute-start.3 = (bf16[400,256]{1,0:T(8,128)(2,1)S(1)}, bf16[400,256]{1,0:T(8,128)(2,1)S(1)}, u32[]{:S(2)}, u32[]{:S(2)}) collective-permute-start(bf16[400,256]{1,0:T(8,128)(2,1)S(1)} %get-tuple-element.28), channel_id=1, source_target_pairs={{0,1},{1,0},{2,3},{3,2},{4,5},{5,4},{6,7},{7,6},{8,9},{9,8},{10,11... | collective-permute-start | bytes 614408 | tf_op jit(solution)/shard_map/ppermute | solution.py:38
  22.6 1.0 %copy-start.5 = (bf16[400,256]{1,0:T(8,128)(2,1)}, bf16[400,256]{1,0:T(8,128)(2,1)S(1)}, u32[]{:S(2)}) copy-start(bf16[400,256]{1,0:T(8,128)(2,1)S(1)} %get-tuple-element.25.left_ref) | copy-start | bytes 614404
  22.6 1.0 %copy-start.6 = (bf16[400,256]{1,0:T(8,128)(2,1)}, bf16[400,256]{1,0:T(8,128)(2,1)S(1)}, u32[]{:S(2)}) copy-start(bf16[400,256]{1,0:T(8,128)(2,1)S(1)} %get-tuple-element.26.right_ref) | copy-start | bytes 614404
  39.1 2.3 %collective-permute-start.4 = (bf16[3,64,1600]{2,1,0:T(8,128)(2,1)}, bf16[3,64,1600]{2,1,0:T(8,128)(2,1)S(1)}, u32[]{:S(2)}, u32[]{:S(2)}) collective-permute-start(bf16[3,64,1600]{2,1,0:T(8,128)(2,1)} %get-tuple-element.11), channel_id=1, source_target_pairs={{0,1},{1,0},{2,3},{3,2},{4,5},{5,4},{6,7},{7,6},{8,9},{9,8},{10,11... | collective-permute-start | bytes 1843208 | tf_op jit(solution)/shard_map/ppermute | solution.py:49
  39.1 11.9 %collective-permute-start.5 = (bf16[3,64,1600]{2,1,0:T(8,128)(2,1)}, bf16[3,64,1600]{2,1,0:T(8,128)(2,1)S(1)}, u32[]{:S(2)}, u32[]{:S(2)}) collective-permute-start(bf16[3,64,1600]{2,1,0:T(8,128)(2,1)} %get-tuple-element.12), channel_id=1, source_target_pairs={{1,2},{2,1},{5,6},{6,5},{9,10},{10,9},{13,14},{14,13},{17,18},{18,... | collective-permute-start | bytes 1843208 | tf_op jit(solution)/shard_map/ppermute | solution.py:49
  41.4 9.6 %copy-start.1 = (bf16[3,64,1600]{2,1,0:T(8,128)(2,1)}, bf16[3,64,1600]{2,1,0:T(8,128)(2,1)S(1)}, u32[]{:S(2)}) copy-start(bf16[3,64,1600]{2,1,0:T(8,128)(2,1)S(1)} %collective-permute-done.4.a_ref) | copy-start | bytes 1843204
  51.0 0.8 %copy-start.2 = (bf16[3,64,1600]{2,1,0:T(8,128)(2,1)}, bf16[3,64,1600]{2,1,0:T(8,128)(2,1)S(1)}, u32[]{:S(2)}) copy-start(bf16[3,64,1600]{2,1,0:T(8,128)(2,1)S(1)} %collective-permute-done.5.b_ref) | copy-start | bytes 1843204
  55.1 6.9 %collective-permute-start.6 = (bf16[64,2240]{1,0:T(8,128)(2,1)}, bf16[64,2240]{1,0:T(8,128)(2,1)S(1)}, u32[]{:S(2)}, u32[]{:S(2)}) collective-permute-start(bf16[64,2240]{1,0:T(8,128)(2,1)} %get-tuple-element.13), channel_id=1, source_target_pairs={{0,4},{4,0},{8,12},{12,8},{16,20},{20,16},{24,28},{28,24},{1,5},{5... | collective-permute-start | bytes 860168 | tf_op jit(solution)/shard_map/ppermute | solution.py:49
  56.4 9.7 %collective-permute-start.7 = (bf16[64,2240]{1,0:T(8,128)(2,1)}, bf16[64,2240]{1,0:T(8,128)(2,1)S(1)}, u32[]{:S(2)}, u32[]{:S(2)}) collective-permute-start(bf16[64,2240]{1,0:T(8,128)(2,1)} %get-tuple-element.14), channel_id=1, source_target_pairs={{4,8},{12,16},{20,24},{8,4},{16,12},{24,20},{5,9},{13,17},{21,25},... | collective-permute-start | bytes 860168 | tf_op jit(solution)/shard_map/ppermute | solution.py:49
  62.0 4.1 %copy-start.7 = (bf16[64,2240]{1,0:T(8,128)(2,1)}, bf16[64,2240]{1,0:T(8,128)(2,1)S(1)}, u32[]{:S(2)}) copy-start(bf16[64,2240]{1,0:T(8,128)(2,1)S(1)} %collective-permute-done.6.a_ref) | copy-start | bytes 860164
  66.1 0.7 %copy-start.8 = (bf16[64,2240]{1,0:T(8,128)(2,1)}, bf16[64,2240]{1,0:T(8,128)(2,1)S(1)}, u32[]{:S(2)}) copy-start(bf16[64,2240]{1,0:T(8,128)(2,1)S(1)} %collective-permute-done.7.b_ref) | copy-start | bytes 860164

commit v17 on v14

--- a/solution.py
+++ b/solution.py
@@ -89,10 +89,10 @@
 
     dpt_ref[...] = jnp.zeros(dpt_ref.shape, jnp.float32)
     for i in range(patches):
-        flipped = own_ref[i].astype(jnp.float32).T
+        flipped = own_ref[i].T
         for p in range(KP):
             start = pl.multiple_of(home_ref[i // AG, i % AG, p] * B, B)
-            dpt_ref[pl.ds(start, B), i * B:(i + 1) * B] += flipped[p * B:(p + 1) * B, :]
+            dpt_ref[pl.ds(start, B), i * B:(i + 1) * B] += flipped[p * B:(p + 1) * B, :].astype(jnp.float32)
 
     prod = prod_ref[...]
     group = HOME * B

time: 68.6 us -> 68.5 us (level)
  transfers between devices with their start and end apart: 8 -> 8, of which waited for: 6 -> 7; matrix products, arithmetic and copies ran while one was open for 3% -> 3% of each run, Pallas kernels for 5% -> 5%
where the time goes in v17:
time: 68.5 us; the launch traced here: 68.1 us
  Pallas kernels  23.9 us (35%)
  waiting for transfers between devices  23.5 us (34%)
  starting transfers between devices  12.7 us (19%)
  local copies, waits for them, and re-layouts  3.97 us (6%)
  other arithmetic  3.76 us (5%)
    pallas_call x1, Pallas kernels, per_device(): pl.pallas_call(galerkin_kernel, out_shape=(jax.ShapeDtypeStruct((HOME, B,...  15.4 us
    ppermute x2, waiting for transfers between devices, swap_rounds(): lax.ppermute(second, axis, pairs_b)  13.8 us
    ppermute x2, waiting for transfers between devices, exchange(): got_second = lax.ppermute(jnp.where(even, to_prev, to_next), axis, second)  6.29 us
    ppermute x2, starting transfers between devices, exchange(): got_second = lax.ppermute(jnp.where(even, to_prev, to_next), axis, second)  5.32 us
    ppermute x2, starting transfers between devices, swap_rounds(): lax.ppermute(second, axis, pairs_b)  4.19 us
    pallas_call x1, Pallas kernels, per_device(): pl.pallas_call(fold_cols_send_kernel, out_shape=(jax.ShapeDtypeStruct((B,...  3.25 us
    pallas_call x1, Pallas kernels, per_device(): pl.pallas_call(fold_cols_keep_kernel, out_shape=jax.ShapeDtypeStruct((B,...  3.1 us
    ppermute x2, waiting for transfers between devices, exchange(): got_first = lax.ppermute(jnp.where(even, to_next, to_prev), axis, first)  2.89 us
  transfers between devices with their start and end apart: 8, of which 7 were waited for; matrix products, arithmetic and copies ran while one was open for 3% of the time, Pallas kernels for 5%

profile of v17, /device:TPU:20, one launch (start us, length us, event | category | flops | bytes accessed | tf_op | source)
XLA Modules:
  0.0 68.1 jit_solution(3576771689596645663)
XLA Ops:
  0.0 0.0 copy-start
  0.0 1.4 %fusion.27 = (bf16[4,4,4]{2,1,0:T(4,128)(2,1)S(1)}, s32[4,4,4]{2,1,0:T(4,128)S(1)}, s32[4,4,4]{2,1,0:T(4,128)}) fusion(s32[]{:T(128)S(6)} %axis_index.14, s32[]{:T(128)S(6)} %axis_index.33, s32[4,4,4]{2,1,0:T(4,128)} %param.10, s32[4,4]{1,0:T(4,128)} %param.11), kind=kLoop, calls=%fused_computation.73 | loop fusion | flops 2112 | bytes 968 | tf_op jit(solution)/shard_map/convert.7
  1.4 0.1 convert_element_type.106
  1.5 0.1 convert_element_type.107
  1.6 1.0 %fusion.28 = (bf16[1,4,64,256]{3,2,1,0:T(8,128)(2,1)S(1)}, bf16[1,4,64,256]{3,2,1,0:T(8,128)(2,1)S(1)}) fusion(bf16[4,4,64,256]{3,2,1,0:T(8,128)(2,1)} %param.9), kind=kLoop, calls=%fused_computation.74 | loop fusion | bytes 524288 | tf_op jit(solution)/shard_map/slice | solution.py:193
  2.6 0.1 broadcast_select_fusion.7
  2.7 3.3 %collective-permute-start = (bf16[272,256]{1,0:T(8,128)(2,1)S(1)}, bf16[272,256]{1,0:T(8,128)(2,1)S(1)}, u32[]{:S(2)}, u32[]{:S(2)}) collective-permute-start(bf16[272,256]{1,0:T(8,128)(2,1)S(1)} %get-tuple-element.29), channel_id=1, source_target_pairs={{4,8},{12,16},{20,24},{8,4},{16,12},{24,20},{5,9},{13,17},{21,25},... | collective-permute-start | bytes 417800 | tf_op jit(solution)/shard_map/ppermute | solution.py:39
  5.9 1.7 %collective-permute-start.1 = (bf16[272,256]{1,0:T(8,128)(2,1)S(1)}, bf16[272,256]{1,0:T(8,128)(2,1)S(1)}, u32[]{:S(2)}, u32[]{:S(2)}) collective-permute-start(bf16[272,256]{1,0:T(8,128)(2,1)S(1)} %get-tuple-element.30), channel_id=1, source_target_pairs={{0,4},{4,0},{8,12},{12,8},{16,20},{20,16},{24,28},{28,24},{1,5},{5... | collective-permute-start | bytes 417800 | tf_op jit(solution)/shard_map/ppermute | solution.py:38
  7.7 1.3 %add_clamp_fusion.pos_ref = s32[4,4,9]{2,1,0:T(4,128)} fusion(s32[4,4,9]{2,1,0:T(4,128)} %param.7, s32[]{:T(128)S(6)} %mul.33, s32[]{:T(128)S(6)} %mul.30), kind=kLoop, calls=%fused_computation.49 | loop fusion | flops 3744 | bytes 1160 | tf_op jit(solution)/shard_map/jit(clip)/min | solution.py:213
  9.0 0.6 pad_add_fusion.par_ref
  9.5 1.4 %collective-permute-done = bf16[272,256]{1,0:T(8,128)(2,1)S(1)} collective-permute-done((bf16[272,256]{1,0:T(8,128)(2,1)S(1)}, bf16[272,256]{1,0:T(8,128)(2,1)S(1)}, u32[]{:S(2)}, u32[]{:S(2)}) %collective-permute-start) | collective-permute-done | bytes 139296 | tf_op jit(solution)/shard_map/ppermute | solution.py:39
  11.0 2.9 %collective-permute-done.1 = bf16[272,256]{1,0:T(8,128)(2,1)S(1)} collective-permute-done((bf16[272,256]{1,0:T(8,128)(2,1)S(1)}, bf16[272,256]{1,0:T(8,128)(2,1)S(1)}, u32[]{:S(2)}, u32[]{:S(2)}) %collective-permute-start.1) | collective-permute-done | bytes 139296 | tf_op jit(solution)/shard_map/ppermute | solution.py:38
  13.9 0.0 copy-start.3
  13.9 0.0 copy-start.4
  14.0 0.1 reshape.196
  14.0 0.1 reshape.197
  14.2 0.1 convert_element_type.112
  14.3 0.1 convert_element_type.113
  14.3 0.0 copy-done
  14.4 0.1 pad_maximum_fusion.2
  14.4 0.1 broadcast_select_fusion.3
  14.5 2.0 %collective-permute-start.2 = (bf16[400,256]{1,0:T(8,128)(2,1)S(1)}, bf16[400,256]{1,0:T(8,128)(2,1)S(1)}, u32[]{:S(2)}, u32[]{:S(2)}) collective-permute-start(bf16[400,256]{1,0:T(8,128)(2,1)S(1)} %get-tuple-element.25), channel_id=1, source_target_pairs={{1,2},{2,1},{5,6},{6,5},{9,10},{10,9},{13,14},{14,13},{17,18},{18,... | collective-permute-start | bytes 614408 | tf_op jit(solution)/shard_map/ppermute | solution.py:39
  16.5 0.1 collective-permute-start.3
  16.6 0.1 add_add_fusion.1
  16.7 4.9 %collective-permute-done.2 = bf16[400,256]{1,0:T(8,128)(2,1)S(1)} collective-permute-done((bf16[400,256]{1,0:T(8,128)(2,1)S(1)}, bf16[400,256]{1,0:T(8,128)(2,1)S(1)}, u32[]{:S(2)}, u32[]{:S(2)}) %collective-permute-start.2) | collective-permute-done | bytes 204832 | tf_op jit(solution)/shard_map/ppermute | solution.py:39
  21.6 0.0 collective-permute-done.3
  21.6 0.0 copy-done.3
  21.6 0.0 copy-done.4
  21.6 0.0 copy-start.5
  21.6 0.0 copy-start.6
  21.7 0.1 reshape.200
  21.8 0.1 reshape.201
  21.9 0.1 fusion.8
  21.9 0.7 min.34.nslot_ref
  22.6 0.0 copy-done.5
  22.6 0.0 copy-done.6
  22.6 15.4 %shard_map.64 = (f32[3,64,1600]{2,1,0:T(8,128)}, bf16[3,64,1600]{2,1,0:T(8,128)(2,1)}, bf16[3,64,1600]{2,1,0:T(8,128)(2,1)}) custom-call(s32[2]{0:T(128)} %pad_add_fusion.par_ref, s32[4,4,9]{2,1,0:T(4,128)} %add_clamp_fusion.pos_ref, s32[144]{0:T(256)} %min.34.nslot_ref, s32[4,4]{1,0:T(4,128)} %count_ref.1, s32[4,4,4]{2,1,0:T(4,128)} %get-tuple-element.31.home_ref, ...), custom_call_target="tpu_custom_call" | custom-call | tf_op jit(solution)/shard_map/pallas_call | solution.py:220
  38.0 0.0 collective-permute-start.4
  38.0 1.9 %collective-permute-start.5 = (bf16[3,64,1600]{2,1,0:T(8,128)(2,1)}, bf16[3,64,1600]{2,1,0:T(8,128)(2,1)S(1)}, u32[]{:S(2)}, u32[]{:S(2)}) collective-permute-start(bf16[3,64,1600]{2,1,0:T(8,128)(2,1)} %get-tuple-element.12), channel_id=1, source_target_pairs={{1,2},{2,1},{5,6},{6,5},{9,10},{10,9},{13,14},{14,13},{17,18},{18,... | collective-permute-start | bytes 1843208 | tf_op jit(solution)/shard_map/ppermute | solution.py:49
  39.9 0.4 collective-permute-done.4.a_ref
  40.3 0.0 copy-start.1
  40.3 9.6 %collective-permute-done.5.b_ref = bf16[3,64,1600]{2,1,0:T(8,128)(2,1)S(1)} collective-permute-done((bf16[3,64,1600]{2,1,0:T(8,128)(2,1)}, bf16[3,64,1600]{2,1,0:T(8,128)(2,1)S(1)}, u32[]{:S(2)}, u32[]{:S(2)}) %collective-permute-start.5) | collective-permute-done | bytes 614432 | tf_op jit(solution)/shard_map/ppermute | solution.py:49
  50.0 0.0 copy-start.2
  50.0 0.0 copy-done.1
  50.0 0.8 %copy-done.2 = bf16[3,64,1600]{2,1,0:T(8,128)(2,1)} copy-done((bf16[3,64,1600]{2,1,0:T(8,128)(2,1)}, bf16[3,64,1600]{2,1,0:T(8,128)(2,1)S(1)}, u32[]{:S(2)}) %copy-start.2) | copy-done | bytes 614424
  50.8 3.3 %shard_map.66 = (bf16[64,2240]{1,0:T(8,128)(2,1)}, bf16[64,2240]{1,0:T(8,128)(2,1)}) custom-call(s32[2]{0:T(128)} %pad_add_fusion.par_ref, f32[3,64,1600]{2,1,0:T(8,128)} %get-tuple-element.10.keep_ref, bf16[3,64,1600]{2,1,0:T(8,128)(2,1)} %copy-done.1, bf16[3,64,1600]{2,1,0:T(8,128)(2,1)} %copy-done.2), custom_call_target="tpu_custom_call" | custom-call | tf_op jit(solution)/shard_map/pallas_call | solution.py:250
  54.0 1.4 %collective-permute-start.6 = (bf16[64,2240]{1,0:T(8,128)(2,1)}, bf16[64,2240]{1,0:T(8,128)(2,1)S(1)}, u32[]{:S(2)}, u32[]{:S(2)}) collective-permute-start(bf16[64,2240]{1,0:T(8,128)(2,1)} %get-tuple-element.13), channel_id=1, source_target_pairs={{0,4},{4,0},{8,12},{12,8},{16,20},{20,16},{24,28},{28,24},{1,5},{5... | collective-permute-start | bytes 860168 | tf_op jit(solution)/shard_map/ppermute | solution.py:49
  55.5 2.3 %collective-permute-start.7 = (bf16[64,2240]{1,0:T(8,128)(2,1)}, bf16[64,2240]{1,0:T(8,128)(2,1)S(1)}, u32[]{:S(2)}, u32[]{:S(2)}) collective-permute-start(bf16[64,2240]{1,0:T(8,128)(2,1)} %get-tuple-element.14), channel_id=1, source_target_pairs={{4,8},{12,16},{20,24},{8,4},{16,12},{24,20},{5,9},{13,17},{21,25},... | collective-permute-start | bytes 860168 | tf_op jit(solution)/shard_map/ppermute | solution.py:49
  57.7 3.1 %shard_map.65.keep_ref = f32[64,3136]{1,0:T(8,128)} custom-call(s32[2]{0:T(128)} %pad_add_fusion.par_ref, f32[3,64,1600]{2,1,0:T(8,128)} %get-tuple-element.10.keep_ref, bf16[3,64,1600]{2,1,0:T(8,128)(2,1)} %copy-done.1, bf16[3,64,1600]{2,1,0:T(8,128)(2,1)} %copy-done.2), custom_call_target="tpu_custom_call" | custom-call | tf_op jit(solution)/shard_map/pallas_call | solution.py:259
  60.8 0.1 collective-permute-done.6.a_ref
  61.0 0.0 copy-start.7
  61.0 4.2 %collective-permute-done.7.b_ref = bf16[64,2240]{1,0:T(8,128)(2,1)S(1)} collective-permute-done((bf16[64,2240]{1,0:T(8,128)(2,1)}, bf16[64,2240]{1,0:T(8,128)(2,1)S(1)}, u32[]{:S(2)}, u32[]{:S(2)}) %collective-permute-start.7) | collective-permute-done | bytes 286752 | tf_op jit(solution)/shard_map/ppermute | solution.py:49
  65.2 0.0 copy-done.7
  65.2 0.0 copy-start.8
  65.2 0.7 %copy-done.8 = bf16[64,2240]{1,0:T(8,128)(2,1)} copy-done((bf16[64,2240]{1,0:T(8,128)(2,1)}, bf16[64,2240]{1,0:T(8,128)(2,1)S(1)}, u32[]{:S(2)}) %copy-start.8) | copy-done | bytes 286744
  65.9 2.2 %shard_map.67 = bf16[64,3136]{1,0:T(8,128)(2,1)} custom-call(s32[2]{0:T(128)} %pad_add_fusion.par_ref, f32[64,3136]{1,0:T(8,128)} %shard_map.65.keep_ref, bf16[64,2240]{1,0:T(8,128)(2,1)} %copy-done.7, bf16[64,2240]{1,0:T(8,128)(2,1)} %copy-done.8), custom_call_target="tpu_custom_call" | custom-call | tf_op jit(solution)/shard_map/pallas_call | solution.py:266
  (11 shorter events, 0.2 us)
Async XLA Ops:
  0.0 14.3 %copy-start = (bf16[4,4,64,256]{3,2,1,0:T(8,128)(2,1)S(1)}, bf16[4,4,64,256]{3,2,1,0:T(8,128)(2,1)}, u32[]{:S(2)}) copy-start(bf16[4,4,64,256]{3,2,1,0:T(8,128)(2,1)} %param.9) | copy-start | bytes 1572868
  2.7 8.3 %collective-permute-start = (bf16[272,256]{1,0:T(8,128)(2,1)S(1)}, bf16[272,256]{1,0:T(8,128)(2,1)S(1)}, u32[]{:S(2)}, u32[]{:S(2)}) collective-permute-start(bf16[272,256]{1,0:T(8,128)(2,1)S(1)} %get-tuple-element.29), channel_id=1, source_target_pairs={{4,8},{12,16},{20,24},{8,4},{16,12},{24,20},{5,9},{13,17},{21,25},... | collective-permute-start | bytes 417800 | tf_op jit(solution)/shard_map/ppermute | solution.py:39
  5.9 7.9 %collective-permute-start.1 = (bf16[272,256]{1,0:T(8,128)(2,1)S(1)}, bf16[272,256]{1,0:T(8,128)(2,1)S(1)}, u32[]{:S(2)}, u32[]{:S(2)}) collective-permute-start(bf16[272,256]{1,0:T(8,128)(2,1)S(1)} %get-tuple-element.30), channel_id=1, source_target_pairs={{0,4},{4,0},{8,12},{12,8},{16,20},{20,16},{24,28},{28,24},{1,5},{5... | collective-permute-start | bytes 417800 | tf_op jit(solution)/shard_map/ppermute | solution.py:38
  13.9 7.7 %copy-start.3 = (bf16[272,256]{1,0:T(8,128)(2,1)}, bf16[272,256]{1,0:T(8,128)(2,1)S(1)}, u32[]{:S(2)}) copy-start(bf16[272,256]{1,0:T(8,128)(2,1)S(1)} %get-tuple-element.27.above_ref) | copy-start | bytes 417796
  13.9 7.7 %copy-start.4 = (bf16[272,256]{1,0:T(8,128)(2,1)}, bf16[272,256]{1,0:T(8,128)(2,1)S(1)}, u32[]{:S(2)}) copy-start(bf16[272,256]{1,0:T(8,128)(2,1)S(1)} %get-tuple-element.28.below_ref) | copy-start | bytes 417796
  14.5 7.1 %collective-permute-start.2 = (bf16[400,256]{1,0:T(8,128)(2,1)S(1)}, bf16[400,256]{1,0:T(8,128)(2,1)S(1)}, u32[]{:S(2)}, u32[]{:S(2)}) collective-permute-start(bf16[400,256]{1,0:T(8,128)(2,1)S(1)} %get-tuple-element.25), channel_id=1, source_target_pairs={{1,2},{2,1},{5,6},{6,5},{9,10},{10,9},{13,14},{14,13},{17,18},{18,... | collective-permute-start | bytes 614408 | tf_op jit(solution)/shard_map/ppermute | solution.py:39
  16.5 5.0 %collective-permute-start.3 = (bf16[400,256]{1,0:T(8,128)(2,1)S(1)}, bf16[400,256]{1,0:T(8,128)(2,1)S(1)}, u32[]{:S(2)}, u32[]{:S(2)}) collective-permute-start(bf16[400,256]{1,0:T(8,128)(2,1)S(1)} %get-tuple-element.26), channel_id=1, source_target_pairs={{0,1},{1,0},{2,3},{3,2},{4,5},{5,4},{6,7},{7,6},{8,9},{9,8},{10,11... | collective-permute-start | bytes 614408 | tf_op jit(solution)/shard_map/ppermute | solution.py:38
  21.6 1.0 %copy-start.5 = (bf16[400,256]{1,0:T(8,128)(2,1)}, bf16[400,256]{1,0:T(8,128)(2,1)S(1)}, u32[]{:S(2)}) copy-start(bf16[400,256]{1,0:T(8,128)(2,1)S(1)} %get-tuple-element.23.left_ref) | copy-start | bytes 614404
  21.6 1.0 %copy-start.6 = (bf16[400,256]{1,0:T(8,128)(2,1)}, bf16[400,256]{1,0:T(8,128)(2,1)S(1)}, u32[]{:S(2)}) copy-start(bf16[400,256]{1,0:T(8,128)(2,1)S(1)} %get-tuple-element.24.right_ref) | copy-start | bytes 614404
  38.0 2.3 %collective-permute-start.4 = (bf16[3,64,1600]{2,1,0:T(8,128)(2,1)}, bf16[3,64,1600]{2,1,0:T(8,128)(2,1)S(1)}, u32[]{:S(2)}, u32[]{:S(2)}) collective-permute-start(bf16[3,64,1600]{2,1,0:T(8,128)(2,1)} %get-tuple-element.11), channel_id=1, source_target_pairs={{0,1},{1,0},{2,3},{3,2},{4,5},{5,4},{6,7},{7,6},{8,9},{9,8},{10,11... | collective-permute-start | bytes 1843208 | tf_op jit(solution)/shard_map/ppermute | solution.py:49
  38.0 11.9 %collective-permute-start.5 = (bf16[3,64,1600]{2,1,0:T(8,128)(2,1)}, bf16[3,64,1600]{2,1,0:T(8,128)(2,1)S(1)}, u32[]{:S(2)}, u32[]{:S(2)}) collective-permute-start(bf16[3,64,1600]{2,1,0:T(8,128)(2,1)} %get-tuple-element.12), channel_id=1, source_target_pairs={{1,2},{2,1},{5,6},{6,5},{9,10},{10,9},{13,14},{14,13},{17,18},{18,... | collective-permute-start | bytes 1843208 | tf_op jit(solution)/shard_map/ppermute | solution.py:49
  40.3 9.6 %copy-start.1 = (bf16[3,64,1600]{2,1,0:T(8,128)(2,1)}, bf16[3,64,1600]{2,1,0:T(8,128)(2,1)S(1)}, u32[]{:S(2)}) copy-start(bf16[3,64,1600]{2,1,0:T(8,128)(2,1)S(1)} %collective-permute-done.4.a_ref) | copy-start | bytes 1843204
  50.0 0.8 %copy-start.2 = (bf16[3,64,1600]{2,1,0:T(8,128)(2,1)}, bf16[3,64,1600]{2,1,0:T(8,128)(2,1)S(1)}, u32[]{:S(2)}) copy-start(bf16[3,64,1600]{2,1,0:T(8,128)(2,1)S(1)} %collective-permute-done.5.b_ref) | copy-start | bytes 1843204
  54.0 6.9 %collective-permute-start.6 = (bf16[64,2240]{1,0:T(8,128)(2,1)}, bf16[64,2240]{1,0:T(8,128)(2,1)S(1)}, u32[]{:S(2)}, u32[]{:S(2)}) collective-permute-start(bf16[64,2240]{1,0:T(8,128)(2,1)} %get-tuple-element.13), channel_id=1, source_target_pairs={{0,4},{4,0},{8,12},{12,8},{16,20},{20,16},{24,28},{28,24},{1,5},{5... | collective-permute-start | bytes 860168 | tf_op jit(solution)/shard_map/ppermute | solution.py:49
  55.5 9.7 %collective-permute-start.7 = (bf16[64,2240]{1,0:T(8,128)(2,1)}, bf16[64,2240]{1,0:T(8,128)(2,1)S(1)}, u32[]{:S(2)}, u32[]{:S(2)}) collective-permute-start(bf16[64,2240]{1,0:T(8,128)(2,1)} %get-tuple-element.14), channel_id=1, source_target_pairs={{4,8},{12,16},{20,24},{8,4},{16,12},{24,20},{5,9},{13,17},{21,25},... | collective-permute-start | bytes 860168 | tf_op jit(solution)/shard_map/ppermute | solution.py:49
  61.0 4.2 %copy-start.7 = (bf16[64,2240]{1,0:T(8,128)(2,1)}, bf16[64,2240]{1,0:T(8,128)(2,1)S(1)}, u32[]{:S(2)}) copy-start(bf16[64,2240]{1,0:T(8,128)(2,1)S(1)} %collective-permute-done.6.a_ref) | copy-start | bytes 860164
  65.2 0.7 %copy-start.8 = (bf16[64,2240]{1,0:T(8,128)(2,1)}, bf16[64,2240]{1,0:T(8,128)(2,1)S(1)}, u32[]{:S(2)}) copy-start(bf16[64,2240]{1,0:T(8,128)(2,1)S(1)} %collective-permute-done.7.b_ref) | copy-start | bytes 860164

commit v18 on v17

--- a/solution.py
+++ b/solution.py
@@ -66,7 +66,7 @@
         p_ref[x * hc + hc - 1] = right_ref[x * B:(x + 1) * B]
 
     def one_patch(i, carry):
-        acc_ref[...] = jnp.zeros(acc_ref.shape, jnp.float32)
+        acc_ref[:TRASH] = jnp.zeros((TRASH, B, B), jnp.float32)
         x = i // AG
         y = i % AG
         count = count_ref[x, y]
@@ -87,7 +87,7 @@
 
     lax.fori_loop(0, patches, one_patch, 0)
 
-    dpt_ref[...] = jnp.zeros(dpt_ref.shape, jnp.float32)
+    dpt_ref[:HOME * HOME * B] = jnp.zeros((HOME * HOME * B, dpt_ref.shape[1]), jnp.float32)
     for i in range(patches):
         flipped = own_ref[i].T
         for p in range(KP):

time: 68.5 us -> 68.5 us (level)
  no operation moved by 1% of the time
where the time goes in v18:
time: 68.5 us; the launch traced here: 67.8 us
  Pallas kernels  23.9 us (35%)
  waiting for transfers between devices  23.2 us (34%)
  starting transfers between devices  12.7 us (19%)
  local copies, waits for them, and re-layouts  3.97 us (6%)
  other arithmetic  3.76 us (5%)
    pallas_call x1, Pallas kernels, per_device(): pl.pallas_call(galerkin_kernel, out_shape=(jax.ShapeDtypeStruct((HOME, B,...  15.4 us
    ppermute x2, waiting for transfers between devices, swap_rounds(): lax.ppermute(second, axis, pairs_b)  13.5 us
    ppermute x2, waiting for transfers between devices, exchange(): got_second = lax.ppermute(jnp.where(even, to_prev, to_next), axis, second)  6.29 us
    ppermute x2, starting transfers between devices, exchange(): got_second = lax.ppermute(jnp.where(even, to_prev, to_next), axis, second)  5.32 us
    ppermute x2, starting transfers between devices, swap_rounds(): lax.ppermute(second, axis, pairs_b)  4.48 us
    pallas_call x1, Pallas kernels, per_device(): pl.pallas_call(fold_cols_send_kernel, out_shape=(jax.ShapeDtypeStruct((B,...  3.25 us
    pallas_call x1, Pallas kernels, per_device(): pl.pallas_call(fold_cols_keep_kernel, out_shape=jax.ShapeDtypeStruct((B,...  3.1 us
    ppermute x2, waiting for transfers between devices, exchange(): got_first = lax.ppermute(jnp.where(even, to_next, to_prev), axis, first)  2.89 us
  transfers between devices with their start and end apart: 8, of which 7 were waited for; matrix products, arithmetic and copies ran while one was open for 3% of the time, Pallas kernels for 5%

profile of v18, /device:TPU:20, one launch (start us, length us, event | category | flops | bytes accessed | tf_op | source)
XLA Modules:
  0.0 67.8 jit_solution(18154004405769763168)
XLA Ops:
  0.0 0.0 copy-start
  0.0 1.4 %fusion.27 = (bf16[4,4,4]{2,1,0:T(4,128)(2,1)S(1)}, s32[4,4,4]{2,1,0:T(4,128)S(1)}, s32[4,4,4]{2,1,0:T(4,128)}) fusion(s32[]{:T(128)S(6)} %axis_index.14, s32[]{:T(128)S(6)} %axis_index.33, s32[4,4,4]{2,1,0:T(4,128)} %param.10, s32[4,4]{1,0:T(4,128)} %param.11), kind=kLoop, calls=%fused_computation.73 | loop fusion | flops 2112 | bytes 968 | tf_op jit(solution)/shard_map/convert.7
  1.4 0.1 convert_element_type.106
  1.5 0.1 convert_element_type.107
  1.6 1.0 %fusion.28 = (bf16[1,4,64,256]{3,2,1,0:T(8,128)(2,1)S(1)}, bf16[1,4,64,256]{3,2,1,0:T(8,128)(2,1)S(1)}) fusion(bf16[4,4,64,256]{3,2,1,0:T(8,128)(2,1)} %param.9), kind=kLoop, calls=%fused_computation.74 | loop fusion | bytes 524288 | tf_op jit(solution)/shard_map/slice | solution.py:193
  2.6 0.1 broadcast_select_fusion.7
  2.7 3.3 %collective-permute-start = (bf16[272,256]{1,0:T(8,128)(2,1)S(1)}, bf16[272,256]{1,0:T(8,128)(2,1)S(1)}, u32[]{:S(2)}, u32[]{:S(2)}) collective-permute-start(bf16[272,256]{1,0:T(8,128)(2,1)S(1)} %get-tuple-element.29), channel_id=1, source_target_pairs={{4,8},{12,16},{20,24},{8,4},{16,12},{24,20},{5,9},{13,17},{21,25},... | collective-permute-start | bytes 417800 | tf_op jit(solution)/shard_map/ppermute | solution.py:39
  5.9 1.7 %collective-permute-start.1 = (bf16[272,256]{1,0:T(8,128)(2,1)S(1)}, bf16[272,256]{1,0:T(8,128)(2,1)S(1)}, u32[]{:S(2)}, u32[]{:S(2)}) collective-permute-start(bf16[272,256]{1,0:T(8,128)(2,1)S(1)} %get-tuple-element.30), channel_id=1, source_target_pairs={{0,4},{4,0},{8,12},{12,8},{16,20},{20,16},{24,28},{28,24},{1,5},{5... | collective-permute-start | bytes 417800 | tf_op jit(solution)/shard_map/ppermute | solution.py:38
  7.7 1.3 %add_clamp_fusion.pos_ref = s32[4,4,9]{2,1,0:T(4,128)} fusion(s32[4,4,9]{2,1,0:T(4,128)} %param.7, s32[]{:T(128)S(6)} %mul.33, s32[]{:T(128)S(6)} %mul.30), kind=kLoop, calls=%fused_computation.49 | loop fusion | flops 3744 | bytes 1160 | tf_op jit(solution)/shard_map/jit(clip)/min | solution.py:213
  9.0 0.6 pad_add_fusion.par_ref
  9.5 1.4 %collective-permute-done = bf16[272,256]{1,0:T(8,128)(2,1)S(1)} collective-permute-done((bf16[272,256]{1,0:T(8,128)(2,1)S(1)}, bf16[272,256]{1,0:T(8,128)(2,1)S(1)}, u32[]{:S(2)}, u32[]{:S(2)}) %collective-permute-start) | collective-permute-done | bytes 139296 | tf_op jit(solution)/shard_map/ppermute | solution.py:39
  11.0 2.9 %collective-permute-done.1 = bf16[272,256]{1,0:T(8,128)(2,1)S(1)} collective-permute-done((bf16[272,256]{1,0:T(8,128)(2,1)S(1)}, bf16[272,256]{1,0:T(8,128)(2,1)S(1)}, u32[]{:S(2)}, u32[]{:S(2)}) %collective-permute-start.1) | collective-permute-done | bytes 139296 | tf_op jit(solution)/shard_map/ppermute | solution.py:38
  13.9 0.0 copy-start.3
  13.9 0.0 copy-start.4
  14.0 0.1 reshape.196
  14.0 0.1 reshape.197
  14.2 0.1 convert_element_type.112
  14.3 0.1 convert_element_type.113
  14.3 0.0 copy-done
  14.4 0.1 pad_maximum_fusion.2
  14.4 0.1 broadcast_select_fusion.3
  14.5 2.0 %collective-permute-start.2 = (bf16[400,256]{1,0:T(8,128)(2,1)S(1)}, bf16[400,256]{1,0:T(8,128)(2,1)S(1)}, u32[]{:S(2)}, u32[]{:S(2)}) collective-permute-start(bf16[400,256]{1,0:T(8,128)(2,1)S(1)} %get-tuple-element.25), channel_id=1, source_target_pairs={{1,2},{2,1},{5,6},{6,5},{9,10},{10,9},{13,14},{14,13},{17,18},{18,... | collective-permute-start | bytes 614408 | tf_op jit(solution)/shard_map/ppermute | solution.py:39
  16.5 0.1 collective-permute-start.3
  16.6 0.1 add_add_fusion.1
  16.7 4.9 %collective-permute-done.2 = bf16[400,256]{1,0:T(8,128)(2,1)S(1)} collective-permute-done((bf16[400,256]{1,0:T(8,128)(2,1)S(1)}, bf16[400,256]{1,0:T(8,128)(2,1)S(1)}, u32[]{:S(2)}, u32[]{:S(2)}) %collective-permute-start.2) | collective-permute-done | bytes 204832 | tf_op jit(solution)/shard_map/ppermute | solution.py:39
  21.6 0.0 collective-permute-done.3
  21.6 0.0 copy-done.3
  21.6 0.0 copy-done.4
  21.6 0.0 copy-start.5
  21.6 0.0 copy-start.6
  21.7 0.1 reshape.200
  21.8 0.1 reshape.201
  21.9 0.1 fusion.8
  21.9 0.7 min.34.nslot_ref
  22.6 0.0 copy-done.5
  22.6 0.0 copy-done.6
  22.6 15.4 %shard_map.64 = (f32[3,64,1600]{2,1,0:T(8,128)}, bf16[3,64,1600]{2,1,0:T(8,128)(2,1)}, bf16[3,64,1600]{2,1,0:T(8,128)(2,1)}) custom-call(s32[2]{0:T(128)} %pad_add_fusion.par_ref, s32[4,4,9]{2,1,0:T(4,128)} %add_clamp_fusion.pos_ref, s32[144]{0:T(256)} %min.34.nslot_ref, s32[4,4]{1,0:T(4,128)} %count_ref.1, s32[4,4,4]{2,1,0:T(4,128)} %get-tuple-element.31.home_ref, ...), custom_call_target="tpu_custom_call" | custom-call | tf_op jit(solution)/shard_map/pallas_call | solution.py:220
  38.0 0.0 collective-permute-start.4
  38.0 1.9 %collective-permute-start.5 = (bf16[3,64,1600]{2,1,0:T(8,128)(2,1)}, bf16[3,64,1600]{2,1,0:T(8,128)(2,1)S(1)}, u32[]{:S(2)}, u32[]{:S(2)}) collective-permute-start(bf16[3,64,1600]{2,1,0:T(8,128)(2,1)} %get-tuple-element.12), channel_id=1, source_target_pairs={{1,2},{2,1},{5,6},{6,5},{9,10},{10,9},{13,14},{14,13},{17,18},{18,... | collective-permute-start | bytes 1843208 | tf_op jit(solution)/shard_map/ppermute | solution.py:49
  40.0 0.3 collective-permute-done.4.a_ref
  40.3 0.0 copy-start.1
  40.3 9.6 %collective-permute-done.5.b_ref = bf16[3,64,1600]{2,1,0:T(8,128)(2,1)S(1)} collective-permute-done((bf16[3,64,1600]{2,1,0:T(8,128)(2,1)}, bf16[3,64,1600]{2,1,0:T(8,128)(2,1)S(1)}, u32[]{:S(2)}, u32[]{:S(2)}) %collective-permute-start.5) | collective-permute-done | bytes 614432 | tf_op jit(solution)/shard_map/ppermute | solution.py:49
  50.0 0.0 copy-start.2
  50.0 0.0 copy-done.1
  50.0 0.8 %copy-done.2 = bf16[3,64,1600]{2,1,0:T(8,128)(2,1)} copy-done((bf16[3,64,1600]{2,1,0:T(8,128)(2,1)}, bf16[3,64,1600]{2,1,0:T(8,128)(2,1)S(1)}, u32[]{:S(2)}) %copy-start.2) | copy-done | bytes 614424
  50.8 3.3 %shard_map.66 = (bf16[64,2240]{1,0:T(8,128)(2,1)}, bf16[64,2240]{1,0:T(8,128)(2,1)}) custom-call(s32[2]{0:T(128)} %pad_add_fusion.par_ref, f32[3,64,1600]{2,1,0:T(8,128)} %get-tuple-element.10.keep_ref, bf16[3,64,1600]{2,1,0:T(8,128)(2,1)} %copy-done.1, bf16[3,64,1600]{2,1,0:T(8,128)(2,1)} %copy-done.2), custom_call_target="tpu_custom_call" | custom-call | tf_op jit(solution)/shard_map/pallas_call | solution.py:250
  54.0 1.1 %collective-permute-start.6 = (bf16[64,2240]{1,0:T(8,128)(2,1)}, bf16[64,2240]{1,0:T(8,128)(2,1)S(1)}, u32[]{:S(2)}, u32[]{:S(2)}) collective-permute-start(bf16[64,2240]{1,0:T(8,128)(2,1)} %get-tuple-element.13), channel_id=1, source_target_pairs={{0,4},{4,0},{8,12},{12,8},{16,20},{20,16},{24,28},{28,24},{1,5},{5... | collective-permute-start | bytes 860168 | tf_op jit(solution)/shard_map/ppermute | solution.py:49
  55.1 2.6 %collective-permute-start.7 = (bf16[64,2240]{1,0:T(8,128)(2,1)}, bf16[64,2240]{1,0:T(8,128)(2,1)S(1)}, u32[]{:S(2)}, u32[]{:S(2)}) collective-permute-start(bf16[64,2240]{1,0:T(8,128)(2,1)} %get-tuple-element.14), channel_id=1, source_target_pairs={{4,8},{12,16},{20,24},{8,4},{16,12},{24,20},{5,9},{13,17},{21,25},... | collective-permute-start | bytes 860168 | tf_op jit(solution)/shard_map/ppermute | solution.py:49
  57.7 3.1 %shard_map.65.keep_ref = f32[64,3136]{1,0:T(8,128)} custom-call(s32[2]{0:T(128)} %pad_add_fusion.par_ref, f32[3,64,1600]{2,1,0:T(8,128)} %get-tuple-element.10.keep_ref, bf16[3,64,1600]{2,1,0:T(8,128)(2,1)} %copy-done.1, bf16[3,64,1600]{2,1,0:T(8,128)(2,1)} %copy-done.2), custom_call_target="tpu_custom_call" | custom-call | tf_op jit(solution)/shard_map/pallas_call | solution.py:259
  60.8 0.2 collective-permute-done.6.a_ref
  61.0 0.0 copy-start.7
  61.0 3.9 %collective-permute-done.7.b_ref = bf16[64,2240]{1,0:T(8,128)(2,1)S(1)} collective-permute-done((bf16[64,2240]{1,0:T(8,128)(2,1)}, bf16[64,2240]{1,0:T(8,128)(2,1)S(1)}, u32[]{:S(2)}, u32[]{:S(2)}) %collective-permute-start.7) | collective-permute-done | bytes 286752 | tf_op jit(solution)/shard_map/ppermute | solution.py:49
  64.9 0.0 copy-done.7
  64.9 0.0 copy-start.8
  64.9 0.7 %copy-done.8 = bf16[64,2240]{1,0:T(8,128)(2,1)} copy-done((bf16[64,2240]{1,0:T(8,128)(2,1)}, bf16[64,2240]{1,0:T(8,128)(2,1)S(1)}, u32[]{:S(2)}) %copy-start.8) | copy-done | bytes 286744
  65.6 2.2 %shard_map.67 = bf16[64,3136]{1,0:T(8,128)(2,1)} custom-call(s32[2]{0:T(128)} %pad_add_fusion.par_ref, f32[64,3136]{1,0:T(8,128)} %shard_map.65.keep_ref, bf16[64,2240]{1,0:T(8,128)(2,1)} %copy-done.7, bf16[64,2240]{1,0:T(8,128)(2,1)} %copy-done.8), custom_call_target="tpu_custom_call" | custom-call | tf_op jit(solution)/shard_map/pallas_call | solution.py:266
  (11 shorter events, 0.2 us)
Async XLA Ops:
  0.0 14.3 %copy-start = (bf16[4,4,64,256]{3,2,1,0:T(8,128)(2,1)S(1)}, bf16[4,4,64,256]{3,2,1,0:T(8,128)(2,1)}, u32[]{:S(2)}) copy-start(bf16[4,4,64,256]{3,2,1,0:T(8,128)(2,1)} %param.9) | copy-start | bytes 1572868
  2.7 8.3 %collective-permute-start = (bf16[272,256]{1,0:T(8,128)(2,1)S(1)}, bf16[272,256]{1,0:T(8,128)(2,1)S(1)}, u32[]{:S(2)}, u32[]{:S(2)}) collective-permute-start(bf16[272,256]{1,0:T(8,128)(2,1)S(1)} %get-tuple-element.29), channel_id=1, source_target_pairs={{4,8},{12,16},{20,24},{8,4},{16,12},{24,20},{5,9},{13,17},{21,25},... | collective-permute-start | bytes 417800 | tf_op jit(solution)/shard_map/ppermute | solution.py:39
  5.9 7.9 %collective-permute-start.1 = (bf16[272,256]{1,0:T(8,128)(2,1)S(1)}, bf16[272,256]{1,0:T(8,128)(2,1)S(1)}, u32[]{:S(2)}, u32[]{:S(2)}) collective-permute-start(bf16[272,256]{1,0:T(8,128)(2,1)S(1)} %get-tuple-element.30), channel_id=1, source_target_pairs={{0,4},{4,0},{8,12},{12,8},{16,20},{20,16},{24,28},{28,24},{1,5},{5... | collective-permute-start | bytes 417800 | tf_op jit(solution)/shard_map/ppermute | solution.py:38
  13.9 7.7 %copy-start.3 = (bf16[272,256]{1,0:T(8,128)(2,1)}, bf16[272,256]{1,0:T(8,128)(2,1)S(1)}, u32[]{:S(2)}) copy-start(bf16[272,256]{1,0:T(8,128)(2,1)S(1)} %get-tuple-element.27.above_ref) | copy-start | bytes 417796
  13.9 7.7 %copy-start.4 = (bf16[272,256]{1,0:T(8,128)(2,1)}, bf16[272,256]{1,0:T(8,128)(2,1)S(1)}, u32[]{:S(2)}) copy-start(bf16[272,256]{1,0:T(8,128)(2,1)S(1)} %get-tuple-element.28.below_ref) | copy-start | bytes 417796
  14.5 7.1 %collective-permute-start.2 = (bf16[400,256]{1,0:T(8,128)(2,1)S(1)}, bf16[400,256]{1,0:T(8,128)(2,1)S(1)}, u32[]{:S(2)}, u32[]{:S(2)}) collective-permute-start(bf16[400,256]{1,0:T(8,128)(2,1)S(1)} %get-tuple-element.25), channel_id=1, source_target_pairs={{1,2},{2,1},{5,6},{6,5},{9,10},{10,9},{13,14},{14,13},{17,18},{18,... | collective-permute-start | bytes 614408 | tf_op jit(solution)/shard_map/ppermute | solution.py:39
  16.5 5.0 %collective-permute-start.3 = (bf16[400,256]{1,0:T(8,128)(2,1)S(1)}, bf16[400,256]{1,0:T(8,128)(2,1)S(1)}, u32[]{:S(2)}, u32[]{:S(2)}) collective-permute-start(bf16[400,256]{1,0:T(8,128)(2,1)S(1)} %get-tuple-element.26), channel_id=1, source_target_pairs={{0,1},{1,0},{2,3},{3,2},{4,5},{5,4},{6,7},{7,6},{8,9},{9,8},{10,11... | collective-permute-start | bytes 614408 | tf_op jit(solution)/shard_map/ppermute | solution.py:38
  21.6 1.0 %copy-start.5 = (bf16[400,256]{1,0:T(8,128)(2,1)}, bf16[400,256]{1,0:T(8,128)(2,1)S(1)}, u32[]{:S(2)}) copy-start(bf16[400,256]{1,0:T(8,128)(2,1)S(1)} %get-tuple-element.23.left_ref) | copy-start | bytes 614404
  21.6 1.0 %copy-start.6 = (bf16[400,256]{1,0:T(8,128)(2,1)}, bf16[400,256]{1,0:T(8,128)(2,1)S(1)}, u32[]{:S(2)}) copy-start(bf16[400,256]{1,0:T(8,128)(2,1)S(1)} %get-tuple-element.24.right_ref) | copy-start | bytes 614404
  38.0 2.3 %collective-permute-start.4 = (bf16[3,64,1600]{2,1,0:T(8,128)(2,1)}, bf16[3,64,1600]{2,1,0:T(8,128)(2,1)S(1)}, u32[]{:S(2)}, u32[]{:S(2)}) collective-permute-start(bf16[3,64,1600]{2,1,0:T(8,128)(2,1)} %get-tuple-element.11), channel_id=1, source_target_pairs={{0,1},{1,0},{2,3},{3,2},{4,5},{5,4},{6,7},{7,6},{8,9},{9,8},{10,11... | collective-permute-start | bytes 1843208 | tf_op jit(solution)/shard_map/ppermute | solution.py:49
  38.0 11.9 %collective-permute-start.5 = (bf16[3,64,1600]{2,1,0:T(8,128)(2,1)}, bf16[3,64,1600]{2,1,0:T(8,128)(2,1)S(1)}, u32[]{:S(2)}, u32[]{:S(2)}) collective-permute-start(bf16[3,64,1600]{2,1,0:T(8,128)(2,1)} %get-tuple-element.12), channel_id=1, source_target_pairs={{1,2},{2,1},{5,6},{6,5},{9,10},{10,9},{13,14},{14,13},{17,18},{18,... | collective-permute-start | bytes 1843208 | tf_op jit(solution)/shard_map/ppermute | solution.py:49
  40.3 9.6 %copy-start.1 = (bf16[3,64,1600]{2,1,0:T(8,128)(2,1)}, bf16[3,64,1600]{2,1,0:T(8,128)(2,1)S(1)}, u32[]{:S(2)}) copy-start(bf16[3,64,1600]{2,1,0:T(8,128)(2,1)S(1)} %collective-permute-done.4.a_ref) | copy-start | bytes 1843204
  50.0 0.8 %copy-start.2 = (bf16[3,64,1600]{2,1,0:T(8,128)(2,1)}, bf16[3,64,1600]{2,1,0:T(8,128)(2,1)S(1)}, u32[]{:S(2)}) copy-start(bf16[3,64,1600]{2,1,0:T(8,128)(2,1)S(1)} %collective-permute-done.5.b_ref) | copy-start | bytes 1843204
  54.0 6.9 %collective-permute-start.6 = (bf16[64,2240]{1,0:T(8,128)(2,1)}, bf16[64,2240]{1,0:T(8,128)(2,1)S(1)}, u32[]{:S(2)}, u32[]{:S(2)}) collective-permute-start(bf16[64,2240]{1,0:T(8,128)(2,1)} %get-tuple-element.13), channel_id=1, source_target_pairs={{0,4},{4,0},{8,12},{12,8},{16,20},{20,16},{24,28},{28,24},{1,5},{5... | collective-permute-start | bytes 860168 | tf_op jit(solution)/shard_map/ppermute | solution.py:49
  55.1 9.7 %collective-permute-start.7 = (bf16[64,2240]{1,0:T(8,128)(2,1)}, bf16[64,2240]{1,0:T(8,128)(2,1)S(1)}, u32[]{:S(2)}, u32[]{:S(2)}) collective-permute-start(bf16[64,2240]{1,0:T(8,128)(2,1)} %get-tuple-element.14), channel_id=1, source_target_pairs={{4,8},{12,16},{20,24},{8,4},{16,12},{24,20},{5,9},{13,17},{21,25},... | collective-permute-start | bytes 860168 | tf_op jit(solution)/shard_map/ppermute | solution.py:49
  61.0 3.9 %copy-start.7 = (bf16[64,2240]{1,0:T(8,128)(2,1)}, bf16[64,2240]{1,0:T(8,128)(2,1)S(1)}, u32[]{:S(2)}) copy-start(bf16[64,2240]{1,0:T(8,128)(2,1)S(1)} %collective-permute-done.6.a_ref) | copy-start | bytes 860164
  64.9 0.7 %copy-start.8 = (bf16[64,2240]{1,0:T(8,128)(2,1)}, bf16[64,2240]{1,0:T(8,128)(2,1)S(1)}, u32[]{:S(2)}) copy-start(bf16[64,2240]{1,0:T(8,128)(2,1)S(1)} %collective-permute-done.7.b_ref) | copy-start | bytes 860164
